TPU v7x, 256 devices: a whole 4x4x8 slice. The times are simulated.
256 devices in a mesh: dm: 32 (over x_lo, z, core), beam: 8 (over y, x_hi).
Axes of the slice: x: 4 (x_hi: 2, x_lo: 2; x = x_hi * 2 + x_lo), y: 4, z: 8, core: 2. Of those that a mesh axis runs over, the one named last changes fastest.
Arguments:
- voltages: bfloat16 [4096, 8, 2, 256], P(('beam', 'dm')), may hold values from -6 to 6
- responses: bfloat16 [128, 4096, 2, 256], P('dm', 'beam'), may hold values from -6 to 6
- chirp_len: int32 [128], P('dm'), may hold values from 1 to 128, as said below
Outputs:
- detected: bfloat16 [128, 8, 262144], P('dm', 'beam')
Inputs may be any that keep to these rules, and one draw needn't show every extreme that they name: `chirp_len`: some trial has the longest chirp 256 // 2 and some trial a chirp of 1 sample.
All inputs are finite; a program needn't handle non-finite values.
Results may differ from a plain program's by a relative error of at most 0.0054.
Values may be sent and summed in bfloat16 or wider, within the bound.
No kernel may reach another device: no remote copies, remote signals or barrier semaphores. Data moves between devices by JAX's collectives and lax.ppermute only.
A program may use at most 128 MiB of HBM per device.

v0:
```python
import math

import jax
import jax.numpy as jnp
from jax import lax
from jax.sharding import PartitionSpec as P

RATE = 4


def dft_tables(length):
    sample = jnp.arange(length, dtype=jnp.int32)
    phases = sample[:, None] * sample[None, :] % length
    angles = phases.astype(jnp.float32) * (2.0 * math.pi / length)
    cosine = jnp.cos(angles) / math.sqrt(length)
    sine_part = jnp.sin(angles) / math.sqrt(length)
    forward = jnp.concatenate(
        [jnp.concatenate([cosine, -sine_part], 1), jnp.concatenate([sine_part, cosine], 1)], 0
    )
    backward = jnp.concatenate(
        [jnp.concatenate([cosine, sine_part], 1), jnp.concatenate([-sine_part, cosine], 1)], 0
    )
    return (forward.astype(jnp.bfloat16), backward.astype(jnp.bfloat16))


def spectrum(signal, forward):
    length = signal.shape[-1]
    flattened = signal.reshape(-1, 2 * length)
    result = jnp.dot(flattened, forward, preferred_element_type=jnp.float32)
    return result.astype(jnp.bfloat16).reshape(signal.shape)


def detect(spectra, response, lengths, backward, rate):
    chans = spectra.shape[0]
    beam_count = spectra.shape[1]
    length = spectra.shape[-1]
    samples_out = length // rate
    spec_re = spectra[:, :, 0, :].astype(jnp.float32)
    spec_im = spectra[:, :, 1, :].astype(jnp.float32)
    sample = jnp.arange(length, dtype=jnp.int32)

    def one_trial(trial):
        filter_row, chirp = trial
        resp_re = filter_row[:, 0, :].astype(jnp.float32)[:, None, :]
        resp_im = filter_row[:, 1, :].astype(jnp.float32)[:, None, :]
        real_part = resp_re * spec_re - resp_im * spec_im
        imag_part = resp_re * spec_im + resp_im * spec_re
        joined = jnp.concatenate([real_part, imag_part], -1).astype(jnp.bfloat16)
        series = jnp.dot(
            joined.reshape(-1, 2 * length), backward, preferred_element_type=jnp.float32
        )
        series = series.reshape(chans, beam_count, 2 * length)
        powers = series[..., :length] ** 2 + series[..., length:] ** 2
        valid_mask = sample >= chirp
        powers = jnp.where(valid_mask[None, None, :], powers, jnp.float32(0.0))
        binned = powers.reshape(chans, beam_count, samples_out, rate).sum(-1) / rate
        return jnp.transpose(binned, (1, 0, 2)).astype(jnp.bfloat16)

    return lax.map(one_trial, (response, lengths))


def shards(voltages, responses, chirp_len):
    length = voltages.shape[-1]
    forward, backward = dft_tables(length)
    trial_count = responses.shape[0]
    prepared = spectrum(lax.all_gather(voltages, "dm", axis=0, tiled=True), forward)
    detected = detect(prepared, responses, chirp_len, backward, RATE)
    flattened = detected.reshape(trial_count, detected.shape[1], -1)
    return lax.all_to_all(flattened, "beam", split_axis=1, concat_axis=2, tiled=True)


def solution(mesh):
    placed = (P(("beam", "dm"), None, None, None), P("dm", "beam", None, None), P("dm"))
    return jax.shard_map(
        shards, mesh=mesh, in_specs=placed, out_specs=P("dm", "beam", None), check_vma=False
    )
```

profile of v0, /device:TPU:1, one launch (start us, length us, event | category | flops | bytes accessed | tf_op | source)
XLA Modules:
  0.0 263.4 jit_solution(4098460005403602583)
XLA Ops:
  11.1 68.8 %all-gather.2.cloned.1.call-done = bf16[512,8,2,256]{3,1,2,0:T(8,128)(2,1)} async-done(((bf16[16,8,2,256]{3,1,2,0:T(8,128)(2,1)}), bf16[512,8,2,256]{3,1,2,0:T(8,128)(2,1)}) %all-gather.2.cloned.1.call-update) | async-done | bytes 4194320 | tf_op jit(solution)/shard_map/all_gather | solution.py:66
  79.9 6.5 %fusion.14 = bf16[4096,512]{0,1:T(8,128)(2,1)} fusion(bf16[4096,512]{1,0:T(8,128)(2,1)} %bitcast.54, bf16[256,256]{0,1:T(8,128)(2,1)S(1)} %get-tuple-element.106, bf16[256,256]{0,1:T(8,128)(2,1)S(1)} %fusion.26, bf16[256,256]{0,1:T(8,128)(2,1)S(1)} %get-tuple-element.105), kind=kOutput, calls=%fused_computation.24 | convolution fusion | flops 2151677952 | bytes 8781824 | tf_op jit(solution)/shard_map/dot_general | solution.py:29
  86.4 6.5 %copy.12 = bf16[4096,512]{1,0:T(8,128)(2,1)} copy(bf16[4096,512]{0,1:T(8,128)(2,1)} %fusion.14) | data formatting | bytes 8388608 | tf_op jit(solution)/shard_map/convert_element_type | solution.py:30
  92.9 7.0 %reshape.32 = bf16[512,8,2,256]{3,2,1,0:T(2,128)(2,1)} reshape(bf16[4096,512]{1,0:T(8,128)(2,1)} %copy.12) | data formatting | bytes 8388608 | tf_op jit(solution)/shard_map/reshape | solution.py:30
  99.9 8.8 %slice_convert_fusion = (f32[512,8,1,256]{3,2,1,0:T(1,128)S(1)}, f32[512,8,1,256]{3,2,1,0:T(1,128)S(1)}) fusion(bf16[512,8,2,256]{3,2,1,0:T(2,128)(2,1)} %reshape.32), kind=kLoop, calls=%fused_computation.25 | loop fusion | flops 2097152 | bytes 12582912 | tf_op jit(solution)/shard_map/convert_element_type | solution.py:39
  115.2 96.9 %while.11 = (s32[]{:T(128)}, bf16[4,8,512,64]{2,3,1,0:T(8,128)(2,1)S(1)}, s32[4]{0:T(128)S(1)}, bf16[4,512,2,256]{3,2,1,0:T(2,128)(2,1)}, f32[512,8,256]{2,0,1:T...) while((s32[]{:T(128)}, ...), condition=%wide.region_2.3_spmd.clone, body=%wide.region_0.2_spmd.clone.sunk | while | flops 2170028288 | bytes 58196600 | solution.py:59
  116.7 4.8 %subtract_convert_fusion.2 = (bf16[512,8,256]{2,0,1:T(8,128)(2,1)S(1)}, bf16[512,8,256]{2,0,1:T(8,128)(2,1)S(1)}) fusion(f32[512,8,256]{2,0,1:T(8,128)} %get-tuple-element.181, f32[512,8,256]{2,0,1:T(8,128)} %get-tuple-element.180, f32[512,256]{1,0:T(8,128)S(1)} %get-tuple-element.154, f32[512,256]{1,0:T(8,128)S(1)} %get-tuple-element.155), kind=kLoop, calls=%fused_computation.10.clone.1 | loop fusion | flops 8388608 | bytes 13631488 | tf_op jit(solution)/shard_map/convert.2
  121.5 3.4 %fusion.38 = f32[512,8,512]{0,2,1:T(8,128)S(1)} fusion(bf16[512,8,256]{2,0,1:T(8,128)(2,1)S(1)} %get-tuple-element.156, bf16[512,8,256]{2,0,1:T(8,128)(2,1)S(1)} %get-tuple-element.157, bf16[512,512]{0,1:T(8,128)(2,1)} %get-tuple-element.182), kind=kOutput, calls=%fused_computation.5.clone.1 | convolution fusion | flops 2155872256 | bytes 13107200 | tf_op jit(solution)/shard_map/while/body/eval_jaxpr/dot_general | solution.py:49
  129.3 5.2 %reshape.44 = f32[512,8,64,4]{0,3,2,1:T(4,128)} reshape(f32[512,8,256]{0,2,1:T(8,128)} %fusion.39) | data formatting | bytes 8388608 | tf_op jit(solution)/shard_map/while/body/eval_jaxpr/reshape | solution.py:56
  134.5 4.8 %reduce_sum.11 = f32[512,8,64]{0,2,1:T(8,128)S(1)} reduce(f32[512,8,64,4]{0,3,2,1:T(4,128)} %reshape.44, f32[]{:T(128)} %constant.29.clone.3..sunk), dimensions={3}, to_apply=%region_1.1 | reduce | flops 786432 | bytes 5242884 | tf_op jit(solution)/shard_map/while/body/eval_jaxpr/reduce_sum | solution.py:56
  141.0 4.8 %subtract_convert_fusion.2 = (bf16[512,8,256]{2,0,1:T(8,128)(2,1)S(1)}, bf16[512,8,256]{2,0,1:T(8,128)(2,1)S(1)}) fusion(f32[512,8,256]{2,0,1:T(8,128)} %get-tuple-element.181, f32[512,8,256]{2,0,1:T(8,128)} %get-tuple-element.180, f32[512,256]{1,0:T(8,128)S(1)} %get-tuple-element.154, f32[512,256]{1,0:T(8,128)S(1)} %get-tuple-element.155), kind=kLoop, calls=%fused_computation.10.clone.1 | loop fusion | flops 8388608 | bytes 13631488 | tf_op jit(solution)/shard_map/convert.2
  145.8 3.4 %fusion.38 = f32[512,8,512]{0,2,1:T(8,128)S(1)} fusion(bf16[512,8,256]{2,0,1:T(8,128)(2,1)S(1)} %get-tuple-element.156, bf16[512,8,256]{2,0,1:T(8,128)(2,1)S(1)} %get-tuple-element.157, bf16[512,512]{0,1:T(8,128)(2,1)} %get-tuple-element.182), kind=kOutput, calls=%fused_computation.5.clone.1 | convolution fusion | flops 2155872256 | bytes 13107200 | tf_op jit(solution)/shard_map/while/body/eval_jaxpr/dot_general | solution.py:49
  153.5 5.2 %reshape.44 = f32[512,8,64,4]{0,3,2,1:T(4,128)} reshape(f32[512,8,256]{0,2,1:T(8,128)} %fusion.39) | data formatting | bytes 8388608 | tf_op jit(solution)/shard_map/while/body/eval_jaxpr/reshape | solution.py:56
  158.7 4.8 %reduce_sum.11 = f32[512,8,64]{0,2,1:T(8,128)S(1)} reduce(f32[512,8,64,4]{0,3,2,1:T(4,128)} %reshape.44, f32[]{:T(128)} %constant.29.clone.3..sunk), dimensions={3}, to_apply=%region_1.1 | reduce | flops 786432 | bytes 5242884 | tf_op jit(solution)/shard_map/while/body/eval_jaxpr/reduce_sum | solution.py:56
  165.2 4.8 %subtract_convert_fusion.2 = (bf16[512,8,256]{2,0,1:T(8,128)(2,1)S(1)}, bf16[512,8,256]{2,0,1:T(8,128)(2,1)S(1)}) fusion(f32[512,8,256]{2,0,1:T(8,128)} %get-tuple-element.181, f32[512,8,256]{2,0,1:T(8,128)} %get-tuple-element.180, f32[512,256]{1,0:T(8,128)S(1)} %get-tuple-element.154, f32[512,256]{1,0:T(8,128)S(1)} %get-tuple-element.155), kind=kLoop, calls=%fused_computation.10.clone.1 | loop fusion | flops 8388608 | bytes 13631488 | tf_op jit(solution)/shard_map/convert.2
  170.0 3.4 %fusion.38 = f32[512,8,512]{0,2,1:T(8,128)S(1)} fusion(bf16[512,8,256]{2,0,1:T(8,128)(2,1)S(1)} %get-tuple-element.156, bf16[512,8,256]{2,0,1:T(8,128)(2,1)S(1)} %get-tuple-element.157, bf16[512,512]{0,1:T(8,128)(2,1)} %get-tuple-element.182), kind=kOutput, calls=%fused_computation.5.clone.1 | convolution fusion | flops 2155872256 | bytes 13107200 | tf_op jit(solution)/shard_map/while/body/eval_jaxpr/dot_general | solution.py:49
  177.8 5.2 %reshape.44 = f32[512,8,64,4]{0,3,2,1:T(4,128)} reshape(f32[512,8,256]{0,2,1:T(8,128)} %fusion.39) | data formatting | bytes 8388608 | tf_op jit(solution)/shard_map/while/body/eval_jaxpr/reshape | solution.py:56
  183.0 4.8 %reduce_sum.11 = f32[512,8,64]{0,2,1:T(8,128)S(1)} reduce(f32[512,8,64,4]{0,3,2,1:T(4,128)} %reshape.44, f32[]{:T(128)} %constant.29.clone.3..sunk), dimensions={3}, to_apply=%region_1.1 | reduce | flops 786432 | bytes 5242884 | tf_op jit(solution)/shard_map/while/body/eval_jaxpr/reduce_sum | solution.py:56
  189.5 4.8 %subtract_convert_fusion.2 = (bf16[512,8,256]{2,0,1:T(8,128)(2,1)S(1)}, bf16[512,8,256]{2,0,1:T(8,128)(2,1)S(1)}) fusion(f32[512,8,256]{2,0,1:T(8,128)} %get-tuple-element.181, f32[512,8,256]{2,0,1:T(8,128)} %get-tuple-element.180, f32[512,256]{1,0:T(8,128)S(1)} %get-tuple-element.154, f32[512,256]{1,0:T(8,128)S(1)} %get-tuple-element.155), kind=kLoop, calls=%fused_computation.10.clone.1 | loop fusion | flops 8388608 | bytes 13631488 | tf_op jit(solution)/shard_map/convert.2
  194.2 3.4 %fusion.38 = f32[512,8,512]{0,2,1:T(8,128)S(1)} fusion(bf16[512,8,256]{2,0,1:T(8,128)(2,1)S(1)} %get-tuple-element.156, bf16[512,8,256]{2,0,1:T(8,128)(2,1)S(1)} %get-tuple-element.157, bf16[512,512]{0,1:T(8,128)(2,1)} %get-tuple-element.182), kind=kOutput, calls=%fused_computation.5.clone.1 | convolution fusion | flops 2155872256 | bytes 13107200 | tf_op jit(solution)/shard_map/while/body/eval_jaxpr/dot_general | solution.py:49
  202.0 5.2 %reshape.44 = f32[512,8,64,4]{0,3,2,1:T(4,128)} reshape(f32[512,8,256]{0,2,1:T(8,128)} %fusion.39) | data formatting | bytes 8388608 | tf_op jit(solution)/shard_map/while/body/eval_jaxpr/reshape | solution.py:56
  207.2 4.8 %reduce_sum.11 = f32[512,8,64]{0,2,1:T(8,128)S(1)} reduce(f32[512,8,64,4]{0,3,2,1:T(4,128)} %reshape.44, f32[]{:T(128)} %constant.29.clone.3..sunk), dimensions={3}, to_apply=%region_1.1 | reduce | flops 786432 | bytes 5242884 | tf_op jit(solution)/shard_map/while/body/eval_jaxpr/reduce_sum | solution.py:56
  215.3 6.3 %reshape.42 = bf16[4,8,32768]{2,0,1:T(4,128)(2,1)S(1)} reshape(bf16[4,8,512,64]{3,2,0,1:T(8,128)(2,1)} %copy.20) | data formatting | bytes 4194304 | tf_op jit(solution)/shard_map/reshape | solution.py:68
  221.6 33.6 %all_to_all.12 = bf16[4,8,32768]{2,0,1:T(4,128)(2,1)S(1)} all-to-all(bf16[4,8,32768]{2,0,1:T(4,128)(2,1)S(1)} %reshape.42), channel_id=1, replica_groups=mesh['dm'=32,'beam'=8] {'beam'}, dimensions={1} | all-to-all | bytes 4194304 | tf_op jit(solution)/shard_map/all_to_all | solution.py:69
  (41 shorter events, 39.7 us)
Async XLA Ops:
  6.5 73.4 %all-gather.2.cloned.1.call-start = ((), (), s32[]{:S(2)}) async-start(), calls=%async_computation.1 | async-start | bytes 4325376 | tf_op jit(solution)/shard_map/all_gather | solution.py:66
  111.9 3.2 %copy-start = (s32[4]{0:T(128)S(1)}, s32[4]{0:T(128)}, u32[]{:S(2)}) copy-start(s32[4]{0:T(128)} %param.7) | copy-start | bytes 52
Sparse Core Ops, SparseCore 0:
  9.2 70.6 all-gather.1
where the time goes:
time: 265 us; the launch traced here: 263 us
  waiting for transfers between devices  68.8 us (26%)
  other arithmetic  65.7 us (25%)
  local copies, waits for them, and re-layouts  61.3 us (23%)
  blocking collectives  33.6 us (13%)
  matrix products  20.2 us (8%)
  between operations  13.4 us (5%)
    all_gather x1, waiting for transfers between devices, shards(): lax.all_gather(voltages, 'dm', axis=0, tiled=True)  68.8 us
    all_to_all x1, blocking collectives, shards(): lax.all_to_all(flattened, 'beam', split_axis=1, concat_axis=2, tiled=True)  33.6 us
    another operation x6, other arithmetic  21.1 us
    reshape x4, local copies, waits for them, and re-layouts, one_trial(): binned = powers.reshape(chans, beam_count, samples_out, rate).sum(-1) / rate  20.7 us
    reduce_sum x4, other arithmetic, one_trial(): binned = powers.reshape(chans, beam_count, samples_out, rate).sum(-1) / rate  19.1 us
    dot_general x4, matrix products, one_trial(): jnp.dot(joined.reshape(-1, 2 * length), backward, preferred_element_type=...  13.7 us
    select_n x4, other arithmetic, one_trial(): powers = jnp.where(valid_mask[None, None, :], powers, jnp.float32(0.0))  12.5 us
    reshape x2, local copies, waits for them, and re-layouts, shards(): flattened = detected.reshape(trial_count, detected.shape[1], -1)  9.45 us
  transfers between devices with their start and end apart: 1, of which 1 were waited for; matrix products, arithmetic and copies ran while one was open for 1% of the time, Pallas kernels for 0%

commit v1 on v0

v1 whole, which is shorter than its diff:
```python
import functools
import math

import jax
import jax.numpy as jnp
from jax import lax
from jax.experimental import pallas as pl
from jax.experimental.pallas import tpu as pltpu
from jax.sharding import PartitionSpec as P

RATE = 4
CHAN_BLOCK = 256


def dft_tables(length):
    sample = jnp.arange(length, dtype=jnp.int32)
    phases = sample[:, None] * sample[None, :] % length
    angles = phases.astype(jnp.float32) * (2.0 * math.pi / length)
    cosine = jnp.cos(angles) / math.sqrt(length)
    sine_part = jnp.sin(angles) / math.sqrt(length)
    forward = jnp.concatenate(
        [jnp.concatenate([cosine, -sine_part], 1), jnp.concatenate([sine_part, cosine], 1)], 0
    )
    backward = jnp.concatenate(
        [jnp.concatenate([cosine, sine_part], 1), jnp.concatenate([-sine_part, cosine], 1)], 0
    )
    return (forward.astype(jnp.bfloat16), backward.astype(jnp.bfloat16))


def sample_order(length, rate):
    pos = jnp.arange(length, dtype=jnp.int32)
    bins = length // rate
    return rate * (pos % bins) + pos // bins


def detect_kernel(chirp_ref, spec_ref, resp_ref, back_ref, out_ref, pair_ref):
    d = pl.program_id(1)
    beams, chans, width = spec_ref.shape
    length = width // 2
    bins = length // RATE
    x = spec_ref[...]
    xr = x[:, :, :length].astype(jnp.float32)
    xi = x[:, :, length:].astype(jnp.float32)
    h = resp_ref[0]
    hr = h[:, :length].astype(jnp.float32)[None]
    hi = h[:, length:].astype(jnp.float32)[None]
    fr = hr * xr - hi * xi
    fi = hr * xi + hi * xr
    joined = jnp.concatenate([fr, fi], -1).reshape(beams * chans, width).astype(jnp.bfloat16)
    series = jnp.dot(joined, back_ref[...], preferred_element_type=jnp.float32)
    powers = series[:, :length] ** 2 + series[:, length:] ** 2
    pos = lax.broadcasted_iota(jnp.int32, (1, length), 1)
    t = RATE * (pos % bins) + pos // bins
    powers = jnp.where(t >= chirp_ref[d], powers, jnp.float32(0.0))
    half = powers[:, : length // 2] + powers[:, length // 2 :]
    pair_ref[...] = half + pltpu.roll(half, bins, 1)
    rows = beams * chans // 2
    even = pair_ref[pl.ds(0, rows, stride=2), :]
    odd = pair_ref[pl.ds(1, rows, stride=2), :]
    lane = lax.broadcasted_iota(jnp.int32, (1, 2 * bins), 1)
    both = jnp.where(lane < bins, even, odd) / RATE
    out_ref[0] = both.reshape(beams, chans // 2, 2 * bins).astype(out_ref.dtype)


def detect(spectra, responses, chirp_len, backward):
    beams, chans, width = spectra.shape
    trials = responses.shape[0]
    length = width // 2
    bins = length // RATE
    block = min(CHAN_BLOCK, chans)
    grid = (chans // block, trials)
    flops = 2 * trials * beams * chans * width * width
    bytes_accessed = 2 * (spectra.size + responses.size + backward.size + trials * beams * chans * bins)
    return pl.pallas_call(
        detect_kernel,
        out_shape=jax.ShapeDtypeStruct((trials, beams, chans // 2, 2 * bins), jnp.bfloat16),
        grid_spec=pltpu.PrefetchScalarGridSpec(
            num_scalar_prefetch=1,
            grid=grid,
            in_specs=[
                pl.BlockSpec((beams, block, width), lambda c, d, cl: (0, c, 0)),
                pl.BlockSpec((1, block, width), lambda c, d, cl: (d, c, 0)),
                pl.BlockSpec((width, width), lambda c, d, cl: (0, 0)),
            ],
            out_specs=pl.BlockSpec((1, beams, block // 2, 2 * bins), lambda c, d, cl: (d, 0, c, 0)),
            scratch_shapes=[pltpu.VMEM((beams * block, 2 * bins), jnp.float32)],
        ),
        compiler_params=pltpu.CompilerParams(
            dimension_semantics=("arbitrary", "arbitrary"), vmem_limit_bytes=48 * 1024 * 1024
        ),
        cost_estimate=pl.CostEstimate(flops=flops, transcendentals=0, bytes_accessed=bytes_accessed),
    )(chirp_len, spectra, responses, backward)


def shards(voltages, responses, chirp_len):
    chans_local, beams, _, length = voltages.shape
    trials, chans = responses.shape[0], responses.shape[1]
    forward, backward = dft_tables(length)
    order = sample_order(length, RATE)
    backward = jnp.concatenate([backward[:, order], backward[:, length + order]], 1)
    local = jnp.dot(
        voltages.reshape(-1, 2 * length), forward, preferred_element_type=jnp.float32
    ).astype(jnp.bfloat16)
    local = local.reshape(chans_local, beams, 2 * length).transpose(1, 0, 2)
    spectra = lax.all_gather(local, "dm", axis=1, tiled=True)
    detected = detect(spectra, responses.reshape(trials, chans, 2 * length), chirp_len, backward)
    flattened = detected.reshape(trials, beams, -1)
    return lax.all_to_all(flattened, "beam", split_axis=1, concat_axis=2, tiled=True)


def solution(mesh):
    placed = (P(("beam", "dm"), None, None, None), P("dm", "beam", None, None), P("dm"))
    return jax.shard_map(
        shards, mesh=mesh, in_specs=placed, out_specs=P("dm", "beam", None), check_vma=False
    )
```

time: 265 us -> 145 us (0.55)
  other arithmetic: 65.7 us -> 2.2 us
  local copies, waits for them, and re-layouts: 61.3 us -> 14.4 us
  matrix products: 20.2 us -> 0.31 us
  Pallas kernels: 0 us -> 15.8 us
  waiting for transfers between devices: 68.8 us -> 65 us
    reshape x7 -> x4, local copies, waits for them, and re-layouts: 37.1 us -> 8.3 us  [the longest x2 4.44 us: shards(): flattened = detected.reshape(trials, beams, -1)]
    dot_general x5 -> x1, matrix products: 20.2 us -> 0.31 us  [shards(): jnp.dot(voltages.reshape(-1, 2 * length), forward, preferred_element_type...]
    reduce_sum x4 -> x0, other arithmetic: 19.1 us -> none  [one_trial(): binned = powers.reshape(chans, beam_count, samples_out, rate).sum(-1) / rate]
    another operation x6 -> x2, other arithmetic: 21.1 us -> 2.1 us
    pallas_call x0 -> x1, Pallas kernels: none -> 15.8 us  [detect(): pl.pallas_call(detect_kernel, out_shape=jax.ShapeDtypeStruct((trials, bea...]
    select_n x4 -> x2, other arithmetic: 12.5 us -> 0.02 us  [the longest x1 0.01 us: shards(): backward[:, length + order]]
    convert_element_type x1 -> x0, other arithmetic: 8.82 us -> none  [detect(): spec_im = spectra[:, :, 1, :].astype(jnp.float32)]
    dynamic_slice x12 -> x0, local copies, waits for them, and re-layouts: 8.36 us -> none  [detect(): return lax.map(one_trial, (response, lengths))]
  transfers between devices with their start and end apart: 1 -> 1, of which waited for: 1 -> 1; matrix products, arithmetic and copies ran while one was open for 1% -> 4% of each run, Pallas kernels for 0% -> 0%
where the time goes in v1:
time: 145 us
  waiting for transfers between devices  65 us (45%)
  blocking collectives  33.6 us (23%)
  Pallas kernels  15.8 us (11%)
  local copies, waits for them, and re-layouts  14.4 us (10%)
  between operations  13.5 us (9%)
  other arithmetic  2.2 us (2%)
    all_gather x1, waiting for transfers between devices, shards(): spectra = lax.all_gather(local, 'dm', axis=1, tiled=True)  65 us
    all_to_all x1, blocking collectives, shards(): lax.all_to_all(flattened, 'beam', split_axis=1, concat_axis=2, tiled=True)  33.6 us
    pallas_call x1, Pallas kernels, detect(): pl.pallas_call(detect_kernel, out_shape=jax.ShapeDtypeStruct((trials, bea...  15.8 us
    reshape x2, local copies, waits for them, and re-layouts, shards(): flattened = detected.reshape(trials, beams, -1)  4.44 us
    unnamed x6, local copies, waits for them, and re-layouts  3.56 us
    reshape x1, local copies, waits for them, and re-layouts, shards(): responses.reshape(trials, chans, 2 * length)  3.16 us
  transfers between devices with their start and end apart: 1, of which 1 were waited for; matrix products, arithmetic and copies ran while one was open for 4% of the time, Pallas kernels for 0%

profile of v1, /device:TPU:1, one launch (start us, length us, event | category | flops | bytes accessed | tf_op | source)
XLA Modules:
  0.0 144.8 jit_solution(17532778282149457161)
XLA Ops:
  6.5 0.0 all-gather.2.cloned.1.call-start
  6.5 1.0 fusion.12
  7.5 1.1 negate_convert_fusion
  8.6 0.9 copy.13
  9.6 0.3 fusion
  9.9 0.7 copy.15
  10.6 0.0 all-gather.2.cloned.1.call-update
  10.7 1.2 gather_fusion.1
  11.9 1.2 gather_fusion
  13.0 0.1 copy.10
  13.2 0.1 copy.11
  13.3 0.0 copy-start.1
  13.3 3.2 %reshape.94.resp_ref = bf16[4,512,512]{2,1,0:T(8,128)(2,1)S(1)} reshape(bf16[4,512,2,256]{3,2,1,0:T(2,128)(2,1)} %param.4) | data formatting | bytes 4194304 | tf_op jit(solution)/shard_map/reshape | solution.py:106
  16.5 65.0 %all-gather.2.cloned.1.call-done.spec_ref = bf16[8,512,512]{2,1,0:T(8,128)(2,1)} async-done(((bf16[8,16,512]{2,1,0:T(8,128)(2,1)}), bf16[8,512,512]{2,1,0:T(8,128)(2,1)}) %all-gather.2.cloned.1.call-update) | async-done | bytes 4194320 | tf_op jit(solution)/shard_map/all_gather | solution.py:105
  81.5 0.0 copy-done.1
  81.5 15.8 %shard_map.37 = bf16[4,8,256,128]{3,2,1,0:T(8,128)(2,1)S(1)} custom-call(s32[4]{0:T(128)S(1)} %copy-done.1, bf16[8,512,512]{2,1,0:T(8,128)(2,1)} %all-gather.2.cloned.1.call-done.spec_ref, bf16[4,512,512]{2,1,0:T(8,128)(2,1)S(1)} %reshape.94.resp_ref, bf16[512,512]{1,0:T(8,128)(2,1)S(1)} %pad_maximum_fusion.5.back_ref), custom_call_target="tpu_custom_call" | custom-call | flops 8589934592 | bytes 8912896 | tf_op jit(solution)/shard_map/pallas_call | solution.py:74
  97.3 0.0 copy-start
  97.3 1.3 copy-done
  98.6 2.8 %reshape.95 = bf16[4,8,32768]{2,1,0:T(8,128)(2,1)S(1)} reshape(bf16[4,8,256,128]{3,2,1,0:T(8,128)(2,1)} %copy-done) | data formatting | bytes 4194304 | tf_op jit(solution)/shard_map/reshape | solution.py:107
  101.4 1.6 %copy.12 = bf16[4,8,32768]{2,0,1:T(4,128)(2,1)S(1)} copy(bf16[4,8,32768]{2,1,0:T(8,128)(2,1)S(1)} %reshape.95) | data formatting | bytes 4194304 | tf_op jit(solution)/shard_map/reshape | solution.py:107
  103.0 33.6 %all_to_all.12 = bf16[4,8,32768]{2,0,1:T(4,128)(2,1)S(1)} all-to-all(bf16[4,8,32768]{2,0,1:T(4,128)(2,1)S(1)} %copy.12), channel_id=1, replica_groups=mesh['dm'=32,'beam'=8] {'beam'}, dimensions={1} | all-to-all | bytes 4194304 | tf_op jit(solution)/shard_map/all_to_all | solution.py:108
  136.6 1.3 copy.17
  (6 shorter events, 0.1 us)
Async XLA Ops:
  6.5 74.9 %all-gather.2.cloned.1.call-start = ((), (), s32[]{:S(2)}) async-start(), calls=%async_computation.1 | async-start | bytes 4325376 | tf_op jit(solution)/shard_map/all_gather | solution.py:105
  13.3 68.2 %copy-start.1 = (s32[4]{0:T(128)S(1)}, s32[4]{0:T(128)}, u32[]{:S(2)}) copy-start(s32[4]{0:T(128)} %chirp_ref.1) | copy-start | bytes 52
  97.3 1.3 copy-start
Sparse Core Ops, SparseCore 0:
  10.7 70.7 all-gather.1

commit v2 on v1

--- a/solution.py
+++ b/solution.py
@@ -92,9 +92,51 @@
     )(chirp_len, spectra, responses, backward)
 
 
+def coords(index, z_count):
+    return index // (2 * z_count), (index // 2) % z_count, index % 2
+
+
+def flat(x_lo, z, core, z_count):
+    return (x_lo * z_count + z % z_count) * 2 + core
+
+
+def moves(count, step):
+    z_count = count // 4
+    pairs = []
+    for index in range(count):
+        x_lo, z, core = coords(index, z_count)
+        pairs.append((index, step(x_lo, z, core, z_count)))
+    return pairs
+
+
+def gather_spectra(own, count):
+    z_count = count // 4
+    across = moves(count, lambda x, z, c, n: flat(1 - x, z, c, n))
+    up = moves(count, lambda x, z, c, n: flat(x, z + 1, c, n))
+    down = moves(count, lambda x, z, c, n: flat(x, z - 1, c, n))
+    partner = moves(count, lambda x, z, c, n: flat(x, z, 1 - c, n))
+    pair = jnp.stack([own, lax.ppermute(own, "dm", across)])
+    from_below = [pair]
+    from_above = [pair]
+    for _ in range(z_count // 2 - 1):
+        from_below.append(lax.ppermute(from_below[-1], "dm", up))
+        from_above.append(lax.ppermute(from_above[-1], "dm", down))
+    far = jnp.stack(
+        [lax.ppermute(from_below[-1][0], "dm", up), lax.ppermute(from_above[-1][1], "dm", down)]
+    )
+    column = jnp.stack(from_above + [far] + from_below[:0:-1])
+    both = jnp.stack([column, lax.ppermute(column, "dm", partner)])
+    x_me, z_me, c_me = coords(lax.axis_index("dm"), z_count)
+    shard = jnp.arange(count, dtype=jnp.int32)
+    x_n, z_n, c_n = coords(shard, z_count)
+    rel = ((c_n ^ c_me) * z_count + (z_n - z_me) % z_count) * 2 + (x_n ^ x_me)
+    return jnp.take(both.reshape((count,) + own.shape), rel, axis=0)
+
+
 def shards(voltages, responses, chirp_len):
     chans_local, beams, _, length = voltages.shape
     trials, chans = responses.shape[0], responses.shape[1]
+    count = chans // chans_local
     forward, backward = dft_tables(length)
     order = sample_order(length, RATE)
     backward = jnp.concatenate([backward[:, order], backward[:, length + order]], 1)
@@ -102,7 +144,8 @@
         voltages.reshape(-1, 2 * length), forward, preferred_element_type=jnp.float32
     ).astype(jnp.bfloat16)
     local = local.reshape(chans_local, beams, 2 * length).transpose(1, 0, 2)
-    spectra = lax.all_gather(local, "dm", axis=1, tiled=True)
+    gathered = gather_spectra(local, count)
+    spectra = gathered.transpose(1, 0, 2, 3).reshape(beams, chans, 2 * length)
     detected = detect(spectra, responses.reshape(trials, chans, 2 * length), chirp_len, backward)
     flattened = detected.reshape(trials, beams, -1)
     return lax.all_to_all(flattened, "beam", split_axis=1, concat_axis=2, tiled=True)

time: 145 us -> 127 us (0.88)
  waiting for transfers between devices: 65 us -> 14.7 us
  starting transfers between devices: 0.01 us -> 22.5 us
  local copies, waits for them, and re-layouts: 14.4 us -> 29.2 us
  between operations: 13.5 us -> 0.2 us
  other arithmetic: 2.2 us -> 8.97 us
    all_gather x1 -> x0, waiting for transfers between devices: 65 us -> none  [shards(): spectra = lax.all_gather(local, 'dm', axis=1, tiled=True)]
    ppermute x0 -> x10, starting transfers between devices: none -> 22.5 us  [the longest x3 9.37 us: gather_spectra(): from_above.append(lax.ppermute(from_above[-1], 'dm', down))]
    ppermute x0 -> x10, waiting for transfers between devices: none -> 14.7 us  [the longest x3 10.9 us: gather_spectra(): from_below.append(lax.ppermute(from_below[-1], 'dm', up))]
    gather x0 -> x1, local copies, waits for them, and re-layouts: none -> 4.98 us  [gather_spectra(): return jnp.take(both.reshape((count,) + own.shape), rel, axis=0)]
    another operation x0 -> x2, local copies, waits for them, and re-layouts: none -> 4.51 us  [the longest x1 3.79 us: gather_spectra(): both = jnp.stack([column, lax.ppermute(column, 'dm', partner)])]
    unnamed x6 -> x11, local copies, waits for them, and re-layouts: 3.56 us -> 7.16 us
    select_n x0 -> x2, other arithmetic: none -> 2.68 us  [gather_spectra(): return jnp.take(both.reshape((count,) + own.shape), rel, axis=0)]
    another operation x2 -> x4, other arithmetic: 2.1 us -> 4.73 us  [the longest x1 2.61 us: gather_spectra(): both = jnp.stack([column, lax.ppermute(column, 'dm', partner)])]
  transfers between devices with their start and end apart: 1 -> 10, of which waited for: 1 -> 7; matrix products, arithmetic and copies ran while one was open for 4% -> 7% of each run, Pallas kernels for 0% -> 0%
where the time goes in v2:
time: 127 us; the launch traced here: 126 us
  blocking collectives  34.7 us (27%)
  local copies, waits for them, and re-layouts  29.2 us (23%)
  starting transfers between devices  22.5 us (18%)
  Pallas kernels  15.7 us (12%)
  waiting for transfers between devices  14.7 us (12%)
  other arithmetic  8.97 us (7%)
    all_to_all x1, blocking collectives, shards(): lax.all_to_all(flattened, 'beam', split_axis=1, concat_axis=2, tiled=True)  34.7 us
    pallas_call x1, Pallas kernels, detect(): pl.pallas_call(detect_kernel, out_shape=jax.ShapeDtypeStruct((trials, bea...  15.7 us
    ppermute x3, waiting for transfers between devices, gather_spectra(): from_below.append(lax.ppermute(from_below[-1], 'dm', up))  10.9 us
    ppermute x3, starting transfers between devices, gather_spectra(): from_above.append(lax.ppermute(from_above[-1], 'dm', down))  9.37 us
    unnamed x11, local copies, waits for them, and re-layouts  7.16 us
    ppermute x1, starting transfers between devices, gather_spectra(): both = jnp.stack([column, lax.ppermute(column, 'dm', partner)])  5.26 us
    gather x1, local copies, waits for them, and re-layouts, gather_spectra(): return jnp.take(both.reshape((count,) + own.shape), rel, axis=0)  4.98 us
    reshape x2, local copies, waits for them, and re-layouts, shards(): flattened = detected.reshape(trials, beams, -1)  4.44 us
  transfers between devices with their start and end apart: 10, of which 7 were waited for; matrix products, arithmetic and copies ran while one was open for 7% of the time, Pallas kernels for 0%

profile of v2, /device:TPU:1, one launch (start us, length us, event | category | flops | bytes accessed | tf_op | source)
XLA Modules:
  0.0 126.4 jit_solution(14768355077277888111)
XLA Ops:
  3.3 2.1 %collective-permute-start = (bf16[8,16,512]{2,0,1:T(8,128)(2,1)S(1)}, bf16[8,16,512]{2,0,1:T(8,128)(2,1)S(1)}, u32[]{:S(2)}, u32[]{:S(2)}) collective-permute-start(bf16[8,16,512]{2,0,1:T(8,128)(2,1)S(1)} %bitcast.56), channel_id=1, source_target_pairs={{0,128},{8,136},{16,144},{24,152},{32,160},{40,168},{48,176},{56,1... | collective-permute-start | bytes 393224 | tf_op jit(solution)/shard_map/ppermute | solution.py:118
  5.5 2.4 %collective-permute-done = bf16[8,16,512]{2,0,1:T(8,128)(2,1)S(1)} collective-permute-done((bf16[8,16,512]{2,0,1:T(8,128)(2,1)S(1)}, bf16[8,16,512]{2,0,1:T(8,128)(2,1)S(1)}, u32[]{:S(2)}, u32[]{:S(2)}) %collective-permute-start) | collective-permute-done | bytes 131104 | tf_op jit(solution)/shard_map/ppermute | solution.py:118
  7.8 2.5 %collective-permute-start.4 = (bf16[2,8,16,512]{3,1,2,0:T(8,128)(2,1)S(1)}, bf16[2,8,16,512]{3,1,2,0:T(8,128)(2,1)S(1)}, u32[]{:S(2)}, u32[]{:S(2)}) collective-permute-start(bf16[2,8,16,512]{3,1,2,0:T(8,128)(2,1)S(1)} %pad_maximum_fusion.7), channel_id=1, source_target_pairs={{0,16},{8,24},{16,32},{24,40},{32,48},{40,56},{48,64},{56,72},{64,... | collective-permute-start | bytes 786440 | tf_op jit(solution)/shard_map/ppermute | solution.py:122
  10.4 4.0 %collective-permute-start.1 = (bf16[2,8,16,512]{3,1,2,0:T(8,128)(2,1)S(1)}, bf16[2,8,16,512]{3,1,2,0:T(8,128)(2,1)S(1)}, u32[]{:S(2)}, u32[]{:S(2)}) collective-permute-start(bf16[2,8,16,512]{3,1,2,0:T(8,128)(2,1)S(1)} %pad_maximum_fusion.7), channel_id=1, source_target_pairs={{0,112},{8,120},{16,0},{24,8},{32,16},{40,24},{48,32},{56,40},{64,... | collective-permute-start | bytes 786440 | tf_op jit(solution)/shard_map/ppermute | solution.py:123
  14.4 5.1 %collective-permute-done.4 = bf16[2,8,16,512]{3,1,2,0:T(8,128)(2,1)S(1)} collective-permute-done((bf16[2,8,16,512]{3,1,2,0:T(8,128)(2,1)S(1)}, bf16[2,8,16,512]{3,1,2,0:T(8,128)(2,1)S(1)}, u32[]{:S(2)}, u32[]{:S(2)}) %collective-permute-start.4) | collective-permute-done | bytes 262176 | tf_op jit(solution)/shard_map/ppermute | solution.py:122
  19.5 2.7 %collective-permute-start.2 = (bf16[2,8,16,512]{3,1,2,0:T(8,128)(2,1)S(1)}, bf16[2,8,16,512]{3,1,2,0:T(8,128)(2,1)S(1)}, u32[]{:S(2)}, u32[]{:S(2)}) collective-permute-start(bf16[2,8,16,512]{3,1,2,0:T(8,128)(2,1)S(1)} %collective-permute-done.1), channel_id=1, source_target_pairs={{0,112},{8,120},{16,0},{24,8},{32,16},{40,24},{48,32},{56,40},{64,... | collective-permute-start | bytes 786440 | tf_op jit(solution)/shard_map/ppermute | solution.py:123
  22.8 3.6 %collective-permute-done.5 = bf16[2,8,16,512]{3,1,2,0:T(8,128)(2,1)S(1)} collective-permute-done((bf16[2,8,16,512]{3,1,2,0:T(8,128)(2,1)S(1)}, bf16[2,8,16,512]{3,1,2,0:T(8,128)(2,1)S(1)}, u32[]{:S(2)}, u32[]{:S(2)}) %collective-permute-start.5) | collective-permute-done | bytes 262176 | tf_op jit(solution)/shard_map/ppermute | solution.py:122
  27.1 2.7 %collective-permute-start.3 = (bf16[2,8,16,512]{3,1,2,0:T(8,128)(2,1)S(1)}, bf16[2,8,16,512]{3,1,2,0:T(8,128)(2,1)S(1)}, u32[]{:S(2)}, u32[]{:S(2)}) collective-permute-start(bf16[2,8,16,512]{3,1,2,0:T(8,128)(2,1)S(1)} %collective-permute-done.2), channel_id=1, source_target_pairs={{0,112},{8,120},{16,0},{24,8},{32,16},{40,24},{48,32},{56,40},{64,... | collective-permute-start | bytes 786440 | tf_op jit(solution)/shard_map/ppermute | solution.py:123
  30.5 2.3 %collective-permute-done.6 = bf16[2,8,16,512]{3,1,2,0:T(8,128)(2,1)S(1)} collective-permute-done((bf16[2,8,16,512]{3,1,2,0:T(8,128)(2,1)S(1)}, bf16[2,8,16,512]{3,1,2,0:T(8,128)(2,1)S(1)}, u32[]{:S(2)}, u32[]{:S(2)}) %collective-permute-start.6) | collective-permute-done | bytes 262176 | tf_op jit(solution)/shard_map/ppermute | solution.py:122
  33.1 3.2 %collective-permute-start.8 = (bf16[8,16,512]{2,0,1:T(8,128)(2,1)S(1)}, bf16[8,16,512]{2,0,1:T(8,128)(2,1)S(1)}, u32[]{:S(2)}, u32[]{:S(2)}) collective-permute-start(bf16[8,16,512]{2,0,1:T(8,128)(2,1)S(1)} %slice_bitcast_fusion), channel_id=1, source_target_pairs={{0,112},{8,120},{16,0},{24,8},{32,16},{40,24},{48,32},{56,40},{64,... | collective-permute-start | bytes 393224 | tf_op jit(solution)/shard_map/ppermute | solution.py:125
  41.2 5.3 %collective-permute-start.9 = (bf16[8,2,8,16,512]{4,2,3,1,0:T(8,128)(2,1)}, bf16[8,2,8,16,512]{4,2,3,1,0:T(8,128)(2,1)}, u32[]{:S(2)}, u32[]{:S(2)}) collective-permute-start(bf16[8,2,8,16,512]{4,2,3,1,0:T(8,128)(2,1)} %bitcast_dynamic-update-slice_fusion), channel_id=1, source_target_pairs={{0,8},{8,0},{16,24},{24,16},{32,40},{40,32},{48,56},{56,48},{64,72... | collective-permute-start | bytes 6291464 | tf_op jit(solution)/shard_map/ppermute | solution.py:128
  46.5 1.2 gather_fusion.1
  49.1 3.2 %reshape.276.resp_ref = bf16[4,512,512]{2,1,0:T(8,128)(2,1)S(1)} reshape(bf16[4,512,2,256]{3,2,1,0:T(2,128)(2,1)} %param.4) | data formatting | bytes 4194304 | tf_op jit(solution)/shard_map/reshape | solution.py:149
  52.4 2.6 %pad_maximum_fusion = bf16[2,8,2,8,16,512]{5,3,4,2,1,0:T(8,128)(2,1)S(1)} fusion(bf16[1,8,2,8,16,512]{5,3,4,2,1,0:T(8,128)(2,1)} %bitcast.20, bf16[1,8,2,8,16,512]{5,3,4,2,1,0:T(8,128)(2,1)} %bitcast.19), kind=kLoop, calls=%fused_computation.3 | loop fusion | flops 2097152 | bytes 8388608 | tf_op jit(solution)/shard_map/stack | solution.py:128
  55.0 3.8 %copy.10 = bf16[2,8,2,8,16,512]{5,4,3,2,1,0:T(8,128)(2,1)} copy(bf16[2,8,2,8,16,512]{5,3,4,2,1,0:T(8,128)(2,1)S(1)} %pad_maximum_fusion) | data formatting | bytes 8388608 | tf_op jit(solution)/shard_map/stack | solution.py:128
  58.8 5.0 %gather_fusion = bf16[32,8,16,512]{3,2,1,0:T(8,128)(2,1)} fusion(bf16[32,8,16,512]{3,2,1,0:T(8,128)(2,1)} %bitcast.51, s32[1024]{0:T(1024)S(1)} %pad_clamp_fusion.2), kind=kCustom, calls=%fused_computation | custom fusion | bytes 8388736 | tf_op jit(solution)/shard_map/jit(_take)/gather | solution.py:133
  63.8 2.6 %select_bitcast_fusion = bf16[8,32,16,512]{3,2,0,1:T(8,128)(2,1)S(1)} fusion(bf16[32,8,16,512]{3,2,1,0:T(8,128)(2,1)} %gather_fusion, pred[32]{0:T(512)(128)(4,1)S(1)} %compare_and_fusion), kind=kLoop, calls=%fused_computation.4 | loop fusion | flops 2097152 | bytes 8388640 | tf_op jit(solution)/shard_map/jit(_take)/select_n | solution.py:133
  66.4 2.4 %copy.11 = bf16[8,32,16,512]{3,2,1,0:T(8,128)(2,1)} copy(bf16[8,32,16,512]{3,2,0,1:T(8,128)(2,1)S(1)} %select_bitcast_fusion) | data formatting | bytes 8388608 | tf_op jit(solution)/shard_map/jit(_take)/select_n | solution.py:133
  68.8 15.7 %shard_map.37 = bf16[4,8,256,128]{3,2,1,0:T(8,128)(2,1)S(1)} custom-call(s32[4]{0:T(128)S(1)} %copy-done.1, bf16[8,512,512]{2,1,0:T(8,128)(2,1)} %bitcast.53, bf16[4,512,512]{2,1,0:T(8,128)(2,1)S(1)} %reshape.276.resp_ref, bf16[512,512]{1,0:T(8,128)(2,1)S(1)} %pad_maximum_fusion.6.back_ref), custom_call_target="tpu_custom_call" | custom-call | flops 8589934592 | bytes 8912896 | tf_op jit(solution)/shard_map/pallas_call | solution.py:74
  84.6 1.3 %copy-done = bf16[4,8,256,128]{3,2,1,0:T(8,128)(2,1)} copy-done((bf16[4,8,256,128]{3,2,1,0:T(8,128)(2,1)}, bf16[4,8,256,128]{3,2,1,0:T(8,128)(2,1)S(1)}, u32[]{:S(2)}) %copy-start) | copy-done | bytes 2097176
  85.9 2.8 %reshape.277 = bf16[4,8,32768]{2,1,0:T(8,128)(2,1)S(1)} reshape(bf16[4,8,256,128]{3,2,1,0:T(8,128)(2,1)} %copy-done) | data formatting | bytes 4194304 | tf_op jit(solution)/shard_map/reshape | solution.py:150
  88.7 1.6 %copy.14 = bf16[4,8,32768]{2,0,1:T(4,128)(2,1)S(1)} copy(bf16[4,8,32768]{2,1,0:T(8,128)(2,1)S(1)} %reshape.277) | data formatting | bytes 4194304 | tf_op jit(solution)/shard_map/reshape | solution.py:150
  90.3 34.7 %all_to_all.12 = bf16[4,8,32768]{2,0,1:T(4,128)(2,1)S(1)} all-to-all(bf16[4,8,32768]{2,0,1:T(4,128)(2,1)S(1)} %copy.14), channel_id=1, replica_groups=mesh['dm'=32,'beam'=8] {'beam'}, dimensions={1} | all-to-all | bytes 4194304 | tf_op jit(solution)/shard_map/all_to_all | solution.py:151
  125.1 1.3 %copy.24 = bf16[4,1,262144]{2,0,1:T(4,128)(2,1)} copy(bf16[4,1,262144]{2,0,1:T(4,128)(2,1)S(1)} %bitcast.52) | data formatting | bytes 4194304
  (38 shorter events, 12.2 us)
Async XLA Ops:
  3.3 4.5 %collective-permute-start = (bf16[8,16,512]{2,0,1:T(8,128)(2,1)S(1)}, bf16[8,16,512]{2,0,1:T(8,128)(2,1)S(1)}, u32[]{:S(2)}, u32[]{:S(2)}) collective-permute-start(bf16[8,16,512]{2,0,1:T(8,128)(2,1)S(1)} %bitcast.56), channel_id=1, source_target_pairs={{0,128},{8,136},{16,144},{24,152},{32,160},{40,168},{48,176},{56,1... | collective-permute-start | bytes 393224 | tf_op jit(solution)/shard_map/ppermute | solution.py:118
  7.8 11.6 %collective-permute-start.4 = (bf16[2,8,16,512]{3,1,2,0:T(8,128)(2,1)S(1)}, bf16[2,8,16,512]{3,1,2,0:T(8,128)(2,1)S(1)}, u32[]{:S(2)}, u32[]{:S(2)}) collective-permute-start(bf16[2,8,16,512]{3,1,2,0:T(8,128)(2,1)S(1)} %pad_maximum_fusion.7), channel_id=1, source_target_pairs={{0,16},{8,24},{16,32},{24,40},{32,48},{40,56},{48,64},{56,72},{64,... | collective-permute-start | bytes 786440 | tf_op jit(solution)/shard_map/ppermute | solution.py:122
  10.4 9.1 %collective-permute-start.1 = (bf16[2,8,16,512]{3,1,2,0:T(8,128)(2,1)S(1)}, bf16[2,8,16,512]{3,1,2,0:T(8,128)(2,1)S(1)}, u32[]{:S(2)}, u32[]{:S(2)}) collective-permute-start(bf16[2,8,16,512]{3,1,2,0:T(8,128)(2,1)S(1)} %pad_maximum_fusion.7), channel_id=1, source_target_pairs={{0,112},{8,120},{16,0},{24,8},{32,16},{40,24},{48,32},{56,40},{64,... | collective-permute-start | bytes 786440 | tf_op jit(solution)/shard_map/ppermute | solution.py:123
  19.4 7.0 %collective-permute-start.5 = (bf16[2,8,16,512]{3,1,2,0:T(8,128)(2,1)S(1)}, bf16[2,8,16,512]{3,1,2,0:T(8,128)(2,1)S(1)}, u32[]{:S(2)}, u32[]{:S(2)}) collective-permute-start(bf16[2,8,16,512]{3,1,2,0:T(8,128)(2,1)S(1)} %collective-permute-done.4), channel_id=1, source_target_pairs={{0,16},{8,24},{16,32},{24,40},{32,48},{40,56},{48,64},{56,72},{64,... | collective-permute-start | bytes 786440 | tf_op jit(solution)/shard_map/ppermute | solution.py:122
  19.5 7.7 %collective-permute-start.2 = (bf16[2,8,16,512]{3,1,2,0:T(8,128)(2,1)S(1)}, bf16[2,8,16,512]{3,1,2,0:T(8,128)(2,1)S(1)}, u32[]{:S(2)}, u32[]{:S(2)}) collective-permute-start(bf16[2,8,16,512]{3,1,2,0:T(8,128)(2,1)S(1)} %collective-permute-done.1), channel_id=1, source_target_pairs={{0,112},{8,120},{16,0},{24,8},{32,16},{40,24},{48,32},{56,40},{64,... | collective-permute-start | bytes 786440 | tf_op jit(solution)/shard_map/ppermute | solution.py:123
  26.4 6.4 %collective-permute-start.6 = (bf16[2,8,16,512]{3,1,2,0:T(8,128)(2,1)S(1)}, bf16[2,8,16,512]{3,1,2,0:T(8,128)(2,1)S(1)}, u32[]{:S(2)}, u32[]{:S(2)}) collective-permute-start(bf16[2,8,16,512]{3,1,2,0:T(8,128)(2,1)S(1)} %collective-permute-done.5), channel_id=1, source_target_pairs={{0,16},{8,24},{16,32},{24,40},{32,48},{40,56},{48,64},{56,72},{64,... | collective-permute-start | bytes 786440 | tf_op jit(solution)/shard_map/ppermute | solution.py:122
  27.1 6.0 %collective-permute-start.3 = (bf16[2,8,16,512]{3,1,2,0:T(8,128)(2,1)S(1)}, bf16[2,8,16,512]{3,1,2,0:T(8,128)(2,1)S(1)}, u32[]{:S(2)}, u32[]{:S(2)}) collective-permute-start(bf16[2,8,16,512]{3,1,2,0:T(8,128)(2,1)S(1)} %collective-permute-done.2), channel_id=1, source_target_pairs={{0,112},{8,120},{16,0},{24,8},{32,16},{40,24},{48,32},{56,40},{64,... | collective-permute-start | bytes 786440 | tf_op jit(solution)/shard_map/ppermute | solution.py:123
  32.9 5.1 %collective-permute-start.7 = (bf16[8,16,512]{2,0,1:T(8,128)(2,1)S(1)}, bf16[8,16,512]{2,0,1:T(8,128)(2,1)S(1)}, u32[]{:S(2)}, u32[]{:S(2)}) collective-permute-start(bf16[8,16,512]{2,0,1:T(8,128)(2,1)S(1)} %slice_bitcast_fusion.1), channel_id=1, source_target_pairs={{0,16},{8,24},{16,32},{24,40},{32,48},{40,56},{48,64},{56,72},{64,... | collective-permute-start | bytes 393224 | tf_op jit(solution)/shard_map/ppermute | solution.py:125
  33.1 5.1 %collective-permute-start.8 = (bf16[8,16,512]{2,0,1:T(8,128)(2,1)S(1)}, bf16[8,16,512]{2,0,1:T(8,128)(2,1)S(1)}, u32[]{:S(2)}, u32[]{:S(2)}) collective-permute-start(bf16[8,16,512]{2,0,1:T(8,128)(2,1)S(1)} %slice_bitcast_fusion), channel_id=1, source_target_pairs={{0,112},{8,120},{16,0},{24,8},{32,16},{40,24},{48,32},{56,40},{64,... | collective-permute-start | bytes 393224 | tf_op jit(solution)/shard_map/ppermute | solution.py:125
  41.2 11.2 %collective-permute-start.9 = (bf16[8,2,8,16,512]{4,2,3,1,0:T(8,128)(2,1)}, bf16[8,2,8,16,512]{4,2,3,1,0:T(8,128)(2,1)}, u32[]{:S(2)}, u32[]{:S(2)}) collective-permute-start(bf16[8,2,8,16,512]{4,2,3,1,0:T(8,128)(2,1)} %bitcast_dynamic-update-slice_fusion), channel_id=1, source_target_pairs={{0,8},{8,0},{16,24},{24,16},{32,40},{40,32},{48,56},{56,48},{64,72... | collective-permute-start | bytes 6291464 | tf_op jit(solution)/shard_map/ppermute | solution.py:128
  66.4 2.4 %copy-start.1 = (s32[4]{0:T(128)S(1)}, s32[4]{0:T(128)}, u32[]{:S(2)}) copy-start(s32[4]{0:T(128)} %chirp_ref.1) | copy-start | bytes 52
  84.6 1.3 %copy-start = (bf16[4,8,256,128]{3,2,1,0:T(8,128)(2,1)}, bf16[4,8,256,128]{3,2,1,0:T(8,128)(2,1)S(1)}, u32[]{:S(2)}) copy-start(bf16[4,8,256,128]{3,2,1,0:T(8,128)(2,1)S(1)} %shard_map.37) | copy-start | bytes 6291460

commit v3 on v2

v3 whole, which is shorter than its diff:
```python
import functools
import math

import jax
import jax.numpy as jnp
from jax import lax
from jax.experimental import pallas as pl
from jax.experimental.pallas import tpu as pltpu
from jax.sharding import PartitionSpec as P

RATE = 4
CHAN_BLOCK = 256


def dft_tables(length):
    sample = jnp.arange(length, dtype=jnp.int32)
    phases = sample[:, None] * sample[None, :] % length
    angles = phases.astype(jnp.float32) * (2.0 * math.pi / length)
    cosine = jnp.cos(angles) / math.sqrt(length)
    sine_part = jnp.sin(angles) / math.sqrt(length)
    forward = jnp.concatenate(
        [jnp.concatenate([cosine, -sine_part], 1), jnp.concatenate([sine_part, cosine], 1)], 0
    )
    backward = jnp.concatenate(
        [jnp.concatenate([cosine, sine_part], 1), jnp.concatenate([-sine_part, cosine], 1)], 0
    )
    return (forward.astype(jnp.bfloat16), backward.astype(jnp.bfloat16))


def sample_order(length, rate):
    pos = jnp.arange(length, dtype=jnp.int32)
    bins = length // rate
    return rate * (pos % bins) + pos // bins


def detect_kernel(chirp_ref, table_ref, swap_ref, mine_ref, theirs_ref, resp_ref, back_ref, out_ref, pair_ref):
    _, beams, chans_local, width = mine_ref.shape
    trials = resp_ref.shape[0]
    length = width // 2
    bins = length // RATE
    chans = 2 * chans_local
    keep = swap_ref[0] == 0
    mine = mine_ref[0]
    theirs = theirs_ref[0]
    x = jnp.concatenate([jnp.where(keep, mine, theirs), jnp.where(keep, theirs, mine)], axis=1)
    xr = x[:, :, :length].astype(jnp.float32)
    xi = x[:, :, length:].astype(jnp.float32)
    back = back_ref[...]
    pos = lax.broadcasted_iota(jnp.int32, (1, length), 1)
    t = RATE * (pos % bins) + pos // bins
    lane = lax.broadcasted_iota(jnp.int32, (1, 2 * bins), 1)
    rows = beams * chans // 2
    for d in range(trials):
        h = resp_ref[d]
        hr = h[:, :length].astype(jnp.float32)[None]
        hi = h[:, length:].astype(jnp.float32)[None]
        fr = hr * xr - hi * xi
        fi = hr * xi + hi * xr
        joined = jnp.concatenate([fr, fi], -1).reshape(beams * chans, width).astype(jnp.bfloat16)
        series = jnp.dot(joined, back, preferred_element_type=jnp.float32)
        powers = series[:, :length] ** 2 + series[:, length:] ** 2
        powers = jnp.where(t >= chirp_ref[d], powers, jnp.float32(0.0))
        half = powers[:, : length // 2] + powers[:, length // 2 :]
        pair_ref[...] = half + pltpu.roll(half, bins, 1)
        even = pair_ref[pl.ds(0, rows, stride=2), :]
        odd = pair_ref[pl.ds(1, rows, stride=2), :]
        both = jnp.where(lane < bins, even, odd) / RATE
        out_ref[d] = both.reshape(beams, chans // 2, 2 * bins).astype(out_ref.dtype)


def detect(table, swap, mine, theirs, responses, chirp_len, backward):
    blocks, beams, chans_local, width = mine.shape
    trials, chans = responses.shape[0], responses.shape[1]
    length = width // 2
    bins = length // RATE
    step = 2 * chans_local
    flops = 2 * trials * beams * chans * width * width
    bytes_accessed = 2 * (2 * mine.size + responses.size + backward.size + trials * beams * chans * bins)
    return pl.pallas_call(
        detect_kernel,
        out_shape=jax.ShapeDtypeStruct((trials, beams, chans // 2, 2 * bins), jnp.bfloat16),
        grid_spec=pltpu.PrefetchScalarGridSpec(
            num_scalar_prefetch=3,
            grid=(chans // step,),
            in_specs=[
                pl.BlockSpec((1, beams, chans_local, width), lambda n, cl, tb, sw: (tb[n], 0, 0, 0)),
                pl.BlockSpec((1, beams, chans_local, width), lambda n, cl, tb, sw: (tb[n], 0, 0, 0)),
                pl.BlockSpec((trials, step, width), lambda n, cl, tb, sw: (0, n, 0)),
                pl.BlockSpec((width, width), lambda n, cl, tb, sw: (0, 0)),
            ],
            out_specs=pl.BlockSpec(
                (trials, beams, step // 2, 2 * bins), lambda n, cl, tb, sw: (0, 0, n, 0)
            ),
            scratch_shapes=[pltpu.VMEM((beams * step, 2 * bins), jnp.float32)],
        ),
        compiler_params=pltpu.CompilerParams(
            dimension_semantics=("arbitrary",), vmem_limit_bytes=48 * 1024 * 1024
        ),
        cost_estimate=pl.CostEstimate(flops=flops, transcendentals=0, bytes_accessed=bytes_accessed),
    )(chirp_len, table, swap, mine, theirs, responses, backward)


def coords(index, z_count):
    return index // (2 * z_count), (index // 2) % z_count, index % 2


def flat(x_lo, z, core, z_count):
    return (x_lo * z_count + z % z_count) * 2 + core


def moves(count, step):
    z_count = count // 4
    pairs = []
    for index in range(count):
        x_lo, z, core = coords(index, z_count)
        pairs.append((index, step(x_lo, z, core, z_count)))
    return pairs


def gather_spectra(own, count):
    z_count = count // 4
    across = moves(count, lambda x, z, c, n: flat(1 - x, z, c, n))
    up = moves(count, lambda x, z, c, n: flat(x, z + 1, c, n))
    down = moves(count, lambda x, z, c, n: flat(x, z - 1, c, n))
    partner = moves(count, lambda x, z, c, n: flat(x, z, 1 - c, n))
    pair = jnp.stack([own, lax.ppermute(own, "dm", across)])
    from_below = [pair]
    from_above = [pair]
    for _ in range(z_count // 2 - 1):
        from_below.append(lax.ppermute(from_below[-1], "dm", up))
        from_above.append(lax.ppermute(from_above[-1], "dm", down))
    far = jnp.stack(
        [lax.ppermute(from_below[-1][0], "dm", up), lax.ppermute(from_above[-1][1], "dm", down)]
    )
    column = jnp.stack(from_above + [far] + from_below[:0:-1])
    column = column.reshape((2 * z_count,) + own.shape)
    return column, lax.ppermute(column, "dm", partner)


def shards(voltages, responses, chirp_len):
    chans_local, beams, _, length = voltages.shape
    trials, chans = responses.shape[0], responses.shape[1]
    count = chans // chans_local
    z_count = count // 4
    forward, backward = dft_tables(length)
    order = sample_order(length, RATE)
    backward = jnp.concatenate([backward[:, order], backward[:, length + order]], 1)
    local = jnp.dot(
        voltages.reshape(-1, 2 * length), forward, preferred_element_type=jnp.float32
    ).astype(jnp.bfloat16)
    local = local.reshape(chans_local, beams, 2 * length).transpose(1, 0, 2)
    mine, theirs = gather_spectra(local, count)
    x_me, z_me, c_me = coords(lax.axis_index("dm"), z_count)
    block = jnp.arange(count // 2, dtype=jnp.int32)
    table = ((block % z_count - z_me) % z_count) * 2 + ((block // z_count) ^ x_me)
    swap = jnp.reshape(c_me, (1,)).astype(jnp.int32)
    detected = detect(
        table, swap, mine, theirs, responses.reshape(trials, chans, 2 * length), chirp_len, backward
    )
    flattened = detected.reshape(trials, beams, -1)
    return lax.all_to_all(flattened, "beam", split_axis=1, concat_axis=2, tiled=True)


def solution(mesh):
    placed = (P(("beam", "dm"), None, None, None), P("dm", "beam", None, None), P("dm"))
    return jax.shard_map(
        shards, mesh=mesh, in_specs=placed, out_specs=P("dm", "beam", None), check_vma=False
    )
```

time: 127 us -> 115 us (0.906)
  local copies, waits for them, and re-layouts: 29.2 us -> 16.5 us
  other arithmetic: 8.97 us -> 2.27 us
  waiting for transfers between devices: 14.7 us -> 18.5 us
  starting transfers between devices: 22.5 us -> 24.9 us
    ppermute x3, waiting for transfers between devices: 10.9 us -> 0.02 us  [gather_spectra(): from_below.append(lax.ppermute(from_below[-1], 'dm', up))]
    ppermute x3, waiting for transfers between devices: 0.18 us -> 10.6 us  [gather_spectra(): from_above.append(lax.ppermute(from_above[-1], 'dm', down))]
    gather x1 -> x0, local copies, waits for them, and re-layouts: 4.98 us -> none  [gather_spectra(): return jnp.take(both.reshape((count,) + own.shape), rel, axis=0)]
    another operation x1 -> x0, local copies, waits for them, and re-layouts: 3.79 us -> none  [gather_spectra(): both = jnp.stack([column, lax.ppermute(column, 'dm', partner)])]
    ppermute x3, starting transfers between devices: 9.37 us -> 13 us  [gather_spectra(): from_above.append(lax.ppermute(from_above[-1], 'dm', down))]
    unnamed x11 -> x13, local copies, waits for them, and re-layouts: 7.16 us -> 3.94 us
    select_n x2 -> x0, other arithmetic: 2.68 us -> none  [gather_spectra(): return jnp.take(both.reshape((count,) + own.shape), rel, axis=0)]
    another operation x3 -> x2, other arithmetic: 4.7 us -> 2.1 us  [the longest x1 2.61 us: gather_spectra(): both = jnp.stack([column, lax.ppermute(column, 'dm', partner)])]
  transfers between devices with their start and end apart: 10 -> 10, of which waited for: 7 -> 6; matrix products, arithmetic and copies ran while one was open for 7% -> 6% of each run, Pallas kernels for 0% -> 0%
where the time goes in v3:
time: 115 us; the launch traced here: 114 us
  blocking collectives  34.7 us (30%)
  starting transfers between devices  24.9 us (22%)
  waiting for transfers between devices  18.5 us (16%)
  Pallas kernels  16.9 us (15%)
  local copies, waits for them, and re-layouts  16.5 us (14%)
  other arithmetic  2.27 us (2%)
    all_to_all x1, blocking collectives, shards(): lax.all_to_all(flattened, 'beam', split_axis=1, concat_axis=2, tiled=True)  34.7 us
    pallas_call x1, Pallas kernels, detect(): pl.pallas_call(detect_kernel, out_shape=jax.ShapeDtypeStruct((trials, bea...  16.9 us
    ppermute x3, starting transfers between devices, gather_spectra(): from_above.append(lax.ppermute(from_above[-1], 'dm', down))  13 us
    ppermute x3, waiting for transfers between devices, gather_spectra(): from_above.append(lax.ppermute(from_above[-1], 'dm', down))  10.6 us
    ppermute x1, starting transfers between devices, gather_spectra(): return (column, lax.ppermute(column, 'dm', partner))  6.39 us
    reshape x2, local copies, waits for them, and re-layouts, shards(): flattened = detected.reshape(trials, beams, -1)  5.5 us
    reshape x1, local copies, waits for them, and re-layouts, shards(): responses.reshape(trials, chans, 2 * length)  4.37 us
    unnamed x13, local copies, waits for them, and re-layouts  3.94 us
  transfers between devices with their start and end apart: 10, of which 6 were waited for; matrix products, arithmetic and copies ran while one was open for 6% of the time, Pallas kernels for 0%

profile of v3, /device:TPU:1, one launch (start us, length us, event | category | flops | bytes accessed | tf_op | source)
XLA Modules:
  0.0 114.2 jit_solution(7602028477823235803)
XLA Ops:
  0.0 1.0 fusion.13
  1.0 1.1 negate_convert_fusion
  2.1 0.9 copy.14
  3.4 2.1 %collective-permute-start = (bf16[8,16,512]{2,1,0:T(8,128)(2,1)S(1)}, bf16[8,16,512]{2,1,0:T(8,128)(2,1)S(1)}, u32[]{:S(2)}, u32[]{:S(2)}) collective-permute-start(bf16[8,16,512]{2,1,0:T(8,128)(2,1)S(1)} %bitcast.51), channel_id=1, source_target_pairs={{0,128},{8,136},{16,144},{24,152},{32,160},{40,168},{48,176},{56,1... | collective-permute-start | bytes 393224 | tf_op jit(solution)/shard_map/ppermute | solution.py:126
  5.5 2.4 %collective-permute-done = bf16[8,16,512]{2,1,0:T(8,128)(2,1)S(1)} collective-permute-done((bf16[8,16,512]{2,1,0:T(8,128)(2,1)S(1)}, bf16[8,16,512]{2,1,0:T(8,128)(2,1)S(1)}, u32[]{:S(2)}, u32[]{:S(2)}) %collective-permute-start) | collective-permute-done | bytes 131104 | tf_op jit(solution)/shard_map/ppermute | solution.py:126
  7.9 6.5 %collective-permute-start.1 = (bf16[2,8,16,512]{3,2,1,0:T(8,128)(2,1)S(1)}, bf16[2,8,16,512]{3,2,1,0:T(8,128)(2,1)S(1)}, u32[]{:S(2)}, u32[]{:S(2)}) collective-permute-start(bf16[2,8,16,512]{3,2,1,0:T(8,128)(2,1)S(1)} %pad_maximum_fusion.6), channel_id=1, source_target_pairs={{0,112},{8,120},{16,0},{24,8},{32,16},{40,24},{48,32},{56,40},{64,... | collective-permute-start | bytes 786440 | tf_op jit(solution)/shard_map/ppermute | solution.py:131
  14.4 4.1 %collective-permute-done.1 = bf16[2,8,16,512]{3,2,1,0:T(8,128)(2,1)S(1)} collective-permute-done((bf16[2,8,16,512]{3,2,1,0:T(8,128)(2,1)S(1)}, bf16[2,8,16,512]{3,2,1,0:T(8,128)(2,1)S(1)}, u32[]{:S(2)}, u32[]{:S(2)}) %collective-permute-start.1) | collective-permute-done | bytes 262176 | tf_op jit(solution)/shard_map/ppermute | solution.py:131
  18.5 3.4 %collective-permute-start.2 = (bf16[2,8,16,512]{3,2,1,0:T(8,128)(2,1)S(1)}, bf16[2,8,16,512]{3,2,1,0:T(8,128)(2,1)S(1)}, u32[]{:S(2)}, u32[]{:S(2)}) collective-permute-start(bf16[2,8,16,512]{3,2,1,0:T(8,128)(2,1)S(1)} %collective-permute-done.1), channel_id=1, source_target_pairs={{0,112},{8,120},{16,0},{24,8},{32,16},{40,24},{48,32},{56,40},{64,... | collective-permute-start | bytes 786440 | tf_op jit(solution)/shard_map/ppermute | solution.py:131
  21.9 3.3 %collective-permute-done.2 = bf16[2,8,16,512]{3,2,1,0:T(8,128)(2,1)S(1)} collective-permute-done((bf16[2,8,16,512]{3,2,1,0:T(8,128)(2,1)S(1)}, bf16[2,8,16,512]{3,2,1,0:T(8,128)(2,1)S(1)}, u32[]{:S(2)}, u32[]{:S(2)}) %collective-permute-start.2) | collective-permute-done | bytes 262176 | tf_op jit(solution)/shard_map/ppermute | solution.py:131
  25.2 3.1 %collective-permute-start.3 = (bf16[2,8,16,512]{3,2,1,0:T(8,128)(2,1)S(1)}, bf16[2,8,16,512]{3,2,1,0:T(8,128)(2,1)S(1)}, u32[]{:S(2)}, u32[]{:S(2)}) collective-permute-start(bf16[2,8,16,512]{3,2,1,0:T(8,128)(2,1)S(1)} %collective-permute-done.2), channel_id=1, source_target_pairs={{0,112},{8,120},{16,0},{24,8},{32,16},{40,24},{48,32},{56,40},{64,... | collective-permute-start | bytes 786440 | tf_op jit(solution)/shard_map/ppermute | solution.py:131
  28.5 3.2 %collective-permute-done.3 = bf16[2,8,16,512]{3,2,1,0:T(8,128)(2,1)S(1)} collective-permute-done((bf16[2,8,16,512]{3,2,1,0:T(8,128)(2,1)S(1)}, bf16[2,8,16,512]{3,2,1,0:T(8,128)(2,1)S(1)}, u32[]{:S(2)}, u32[]{:S(2)}) %collective-permute-start.3) | collective-permute-done | bytes 262176 | tf_op jit(solution)/shard_map/ppermute | solution.py:131
  31.7 3.2 %collective-permute-start.8 = (bf16[8,16,512]{2,1,0:T(8,128)(2,1)S(1)}, bf16[8,16,512]{2,1,0:T(8,128)(2,1)S(1)}, u32[]{:S(2)}, u32[]{:S(2)}) collective-permute-start(bf16[8,16,512]{2,1,0:T(8,128)(2,1)S(1)} %slice_bitcast_fusion), channel_id=1, source_target_pairs={{0,112},{8,120},{16,0},{24,8},{32,16},{40,24},{48,32},{56,40},{64,... | collective-permute-start | bytes 393224 | tf_op jit(solution)/shard_map/ppermute | solution.py:133
  35.0 2.0 %collective-permute-done.8 = bf16[8,16,512]{2,1,0:T(8,128)(2,1)S(1)} collective-permute-done((bf16[8,16,512]{2,1,0:T(8,128)(2,1)S(1)}, bf16[8,16,512]{2,1,0:T(8,128)(2,1)S(1)}, u32[]{:S(2)}, u32[]{:S(2)}) %collective-permute-start.8) | collective-permute-done | bytes 131104 | tf_op jit(solution)/shard_map/ppermute | solution.py:133
  37.1 3.5 %collective-permute-done.7 = bf16[8,16,512]{2,1,0:T(8,128)(2,1)S(1)} collective-permute-done((bf16[8,16,512]{2,1,0:T(8,128)(2,1)S(1)}, bf16[8,16,512]{2,1,0:T(8,128)(2,1)S(1)}, u32[]{:S(2)}, u32[]{:S(2)}) %collective-permute-start.7) | collective-permute-done | bytes 131104 | tf_op jit(solution)/shard_map/ppermute | solution.py:133
  40.7 6.4 %collective-permute-start.9 = (bf16[16,8,16,512]{3,2,1,0:T(8,128)(2,1)S(1)}, bf16[16,8,16,512]{3,2,1,0:T(8,128)(2,1)}, u32[]{:S(2)}, u32[]{:S(2)}) collective-permute-start(bf16[16,8,16,512]{3,2,1,0:T(8,128)(2,1)S(1)} %bitcast.48), channel_id=1, source_target_pairs={{0,8},{8,0},{16,24},{24,16},{32,40},{40,32},{48,56},{56,48},{64,72... | collective-permute-start | bytes 6291464 | tf_op jit(solution)/shard_map/ppermute | solution.py:137
  47.2 1.2 %gather_fusion.1 = bf16[256,512]{1,0:T(8,128)(2,1)S(1)} fusion(bf16[512,512]{0,1:T(8,128)(2,1)S(1)} %fusion.3, s32[1024]{0:T(1024)S(1)} %get-tuple-element.9), kind=kCustom, calls=%fused_computation.1 | custom fusion | bytes 525312 | tf_op jit(solution)/shard_map/gather | solution.py:147
  48.3 1.2 %gather_fusion = bf16[256,512]{1,0:T(8,128)(2,1)S(1)} fusion(bf16[512,512]{0,1:T(8,128)(2,1)S(1)} %fusion.3, s32[1024]{0:T(1024)S(1)} %get-tuple-element.10), kind=kCustom, calls=%fused_computation | custom fusion | bytes 525312 | tf_op jit(solution)/shard_map/gather | solution.py:147
  49.8 4.4 %reshape.102.resp_ref = bf16[4,512,512]{2,1,0:T(8,128)(2,1)} reshape(bf16[4,512,2,256]{3,2,1,0:T(2,128)(2,1)} %param.4) | data formatting | bytes 4194304 | tf_op jit(solution)/shard_map/reshape | solution.py:158
  54.2 1.6 %copy-done.1 = bf16[8,2,8,16,512]{4,3,2,1,0:T(8,128)(2,1)S(1)} copy-done((bf16[8,2,8,16,512]{4,3,2,1,0:T(8,128)(2,1)S(1)}, bf16[8,2,8,16,512]{4,3,2,1,0:T(8,128)(2,1)}, u32[]{:S(2)}) %copy-start.1) | copy-done | bytes 2097176
  55.8 16.9 %shard_map.37 = bf16[4,8,256,128]{3,2,1,0:T(8,128)(2,1)S(1)} custom-call(s32[4]{0:T(128)S(1)} %copy-done.2, s32[16]{0:T(128)S(1)} %fusion.18.table_ref, s32[1]{0:T(128)} %bitcast.swap_ref, bf16[16,8,16,512]{3,2,1,0:T(8,128)(2,1)S(1)} %bitcast.49, bf16[16,8,16,512]{3,2,1,0:T(8,128)(2,1)} %collective-permute-done.9.theirs_ref, ...), custom_call_target="tpu_custom_call" | custom-call | flops 8589934592 | bytes 8912896 | tf_op jit(solution)/shard_map/pallas_call | solution.py:79
  72.8 2.3 %reshape.103 = bf16[4,8,32768]{2,1,0:T(8,128)(2,1)} reshape(bf16[4,8,256,128]{3,2,1,0:T(8,128)(2,1)S(1)} %shard_map.37) | data formatting | bytes 4194304 | tf_op jit(solution)/shard_map/reshape | solution.py:160
  75.0 3.2 %copy.13 = bf16[4,8,32768]{2,0,1:T(4,128)(2,1)S(1)} copy(bf16[4,8,32768]{2,1,0:T(8,128)(2,1)} %reshape.103) | data formatting | bytes 4194304 | tf_op jit(solution)/shard_map/reshape | solution.py:160
  78.3 34.7 %all_to_all.12 = bf16[4,8,32768]{2,0,1:T(4,128)(2,1)S(1)} all-to-all(bf16[4,8,32768]{2,0,1:T(4,128)(2,1)S(1)} %copy.13), channel_id=1, replica_groups=mesh['dm'=32,'beam'=8] {'beam'}, dimensions={1} | all-to-all | bytes 4194304 | tf_op jit(solution)/shard_map/all_to_all | solution.py:161
  112.9 1.3 %copy.26 = bf16[4,1,262144]{2,0,1:T(4,128)(2,1)} copy(bf16[4,1,262144]{2,0,1:T(4,128)(2,1)S(1)} %bitcast.50) | data formatting | bytes 4194304
  (34 shorter events, 1.1 us)
Async XLA Ops:
  3.4 4.5 %collective-permute-start = (bf16[8,16,512]{2,1,0:T(8,128)(2,1)S(1)}, bf16[8,16,512]{2,1,0:T(8,128)(2,1)S(1)}, u32[]{:S(2)}, u32[]{:S(2)}) collective-permute-start(bf16[8,16,512]{2,1,0:T(8,128)(2,1)S(1)} %bitcast.51), channel_id=1, source_target_pairs={{0,128},{8,136},{16,144},{24,152},{32,160},{40,168},{48,176},{56,1... | collective-permute-start | bytes 393224 | tf_op jit(solution)/shard_map/ppermute | solution.py:126
  7.9 10.6 %collective-permute-start.1 = (bf16[2,8,16,512]{3,2,1,0:T(8,128)(2,1)S(1)}, bf16[2,8,16,512]{3,2,1,0:T(8,128)(2,1)S(1)}, u32[]{:S(2)}, u32[]{:S(2)}) collective-permute-start(bf16[2,8,16,512]{3,2,1,0:T(8,128)(2,1)S(1)} %pad_maximum_fusion.6), channel_id=1, source_target_pairs={{0,112},{8,120},{16,0},{24,8},{32,16},{40,24},{48,32},{56,40},{64,... | collective-permute-start | bytes 786440 | tf_op jit(solution)/shard_map/ppermute | solution.py:131
  14.4 7.5 %collective-permute-start.4 = (bf16[2,8,16,512]{3,2,1,0:T(8,128)(2,1)S(1)}, bf16[2,8,16,512]{3,2,1,0:T(8,128)(2,1)S(1)}, u32[]{:S(2)}, u32[]{:S(2)}) collective-permute-start(bf16[2,8,16,512]{3,2,1,0:T(8,128)(2,1)S(1)} %pad_maximum_fusion.6), channel_id=1, source_target_pairs={{0,16},{8,24},{16,32},{24,40},{32,48},{40,56},{48,64},{56,72},{64,... | collective-permute-start | bytes 786440 | tf_op jit(solution)/shard_map/ppermute | solution.py:130
  18.5 6.7 %collective-permute-start.2 = (bf16[2,8,16,512]{3,2,1,0:T(8,128)(2,1)S(1)}, bf16[2,8,16,512]{3,2,1,0:T(8,128)(2,1)S(1)}, u32[]{:S(2)}, u32[]{:S(2)}) collective-permute-start(bf16[2,8,16,512]{3,2,1,0:T(8,128)(2,1)S(1)} %collective-permute-done.1), channel_id=1, source_target_pairs={{0,112},{8,120},{16,0},{24,8},{32,16},{40,24},{48,32},{56,40},{64,... | collective-permute-start | bytes 786440 | tf_op jit(solution)/shard_map/ppermute | solution.py:131
  21.9 6.5 %collective-permute-start.5 = (bf16[2,8,16,512]{3,2,1,0:T(8,128)(2,1)S(1)}, bf16[2,8,16,512]{3,2,1,0:T(8,128)(2,1)S(1)}, u32[]{:S(2)}, u32[]{:S(2)}) collective-permute-start(bf16[2,8,16,512]{3,2,1,0:T(8,128)(2,1)S(1)} %collective-permute-done.4), channel_id=1, source_target_pairs={{0,16},{8,24},{16,32},{24,40},{32,48},{40,56},{48,64},{56,72},{64,... | collective-permute-start | bytes 786440 | tf_op jit(solution)/shard_map/ppermute | solution.py:130
  25.2 6.4 %collective-permute-start.3 = (bf16[2,8,16,512]{3,2,1,0:T(8,128)(2,1)S(1)}, bf16[2,8,16,512]{3,2,1,0:T(8,128)(2,1)S(1)}, u32[]{:S(2)}, u32[]{:S(2)}) collective-permute-start(bf16[2,8,16,512]{3,2,1,0:T(8,128)(2,1)S(1)} %collective-permute-done.2), channel_id=1, source_target_pairs={{0,112},{8,120},{16,0},{24,8},{32,16},{40,24},{48,32},{56,40},{64,... | collective-permute-start | bytes 786440 | tf_op jit(solution)/shard_map/ppermute | solution.py:131
  28.4 6.5 %collective-permute-start.6 = (bf16[2,8,16,512]{3,2,1,0:T(8,128)(2,1)S(1)}, bf16[2,8,16,512]{3,2,1,0:T(8,128)(2,1)S(1)}, u32[]{:S(2)}, u32[]{:S(2)}) collective-permute-start(bf16[2,8,16,512]{3,2,1,0:T(8,128)(2,1)S(1)} %collective-permute-done.5), channel_id=1, source_target_pairs={{0,16},{8,24},{16,32},{24,40},{32,48},{40,56},{48,64},{56,72},{64,... | collective-permute-start | bytes 786440 | tf_op jit(solution)/shard_map/ppermute | solution.py:130
  31.7 5.4 %collective-permute-start.8 = (bf16[8,16,512]{2,1,0:T(8,128)(2,1)S(1)}, bf16[8,16,512]{2,1,0:T(8,128)(2,1)S(1)}, u32[]{:S(2)}, u32[]{:S(2)}) collective-permute-start(bf16[8,16,512]{2,1,0:T(8,128)(2,1)S(1)} %slice_bitcast_fusion), channel_id=1, source_target_pairs={{0,112},{8,120},{16,0},{24,8},{32,16},{40,24},{48,32},{56,40},{64,... | collective-permute-start | bytes 393224 | tf_op jit(solution)/shard_map/ppermute | solution.py:133
  34.9 5.7 %collective-permute-start.7 = (bf16[8,16,512]{2,1,0:T(8,128)(2,1)S(1)}, bf16[8,16,512]{2,1,0:T(8,128)(2,1)S(1)}, u32[]{:S(2)}, u32[]{:S(2)}) collective-permute-start(bf16[8,16,512]{2,1,0:T(8,128)(2,1)S(1)} %slice_bitcast_fusion.1), channel_id=1, source_target_pairs={{0,16},{8,24},{16,32},{24,40},{32,48},{40,56},{48,64},{56,72},{64,... | collective-permute-start | bytes 393224 | tf_op jit(solution)/shard_map/ppermute | solution.py:133
  40.7 8.8 %copy-start = (bf16[8,2,8,16,512]{4,3,2,1,0:T(8,128)(2,1)}, bf16[8,2,8,16,512]{4,3,2,1,0:T(8,128)(2,1)S(1)}, u32[]{:S(2)}) copy-start(bf16[8,2,8,16,512]{4,3,2,1,0:T(8,128)(2,1)S(1)} %bitcast_dynamic-update-slice_fusion) | copy-start | bytes 6291460
  40.7 13.5 %collective-permute-start.9 = (bf16[16,8,16,512]{3,2,1,0:T(8,128)(2,1)S(1)}, bf16[16,8,16,512]{3,2,1,0:T(8,128)(2,1)}, u32[]{:S(2)}, u32[]{:S(2)}) collective-permute-start(bf16[16,8,16,512]{3,2,1,0:T(8,128)(2,1)S(1)} %bitcast.48), channel_id=1, source_target_pairs={{0,8},{8,0},{16,24},{24,16},{32,40},{40,32},{48,56},{56,48},{64,72... | collective-permute-start | bytes 6291464 | tf_op jit(solution)/shard_map/ppermute | solution.py:137
  49.7 4.5 %copy-start.2 = (s32[4]{0:T(128)S(1)}, s32[4]{0:T(128)}, u32[]{:S(2)}) copy-start(s32[4]{0:T(128)} %chirp_ref.1) | copy-start | bytes 52
  54.2 1.6 %copy-start.1 = (bf16[8,2,8,16,512]{4,3,2,1,0:T(8,128)(2,1)S(1)}, bf16[8,2,8,16,512]{4,3,2,1,0:T(8,128)(2,1)}, u32[]{:S(2)}) copy-start(bf16[8,2,8,16,512]{4,3,2,1,0:T(8,128)(2,1)} %copy-done) | copy-start | bytes 6291460

commit v4 on v3

--- a/solution.py
+++ b/solution.py
@@ -65,7 +65,7 @@
         even = pair_ref[pl.ds(0, rows, stride=2), :]
         odd = pair_ref[pl.ds(1, rows, stride=2), :]
         both = jnp.where(lane < bins, even, odd) / RATE
-        out_ref[d] = both.reshape(beams, chans // 2, 2 * bins).astype(out_ref.dtype)
+        out_ref[:, d] = both.reshape(beams, chans // 2, 2 * bins).astype(out_ref.dtype)
 
 
 def detect(table, swap, mine, theirs, responses, chirp_len, backward):
@@ -78,7 +78,7 @@
     bytes_accessed = 2 * (2 * mine.size + responses.size + backward.size + trials * beams * chans * bins)
     return pl.pallas_call(
         detect_kernel,
-        out_shape=jax.ShapeDtypeStruct((trials, beams, chans // 2, 2 * bins), jnp.bfloat16),
+        out_shape=jax.ShapeDtypeStruct((beams, trials, chans // 2, 2 * bins), jnp.bfloat16),
         grid_spec=pltpu.PrefetchScalarGridSpec(
             num_scalar_prefetch=3,
             grid=(chans // step,),
@@ -89,7 +89,7 @@
                 pl.BlockSpec((width, width), lambda n, cl, tb, sw: (0, 0)),
             ],
             out_specs=pl.BlockSpec(
-                (trials, beams, step // 2, 2 * bins), lambda n, cl, tb, sw: (0, 0, n, 0)
+                (beams, trials, step // 2, 2 * bins), lambda n, cl, tb, sw: (0, 0, n, 0)
             ),
             scratch_shapes=[pltpu.VMEM((beams * step, 2 * bins), jnp.float32)],
         ),
@@ -149,16 +149,28 @@
         voltages.reshape(-1, 2 * length), forward, preferred_element_type=jnp.float32
     ).astype(jnp.bfloat16)
     local = local.reshape(chans_local, beams, 2 * length).transpose(1, 0, 2)
+    resp = responses.reshape(trials, chans, 2 * length)
+    local, resp, backward = lax.optimization_barrier((local, resp, backward))
     mine, theirs = gather_spectra(local, count)
     x_me, z_me, c_me = coords(lax.axis_index("dm"), z_count)
     block = jnp.arange(count // 2, dtype=jnp.int32)
     table = ((block % z_count - z_me) % z_count) * 2 + ((block // z_count) ^ x_me)
     swap = jnp.reshape(c_me, (1,)).astype(jnp.int32)
-    detected = detect(
-        table, swap, mine, theirs, responses.reshape(trials, chans, 2 * length), chirp_len, backward
-    )
-    flattened = detected.reshape(trials, beams, -1)
-    return lax.all_to_all(flattened, "beam", split_axis=1, concat_axis=2, tiled=True)
+    detected = detect(table, swap, mine, theirs, resp, chirp_len, backward)
+    return exchange_beams(detected.reshape(beams, trials, -1))[:, None]
+
+
+def exchange_beams(detected):
+    beams = detected.shape[0]
+    me = lax.axis_index("beam")
+    pieces = [lax.dynamic_index_in_dim(detected, me, 0, keepdims=False)]
+    for shift in range(1, beams):
+        part = lax.dynamic_index_in_dim(detected, (me + shift) % beams, 0, keepdims=False)
+        pieces.append(lax.ppermute(part, "beam", [(b, (b + shift) % beams) for b in range(beams)]))
+    stacked = jnp.stack(pieces[:1] + pieces[:0:-1])
+    doubled = jnp.concatenate([stacked, stacked], 0)
+    ordered = lax.dynamic_slice_in_dim(doubled, (beams - me) % beams, beams, 0)
+    return ordered.transpose(1, 0, 2).reshape(detected.shape[1], -1)
 
 
 def solution(mesh):

time: 115 us -> 135 us (1.17)
  the two profiles are of different devices: /device:TPU:1 before, /device:TPU:24 now
where the time goes in v4:
time: 135 us; the launch traced here: 134 us
  waiting for transfers between devices  52.7 us (39%)
  starting transfers between devices  31.3 us (23%)
  local copies, waits for them, and re-layouts  30.6 us (23%)
  Pallas kernels  16.9 us (13%)
  other arithmetic  2.27 us (2%)
    ppermute x7, waiting for transfers between devices, exchange_beams(): lax.ppermute(part, 'beam', [(b, (b + shift) % beams) for b in range(beams)])  27 us
    pallas_call x1, Pallas kernels, detect(): pl.pallas_call(detect_kernel, out_shape=jax.ShapeDtypeStruct((beams, tria...  16.9 us
    unnamed x28, local copies, waits for them, and re-layouts  15.9 us
    ppermute x3, starting transfers between devices, gather_spectra(): from_above.append(lax.ppermute(from_above[-1], 'dm', down))  13.3 us
    ppermute x3, waiting for transfers between devices, gather_spectra(): from_above.append(lax.ppermute(from_above[-1], 'dm', down))  12.6 us
    ppermute x7, starting transfers between devices, exchange_beams(): lax.ppermute(part, 'beam', [(b, (b + shift) % beams) for b in range(beams)])  12.2 us
    ppermute x1, waiting for transfers between devices, gather_spectra(): lax.ppermute(from_below[-1][0], 'dm', up)  4.05 us
    ppermute x1, starting transfers between devices, gather_spectra(): lax.ppermute(from_above[-1][1], 'dm', down)  3.77 us
  transfers between devices with their start and end apart: 17, of which 10 were waited for; matrix products, arithmetic and copies ran while one was open for 4% of the time, Pallas kernels for 0%

profile of v4, /device:TPU:24, one launch (start us, length us, event | category | flops | bytes accessed | tf_op | source)
XLA Modules:
  0.0 134.4 jit_solution(13912787494025228093)
XLA Ops:
  6.1 2.6 %reshape.98.resp_ref = bf16[4,512,512]{2,1,0:T(8,128)(2,1)} reshape(bf16[4,512,2,256]{3,2,1,0:T(2,128)(2,1)S(1)} %copy-done.3) | data formatting | bytes 4194304 | tf_op jit(solution)/shard_map/reshape | solution.py:152
  10.3 3.7 %collective-permute-done = bf16[8,16,512]{2,1,0:T(8,128)(2,1)S(1)} collective-permute-done((bf16[8,16,512]{2,1,0:T(8,128)(2,1)S(1)}, bf16[8,16,512]{2,1,0:T(8,128)(2,1)S(1)}, u32[]{:S(2)}, u32[]{:S(2)}) %collective-permute-start) | collective-permute-done | bytes 131104 | tf_op jit(solution)/shard_map/ppermute | solution.py:126
  14.1 5.9 %collective-permute-start.1 = (bf16[2,8,16,512]{3,2,1,0:T(8,128)(2,1)S(1)}, bf16[2,8,16,512]{3,2,1,0:T(8,128)(2,1)S(1)}, u32[]{:S(2)}, u32[]{:S(2)}) collective-permute-start(bf16[2,8,16,512]{3,2,1,0:T(8,128)(2,1)S(1)} %pad_maximum_fusion.6), channel_id=1, source_target_pairs={{0,112},{8,120},{16,0},{24,8},{32,16},{40,24},{48,32},{56,40},{64,... | collective-permute-start | bytes 786440 | tf_op jit(solution)/shard_map/ppermute | solution.py:131
  20.0 4.7 %collective-permute-done.1 = bf16[2,8,16,512]{3,2,1,0:T(8,128)(2,1)S(1)} collective-permute-done((bf16[2,8,16,512]{3,2,1,0:T(8,128)(2,1)S(1)}, bf16[2,8,16,512]{3,2,1,0:T(8,128)(2,1)S(1)}, u32[]{:S(2)}, u32[]{:S(2)}) %collective-permute-start.1) | collective-permute-done | bytes 262176 | tf_op jit(solution)/shard_map/ppermute | solution.py:131
  24.7 3.7 %collective-permute-start.2 = (bf16[2,8,16,512]{3,2,1,0:T(8,128)(2,1)S(1)}, bf16[2,8,16,512]{3,2,1,0:T(8,128)(2,1)S(1)}, u32[]{:S(2)}, u32[]{:S(2)}) collective-permute-start(bf16[2,8,16,512]{3,2,1,0:T(8,128)(2,1)S(1)} %collective-permute-done.1), channel_id=1, source_target_pairs={{0,112},{8,120},{16,0},{24,8},{32,16},{40,24},{48,32},{56,40},{64,... | collective-permute-start | bytes 786440 | tf_op jit(solution)/shard_map/ppermute | solution.py:131
  28.5 3.9 %collective-permute-done.2 = bf16[2,8,16,512]{3,2,1,0:T(8,128)(2,1)S(1)} collective-permute-done((bf16[2,8,16,512]{3,2,1,0:T(8,128)(2,1)S(1)}, bf16[2,8,16,512]{3,2,1,0:T(8,128)(2,1)S(1)}, u32[]{:S(2)}, u32[]{:S(2)}) %collective-permute-start.2) | collective-permute-done | bytes 262176 | tf_op jit(solution)/shard_map/ppermute | solution.py:131
  32.3 3.7 %collective-permute-start.3 = (bf16[2,8,16,512]{3,2,1,0:T(8,128)(2,1)S(1)}, bf16[2,8,16,512]{3,2,1,0:T(8,128)(2,1)S(1)}, u32[]{:S(2)}, u32[]{:S(2)}) collective-permute-start(bf16[2,8,16,512]{3,2,1,0:T(8,128)(2,1)S(1)} %collective-permute-done.2), channel_id=1, source_target_pairs={{0,112},{8,120},{16,0},{24,8},{32,16},{40,24},{48,32},{56,40},{64,... | collective-permute-start | bytes 786440 | tf_op jit(solution)/shard_map/ppermute | solution.py:131
  36.2 4.0 %collective-permute-done.3 = bf16[2,8,16,512]{3,2,1,0:T(8,128)(2,1)S(1)} collective-permute-done((bf16[2,8,16,512]{3,2,1,0:T(8,128)(2,1)S(1)}, bf16[2,8,16,512]{3,2,1,0:T(8,128)(2,1)S(1)}, u32[]{:S(2)}, u32[]{:S(2)}) %collective-permute-start.3) | collective-permute-done | bytes 262176 | tf_op jit(solution)/shard_map/ppermute | solution.py:131
  40.2 3.8 %collective-permute-start.8 = (bf16[8,16,512]{2,1,0:T(8,128)(2,1)S(1)}, bf16[8,16,512]{2,1,0:T(8,128)(2,1)S(1)}, u32[]{:S(2)}, u32[]{:S(2)}) collective-permute-start(bf16[8,16,512]{2,1,0:T(8,128)(2,1)S(1)} %slice_bitcast_fusion), channel_id=1, source_target_pairs={{0,112},{8,120},{16,0},{24,8},{32,16},{40,24},{48,32},{56,40},{64,... | collective-permute-start | bytes 393224 | tf_op jit(solution)/shard_map/ppermute | solution.py:133
  44.4 2.1 %collective-permute-done.8 = bf16[8,16,512]{2,1,0:T(8,128)(2,1)S(1)} collective-permute-done((bf16[8,16,512]{2,1,0:T(8,128)(2,1)S(1)}, bf16[8,16,512]{2,1,0:T(8,128)(2,1)S(1)}, u32[]{:S(2)}, u32[]{:S(2)}) %collective-permute-start.8) | collective-permute-done | bytes 131104 | tf_op jit(solution)/shard_map/ppermute | solution.py:133
  46.5 4.0 %collective-permute-done.7 = bf16[8,16,512]{2,1,0:T(8,128)(2,1)S(1)} collective-permute-done((bf16[8,16,512]{2,1,0:T(8,128)(2,1)S(1)}, bf16[8,16,512]{2,1,0:T(8,128)(2,1)S(1)}, u32[]{:S(2)}, u32[]{:S(2)}) %collective-permute-start.7) | collective-permute-done | bytes 131104 | tf_op jit(solution)/shard_map/ppermute | solution.py:133
  52.3 2.9 %collective-permute-done.9.theirs_ref = bf16[16,8,16,512]{3,2,1,0:T(8,128)(2,1)} collective-permute-done((bf16[16,8,16,512]{3,2,1,0:T(8,128)(2,1)S(1)}, bf16[16,8,16,512]{3,2,1,0:T(8,128)(2,1)}, u32[]{:S(2)}, u32[]{:S(2)}) %collective-permute-start.9) | collective-permute-done | bytes 2097184 | tf_op jit(solution)/shard_map/ppermute | solution.py:137
  55.2 1.6 %copy-done.1 = bf16[8,2,8,16,512]{4,3,2,1,0:T(8,128)(2,1)S(1)} copy-done((bf16[8,2,8,16,512]{4,3,2,1,0:T(8,128)(2,1)S(1)}, bf16[8,2,8,16,512]{4,3,2,1,0:T(8,128)(2,1)}, u32[]{:S(2)}) %copy-start.1) | copy-done | bytes 2097176
  56.8 16.9 %shard_map.37 = bf16[8,4,256,128]{3,2,1,0:T(8,128)(2,1)S(1)} custom-call(s32[4]{0:T(128)S(1)} %copy-done.2, s32[16]{0:T(128)S(1)} %fusion.18.table_ref, s32[1]{0:T(128)} %bitcast.swap_ref, bf16[16,8,16,512]{3,2,1,0:T(8,128)(2,1)S(1)} %bitcast.84, bf16[16,8,16,512]{3,2,1,0:T(8,128)(2,1)} %collective-permute-done.9.theirs_ref, ...), custom_call_target="tpu_custom_call" | custom-call | flops 8589934592 | bytes 8912896 | tf_op jit(solution)/shard_map/pallas_call | solution.py:79
  73.7 2.1 %reshape.100 = bf16[8,4,32768]{2,1,0:T(4,128)(2,1)} reshape(bf16[8,4,256,128]{3,2,1,0:T(8,128)(2,1)S(1)} %shard_map.37) | data formatting | bytes 4194304 | tf_op jit(solution)/shard_map/reshape | solution.py:160
  75.8 2.9 %dynamic-slice_bitcast_fusion = (bf16[4,32768]{1,0:T(4,128)(2,1)S(1)}, bf16[16,4,32768]{2,1,0:T(4,128)(2,1)}, bf16[4,32768]{1,0:T(4,128)(2,1)S(1)}, bf16[4,32768...) fusion(bf16[8,4,32768]{2,1,0:T(4,128)(2,1)} %reshape.100, ...), kind=kLoop, calls=%fused_computation.43 | loop fusion | bytes 4194336 | tf_op jit(solution)/shard_map/jit(dynamic_index_in_dim)/squeeze | solution.py:168
  78.8 3.2 %collective-permute-start.10 = (bf16[4,32768]{1,0:T(4,128)(2,1)S(1)}, bf16[4,32768]{1,0:T(4,128)(2,1)S(1)}, u32[]{:S(2)}, u32[]{:S(2)}) collective-permute-start(bf16[4,32768]{1,0:T(4,128)(2,1)S(1)} %get-tuple-element.18), channel_id=1, source_target_pairs={{0,7},{1,0},{2,1},{3,2},{4,3},{5,4},{6,5},{7,6},{8,15},{9,8},{10,9... | collective-permute-start | bytes 786440 | tf_op jit(solution)/shard_map/ppermute | solution.py:169
  82.3 2.2 %collective-permute-start.15 = (bf16[4,32768]{1,0:T(4,128)(2,1)S(1)}, bf16[4,32768]{1,0:T(4,128)(2,1)S(1)}, u32[]{:S(2)}, u32[]{:S(2)}) collective-permute-start(bf16[4,32768]{1,0:T(4,128)(2,1)S(1)} %get-tuple-element.13), channel_id=1, source_target_pairs={{0,2},{1,3},{2,4},{3,5},{4,6},{5,7},{6,0},{7,1},{8,10},{9,11},{10,... | collective-permute-start | bytes 786440 | tf_op jit(solution)/shard_map/ppermute | solution.py:169
  84.5 3.0 %collective-permute-start.14 = (bf16[4,32768]{1,0:T(4,128)(2,1)S(1)}, bf16[4,32768]{1,0:T(4,128)(2,1)S(1)}, u32[]{:S(2)}, u32[]{:S(2)}) collective-permute-start(bf16[4,32768]{1,0:T(4,128)(2,1)S(1)} %get-tuple-element.14), channel_id=1, source_target_pairs={{0,3},{1,4},{2,5},{3,6},{4,7},{5,0},{6,1},{7,2},{8,11},{9,12},{10,... | collective-permute-start | bytes 786440 | tf_op jit(solution)/shard_map/ppermute | solution.py:169
  87.5 3.5 %collective-permute-start.13 = (bf16[4,32768]{1,0:T(4,128)(2,1)S(1)}, bf16[4,32768]{1,0:T(4,128)(2,1)S(1)}, u32[]{:S(2)}, u32[]{:S(2)}) collective-permute-start(bf16[4,32768]{1,0:T(4,128)(2,1)S(1)} %get-tuple-element.15), channel_id=1, source_target_pairs={{0,4},{1,5},{2,6},{3,7},{4,0},{5,1},{6,2},{7,3},{8,12},{9,13},{10,... | collective-permute-start | bytes 786440 | tf_op jit(solution)/shard_map/ppermute | solution.py:169
  91.8 15.9 %collective-permute-done.11 = bf16[4,32768]{1,0:T(4,128)(2,1)S(1)} collective-permute-done((bf16[4,32768]{1,0:T(4,128)(2,1)S(1)}, bf16[4,32768]{1,0:T(4,128)(2,1)S(1)}, u32[]{:S(2)}, u32[]{:S(2)}) %collective-permute-start.11) | collective-permute-done | bytes 262176 | tf_op jit(solution)/shard_map/ppermute | solution.py:169
  108.5 11.0 %collective-permute-done.12 = bf16[4,32768]{1,0:T(4,128)(2,1)S(1)} collective-permute-done((bf16[4,32768]{1,0:T(4,128)(2,1)S(1)}, bf16[4,32768]{1,0:T(4,128)(2,1)S(1)}, u32[]{:S(2)}, u32[]{:S(2)}) %collective-permute-start.12) | collective-permute-done | bytes 262176 | tf_op jit(solution)/shard_map/ppermute | solution.py:169
  123.5 1.7 %dynamic-slice_dynamic-update-slice_fusion.1 = bf16[16,4,32768]{2,1,0:T(4,128)(2,1)} fusion(bf16[16,4,32768]{2,1,0:T(4,128)(2,1)} %bitcast_dynamic-update-slice_fusion, bf16[8,4,32768]{2,1,0:T(4,128)(2,1)} %reshape.100, s32[]{:T(128)S(6)} %select_n.182), kind=kLoop, calls=%fused_computation.58 | loop fusion | bytes 524292
  130.7 3.6 %constant_dynamic-slice_fusion = bf16[8,4,32768]{2,1,0:T(4,128)(2,1)} fusion(bf16[16,4,32768]{2,1,0:T(4,128)(2,1)} %bitcast_dynamic-update-slice_fusion.1, s32[]{:T(128)S(6)} %select_n.198), kind=kLoop, calls=%fused_computation.68 | loop fusion | bytes 4194308 | tf_op jit(solution)/shard_map/dynamic_slice | solution.py:172
  (64 shorter events, 21.3 us)
Async XLA Ops:
  3.1 3.0 %copy-start.3 = (bf16[4,512,2,256]{3,2,1,0:T(2,128)(2,1)S(1)}, bf16[4,512,2,256]{3,2,1,0:T(2,128)(2,1)}, u32[]{:S(2)}) copy-start(bf16[4,512,2,256]{3,2,1,0:T(2,128)(2,1)} %param.4) | copy-start | bytes 6291460
  8.7 46.5 %copy-start.2 = (s32[4]{0:T(128)S(1)}, s32[4]{0:T(128)}, u32[]{:S(2)}) copy-start(s32[4]{0:T(128)} %chirp_ref.1) | copy-start | bytes 52
  8.7 5.3 %collective-permute-start = (bf16[8,16,512]{2,1,0:T(8,128)(2,1)S(1)}, bf16[8,16,512]{2,1,0:T(8,128)(2,1)S(1)}, u32[]{:S(2)}, u32[]{:S(2)}) collective-permute-start(bf16[8,16,512]{2,1,0:T(8,128)(2,1)S(1)} %bitcast.85), channel_id=1, source_target_pairs={{0,128},{8,136},{16,144},{24,152},{32,160},{40,168},{48,176},{56,1... | collective-permute-start | bytes 393224 | tf_op jit(solution)/shard_map/ppermute | solution.py:126
  14.1 10.6 %collective-permute-start.1 = (bf16[2,8,16,512]{3,2,1,0:T(8,128)(2,1)S(1)}, bf16[2,8,16,512]{3,2,1,0:T(8,128)(2,1)S(1)}, u32[]{:S(2)}, u32[]{:S(2)}) collective-permute-start(bf16[2,8,16,512]{3,2,1,0:T(8,128)(2,1)S(1)} %pad_maximum_fusion.6), channel_id=1, source_target_pairs={{0,112},{8,120},{16,0},{24,8},{32,16},{40,24},{48,32},{56,40},{64,... | collective-permute-start | bytes 786440 | tf_op jit(solution)/shard_map/ppermute | solution.py:131
  20.0 8.4 %collective-permute-start.4 = (bf16[2,8,16,512]{3,2,1,0:T(8,128)(2,1)S(1)}, bf16[2,8,16,512]{3,2,1,0:T(8,128)(2,1)S(1)}, u32[]{:S(2)}, u32[]{:S(2)}) collective-permute-start(bf16[2,8,16,512]{3,2,1,0:T(8,128)(2,1)S(1)} %pad_maximum_fusion.6), channel_id=1, source_target_pairs={{0,16},{8,24},{16,32},{24,40},{32,48},{40,56},{48,64},{56,72},{64,... | collective-permute-start | bytes 786440 | tf_op jit(solution)/shard_map/ppermute | solution.py:130
  24.7 7.6 %collective-permute-start.2 = (bf16[2,8,16,512]{3,2,1,0:T(8,128)(2,1)S(1)}, bf16[2,8,16,512]{3,2,1,0:T(8,128)(2,1)S(1)}, u32[]{:S(2)}, u32[]{:S(2)}) collective-permute-start(bf16[2,8,16,512]{3,2,1,0:T(8,128)(2,1)S(1)} %collective-permute-done.1), channel_id=1, source_target_pairs={{0,112},{8,120},{16,0},{24,8},{32,16},{40,24},{48,32},{56,40},{64,... | collective-permute-start | bytes 786440 | tf_op jit(solution)/shard_map/ppermute | solution.py:131
  28.4 7.6 %collective-permute-start.5 = (bf16[2,8,16,512]{3,2,1,0:T(8,128)(2,1)S(1)}, bf16[2,8,16,512]{3,2,1,0:T(8,128)(2,1)S(1)}, u32[]{:S(2)}, u32[]{:S(2)}) collective-permute-start(bf16[2,8,16,512]{3,2,1,0:T(8,128)(2,1)S(1)} %collective-permute-done.4), channel_id=1, source_target_pairs={{0,16},{8,24},{16,32},{24,40},{32,48},{40,56},{48,64},{56,72},{64,... | collective-permute-start | bytes 786440 | tf_op jit(solution)/shard_map/ppermute | solution.py:130
  32.3 7.9 %collective-permute-start.3 = (bf16[2,8,16,512]{3,2,1,0:T(8,128)(2,1)S(1)}, bf16[2,8,16,512]{3,2,1,0:T(8,128)(2,1)S(1)}, u32[]{:S(2)}, u32[]{:S(2)}) collective-permute-start(bf16[2,8,16,512]{3,2,1,0:T(8,128)(2,1)S(1)} %collective-permute-done.2), channel_id=1, source_target_pairs={{0,112},{8,120},{16,0},{24,8},{32,16},{40,24},{48,32},{56,40},{64,... | collective-permute-start | bytes 786440 | tf_op jit(solution)/shard_map/ppermute | solution.py:131
  36.0 8.2 %collective-permute-start.6 = (bf16[2,8,16,512]{3,2,1,0:T(8,128)(2,1)S(1)}, bf16[2,8,16,512]{3,2,1,0:T(8,128)(2,1)S(1)}, u32[]{:S(2)}, u32[]{:S(2)}) collective-permute-start(bf16[2,8,16,512]{3,2,1,0:T(8,128)(2,1)S(1)} %collective-permute-done.5), channel_id=1, source_target_pairs={{0,16},{8,24},{16,32},{24,40},{32,48},{40,56},{48,64},{56,72},{64,... | collective-permute-start | bytes 786440 | tf_op jit(solution)/shard_map/ppermute | solution.py:130
  40.2 6.3 %collective-permute-start.8 = (bf16[8,16,512]{2,1,0:T(8,128)(2,1)S(1)}, bf16[8,16,512]{2,1,0:T(8,128)(2,1)S(1)}, u32[]{:S(2)}, u32[]{:S(2)}) collective-permute-start(bf16[8,16,512]{2,1,0:T(8,128)(2,1)S(1)} %slice_bitcast_fusion), channel_id=1, source_target_pairs={{0,112},{8,120},{16,0},{24,8},{32,16},{40,24},{48,32},{56,40},{64,... | collective-permute-start | bytes 393224 | tf_op jit(solution)/shard_map/ppermute | solution.py:133
  44.3 6.3 %collective-permute-start.7 = (bf16[8,16,512]{2,1,0:T(8,128)(2,1)S(1)}, bf16[8,16,512]{2,1,0:T(8,128)(2,1)S(1)}, u32[]{:S(2)}, u32[]{:S(2)}) collective-permute-start(bf16[8,16,512]{2,1,0:T(8,128)(2,1)S(1)} %slice_bitcast_fusion.1), channel_id=1, source_target_pairs={{0,16},{8,24},{16,32},{24,40},{32,48},{40,56},{48,64},{56,72},{64,... | collective-permute-start | bytes 393224 | tf_op jit(solution)/shard_map/ppermute | solution.py:133
  50.6 4.6 %collective-permute-start.9 = (bf16[16,8,16,512]{3,2,1,0:T(8,128)(2,1)S(1)}, bf16[16,8,16,512]{3,2,1,0:T(8,128)(2,1)}, u32[]{:S(2)}, u32[]{:S(2)}) collective-permute-start(bf16[16,8,16,512]{3,2,1,0:T(8,128)(2,1)S(1)} %bitcast.83), channel_id=1, source_target_pairs={{0,8},{8,0},{16,24},{24,16},{32,40},{40,32},{48,56},{56,48},{64,72... | collective-permute-start | bytes 6291464 | tf_op jit(solution)/shard_map/ppermute | solution.py:137
  50.9 1.3 copy-start
  55.2 1.6 %copy-start.1 = (bf16[8,2,8,16,512]{4,3,2,1,0:T(8,128)(2,1)S(1)}, bf16[8,2,8,16,512]{4,3,2,1,0:T(8,128)(2,1)}, u32[]{:S(2)}) copy-start(bf16[8,2,8,16,512]{4,3,2,1,0:T(8,128)(2,1)} %copy-done) | copy-start | bytes 6291460
  78.8 12.2 %collective-permute-start.10 = (bf16[4,32768]{1,0:T(4,128)(2,1)S(1)}, bf16[4,32768]{1,0:T(4,128)(2,1)S(1)}, u32[]{:S(2)}, u32[]{:S(2)}) collective-permute-start(bf16[4,32768]{1,0:T(4,128)(2,1)S(1)} %get-tuple-element.18), channel_id=1, source_target_pairs={{0,7},{1,0},{2,1},{3,2},{4,3},{5,4},{6,5},{7,6},{8,15},{9,8},{10,9... | collective-permute-start | bytes 786440 | tf_op jit(solution)/shard_map/ppermute | solution.py:169
  82.0 40.7 %collective-permute-start.16 = (bf16[4,32768]{1,0:T(4,128)(2,1)S(1)}, bf16[4,32768]{1,0:T(4,128)(2,1)S(1)}, u32[]{:S(2)}, u32[]{:S(2)}) collective-permute-start(bf16[4,32768]{1,0:T(4,128)(2,1)S(1)} %get-tuple-element.11), channel_id=1, source_target_pairs={{0,1},{1,2},{2,3},{3,4},{4,5},{5,6},{6,7},{7,0},{8,9},{9,10},{10,1... | collective-permute-start | bytes 786440 | tf_op jit(solution)/shard_map/ppermute | solution.py:169
  82.3 39.6 %collective-permute-start.15 = (bf16[4,32768]{1,0:T(4,128)(2,1)S(1)}, bf16[4,32768]{1,0:T(4,128)(2,1)S(1)}, u32[]{:S(2)}, u32[]{:S(2)}) collective-permute-start(bf16[4,32768]{1,0:T(4,128)(2,1)S(1)} %get-tuple-element.13), channel_id=1, source_target_pairs={{0,2},{1,3},{2,4},{3,5},{4,6},{5,7},{6,0},{7,1},{8,10},{9,11},{10,... | collective-permute-start | bytes 786440 | tf_op jit(solution)/shard_map/ppermute | solution.py:169
  84.5 36.6 %collective-permute-start.14 = (bf16[4,32768]{1,0:T(4,128)(2,1)S(1)}, bf16[4,32768]{1,0:T(4,128)(2,1)S(1)}, u32[]{:S(2)}, u32[]{:S(2)}) collective-permute-start(bf16[4,32768]{1,0:T(4,128)(2,1)S(1)} %get-tuple-element.14), channel_id=1, source_target_pairs={{0,3},{1,4},{2,5},{3,6},{4,7},{5,0},{6,1},{7,2},{8,11},{9,12},{10,... | collective-permute-start | bytes 786440 | tf_op jit(solution)/shard_map/ppermute | solution.py:169
  87.5 32.8 %collective-permute-start.13 = (bf16[4,32768]{1,0:T(4,128)(2,1)S(1)}, bf16[4,32768]{1,0:T(4,128)(2,1)S(1)}, u32[]{:S(2)}, u32[]{:S(2)}) collective-permute-start(bf16[4,32768]{1,0:T(4,128)(2,1)S(1)} %get-tuple-element.15), channel_id=1, source_target_pairs={{0,4},{1,5},{2,6},{3,7},{4,0},{5,1},{6,2},{7,3},{8,12},{9,13},{10,... | collective-permute-start | bytes 786440 | tf_op jit(solution)/shard_map/ppermute | solution.py:169
  91.0 16.7 %collective-permute-start.11 = (bf16[4,32768]{1,0:T(4,128)(2,1)S(1)}, bf16[4,32768]{1,0:T(4,128)(2,1)S(1)}, u32[]{:S(2)}, u32[]{:S(2)}) collective-permute-start(bf16[4,32768]{1,0:T(4,128)(2,1)S(1)} %get-tuple-element.17), channel_id=1, source_target_pairs={{0,6},{1,7},{2,0},{3,1},{4,2},{5,3},{6,4},{7,5},{8,14},{9,15},{10,... | collective-permute-start | bytes 786440 | tf_op jit(solution)/shard_map/ppermute | solution.py:169
  107.7 11.8 %collective-permute-start.12 = (bf16[4,32768]{1,0:T(4,128)(2,1)S(1)}, bf16[4,32768]{1,0:T(4,128)(2,1)S(1)}, u32[]{:S(2)}, u32[]{:S(2)}) collective-permute-start(bf16[4,32768]{1,0:T(4,128)(2,1)S(1)} %get-tuple-element.16), channel_id=1, source_target_pairs={{0,5},{1,6},{2,7},{3,0},{4,1},{5,2},{6,3},{7,4},{8,13},{9,14},{10,... | collective-permute-start | bytes 786440 | tf_op jit(solution)/shard_map/ppermute | solution.py:169

commit v5 on v3

--- a/solution.py
+++ b/solution.py
@@ -70,22 +70,22 @@
 
 def detect(table, swap, mine, theirs, responses, chirp_len, backward):
     blocks, beams, chans_local, width = mine.shape
-    trials, chans = responses.shape[0], responses.shape[1]
+    trials = responses.shape[0]
     length = width // 2
     bins = length // RATE
     step = 2 * chans_local
-    flops = 2 * trials * beams * chans * width * width
-    bytes_accessed = 2 * (2 * mine.size + responses.size + backward.size + trials * beams * chans * bins)
+    flops = 2 * trials * beams * blocks * step * width * width
+    bytes_accessed = 2 * (2 * mine.size + blocks * (trials * step * width + trials * beams * step * bins))
     return pl.pallas_call(
         detect_kernel,
-        out_shape=jax.ShapeDtypeStruct((trials, beams, chans // 2, 2 * bins), jnp.bfloat16),
+        out_shape=jax.ShapeDtypeStruct((trials, beams, blocks * step // 2, 2 * bins), jnp.bfloat16),
         grid_spec=pltpu.PrefetchScalarGridSpec(
             num_scalar_prefetch=3,
-            grid=(chans // step,),
+            grid=(blocks,),
             in_specs=[
-                pl.BlockSpec((1, beams, chans_local, width), lambda n, cl, tb, sw: (tb[n], 0, 0, 0)),
-                pl.BlockSpec((1, beams, chans_local, width), lambda n, cl, tb, sw: (tb[n], 0, 0, 0)),
-                pl.BlockSpec((trials, step, width), lambda n, cl, tb, sw: (0, n, 0)),
+                pl.BlockSpec((1, beams, chans_local, width), lambda n, cl, tb, sw: (n, 0, 0, 0)),
+                pl.BlockSpec((1, beams, chans_local, width), lambda n, cl, tb, sw: (n, 0, 0, 0)),
+                pl.BlockSpec((trials, step, width), lambda n, cl, tb, sw: (0, tb[n], 0)),
                 pl.BlockSpec((width, width), lambda n, cl, tb, sw: (0, 0)),
             ],
             out_specs=pl.BlockSpec(
@@ -117,12 +117,11 @@
     return pairs
 
 
-def gather_spectra(own, count):
+def gather_columns(own, count):
     z_count = count // 4
     across = moves(count, lambda x, z, c, n: flat(1 - x, z, c, n))
     up = moves(count, lambda x, z, c, n: flat(x, z + 1, c, n))
     down = moves(count, lambda x, z, c, n: flat(x, z - 1, c, n))
-    partner = moves(count, lambda x, z, c, n: flat(x, z, 1 - c, n))
     pair = jnp.stack([own, lax.ppermute(own, "dm", across)])
     from_below = [pair]
     from_above = [pair]
@@ -132,9 +131,17 @@
     far = jnp.stack(
         [lax.ppermute(from_below[-1][0], "dm", up), lax.ppermute(from_above[-1][1], "dm", down)]
     )
-    column = jnp.stack(from_above + [far] + from_below[:0:-1])
-    column = column.reshape((2 * z_count,) + own.shape)
-    return column, lax.ppermute(column, "dm", partner)
+    near_count = z_count // 4 + 1
+    near = from_above[:near_count] + from_below[1:near_count]
+    near_offsets = list(range(near_count)) + [-k for k in range(1, near_count)]
+    rest = from_above[near_count:] + [far] + from_below[near_count:]
+    rest_offsets = list(range(near_count, z_count // 2)) + [z_count // 2] + [
+        -k for k in range(near_count, z_count // 2)
+    ]
+    chunks = []
+    for offsets, pieces in ((near_offsets, near), (rest_offsets, rest)):
+        chunks.append((offsets, jnp.stack(pieces).reshape((2 * len(pieces),) + own.shape)))
+    return chunks
 
 
 def shards(voltages, responses, chirp_len):
@@ -149,16 +156,26 @@
         voltages.reshape(-1, 2 * length), forward, preferred_element_type=jnp.float32
     ).astype(jnp.bfloat16)
     local = local.reshape(chans_local, beams, 2 * length).transpose(1, 0, 2)
-    mine, theirs = gather_spectra(local, count)
+    resp = responses.reshape(trials, chans, 2 * length)
     x_me, z_me, c_me = coords(lax.axis_index("dm"), z_count)
-    block = jnp.arange(count // 2, dtype=jnp.int32)
-    table = ((block % z_count - z_me) % z_count) * 2 + ((block // z_count) ^ x_me)
     swap = jnp.reshape(c_me, (1,)).astype(jnp.int32)
-    detected = detect(
-        table, swap, mine, theirs, responses.reshape(trials, chans, 2 * length), chirp_len, backward
-    )
-    flattened = detected.reshape(trials, beams, -1)
-    return lax.all_to_all(flattened, "beam", split_axis=1, concat_axis=2, tiled=True)
+    partner = moves(count, lambda x, z, c, n: flat(x, z, 1 - c, n))
+    outputs = []
+    naturals = []
+    for offsets, mine in gather_columns(local, count):
+        theirs = lax.ppermute(mine, "dm", partner)
+        offs = jnp.array(offsets, dtype=jnp.int32)[:, None]
+        x_rel = jnp.arange(2, dtype=jnp.int32)[None, :]
+        natural = ((x_rel ^ x_me) * z_count + (z_me + offs) % z_count).reshape(-1)
+        detected = detect(natural, swap, mine, theirs, resp, chirp_len, backward)
+        flattened = detected.reshape(trials, beams, -1)
+        moved = lax.all_to_all(flattened, "beam", split_axis=1, concat_axis=2, tiled=True)
+        outputs.append(moved.reshape(trials, beams, natural.shape[0], -1))
+        naturals.append(natural)
+    natural = jnp.concatenate(naturals)
+    place = jnp.zeros_like(natural).at[natural].set(jnp.arange(natural.shape[0], dtype=jnp.int32))
+    joined = jnp.take(jnp.concatenate(outputs, 2), place, axis=2)
+    return joined.reshape(trials, 1, -1)
 
 
 def solution(mesh):

time: 115 us -> 128 us (1.11)
  blocking collectives: 34.7 us -> 0 us
  local copies, waits for them, and re-layouts: 16.5 us -> 30.9 us
  starting transfers between devices: 24.9 us -> 39 us
  waiting for transfers between devices: 18.5 us -> 30.6 us
  other arithmetic: 2.27 us -> 7.7 us
    all_to_all x1 -> x0, blocking collectives: 34.7 us -> none  [shards(): lax.all_to_all(flattened, 'beam', split_axis=1, concat_axis=2, tiled=True)]
    all_to_all x0 -> x2, waiting for transfers between devices: none -> 17.9 us  [shards(): lax.all_to_all(flattened, 'beam', split_axis=1, concat_axis=2, tiled=True)]
    all_to_all x0 -> x2, starting transfers between devices: none -> 13.1 us  [shards(): lax.all_to_all(flattened, 'beam', split_axis=1, concat_axis=2, tiled=True)]
    gather x0 -> x3, local copies, waits for them, and re-layouts: none -> 9.3 us  [shards(): joined = jnp.take(jnp.concatenate(outputs, 2), place, axis=2)]
    ppermute x10 -> x11, waiting for transfers between devices: 18.5 us -> 12.7 us  [the longest x3 7.31 us: gather_columns(): from_below.append(lax.ppermute(from_below[-1], 'dm', up))]
    select_n x0 -> x5, other arithmetic: none -> 2.87 us  [the longest x2 2.77 us: shards(): joined = jnp.take(jnp.concatenate(outputs, 2), place, axis=2)]
    unnamed x13 -> x19, local copies, waits for them, and re-layouts: 3.94 us -> 5.85 us
    concatenate x1, other arithmetic: 0.04 us -> 1.47 us  [shards(): jnp.concatenate([backward[:, order], backward[:, length + order]], 1)]
  transfers between devices with their start and end apart: 10 -> 13, of which waited for: 6 -> 6; matrix products, arithmetic and copies ran while one was open for 6% -> 16% of each run, Pallas kernels for 0% -> 14%
where the time goes in v5:
time: 128 us; the launch traced here: 127 us
  starting transfers between devices  39 us (30%)
  local copies, waits for them, and re-layouts  30.9 us (24%)
  waiting for transfers between devices  30.6 us (24%)
  Pallas kernels  18 us (14%)
  other arithmetic  7.7 us (6%)
    pallas_call x2, Pallas kernels, detect(): pl.pallas_call(detect_kernel, out_shape=jax.ShapeDtypeStruct((trials, bea...  18 us
    all_to_all x2, waiting for transfers between devices, shards(): lax.all_to_all(flattened, 'beam', split_axis=1, concat_axis=2, tiled=True)  17.9 us
    all_to_all x2, starting transfers between devices, shards(): lax.all_to_all(flattened, 'beam', split_axis=1, concat_axis=2, tiled=True)  13.1 us
    ppermute x3, starting transfers between devices, gather_columns(): from_above.append(lax.ppermute(from_above[-1], 'dm', down))  12.5 us
    gather x3, local copies, waits for them, and re-layouts, shards(): joined = jnp.take(jnp.concatenate(outputs, 2), place, axis=2)  9.3 us
    ppermute x2, starting transfers between devices, shards(): theirs = lax.ppermute(mine, 'dm', partner)  8.48 us
    ppermute x3, waiting for transfers between devices, gather_columns(): from_below.append(lax.ppermute(from_below[-1], 'dm', up))  7.31 us
    unnamed x19, local copies, waits for them, and re-layouts  5.85 us
  transfers between devices with their start and end apart: 13, of which 6 were waited for; matrix products, arithmetic and copies ran while one was open for 16% of the time, Pallas kernels for 14%

profile of v5, /device:TPU:1, one launch (start us, length us, event | category | flops | bytes accessed | tf_op | source)
XLA Modules:
  0.0 126.9 jit_solution(12813364208653549408)
XLA Ops:
  3.4 2.1 %collective-permute-start = (bf16[8,16,512]{2,1,0:T(8,128)(2,1)S(1)}, bf16[8,16,512]{2,1,0:T(8,128)(2,1)S(1)}, u32[]{:S(2)}, u32[]{:S(2)}) collective-permute-start(bf16[8,16,512]{2,1,0:T(8,128)(2,1)S(1)} %bitcast.60), channel_id=1, source_target_pairs={{0,128},{8,136},{16,144},{24,152},{32,160},{40,168},{48,176},{56,1... | collective-permute-start | bytes 393224 | tf_op jit(solution)/shard_map/ppermute | solution.py:125
  5.6 2.3 %collective-permute-done = bf16[8,16,512]{2,1,0:T(8,128)(2,1)S(1)} collective-permute-done((bf16[8,16,512]{2,1,0:T(8,128)(2,1)S(1)}, bf16[8,16,512]{2,1,0:T(8,128)(2,1)S(1)}, u32[]{:S(2)}, u32[]{:S(2)}) %collective-permute-start) | collective-permute-done | bytes 131104 | tf_op jit(solution)/shard_map/ppermute | solution.py:125
  7.9 6.5 %collective-permute-start.1 = (bf16[2,8,16,512]{3,2,1,0:T(8,128)(2,1)S(1)}, bf16[2,8,16,512]{3,2,1,0:T(8,128)(2,1)S(1)}, u32[]{:S(2)}, u32[]{:S(2)}) collective-permute-start(bf16[2,8,16,512]{3,2,1,0:T(8,128)(2,1)S(1)} %pad_maximum_fusion.8), channel_id=1, source_target_pairs={{0,112},{8,120},{16,0},{24,8},{32,16},{40,24},{48,32},{56,40},{64,... | collective-permute-start | bytes 786440 | tf_op jit(solution)/shard_map/ppermute | solution.py:130
  15.4 3.1 %collective-permute-done.1 = bf16[2,8,16,512]{3,2,1,0:T(8,128)(2,1)S(1)} collective-permute-done((bf16[2,8,16,512]{3,2,1,0:T(8,128)(2,1)S(1)}, bf16[2,8,16,512]{3,2,1,0:T(8,128)(2,1)S(1)}, u32[]{:S(2)}, u32[]{:S(2)}) %collective-permute-start.1) | collective-permute-done | bytes 262176 | tf_op jit(solution)/shard_map/ppermute | solution.py:130
  18.5 3.4 %collective-permute-start.2 = (bf16[2,8,16,512]{3,2,1,0:T(8,128)(2,1)S(1)}, bf16[2,8,16,512]{3,2,1,0:T(8,128)(2,1)S(1)}, u32[]{:S(2)}, u32[]{:S(2)}) collective-permute-start(bf16[2,8,16,512]{3,2,1,0:T(8,128)(2,1)S(1)} %collective-permute-done.1), channel_id=1, source_target_pairs={{0,112},{8,120},{16,0},{24,8},{32,16},{40,24},{48,32},{56,40},{64,... | collective-permute-start | bytes 786440 | tf_op jit(solution)/shard_map/ppermute | solution.py:130
  23.4 5.0 %collective-permute-done.4 = bf16[2,8,16,512]{3,2,1,0:T(8,128)(2,1)S(1)} collective-permute-done((bf16[2,8,16,512]{3,2,1,0:T(8,128)(2,1)S(1)}, bf16[2,8,16,512]{3,2,1,0:T(8,128)(2,1)S(1)}, u32[]{:S(2)}, u32[]{:S(2)}) %collective-permute-start.4) | collective-permute-done | bytes 262176 | tf_op jit(solution)/shard_map/ppermute | solution.py:129
  28.4 2.7 %collective-permute-start.6 = (bf16[2,8,16,512]{3,2,1,0:T(8,128)(2,1)S(1)}, bf16[2,8,16,512]{3,2,1,0:T(8,128)(2,1)S(1)}, u32[]{:S(2)}, u32[]{:S(2)}) collective-permute-start(bf16[2,8,16,512]{3,2,1,0:T(8,128)(2,1)S(1)} %collective-permute-done.2), channel_id=1, source_target_pairs={{0,112},{8,120},{16,0},{24,8},{32,16},{40,24},{48,32},{56,40},{64,... | collective-permute-start | bytes 786440 | tf_op jit(solution)/shard_map/ppermute | solution.py:130
  32.5 2.3 %collective-permute-done.7 = bf16[2,8,16,512]{3,2,1,0:T(8,128)(2,1)S(1)} collective-permute-done((bf16[2,8,16,512]{3,2,1,0:T(8,128)(2,1)S(1)}, bf16[2,8,16,512]{3,2,1,0:T(8,128)(2,1)S(1)}, u32[]{:S(2)}, u32[]{:S(2)}) %collective-permute-start.7) | collective-permute-done | bytes 262176 | tf_op jit(solution)/shard_map/ppermute | solution.py:129
  34.9 2.7 %collective-permute-start.9 = (bf16[8,16,512]{2,1,0:T(8,128)(2,1)S(1)}, bf16[8,16,512]{2,1,0:T(8,128)(2,1)S(1)}, u32[]{:S(2)}, u32[]{:S(2)}) collective-permute-start(bf16[8,16,512]{2,1,0:T(8,128)(2,1)S(1)} %slice_bitcast_fusion), channel_id=1, source_target_pairs={{0,112},{8,120},{16,0},{24,8},{32,16},{40,24},{48,32},{56,40},{64,... | collective-permute-start | bytes 393224 | tf_op jit(solution)/shard_map/ppermute | solution.py:132
  38.4 6.2 %collective-permute-start.5 = (bf16[10,8,16,512]{3,2,1,0:T(8,128)(2,1)}, bf16[10,8,16,512]{3,2,1,0:T(8,128)(2,1)}, u32[]{:S(2)}, u32[]{:S(2)}) collective-permute-start(bf16[10,8,16,512]{3,2,1,0:T(8,128)(2,1)} %bitcast.12.mine_ref), channel_id=1, source_target_pairs={{0,8},{8,0},{16,24},{24,16},{32,40},{40,32},{48,56},{56,48},{64,72... | collective-permute-start | bytes 3932168 | tf_op jit(solution)/shard_map/ppermute | solution.py:166
  44.7 2.3 %collective-permute-start.10 = (bf16[6,8,16,512]{3,2,1,0:T(8,128)(2,1)S(1)}, bf16[6,8,16,512]{3,2,1,0:T(8,128)(2,1)}, u32[]{:S(2)}, u32[]{:S(2)}) collective-permute-start(bf16[6,8,16,512]{3,2,1,0:T(8,128)(2,1)S(1)} %bitcast.55), channel_id=1, source_target_pairs={{0,8},{8,0},{16,24},{24,16},{32,40},{40,32},{48,56},{56,48},{64,72... | collective-permute-start | bytes 2359304 | tf_op jit(solution)/shard_map/ppermute | solution.py:166
  51.1 3.2 %reshape.285.resp_ref = bf16[4,512,512]{2,1,0:T(8,128)(2,1)S(1)} reshape(bf16[4,512,2,256]{3,2,1,0:T(2,128)(2,1)} %param.6) | data formatting | bytes 4194304 | tf_op jit(solution)/shard_map/reshape | solution.py:159
  54.3 1.5 %pad_maximum_fusion.7.back_ref = bf16[512,512]{1,0:T(8,128)(2,1)S(1)} fusion(bf16[512,256]{1,0:T(8,128)(2,1)} %bitcast.65, bf16[512,256]{1,0:T(8,128)(2,1)} %bitcast.66), kind=kLoop, calls=%fused_computation.17 | loop fusion | flops 1048576 | bytes 1048576 | tf_op jit(solution)/shard_map/concatenate | solution.py:154
  55.8 6.8 %shard_map.56 = bf16[4,8,96,128]{3,2,1,0:T(8,128)(2,1)S(1)} custom-call(s32[4]{0:T(128)S(1)} %copy-done.2, s32[6]{0:T(128)S(1)} %add.238.table_ref, s32[1]{0:T(128)} %bitcast.1.swap_ref, bf16[6,8,16,512]{3,2,1,0:T(8,128)(2,1)S(1)} %bitcast.56, bf16[6,8,16,512]{3,2,1,0:T(8,128)(2,1)} %collective-permute-done.10.theirs_ref, ...), custom_call_target="tpu_custom_call" | custom-call | flops 3221225472 | bytes 3145728 | tf_op jit(solution)/shard_map/pallas_call | solution.py:79
  65.0 1.5 %copy.27 = bf16[4,8,12288]{2,0,1:T(4,128)(2,1)} copy(bf16[4,8,12288]{2,1,0:T(8,128)(2,1)S(1)} %reshape.289) | data formatting | bytes 1572864 | tf_op jit(solution)/shard_map/reshape | solution.py:171
  66.5 6.7 %all-to-all-start.1 = ((bf16[4,8,12288]{2,0,1:T(4,128)(2,1)}), bf16[4,8,12288]{2,0,1:T(4,128)(2,1)S(1)}, u32[]{:S(2)}, u32[]{:S(2)}) async-start(bf16[4,8,12288]{2,0,1:T(4,128)(2,1)} %copy.27), calls=%async_computation.1 | async-start | bytes 1572864 | tf_op jit(solution)/shard_map/all_to_all | solution.py:172
  73.2 11.2 %shard_map.55 = bf16[4,8,160,128]{3,2,1,0:T(8,128)(2,1)S(1)} custom-call(s32[4]{0:T(128)S(1)} %copy-done.2, s32[10]{0:T(128)S(1)} %add.228.table_ref, s32[1]{0:T(128)} %bitcast.1.swap_ref, bf16[10,8,16,512]{3,2,1,0:T(8,128)(2,1)} %bitcast.12.mine_ref, bf16[10,8,16,512]{3,2,1,0:T(8,128)(2,1)} %collective-permute-done.5.theirs_ref, ...), custom_call_target="tpu_custom_call" | custom-call | flops 5368709120 | bytes 5242880 | tf_op jit(solution)/shard_map/pallas_call | solution.py:79
  85.0 2.1 %copy.25 = bf16[4,8,20480]{2,0,1:T(4,128)(2,1)} copy(bf16[4,8,20480]{2,1,0:T(8,128)(2,1)S(1)} %reshape.286) | data formatting | bytes 2621440 | tf_op jit(solution)/shard_map/reshape | solution.py:171
  88.2 6.4 %all-to-all-start = ((bf16[4,8,20480]{2,0,1:T(4,128)(2,1)}), bf16[4,8,20480]{2,0,1:T(4,128)(2,1)S(1)}, u32[]{:S(2)}, u32[]{:S(2)}) async-start(bf16[4,8,20480]{2,0,1:T(4,128)(2,1)} %copy.25), calls=%async_computation | async-start | bytes 2621440 | tf_op jit(solution)/shard_map/all_to_all | solution.py:172
  96.2 17.7 %all-to-all-done = bf16[4,8,20480]{2,0,1:T(4,128)(2,1)S(1)} async-done(((bf16[4,8,20480]{2,0,1:T(4,128)(2,1)}), bf16[4,8,20480]{2,0,1:T(4,128)(2,1)S(1)}, u32[]{:S(2)}, u32[]{:S(2)}) %all-to-all-start) | async-done | bytes 1310752 | tf_op jit(solution)/shard_map/all_to_all | solution.py:172
  114.8 2.0 %gather_fusion.2 = bf16[16,4,8,2048]{3,2,1,0:T(8,128)(2,1)} fusion(bf16[4,8,16,2048]{3,1,2,0:T(8,128)(2,1)S(1)} %pad_maximum_fusion, s32[1024]{0:T(1024)S(1)} %get-tuple-element.9), kind=kCustom, calls=%fused_computation.2 | custom fusion | bytes 4194368 | tf_op jit(solution)/shard_map/jit(_take)/gather | solution.py:177
  116.8 4.1 %copy.29 = bf16[4,8,16,2048]{3,2,1,0:T(8,128)(2,1)} copy(bf16[4,8,16,2048]{3,1,0,2:T(8,128)(2,1)} %bitcast.57) | data formatting | bytes 4194304 | tf_op jit(solution)/shard_map/jit(_take)/gather | solution.py:177
  120.9 3.2 %gather.15 = bf16[4,1,262144]{2,0,1:T(4,128)(2,1)S(1)} reshape(bf16[4,8,16,2048]{3,2,1,0:T(8,128)(2,1)} %copy.29) | data formatting | bytes 4194304 | tf_op jit(solution)/shard_map/jit(_take)/gather | solution.py:177
  124.1 2.8 %broadcast_select_fusion = bf16[4,1,262144]{2,0,1:T(4,128)(2,1)} fusion(bf16[4,1,262144]{2,0,1:T(4,128)(2,1)S(1)} %gather.15, pred[262144]{0:T(1024)(128)(4,1)S(1)} %bitcast.63), kind=kLoop, calls=%fused_computation.5 | loop fusion | flops 1048576 | bytes 4456448 | tf_op jit(solution)/shard_map/jit(_take)/select_n | solution.py:177
  (71 shorter events, 19.0 us)
Async XLA Ops:
  2.1 3.4 %copy-start.6 = (s32[5]{0:T(128)S(1)}, s32[5]{0:T(128)}, u32[]{:S(2)}) copy-start(s32[5]{0:T(128)} %constant.145.clone) | copy-start | bytes 64
  2.1 3.5 %copy-start.5 = (s32[3]{0:T(128)S(1)}, s32[3]{0:T(128)}, u32[]{:S(2)}) copy-start(s32[3]{0:T(128)} %constant.146.clone) | copy-start | bytes 40
  3.4 4.5 %collective-permute-start = (bf16[8,16,512]{2,1,0:T(8,128)(2,1)S(1)}, bf16[8,16,512]{2,1,0:T(8,128)(2,1)S(1)}, u32[]{:S(2)}, u32[]{:S(2)}) collective-permute-start(bf16[8,16,512]{2,1,0:T(8,128)(2,1)S(1)} %bitcast.60), channel_id=1, source_target_pairs={{0,128},{8,136},{16,144},{24,152},{32,160},{40,168},{48,176},{56,1... | collective-permute-start | bytes 393224 | tf_op jit(solution)/shard_map/ppermute | solution.py:125
  7.9 10.6 %collective-permute-start.1 = (bf16[2,8,16,512]{3,2,1,0:T(8,128)(2,1)S(1)}, bf16[2,8,16,512]{3,2,1,0:T(8,128)(2,1)S(1)}, u32[]{:S(2)}, u32[]{:S(2)}) collective-permute-start(bf16[2,8,16,512]{3,2,1,0:T(8,128)(2,1)S(1)} %pad_maximum_fusion.8), channel_id=1, source_target_pairs={{0,112},{8,120},{16,0},{24,8},{32,16},{40,24},{48,32},{56,40},{64,... | collective-permute-start | bytes 786440 | tf_op jit(solution)/shard_map/ppermute | solution.py:130
  14.4 7.5 %collective-permute-start.3 = (bf16[2,8,16,512]{3,2,1,0:T(8,128)(2,1)S(1)}, bf16[2,8,16,512]{3,2,1,0:T(8,128)(2,1)S(1)}, u32[]{:S(2)}, u32[]{:S(2)}) collective-permute-start(bf16[2,8,16,512]{3,2,1,0:T(8,128)(2,1)S(1)} %pad_maximum_fusion.8), channel_id=1, source_target_pairs={{0,16},{8,24},{16,32},{24,40},{32,48},{40,56},{48,64},{56,72},{64,... | collective-permute-start | bytes 786440 | tf_op jit(solution)/shard_map/ppermute | solution.py:129
  18.5 9.9 %collective-permute-start.2 = (bf16[2,8,16,512]{3,2,1,0:T(8,128)(2,1)S(1)}, bf16[2,8,16,512]{3,2,1,0:T(8,128)(2,1)S(1)}, u32[]{:S(2)}, u32[]{:S(2)}) collective-permute-start(bf16[2,8,16,512]{3,2,1,0:T(8,128)(2,1)S(1)} %collective-permute-done.1), channel_id=1, source_target_pairs={{0,112},{8,120},{16,0},{24,8},{32,16},{40,24},{48,32},{56,40},{64,... | collective-permute-start | bytes 786440 | tf_op jit(solution)/shard_map/ppermute | solution.py:130
  21.9 6.4 %collective-permute-start.4 = (bf16[2,8,16,512]{3,2,1,0:T(8,128)(2,1)S(1)}, bf16[2,8,16,512]{3,2,1,0:T(8,128)(2,1)S(1)}, u32[]{:S(2)}, u32[]{:S(2)}) collective-permute-start(bf16[2,8,16,512]{3,2,1,0:T(8,128)(2,1)S(1)} %collective-permute-done.3), channel_id=1, source_target_pairs={{0,16},{8,24},{16,32},{24,40},{32,48},{40,56},{48,64},{56,72},{64,... | collective-permute-start | bytes 786440 | tf_op jit(solution)/shard_map/ppermute | solution.py:129
  28.4 6.4 %collective-permute-start.7 = (bf16[2,8,16,512]{3,2,1,0:T(8,128)(2,1)S(1)}, bf16[2,8,16,512]{3,2,1,0:T(8,128)(2,1)S(1)}, u32[]{:S(2)}, u32[]{:S(2)}) collective-permute-start(bf16[2,8,16,512]{3,2,1,0:T(8,128)(2,1)S(1)} %collective-permute-done.4), channel_id=1, source_target_pairs={{0,16},{8,24},{16,32},{24,40},{32,48},{40,56},{48,64},{56,72},{64,... | collective-permute-start | bytes 786440 | tf_op jit(solution)/shard_map/ppermute | solution.py:129
  28.4 6.5 %collective-permute-start.6 = (bf16[2,8,16,512]{3,2,1,0:T(8,128)(2,1)S(1)}, bf16[2,8,16,512]{3,2,1,0:T(8,128)(2,1)S(1)}, u32[]{:S(2)}, u32[]{:S(2)}) collective-permute-start(bf16[2,8,16,512]{3,2,1,0:T(8,128)(2,1)S(1)} %collective-permute-done.2), channel_id=1, source_target_pairs={{0,112},{8,120},{16,0},{24,8},{32,16},{40,24},{48,32},{56,40},{64,... | collective-permute-start | bytes 786440 | tf_op jit(solution)/shard_map/ppermute | solution.py:130
  34.8 9.7 %collective-permute-start.8 = (bf16[8,16,512]{2,1,0:T(8,128)(2,1)S(1)}, bf16[8,16,512]{2,1,0:T(8,128)(2,1)S(1)}, u32[]{:S(2)}, u32[]{:S(2)}) collective-permute-start(bf16[8,16,512]{2,1,0:T(8,128)(2,1)S(1)} %slice_bitcast_fusion.1), channel_id=1, source_target_pairs={{0,16},{8,24},{16,32},{24,40},{32,48},{40,56},{48,64},{56,72},{64,... | collective-permute-start | bytes 393224 | tf_op jit(solution)/shard_map/ppermute | solution.py:132
  34.9 9.6 %collective-permute-start.9 = (bf16[8,16,512]{2,1,0:T(8,128)(2,1)S(1)}, bf16[8,16,512]{2,1,0:T(8,128)(2,1)S(1)}, u32[]{:S(2)}, u32[]{:S(2)}) collective-permute-start(bf16[8,16,512]{2,1,0:T(8,128)(2,1)S(1)} %slice_bitcast_fusion), channel_id=1, source_target_pairs={{0,112},{8,120},{16,0},{24,8},{32,16},{40,24},{48,32},{56,40},{64,... | collective-permute-start | bytes 393224 | tf_op jit(solution)/shard_map/ppermute | solution.py:132
  38.4 34.8 %collective-permute-start.5 = (bf16[10,8,16,512]{3,2,1,0:T(8,128)(2,1)}, bf16[10,8,16,512]{3,2,1,0:T(8,128)(2,1)}, u32[]{:S(2)}, u32[]{:S(2)}) collective-permute-start(bf16[10,8,16,512]{3,2,1,0:T(8,128)(2,1)} %bitcast.12.mine_ref), channel_id=1, source_target_pairs={{0,8},{8,0},{16,24},{24,16},{32,40},{40,32},{48,56},{56,48},{64,72... | collective-permute-start | bytes 3932168 | tf_op jit(solution)/shard_map/ppermute | solution.py:166
  44.7 11.0 %collective-permute-start.10 = (bf16[6,8,16,512]{3,2,1,0:T(8,128)(2,1)S(1)}, bf16[6,8,16,512]{3,2,1,0:T(8,128)(2,1)}, u32[]{:S(2)}, u32[]{:S(2)}) collective-permute-start(bf16[6,8,16,512]{3,2,1,0:T(8,128)(2,1)S(1)} %bitcast.55), channel_id=1, source_target_pairs={{0,8},{8,0},{16,24},{24,16},{32,40},{40,32},{48,56},{56,48},{64,72... | collective-permute-start | bytes 2359304 | tf_op jit(solution)/shard_map/ppermute | solution.py:166
  51.1 4.7 %copy-start.2 = (s32[4]{0:T(128)S(1)}, s32[4]{0:T(128)}, u32[]{:S(2)}) copy-start(s32[4]{0:T(128)} %chirp_ref.3) | copy-start | bytes 52
  54.2 8.4 %copy-start = (bf16[4,512,512]{2,1,0:T(8,128)(2,1)}, bf16[4,512,512]{2,1,0:T(8,128)(2,1)S(1)}, u32[]{:S(2)}) copy-start(bf16[4,512,512]{2,1,0:T(8,128)(2,1)S(1)} %reshape.285.resp_ref) | copy-start | bytes 6291460
  62.6 0.9 copy-start.1
  66.5 20.8 %all-to-all-start.1 = ((bf16[4,8,12288]{2,0,1:T(4,128)(2,1)}), bf16[4,8,12288]{2,0,1:T(4,128)(2,1)S(1)}, u32[]{:S(2)}, u32[]{:S(2)}) async-start(bf16[4,8,12288]{2,0,1:T(4,128)(2,1)} %copy.27), calls=%async_computation.1 | async-start | bytes 1572864 | tf_op jit(solution)/shard_map/all_to_all | solution.py:172
  87.3 0.9 copy-start.3
  88.2 25.7 %all-to-all-start = ((bf16[4,8,20480]{2,0,1:T(4,128)(2,1)}), bf16[4,8,20480]{2,0,1:T(4,128)(2,1)S(1)}, u32[]{:S(2)}, u32[]{:S(2)}) async-start(bf16[4,8,20480]{2,0,1:T(4,128)(2,1)} %copy.25), calls=%async_computation | async-start | bytes 2621440 | tf_op jit(solution)/shard_map/all_to_all | solution.py:172
  94.6 1.1 copy-start.4

commit v6 on v3

--- a/solution.py
+++ b/solution.py
@@ -68,24 +68,25 @@
         out_ref[d] = both.reshape(beams, chans // 2, 2 * bins).astype(out_ref.dtype)
 
 
-def detect(table, swap, mine, theirs, responses, chirp_len, backward):
+def detect(table, swap, mine, theirs, responses, chirp_len, backward, first, count):
     blocks, beams, chans_local, width = mine.shape
     trials, chans = responses.shape[0], responses.shape[1]
     length = width // 2
     bins = length // RATE
     step = 2 * chans_local
+    chans = count * step
     flops = 2 * trials * beams * chans * width * width
-    bytes_accessed = 2 * (2 * mine.size + responses.size + backward.size + trials * beams * chans * bins)
+    bytes_accessed = 2 * (chans * beams * width + trials * chans * width + trials * beams * chans * bins)
     return pl.pallas_call(
         detect_kernel,
         out_shape=jax.ShapeDtypeStruct((trials, beams, chans // 2, 2 * bins), jnp.bfloat16),
         grid_spec=pltpu.PrefetchScalarGridSpec(
             num_scalar_prefetch=3,
-            grid=(chans // step,),
+            grid=(count,),
             in_specs=[
-                pl.BlockSpec((1, beams, chans_local, width), lambda n, cl, tb, sw: (tb[n], 0, 0, 0)),
-                pl.BlockSpec((1, beams, chans_local, width), lambda n, cl, tb, sw: (tb[n], 0, 0, 0)),
-                pl.BlockSpec((trials, step, width), lambda n, cl, tb, sw: (0, n, 0)),
+                pl.BlockSpec((1, beams, chans_local, width), lambda n, cl, tb, sw: (tb[n + first], 0, 0, 0)),
+                pl.BlockSpec((1, beams, chans_local, width), lambda n, cl, tb, sw: (tb[n + first], 0, 0, 0)),
+                pl.BlockSpec((trials, step, width), lambda n, cl, tb, sw: (0, n + first, 0)),
                 pl.BlockSpec((width, width), lambda n, cl, tb, sw: (0, 0)),
             ],
             out_specs=pl.BlockSpec(
@@ -154,11 +155,15 @@
     block = jnp.arange(count // 2, dtype=jnp.int32)
     table = ((block % z_count - z_me) % z_count) * 2 + ((block // z_count) ^ x_me)
     swap = jnp.reshape(c_me, (1,)).astype(jnp.int32)
-    detected = detect(
-        table, swap, mine, theirs, responses.reshape(trials, chans, 2 * length), chirp_len, backward
-    )
-    flattened = detected.reshape(trials, beams, -1)
-    return lax.all_to_all(flattened, "beam", split_axis=1, concat_axis=2, tiled=True)
+    resp = responses.reshape(trials, chans, 2 * length)
+    halves = []
+    blocks = count // 2
+    for first in (0, blocks // 2):
+        detected = detect(table, swap, mine, theirs, resp, chirp_len, backward, first, blocks // 2)
+        flattened = detected.reshape(trials, beams, -1)
+        moved = lax.all_to_all(flattened, "beam", split_axis=1, concat_axis=2, tiled=True)
+        halves.append(moved.reshape(trials, beams, 1, -1))
+    return jnp.concatenate(halves, 2).reshape(trials, 1, -1)
 
 
 def solution(mesh):

time: 115 us -> 119 us (1.035)
  blocking collectives: 34.7 us -> 19.2 us
  starting transfers between devices: 24.9 us -> 31.2 us
  waiting for transfers between devices: 18.5 us -> 22.8 us
  local copies, waits for them, and re-layouts: 16.5 us -> 20.7 us
  other arithmetic: 2.27 us -> 5.16 us
  Pallas kernels: 16.9 us -> 18.7 us
    all_to_all x1, blocking collectives: 34.7 us -> 19.2 us  [shards(): lax.all_to_all(flattened, 'beam', split_axis=1, concat_axis=2, tiled=True)]
    all_to_all x0 -> x1, starting transfers between devices: none -> 6.65 us  [shards(): lax.all_to_all(flattened, 'beam', split_axis=1, concat_axis=2, tiled=True)]
    all_to_all x0 -> x1, waiting for transfers between devices: none -> 6.37 us  [shards(): lax.all_to_all(flattened, 'beam', split_axis=1, concat_axis=2, tiled=True)]
    reshape x1 -> x2, local copies, waits for them, and re-layouts: 4.37 us -> 7.02 us  [the longest x1 4.37 us: shards(): resp = responses.reshape(trials, chans, 2 * length)]
    concatenate x0 -> x1, local copies, waits for them, and re-layouts: none -> 2.17 us  [shards(): return jnp.concatenate(halves, 2).reshape(trials, 1, -1)]
    ppermute x3, waiting for transfers between devices: 10.6 us -> 8.58 us  [gather_spectra(): from_above.append(lax.ppermute(from_above[-1], 'dm', down))]
    reshape x2 -> x4, local copies, waits for them, and re-layouts: 5.5 us -> 3.59 us  [shards(): flattened = detected.reshape(trials, beams, -1)]
    pallas_call x1 -> x2, Pallas kernels: 16.9 us -> 18.7 us  [detect(): pl.pallas_call(detect_kernel, out_shape=jax.ShapeDtypeStruct((trials, bea...]
  transfers between devices with their start and end apart: 10 -> 11, of which waited for: 6 -> 8; matrix products, arithmetic and copies ran while one was open for 6% -> 10% of each run, Pallas kernels for 0% -> 8%
where the time goes in v6:
time: 119 us; the launch traced here: 118 us
  starting transfers between devices  31.2 us (26%)
  waiting for transfers between devices  22.8 us (19%)
  local copies, waits for them, and re-layouts  20.7 us (17%)
  blocking collectives  19.2 us (16%)
  Pallas kernels  18.7 us (16%)
  other arithmetic  5.16 us (4%)
    all_to_all x1, blocking collectives, shards(): lax.all_to_all(flattened, 'beam', split_axis=1, concat_axis=2, tiled=True)  19.2 us
    pallas_call x2, Pallas kernels, detect(): pl.pallas_call(detect_kernel, out_shape=jax.ShapeDtypeStruct((trials, bea...  18.7 us
    ppermute x3, starting transfers between devices, gather_spectra(): from_above.append(lax.ppermute(from_above[-1], 'dm', down))  13 us
    ppermute x3, waiting for transfers between devices, gather_spectra(): from_above.append(lax.ppermute(from_above[-1], 'dm', down))  8.58 us
    all_to_all x1, starting transfers between devices, shards(): lax.all_to_all(flattened, 'beam', split_axis=1, concat_axis=2, tiled=True)  6.65 us
    all_to_all x1, waiting for transfers between devices, shards(): lax.all_to_all(flattened, 'beam', split_axis=1, concat_axis=2, tiled=True)  6.37 us
    ppermute x1, starting transfers between devices, gather_spectra(): return (column, lax.ppermute(column, 'dm', partner))  6.12 us
    unnamed x8, local copies, waits for them, and re-layouts  4.53 us
  transfers between devices with their start and end apart: 11, of which 8 were waited for; matrix products, arithmetic and copies ran while one was open for 10% of the time, Pallas kernels for 8%

profile of v6, /device:TPU:1, one launch (start us, length us, event | category | flops | bytes accessed | tf_op | source)
XLA Modules:
  0.0 118.1 jit_solution(12135481186372317261)
XLA Ops:
  1.0 1.1 negate_convert_fusion
  3.4 2.1 %collective-permute-start = (bf16[8,16,512]{2,1,0:T(8,128)(2,1)S(1)}, bf16[8,16,512]{2,1,0:T(8,128)(2,1)S(1)}, u32[]{:S(2)}, u32[]{:S(2)}) collective-permute-start(bf16[8,16,512]{2,1,0:T(8,128)(2,1)S(1)} %bitcast.53), channel_id=1, source_target_pairs={{0,128},{8,136},{16,144},{24,152},{32,160},{40,168},{48,176},{56,1... | collective-permute-start | bytes 393224 | tf_op jit(solution)/shard_map/ppermute | solution.py:127
  5.5 2.4 %collective-permute-done = bf16[8,16,512]{2,1,0:T(8,128)(2,1)S(1)} collective-permute-done((bf16[8,16,512]{2,1,0:T(8,128)(2,1)S(1)}, bf16[8,16,512]{2,1,0:T(8,128)(2,1)S(1)}, u32[]{:S(2)}, u32[]{:S(2)}) %collective-permute-start) | collective-permute-done | bytes 131104 | tf_op jit(solution)/shard_map/ppermute | solution.py:127
  7.9 6.5 %collective-permute-start.1 = (bf16[2,8,16,512]{3,2,1,0:T(8,128)(2,1)S(1)}, bf16[2,8,16,512]{3,2,1,0:T(8,128)(2,1)S(1)}, u32[]{:S(2)}, u32[]{:S(2)}) collective-permute-start(bf16[2,8,16,512]{3,2,1,0:T(8,128)(2,1)S(1)} %pad_maximum_fusion.7), channel_id=1, source_target_pairs={{0,112},{8,120},{16,0},{24,8},{32,16},{40,24},{48,32},{56,40},{64,... | collective-permute-start | bytes 786440 | tf_op jit(solution)/shard_map/ppermute | solution.py:132
  14.4 4.1 %collective-permute-done.1 = bf16[2,8,16,512]{3,2,1,0:T(8,128)(2,1)S(1)} collective-permute-done((bf16[2,8,16,512]{3,2,1,0:T(8,128)(2,1)S(1)}, bf16[2,8,16,512]{3,2,1,0:T(8,128)(2,1)S(1)}, u32[]{:S(2)}, u32[]{:S(2)}) %collective-permute-start.1) | collective-permute-done | bytes 262176 | tf_op jit(solution)/shard_map/ppermute | solution.py:132
  18.5 3.4 %collective-permute-start.2 = (bf16[2,8,16,512]{3,2,1,0:T(8,128)(2,1)S(1)}, bf16[2,8,16,512]{3,2,1,0:T(8,128)(2,1)S(1)}, u32[]{:S(2)}, u32[]{:S(2)}) collective-permute-start(bf16[2,8,16,512]{3,2,1,0:T(8,128)(2,1)S(1)} %collective-permute-done.1), channel_id=1, source_target_pairs={{0,112},{8,120},{16,0},{24,8},{32,16},{40,24},{48,32},{56,40},{64,... | collective-permute-start | bytes 786440 | tf_op jit(solution)/shard_map/ppermute | solution.py:132
  22.6 2.6 %collective-permute-done.2 = bf16[2,8,16,512]{3,2,1,0:T(8,128)(2,1)S(1)} collective-permute-done((bf16[2,8,16,512]{3,2,1,0:T(8,128)(2,1)S(1)}, bf16[2,8,16,512]{3,2,1,0:T(8,128)(2,1)S(1)}, u32[]{:S(2)}, u32[]{:S(2)}) %collective-permute-start.2) | collective-permute-done | bytes 262176 | tf_op jit(solution)/shard_map/ppermute | solution.py:132
  25.2 3.1 %collective-permute-start.3 = (bf16[2,8,16,512]{3,2,1,0:T(8,128)(2,1)S(1)}, bf16[2,8,16,512]{3,2,1,0:T(8,128)(2,1)S(1)}, u32[]{:S(2)}, u32[]{:S(2)}) collective-permute-start(bf16[2,8,16,512]{3,2,1,0:T(8,128)(2,1)S(1)} %collective-permute-done.2), channel_id=1, source_target_pairs={{0,112},{8,120},{16,0},{24,8},{32,16},{40,24},{48,32},{56,40},{64,... | collective-permute-start | bytes 786440 | tf_op jit(solution)/shard_map/ppermute | solution.py:132
  29.8 1.9 %collective-permute-done.3 = bf16[2,8,16,512]{3,2,1,0:T(8,128)(2,1)S(1)} collective-permute-done((bf16[2,8,16,512]{3,2,1,0:T(8,128)(2,1)S(1)}, bf16[2,8,16,512]{3,2,1,0:T(8,128)(2,1)S(1)}, u32[]{:S(2)}, u32[]{:S(2)}) %collective-permute-start.3) | collective-permute-done | bytes 262176 | tf_op jit(solution)/shard_map/ppermute | solution.py:132
  31.7 3.2 %collective-permute-start.8 = (bf16[8,16,512]{2,1,0:T(8,128)(2,1)S(1)}, bf16[8,16,512]{2,1,0:T(8,128)(2,1)S(1)}, u32[]{:S(2)}, u32[]{:S(2)}) collective-permute-start(bf16[8,16,512]{2,1,0:T(8,128)(2,1)S(1)} %slice_bitcast_fusion), channel_id=1, source_target_pairs={{0,112},{8,120},{16,0},{24,8},{32,16},{40,24},{48,32},{56,40},{64,... | collective-permute-start | bytes 393224 | tf_op jit(solution)/shard_map/ppermute | solution.py:134
  37.1 4.1 %collective-permute-done.7 = bf16[8,16,512]{2,1,0:T(8,128)(2,1)S(1)} collective-permute-done((bf16[8,16,512]{2,1,0:T(8,128)(2,1)S(1)}, bf16[8,16,512]{2,1,0:T(8,128)(2,1)S(1)}, u32[]{:S(2)}, u32[]{:S(2)}) %collective-permute-start.7) | collective-permute-done | bytes 131104 | tf_op jit(solution)/shard_map/ppermute | solution.py:134
  44.1 6.1 %collective-permute-start.9 = (bf16[16,8,16,512]{3,2,1,0:T(8,128)(2,1)}, bf16[16,8,16,512]{3,2,1,0:T(8,128)(2,1)}, u32[]{:S(2)}, u32[]{:S(2)}) collective-permute-start(bf16[16,8,16,512]{3,2,1,0:T(8,128)(2,1)} %bitcast.18.mine_ref), channel_id=1, source_target_pairs={{0,8},{8,0},{16,24},{24,16},{32,40},{40,32},{48,56},{56,48},{64,72... | collective-permute-start | bytes 6291464 | tf_op jit(solution)/shard_map/ppermute | solution.py:138
  50.3 1.2 gather_fusion.1
  51.4 1.2 gather_fusion
  52.9 4.4 %reshape.113.resp_ref = bf16[4,512,512]{2,1,0:T(8,128)(2,1)} reshape(bf16[4,512,2,256]{3,2,1,0:T(2,128)(2,1)} %param.4) | data formatting | bytes 4194304 | tf_op jit(solution)/shard_map/reshape | solution.py:158
  57.3 9.3 %shard_map.38 = bf16[4,8,128,128]{3,2,1,0:T(8,128)(2,1)S(1)} custom-call(s32[4]{0:T(128)S(1)} %copy-done, s32[16]{0:T(128)S(1)} %fusion.18.table_ref, s32[1]{0:T(128)} %bitcast.swap_ref, bf16[16,8,16,512]{3,2,1,0:T(8,128)(2,1)} %bitcast.18.mine_ref, bf16[16,8,16,512]{3,2,1,0:T(8,128)(2,1)} %collective-permute-done.9.theirs_ref, ...), custom_call_target="tpu_custom_call" | custom-call | flops 4294967296 | bytes 4194304 | tf_op jit(solution)/shard_map/pallas_call | solution.py:80
  67.2 1.8 %copy.21 = bf16[4,8,16384]{2,0,1:T(4,128)(2,1)} copy(bf16[4,8,16384]{2,1,0:T(8,128)(2,1)S(1)} %reshape.115) | data formatting | bytes 2097152 | tf_op jit(solution)/shard_map/reshape | solution.py:163
  69.0 6.6 %all-to-all-start.1 = ((bf16[4,8,16384]{2,0,1:T(4,128)(2,1)}), bf16[4,8,16384]{2,0,1:T(4,128)(2,1)S(1)}, u32[]{:S(2)}, u32[]{:S(2)}) async-start(bf16[4,8,16384]{2,0,1:T(4,128)(2,1)} %copy.21), calls=%async_computation.1 | async-start | bytes 2097152 | tf_op jit(solution)/shard_map/all_to_all | solution.py:164
  75.6 9.3 %shard_map.37 = bf16[4,8,128,128]{3,2,1,0:T(8,128)(2,1)S(1)} custom-call(s32[4]{0:T(128)S(1)} %copy-done, s32[16]{0:T(128)S(1)} %fusion.18.table_ref, s32[1]{0:T(128)} %bitcast.swap_ref, bf16[16,8,16,512]{3,2,1,0:T(8,128)(2,1)} %bitcast.18.mine_ref, bf16[16,8,16,512]{3,2,1,0:T(8,128)(2,1)} %collective-permute-done.9.theirs_ref, ...), custom_call_target="tpu_custom_call" | custom-call | flops 4294967296 | bytes 4194304 | tf_op jit(solution)/shard_map/pallas_call | solution.py:80
  86.2 6.4 %all-to-all-done.1 = bf16[4,8,16384]{2,0,1:T(4,128)(2,1)S(1)} async-done(((bf16[4,8,16384]{2,0,1:T(4,128)(2,1)}), bf16[4,8,16384]{2,0,1:T(4,128)(2,1)S(1)}, u32[]{:S(2)}, u32[]{:S(2)}) %all-to-all-start.1) | async-done | bytes 1048608 | tf_op jit(solution)/shard_map/all_to_all | solution.py:164
  92.6 19.2 %all_to_all.24 = bf16[4,8,16384]{2,0,1:T(4,128)(2,1)S(1)} all-to-all(bf16[4,8,16384]{2,0,1:T(4,128)(2,1)S(1)} %copy.20), channel_id=1, replica_groups=mesh['dm'=32,'beam'=8] {'beam'}, dimensions={1} | all-to-all | bytes 2097152 | tf_op jit(solution)/shard_map/all_to_all | solution.py:164
  111.8 1.5 %pad_maximum_fusion = bf16[4,8,2,16384]{3,0,1,2:T(4,128)(2,1)S(1)} fusion(bf16[4,8,1,16384]{3,0,1,2:T(4,128)(2,1)S(1)} %bitcast.51, bf16[4,8,1,16384]{3,0,1,2:T(4,128)(2,1)S(1)} %bitcast.52), kind=kLoop, calls=%fused_computation.2 | loop fusion | flops 1048576 | bytes 4194304 | tf_op jit(solution)/shard_map/concatenate | solution.py:166
  113.3 2.2 %copy.22 = bf16[4,8,2,16384]{3,2,1,0:T(2,128)(2,1)S(1)} copy(bf16[4,8,2,16384]{3,0,1,2:T(4,128)(2,1)S(1)} %pad_maximum_fusion) | data formatting | bytes 4194304 | tf_op jit(solution)/shard_map/concatenate | solution.py:166
  115.5 2.7 %reshape.116 = bf16[4,1,262144]{2,0,1:T(4,128)(2,1)} reshape(bf16[4,8,2,16384]{3,2,1,0:T(2,128)(2,1)S(1)} %copy.22) | data formatting | bytes 4194304 | tf_op jit(solution)/shard_map/reshape | solution.py:166
  (37 shorter events, 11.7 us)
Async XLA Ops:
  3.4 4.5 %collective-permute-start = (bf16[8,16,512]{2,1,0:T(8,128)(2,1)S(1)}, bf16[8,16,512]{2,1,0:T(8,128)(2,1)S(1)}, u32[]{:S(2)}, u32[]{:S(2)}) collective-permute-start(bf16[8,16,512]{2,1,0:T(8,128)(2,1)S(1)} %bitcast.53), channel_id=1, source_target_pairs={{0,128},{8,136},{16,144},{24,152},{32,160},{40,168},{48,176},{56,1... | collective-permute-start | bytes 393224 | tf_op jit(solution)/shard_map/ppermute | solution.py:127
  7.9 10.6 %collective-permute-start.1 = (bf16[2,8,16,512]{3,2,1,0:T(8,128)(2,1)S(1)}, bf16[2,8,16,512]{3,2,1,0:T(8,128)(2,1)S(1)}, u32[]{:S(2)}, u32[]{:S(2)}) collective-permute-start(bf16[2,8,16,512]{3,2,1,0:T(8,128)(2,1)S(1)} %pad_maximum_fusion.7), channel_id=1, source_target_pairs={{0,112},{8,120},{16,0},{24,8},{32,16},{40,24},{48,32},{56,40},{64,... | collective-permute-start | bytes 786440 | tf_op jit(solution)/shard_map/ppermute | solution.py:132
  14.4 7.5 %collective-permute-start.4 = (bf16[2,8,16,512]{3,2,1,0:T(8,128)(2,1)S(1)}, bf16[2,8,16,512]{3,2,1,0:T(8,128)(2,1)S(1)}, u32[]{:S(2)}, u32[]{:S(2)}) collective-permute-start(bf16[2,8,16,512]{3,2,1,0:T(8,128)(2,1)S(1)} %pad_maximum_fusion.7), channel_id=1, source_target_pairs={{0,16},{8,24},{16,32},{24,40},{32,48},{40,56},{48,64},{56,72},{64,... | collective-permute-start | bytes 786440 | tf_op jit(solution)/shard_map/ppermute | solution.py:131
  18.5 6.7 %collective-permute-start.2 = (bf16[2,8,16,512]{3,2,1,0:T(8,128)(2,1)S(1)}, bf16[2,8,16,512]{3,2,1,0:T(8,128)(2,1)S(1)}, u32[]{:S(2)}, u32[]{:S(2)}) collective-permute-start(bf16[2,8,16,512]{3,2,1,0:T(8,128)(2,1)S(1)} %collective-permute-done.1), channel_id=1, source_target_pairs={{0,112},{8,120},{16,0},{24,8},{32,16},{40,24},{48,32},{56,40},{64,... | collective-permute-start | bytes 786440 | tf_op jit(solution)/shard_map/ppermute | solution.py:132
  21.9 7.2 %collective-permute-start.5 = (bf16[2,8,16,512]{3,2,1,0:T(8,128)(2,1)S(1)}, bf16[2,8,16,512]{3,2,1,0:T(8,128)(2,1)S(1)}, u32[]{:S(2)}, u32[]{:S(2)}) collective-permute-start(bf16[2,8,16,512]{3,2,1,0:T(8,128)(2,1)S(1)} %collective-permute-done.4), channel_id=1, source_target_pairs={{0,16},{8,24},{16,32},{24,40},{32,48},{40,56},{48,64},{56,72},{64,... | collective-permute-start | bytes 786440 | tf_op jit(solution)/shard_map/ppermute | solution.py:131
  25.2 6.4 %collective-permute-start.3 = (bf16[2,8,16,512]{3,2,1,0:T(8,128)(2,1)S(1)}, bf16[2,8,16,512]{3,2,1,0:T(8,128)(2,1)S(1)}, u32[]{:S(2)}, u32[]{:S(2)}) collective-permute-start(bf16[2,8,16,512]{3,2,1,0:T(8,128)(2,1)S(1)} %collective-permute-done.2), channel_id=1, source_target_pairs={{0,112},{8,120},{16,0},{24,8},{32,16},{40,24},{48,32},{56,40},{64,... | collective-permute-start | bytes 786440 | tf_op jit(solution)/shard_map/ppermute | solution.py:132
  29.1 6.4 %collective-permute-start.6 = (bf16[2,8,16,512]{3,2,1,0:T(8,128)(2,1)S(1)}, bf16[2,8,16,512]{3,2,1,0:T(8,128)(2,1)S(1)}, u32[]{:S(2)}, u32[]{:S(2)}) collective-permute-start(bf16[2,8,16,512]{3,2,1,0:T(8,128)(2,1)S(1)} %collective-permute-done.5), channel_id=1, source_target_pairs={{0,16},{8,24},{16,32},{24,40},{32,48},{40,56},{48,64},{56,72},{64,... | collective-permute-start | bytes 786440 | tf_op jit(solution)/shard_map/ppermute | solution.py:131
  31.7 5.4 %collective-permute-start.8 = (bf16[8,16,512]{2,1,0:T(8,128)(2,1)S(1)}, bf16[8,16,512]{2,1,0:T(8,128)(2,1)S(1)}, u32[]{:S(2)}, u32[]{:S(2)}) collective-permute-start(bf16[8,16,512]{2,1,0:T(8,128)(2,1)S(1)} %slice_bitcast_fusion), channel_id=1, source_target_pairs={{0,112},{8,120},{16,0},{24,8},{32,16},{40,24},{48,32},{56,40},{64,... | collective-permute-start | bytes 393224 | tf_op jit(solution)/shard_map/ppermute | solution.py:134
  35.5 5.7 %collective-permute-start.7 = (bf16[8,16,512]{2,1,0:T(8,128)(2,1)S(1)}, bf16[8,16,512]{2,1,0:T(8,128)(2,1)S(1)}, u32[]{:S(2)}, u32[]{:S(2)}) collective-permute-start(bf16[8,16,512]{2,1,0:T(8,128)(2,1)S(1)} %slice_bitcast_fusion.1), channel_id=1, source_target_pairs={{0,16},{8,24},{16,32},{24,40},{32,48},{40,56},{48,64},{56,72},{64,... | collective-permute-start | bytes 393224 | tf_op jit(solution)/shard_map/ppermute | solution.py:134
  44.1 13.2 %collective-permute-start.9 = (bf16[16,8,16,512]{3,2,1,0:T(8,128)(2,1)}, bf16[16,8,16,512]{3,2,1,0:T(8,128)(2,1)}, u32[]{:S(2)}, u32[]{:S(2)}) collective-permute-start(bf16[16,8,16,512]{3,2,1,0:T(8,128)(2,1)} %bitcast.18.mine_ref), channel_id=1, source_target_pairs={{0,8},{8,0},{16,24},{24,16},{32,40},{40,32},{48,56},{56,48},{64,72... | collective-permute-start | bytes 6291464 | tf_op jit(solution)/shard_map/ppermute | solution.py:138
  52.9 4.5 %copy-start = (s32[4]{0:T(128)S(1)}, s32[4]{0:T(128)}, u32[]{:S(2)}) copy-start(s32[4]{0:T(128)} %chirp_ref.3) | copy-start | bytes 52
  69.0 23.7 %all-to-all-start.1 = ((bf16[4,8,16384]{2,0,1:T(4,128)(2,1)}), bf16[4,8,16384]{2,0,1:T(4,128)(2,1)S(1)}, u32[]{:S(2)}, u32[]{:S(2)}) async-start(bf16[4,8,16384]{2,0,1:T(4,128)(2,1)} %copy.21), calls=%async_computation.1 | async-start | bytes 2097152 | tf_op jit(solution)/shard_map/all_to_all | solution.py:164

commit v7 on v3

--- a/solution.py
+++ b/solution.py
@@ -65,7 +65,7 @@
         even = pair_ref[pl.ds(0, rows, stride=2), :]
         odd = pair_ref[pl.ds(1, rows, stride=2), :]
         both = jnp.where(lane < bins, even, odd) / RATE
-        out_ref[d] = both.reshape(beams, chans // 2, 2 * bins).astype(out_ref.dtype)
+        out_ref[:, d] = both.reshape(beams, chans // 2, 2 * bins).astype(out_ref.dtype)
 
 
 def detect(table, swap, mine, theirs, responses, chirp_len, backward):
@@ -78,7 +78,7 @@
     bytes_accessed = 2 * (2 * mine.size + responses.size + backward.size + trials * beams * chans * bins)
     return pl.pallas_call(
         detect_kernel,
-        out_shape=jax.ShapeDtypeStruct((trials, beams, chans // 2, 2 * bins), jnp.bfloat16),
+        out_shape=jax.ShapeDtypeStruct((beams, trials, chans // 2, 2 * bins), jnp.bfloat16),
         grid_spec=pltpu.PrefetchScalarGridSpec(
             num_scalar_prefetch=3,
             grid=(chans // step,),
@@ -89,7 +89,7 @@
                 pl.BlockSpec((width, width), lambda n, cl, tb, sw: (0, 0)),
             ],
             out_specs=pl.BlockSpec(
-                (trials, beams, step // 2, 2 * bins), lambda n, cl, tb, sw: (0, 0, n, 0)
+                (beams, trials, step // 2, 2 * bins), lambda n, cl, tb, sw: (0, 0, n, 0)
             ),
             scratch_shapes=[pltpu.VMEM((beams * step, 2 * bins), jnp.float32)],
         ),
@@ -157,8 +157,8 @@
     detected = detect(
         table, swap, mine, theirs, responses.reshape(trials, chans, 2 * length), chirp_len, backward
     )
-    flattened = detected.reshape(trials, beams, -1)
-    return lax.all_to_all(flattened, "beam", split_axis=1, concat_axis=2, tiled=True)
+    moved = lax.all_to_all(detected.transpose(1, 0, 2, 3), "beam", split_axis=1, concat_axis=2, tiled=True)
+    return moved.reshape(trials, 1, -1)
 
 
 def solution(mesh):

time: 115 us -> 109 us (0.948)
  local copies, waits for them, and re-layouts: 16.5 us -> 10.3 us
    reshape x2 -> x1, local copies, waits for them, and re-layouts: 5.5 us -> 2.09 us  [shards(): return moved.reshape(trials, 1, -1)]
    unnamed x13 -> x8, local copies, waits for them, and re-layouts: 3.94 us -> 1.02 us
  transfers between devices with their start and end apart: 10 -> 10, of which waited for: 6 -> 6; matrix products, arithmetic and copies ran while one was open for 6% -> 7% of each run, Pallas kernels for 0% -> 0%
where the time goes in v7:
time: 109 us; the launch traced here: 108 us
  blocking collectives  34.7 us (32%)
  starting transfers between devices  24.9 us (23%)
  waiting for transfers between devices  18.5 us (17%)
  Pallas kernels  16.9 us (16%)
  local copies, waits for them, and re-layouts  10.3 us (9%)
  other arithmetic  2.27 us (2%)
    all_to_all x1, blocking collectives, shards(): lax.all_to_all(detected.transpose(1, 0, 2, 3), 'beam', split_axis=1, conc...  34.7 us
    pallas_call x1, Pallas kernels, detect(): pl.pallas_call(detect_kernel, out_shape=jax.ShapeDtypeStruct((beams, tria...  16.9 us
    ppermute x3, starting transfers between devices, gather_spectra(): from_above.append(lax.ppermute(from_above[-1], 'dm', down))  13 us
    ppermute x3, waiting for transfers between devices, gather_spectra(): from_above.append(lax.ppermute(from_above[-1], 'dm', down))  10.6 us
    ppermute x1, starting transfers between devices, gather_spectra(): return (column, lax.ppermute(column, 'dm', partner))  6.39 us
    reshape x1, local copies, waits for them, and re-layouts, shards(): responses.reshape(trials, chans, 2 * length)  4.37 us
    ppermute x1, waiting for transfers between devices, gather_spectra(): lax.ppermute(from_below[-1][0], 'dm', up)  3.51 us
    ppermute x1, starting transfers between devices, gather_spectra(): lax.ppermute(from_above[-1][1], 'dm', down)  3.19 us
  transfers between devices with their start and end apart: 10, of which 6 were waited for; matrix products, arithmetic and copies ran while one was open for 7% of the time, Pallas kernels for 0%

profile of v7, /device:TPU:1, one launch (start us, length us, event | category | flops | bytes accessed | tf_op | source)
XLA Modules:
  0.0 108.0 jit_solution(2441025084427279176)
XLA Ops:
  0.0 1.0 fusion.13
  1.0 1.1 %negate_convert_fusion = (bf16[256,256]{0,1:T(8,128)(2,1)S(1)}, bf16[256,256]{0,1:T(8,128)(2,1)S(1)}) fusion(), kind=kLoop, calls=%fused_computation.29 | loop fusion | flops 1245184 | bytes 262144 | tf_op jit(solution)/shard_map/convert.11
  2.1 0.9 copy.11
  3.0 0.3 fusion
  3.4 2.1 %collective-permute-start = (bf16[8,16,512]{2,1,0:T(8,128)(2,1)S(1)}, bf16[8,16,512]{2,1,0:T(8,128)(2,1)S(1)}, u32[]{:S(2)}, u32[]{:S(2)}) collective-permute-start(bf16[8,16,512]{2,1,0:T(8,128)(2,1)S(1)} %bitcast.51), channel_id=1, source_target_pairs={{0,128},{8,136},{16,144},{24,152},{32,160},{40,168},{48,176},{56,1... | collective-permute-start | bytes 393224 | tf_op jit(solution)/shard_map/ppermute | solution.py:126
  5.5 2.4 %collective-permute-done = bf16[8,16,512]{2,1,0:T(8,128)(2,1)S(1)} collective-permute-done((bf16[8,16,512]{2,1,0:T(8,128)(2,1)S(1)}, bf16[8,16,512]{2,1,0:T(8,128)(2,1)S(1)}, u32[]{:S(2)}, u32[]{:S(2)}) %collective-permute-start) | collective-permute-done | bytes 131104 | tf_op jit(solution)/shard_map/ppermute | solution.py:126
  7.9 6.5 %collective-permute-start.1 = (bf16[2,8,16,512]{3,2,1,0:T(8,128)(2,1)S(1)}, bf16[2,8,16,512]{3,2,1,0:T(8,128)(2,1)S(1)}, u32[]{:S(2)}, u32[]{:S(2)}) collective-permute-start(bf16[2,8,16,512]{3,2,1,0:T(8,128)(2,1)S(1)} %pad_maximum_fusion.6), channel_id=1, source_target_pairs={{0,112},{8,120},{16,0},{24,8},{32,16},{40,24},{48,32},{56,40},{64,... | collective-permute-start | bytes 786440 | tf_op jit(solution)/shard_map/ppermute | solution.py:131
  14.4 4.1 %collective-permute-done.1 = bf16[2,8,16,512]{3,2,1,0:T(8,128)(2,1)S(1)} collective-permute-done((bf16[2,8,16,512]{3,2,1,0:T(8,128)(2,1)S(1)}, bf16[2,8,16,512]{3,2,1,0:T(8,128)(2,1)S(1)}, u32[]{:S(2)}, u32[]{:S(2)}) %collective-permute-start.1) | collective-permute-done | bytes 262176 | tf_op jit(solution)/shard_map/ppermute | solution.py:131
  18.5 3.4 %collective-permute-start.2 = (bf16[2,8,16,512]{3,2,1,0:T(8,128)(2,1)S(1)}, bf16[2,8,16,512]{3,2,1,0:T(8,128)(2,1)S(1)}, u32[]{:S(2)}, u32[]{:S(2)}) collective-permute-start(bf16[2,8,16,512]{3,2,1,0:T(8,128)(2,1)S(1)} %collective-permute-done.1), channel_id=1, source_target_pairs={{0,112},{8,120},{16,0},{24,8},{32,16},{40,24},{48,32},{56,40},{64,... | collective-permute-start | bytes 786440 | tf_op jit(solution)/shard_map/ppermute | solution.py:131
  21.9 3.3 %collective-permute-done.2 = bf16[2,8,16,512]{3,2,1,0:T(8,128)(2,1)S(1)} collective-permute-done((bf16[2,8,16,512]{3,2,1,0:T(8,128)(2,1)S(1)}, bf16[2,8,16,512]{3,2,1,0:T(8,128)(2,1)S(1)}, u32[]{:S(2)}, u32[]{:S(2)}) %collective-permute-start.2) | collective-permute-done | bytes 262176 | tf_op jit(solution)/shard_map/ppermute | solution.py:131
  25.2 3.1 %collective-permute-start.3 = (bf16[2,8,16,512]{3,2,1,0:T(8,128)(2,1)S(1)}, bf16[2,8,16,512]{3,2,1,0:T(8,128)(2,1)S(1)}, u32[]{:S(2)}, u32[]{:S(2)}) collective-permute-start(bf16[2,8,16,512]{3,2,1,0:T(8,128)(2,1)S(1)} %collective-permute-done.2), channel_id=1, source_target_pairs={{0,112},{8,120},{16,0},{24,8},{32,16},{40,24},{48,32},{56,40},{64,... | collective-permute-start | bytes 786440 | tf_op jit(solution)/shard_map/ppermute | solution.py:131
  28.5 3.2 %collective-permute-done.3 = bf16[2,8,16,512]{3,2,1,0:T(8,128)(2,1)S(1)} collective-permute-done((bf16[2,8,16,512]{3,2,1,0:T(8,128)(2,1)S(1)}, bf16[2,8,16,512]{3,2,1,0:T(8,128)(2,1)S(1)}, u32[]{:S(2)}, u32[]{:S(2)}) %collective-permute-start.3) | collective-permute-done | bytes 262176 | tf_op jit(solution)/shard_map/ppermute | solution.py:131
  31.7 3.2 %collective-permute-start.8 = (bf16[8,16,512]{2,1,0:T(8,128)(2,1)S(1)}, bf16[8,16,512]{2,1,0:T(8,128)(2,1)S(1)}, u32[]{:S(2)}, u32[]{:S(2)}) collective-permute-start(bf16[8,16,512]{2,1,0:T(8,128)(2,1)S(1)} %slice_bitcast_fusion), channel_id=1, source_target_pairs={{0,112},{8,120},{16,0},{24,8},{32,16},{40,24},{48,32},{56,40},{64,... | collective-permute-start | bytes 393224 | tf_op jit(solution)/shard_map/ppermute | solution.py:133
  35.0 2.0 %collective-permute-done.8 = bf16[8,16,512]{2,1,0:T(8,128)(2,1)S(1)} collective-permute-done((bf16[8,16,512]{2,1,0:T(8,128)(2,1)S(1)}, bf16[8,16,512]{2,1,0:T(8,128)(2,1)S(1)}, u32[]{:S(2)}, u32[]{:S(2)}) %collective-permute-start.8) | collective-permute-done | bytes 131104 | tf_op jit(solution)/shard_map/ppermute | solution.py:133
  37.1 3.5 %collective-permute-done.7 = bf16[8,16,512]{2,1,0:T(8,128)(2,1)S(1)} collective-permute-done((bf16[8,16,512]{2,1,0:T(8,128)(2,1)S(1)}, bf16[8,16,512]{2,1,0:T(8,128)(2,1)S(1)}, u32[]{:S(2)}, u32[]{:S(2)}) %collective-permute-start.7) | collective-permute-done | bytes 131104 | tf_op jit(solution)/shard_map/ppermute | solution.py:133
  40.7 6.4 %collective-permute-start.9 = (bf16[16,8,16,512]{3,2,1,0:T(8,128)(2,1)S(1)}, bf16[16,8,16,512]{3,2,1,0:T(8,128)(2,1)}, u32[]{:S(2)}, u32[]{:S(2)}) collective-permute-start(bf16[16,8,16,512]{3,2,1,0:T(8,128)(2,1)S(1)} %bitcast.49), channel_id=1, source_target_pairs={{0,8},{8,0},{16,24},{24,16},{32,40},{40,32},{48,56},{56,48},{64,72... | collective-permute-start | bytes 6291464 | tf_op jit(solution)/shard_map/ppermute | solution.py:137
  47.1 1.2 %gather_fusion.1 = bf16[256,512]{1,0:T(8,128)(2,1)S(1)} fusion(bf16[512,512]{0,1:T(8,128)(2,1)S(1)} %fusion.3, s32[1024]{0:T(1024)S(1)} %get-tuple-element.9), kind=kCustom, calls=%fused_computation.1 | custom fusion | bytes 525312 | tf_op jit(solution)/shard_map/gather | solution.py:147
  48.3 1.2 %gather_fusion = bf16[256,512]{1,0:T(8,128)(2,1)S(1)} fusion(bf16[512,512]{0,1:T(8,128)(2,1)S(1)} %fusion.3, s32[1024]{0:T(1024)S(1)} %get-tuple-element.10), kind=kCustom, calls=%fused_computation | custom fusion | bytes 525312 | tf_op jit(solution)/shard_map/gather | solution.py:147
  49.6 0.1 copy.9
  49.7 4.4 %reshape.103.resp_ref = bf16[4,512,512]{2,1,0:T(8,128)(2,1)} reshape(bf16[4,512,2,256]{3,2,1,0:T(2,128)(2,1)} %param.4) | data formatting | bytes 4194304 | tf_op jit(solution)/shard_map/reshape | solution.py:158
  54.2 16.9 %shard_map.37 = bf16[8,4,256,128]{3,2,1,0:T(8,128)(2,1)S(1)} custom-call(s32[4]{0:T(128)S(1)} %copy-done, s32[16]{0:T(128)S(1)} %fusion.18.table_ref, s32[1]{0:T(128)} %bitcast.swap_ref, bf16[16,8,16,512]{3,2,1,0:T(8,128)(2,1)S(1)} %bitcast.50, bf16[16,8,16,512]{3,2,1,0:T(8,128)(2,1)} %collective-permute-done.9.theirs_ref, ...), custom_call_target="tpu_custom_call" | custom-call | flops 8589934592 | bytes 8912896 | tf_op jit(solution)/shard_map/pallas_call | solution.py:79
  71.1 34.7 %all_to_all.4 = bf16[4,8,256,128]{3,2,0,1:T(8,128)(2,1)S(1)} all-to-all(bf16[4,8,256,128]{3,2,0,1:T(8,128)(2,1)S(1)} %bitcast.48), channel_id=1, replica_groups=mesh['dm'=32,'beam'=8] {'beam'}, dimensions={1} | all-to-all | bytes 4194304 | tf_op jit(solution)/shard_map/all_to_all | solution.py:160
  105.8 0.1 copy.10
  106.0 2.1 %reshape.104 = bf16[4,1,262144]{2,0,1:T(4,128)(2,1)} reshape(bf16[4,8,256,128]{3,2,1,0:T(8,128)(2,1)S(1)} %copy.10) | data formatting | bytes 4194304 | tf_op jit(solution)/shard_map/reshape | solution.py:161
  (29 shorter events, 0.7 us)
Async XLA Ops:
  3.4 4.5 %collective-permute-start = (bf16[8,16,512]{2,1,0:T(8,128)(2,1)S(1)}, bf16[8,16,512]{2,1,0:T(8,128)(2,1)S(1)}, u32[]{:S(2)}, u32[]{:S(2)}) collective-permute-start(bf16[8,16,512]{2,1,0:T(8,128)(2,1)S(1)} %bitcast.51), channel_id=1, source_target_pairs={{0,128},{8,136},{16,144},{24,152},{32,160},{40,168},{48,176},{56,1... | collective-permute-start | bytes 393224 | tf_op jit(solution)/shard_map/ppermute | solution.py:126
  7.9 10.6 %collective-permute-start.1 = (bf16[2,8,16,512]{3,2,1,0:T(8,128)(2,1)S(1)}, bf16[2,8,16,512]{3,2,1,0:T(8,128)(2,1)S(1)}, u32[]{:S(2)}, u32[]{:S(2)}) collective-permute-start(bf16[2,8,16,512]{3,2,1,0:T(8,128)(2,1)S(1)} %pad_maximum_fusion.6), channel_id=1, source_target_pairs={{0,112},{8,120},{16,0},{24,8},{32,16},{40,24},{48,32},{56,40},{64,... | collective-permute-start | bytes 786440 | tf_op jit(solution)/shard_map/ppermute | solution.py:131
  14.4 7.5 %collective-permute-start.4 = (bf16[2,8,16,512]{3,2,1,0:T(8,128)(2,1)S(1)}, bf16[2,8,16,512]{3,2,1,0:T(8,128)(2,1)S(1)}, u32[]{:S(2)}, u32[]{:S(2)}) collective-permute-start(bf16[2,8,16,512]{3,2,1,0:T(8,128)(2,1)S(1)} %pad_maximum_fusion.6), channel_id=1, source_target_pairs={{0,16},{8,24},{16,32},{24,40},{32,48},{40,56},{48,64},{56,72},{64,... | collective-permute-start | bytes 786440 | tf_op jit(solution)/shard_map/ppermute | solution.py:130
  18.5 6.7 %collective-permute-start.2 = (bf16[2,8,16,512]{3,2,1,0:T(8,128)(2,1)S(1)}, bf16[2,8,16,512]{3,2,1,0:T(8,128)(2,1)S(1)}, u32[]{:S(2)}, u32[]{:S(2)}) collective-permute-start(bf16[2,8,16,512]{3,2,1,0:T(8,128)(2,1)S(1)} %collective-permute-done.1), channel_id=1, source_target_pairs={{0,112},{8,120},{16,0},{24,8},{32,16},{40,24},{48,32},{56,40},{64,... | collective-permute-start | bytes 786440 | tf_op jit(solution)/shard_map/ppermute | solution.py:131
  21.9 6.5 %collective-permute-start.5 = (bf16[2,8,16,512]{3,2,1,0:T(8,128)(2,1)S(1)}, bf16[2,8,16,512]{3,2,1,0:T(8,128)(2,1)S(1)}, u32[]{:S(2)}, u32[]{:S(2)}) collective-permute-start(bf16[2,8,16,512]{3,2,1,0:T(8,128)(2,1)S(1)} %collective-permute-done.4), channel_id=1, source_target_pairs={{0,16},{8,24},{16,32},{24,40},{32,48},{40,56},{48,64},{56,72},{64,... | collective-permute-start | bytes 786440 | tf_op jit(solution)/shard_map/ppermute | solution.py:130
  25.2 6.4 %collective-permute-start.3 = (bf16[2,8,16,512]{3,2,1,0:T(8,128)(2,1)S(1)}, bf16[2,8,16,512]{3,2,1,0:T(8,128)(2,1)S(1)}, u32[]{:S(2)}, u32[]{:S(2)}) collective-permute-start(bf16[2,8,16,512]{3,2,1,0:T(8,128)(2,1)S(1)} %collective-permute-done.2), channel_id=1, source_target_pairs={{0,112},{8,120},{16,0},{24,8},{32,16},{40,24},{48,32},{56,40},{64,... | collective-permute-start | bytes 786440 | tf_op jit(solution)/shard_map/ppermute | solution.py:131
  28.4 6.5 %collective-permute-start.6 = (bf16[2,8,16,512]{3,2,1,0:T(8,128)(2,1)S(1)}, bf16[2,8,16,512]{3,2,1,0:T(8,128)(2,1)S(1)}, u32[]{:S(2)}, u32[]{:S(2)}) collective-permute-start(bf16[2,8,16,512]{3,2,1,0:T(8,128)(2,1)S(1)} %collective-permute-done.5), channel_id=1, source_target_pairs={{0,16},{8,24},{16,32},{24,40},{32,48},{40,56},{48,64},{56,72},{64,... | collective-permute-start | bytes 786440 | tf_op jit(solution)/shard_map/ppermute | solution.py:130
  31.7 5.4 %collective-permute-start.8 = (bf16[8,16,512]{2,1,0:T(8,128)(2,1)S(1)}, bf16[8,16,512]{2,1,0:T(8,128)(2,1)S(1)}, u32[]{:S(2)}, u32[]{:S(2)}) collective-permute-start(bf16[8,16,512]{2,1,0:T(8,128)(2,1)S(1)} %slice_bitcast_fusion), channel_id=1, source_target_pairs={{0,112},{8,120},{16,0},{24,8},{32,16},{40,24},{48,32},{56,40},{64,... | collective-permute-start | bytes 393224 | tf_op jit(solution)/shard_map/ppermute | solution.py:133
  34.9 5.7 %collective-permute-start.7 = (bf16[8,16,512]{2,1,0:T(8,128)(2,1)S(1)}, bf16[8,16,512]{2,1,0:T(8,128)(2,1)S(1)}, u32[]{:S(2)}, u32[]{:S(2)}) collective-permute-start(bf16[8,16,512]{2,1,0:T(8,128)(2,1)S(1)} %slice_bitcast_fusion.1), channel_id=1, source_target_pairs={{0,16},{8,24},{16,32},{24,40},{32,48},{40,56},{48,64},{56,72},{64,... | collective-permute-start | bytes 393224 | tf_op jit(solution)/shard_map/ppermute | solution.py:133
  40.7 13.5 %collective-permute-start.9 = (bf16[16,8,16,512]{3,2,1,0:T(8,128)(2,1)S(1)}, bf16[16,8,16,512]{3,2,1,0:T(8,128)(2,1)}, u32[]{:S(2)}, u32[]{:S(2)}) collective-permute-start(bf16[16,8,16,512]{3,2,1,0:T(8,128)(2,1)S(1)} %bitcast.49), channel_id=1, source_target_pairs={{0,8},{8,0},{16,24},{24,16},{32,40},{40,32},{48,56},{56,48},{64,72... | collective-permute-start | bytes 6291464 | tf_op jit(solution)/shard_map/ppermute | solution.py:137
  49.7 4.5 %copy-start = (s32[4]{0:T(128)S(1)}, s32[4]{0:T(128)}, u32[]{:S(2)}) copy-start(s32[4]{0:T(128)} %chirp_ref.1) | copy-start | bytes 52

commit v8 on v7

--- a/solution.py
+++ b/solution.py
@@ -2,6 +2,8 @@
 import math
 
 import jax
+import ml_dtypes
+import numpy as np
 import jax.numpy as jnp
 from jax import lax
 from jax.experimental import pallas as pl
@@ -25,6 +27,24 @@
         [jnp.concatenate([cosine, sine_part], 1), jnp.concatenate([-sine_part, cosine], 1)], 0
     )
     return (forward.astype(jnp.bfloat16), backward.astype(jnp.bfloat16))
+
+
+def constant_tables(length, rate):
+    sample = np.arange(length, dtype=np.int32)
+    phases = sample[:, None] * sample[None, :] % length
+    angles = phases.astype(np.float32) * np.float32(2.0 * math.pi / length)
+    cosine = np.cos(angles) / np.float32(math.sqrt(length))
+    sine_part = np.sin(angles) / np.float32(math.sqrt(length))
+    forward = np.concatenate(
+        [np.concatenate([cosine, -sine_part], 1), np.concatenate([sine_part, cosine], 1)], 0
+    )
+    backward = np.concatenate(
+        [np.concatenate([cosine, sine_part], 1), np.concatenate([-sine_part, cosine], 1)], 0
+    )
+    pos = np.arange(length)
+    order = rate * (pos % (length // rate)) + pos // (length // rate)
+    backward = np.concatenate([backward[:, order], backward[:, length + order]], 1)
+    return forward.astype(ml_dtypes.bfloat16), backward.astype(ml_dtypes.bfloat16)
 
 
 def sample_order(length, rate):
@@ -142,9 +162,7 @@
     trials, chans = responses.shape[0], responses.shape[1]
     count = chans // chans_local
     z_count = count // 4
-    forward, backward = dft_tables(length)
-    order = sample_order(length, RATE)
-    backward = jnp.concatenate([backward[:, order], backward[:, length + order]], 1)
+    forward, backward = (jnp.asarray(table) for table in constant_tables(length, RATE))
     local = jnp.dot(
         voltages.reshape(-1, 2 * length), forward, preferred_element_type=jnp.float32
     ).astype(jnp.bfloat16)

time: 109 us -> 104 us (0.954)
  local copies, waits for them, and re-layouts: 10.3 us -> 7.77 us
  other arithmetic: 2.27 us -> 0.07 us
    gather x4 -> x0, local copies, waits for them, and re-layouts: 2.57 us -> none  [the longest x2 1.29 us: shards(): backward[:, length + order]]
    another operation x2 -> x0, other arithmetic: 2.1 us -> none
  transfers between devices with their start and end apart: 10 -> 10, of which waited for: 6 -> 6; matrix products, arithmetic and copies ran while one was open for 7% -> 4% of each run, Pallas kernels for 0% -> 0%
where the time goes in v8:
time: 104 us
  blocking collectives  34.6 us (33%)
  starting transfers between devices  24.7 us (24%)
  waiting for transfers between devices  18.5 us (18%)
  Pallas kernels  16.8 us (16%)
  local copies, waits for them, and re-layouts  7.77 us (7%)
  matrix products  1.27 us (1%)
    all_to_all x1, blocking collectives, shards(): lax.all_to_all(detected.transpose(1, 0, 2, 3), 'beam', split_axis=1, conc...  34.6 us
    pallas_call x1, Pallas kernels, detect(): pl.pallas_call(detect_kernel, out_shape=jax.ShapeDtypeStruct((beams, tria...  16.8 us
    ppermute x3, starting transfers between devices, gather_spectra(): from_above.append(lax.ppermute(from_above[-1], 'dm', down))  13 us
    ppermute x3, waiting for transfers between devices, gather_spectra(): from_above.append(lax.ppermute(from_above[-1], 'dm', down))  10.6 us
    ppermute x1, starting transfers between devices, gather_spectra(): return (column, lax.ppermute(column, 'dm', partner))  6.2 us
    reshape x1, local copies, waits for them, and re-layouts, shards(): responses.reshape(trials, chans, 2 * length)  4.43 us
    ppermute x1, waiting for transfers between devices, gather_spectra(): lax.ppermute(from_below[-1][0], 'dm', up)  3.51 us
    ppermute x1, starting transfers between devices, gather_spectra(): lax.ppermute(from_above[-1][1], 'dm', down)  3.19 us
  transfers between devices with their start and end apart: 10, of which 6 were waited for; matrix products, arithmetic and copies ran while one was open for 4% of the time, Pallas kernels for 0%

profile of v8, /device:TPU:1, one launch (start us, length us, event | category | flops | bytes accessed | tf_op | source)
XLA Modules:
  0.0 103.9 jit_solution(16514875360693036426)
XLA Ops:
  0.0 0.9 copy.9
  0.9 1.3 %fusion = bf16[16,8,512]{2,1,0:T(8,128)(2,1)S(1)} fusion(bf16[128,512]{1,0:T(8,128)(2,1)S(1)} %bitcast.51, bf16[512,512]{1,0:T(8,128)(2,1)} %constant.83.clone), kind=kOutput, calls=%fused_computation.1 | convolution fusion | flops 67174400 | bytes 786432 | tf_op jit(solution)/shard_map/dot_general | solution.py:166
  2.3 2.1 %collective-permute-start = (bf16[8,16,512]{2,1,0:T(8,128)(2,1)S(1)}, bf16[8,16,512]{2,1,0:T(8,128)(2,1)S(1)}, u32[]{:S(2)}, u32[]{:S(2)}) collective-permute-start(bf16[8,16,512]{2,1,0:T(8,128)(2,1)S(1)} %bitcast.48), channel_id=1, source_target_pairs={{0,128},{8,136},{16,144},{24,152},{32,160},{40,168},{48,176},{56,1... | collective-permute-start | bytes 393224 | tf_op jit(solution)/shard_map/ppermute | solution.py:146
  4.4 2.4 %collective-permute-done = bf16[8,16,512]{2,1,0:T(8,128)(2,1)S(1)} collective-permute-done((bf16[8,16,512]{2,1,0:T(8,128)(2,1)S(1)}, bf16[8,16,512]{2,1,0:T(8,128)(2,1)S(1)}, u32[]{:S(2)}, u32[]{:S(2)}) %collective-permute-start) | collective-permute-done | bytes 131104 | tf_op jit(solution)/shard_map/ppermute | solution.py:146
  6.8 6.5 %collective-permute-start.1 = (bf16[2,8,16,512]{3,2,1,0:T(8,128)(2,1)S(1)}, bf16[2,8,16,512]{3,2,1,0:T(8,128)(2,1)S(1)}, u32[]{:S(2)}, u32[]{:S(2)}) collective-permute-start(bf16[2,8,16,512]{3,2,1,0:T(8,128)(2,1)S(1)} %pad_maximum_fusion), channel_id=1, source_target_pairs={{0,112},{8,120},{16,0},{24,8},{32,16},{40,24},{48,32},{56,40},{64,... | collective-permute-start | bytes 786440 | tf_op jit(solution)/shard_map/ppermute | solution.py:151
  13.2 4.1 %collective-permute-done.1 = bf16[2,8,16,512]{3,2,1,0:T(8,128)(2,1)S(1)} collective-permute-done((bf16[2,8,16,512]{3,2,1,0:T(8,128)(2,1)S(1)}, bf16[2,8,16,512]{3,2,1,0:T(8,128)(2,1)S(1)}, u32[]{:S(2)}, u32[]{:S(2)}) %collective-permute-start.1) | collective-permute-done | bytes 262176 | tf_op jit(solution)/shard_map/ppermute | solution.py:151
  17.4 3.4 %collective-permute-start.2 = (bf16[2,8,16,512]{3,2,1,0:T(8,128)(2,1)S(1)}, bf16[2,8,16,512]{3,2,1,0:T(8,128)(2,1)S(1)}, u32[]{:S(2)}, u32[]{:S(2)}) collective-permute-start(bf16[2,8,16,512]{3,2,1,0:T(8,128)(2,1)S(1)} %collective-permute-done.1), channel_id=1, source_target_pairs={{0,112},{8,120},{16,0},{24,8},{32,16},{40,24},{48,32},{56,40},{64,... | collective-permute-start | bytes 786440 | tf_op jit(solution)/shard_map/ppermute | solution.py:151
  20.8 0.0 collective-permute-done.4
  20.8 0.0 collective-permute-start.5
  20.8 3.3 %collective-permute-done.2 = bf16[2,8,16,512]{3,2,1,0:T(8,128)(2,1)S(1)} collective-permute-done((bf16[2,8,16,512]{3,2,1,0:T(8,128)(2,1)S(1)}, bf16[2,8,16,512]{3,2,1,0:T(8,128)(2,1)S(1)}, u32[]{:S(2)}, u32[]{:S(2)}) %collective-permute-start.2) | collective-permute-done | bytes 262176 | tf_op jit(solution)/shard_map/ppermute | solution.py:151
  24.1 3.1 %collective-permute-start.3 = (bf16[2,8,16,512]{3,2,1,0:T(8,128)(2,1)S(1)}, bf16[2,8,16,512]{3,2,1,0:T(8,128)(2,1)S(1)}, u32[]{:S(2)}, u32[]{:S(2)}) collective-permute-start(bf16[2,8,16,512]{3,2,1,0:T(8,128)(2,1)S(1)} %collective-permute-done.2), channel_id=1, source_target_pairs={{0,112},{8,120},{16,0},{24,8},{32,16},{40,24},{48,32},{56,40},{64,... | collective-permute-start | bytes 786440 | tf_op jit(solution)/shard_map/ppermute | solution.py:151
  27.2 0.1 collective-permute-start.6
  27.4 3.2 %collective-permute-done.3 = bf16[2,8,16,512]{3,2,1,0:T(8,128)(2,1)S(1)} collective-permute-done((bf16[2,8,16,512]{3,2,1,0:T(8,128)(2,1)S(1)}, bf16[2,8,16,512]{3,2,1,0:T(8,128)(2,1)S(1)}, u32[]{:S(2)}, u32[]{:S(2)}) %collective-permute-start.3) | collective-permute-done | bytes 262176 | tf_op jit(solution)/shard_map/ppermute | solution.py:151
  30.5 3.2 %collective-permute-start.8 = (bf16[8,16,512]{2,1,0:T(8,128)(2,1)S(1)}, bf16[8,16,512]{2,1,0:T(8,128)(2,1)S(1)}, u32[]{:S(2)}, u32[]{:S(2)}) collective-permute-start(bf16[8,16,512]{2,1,0:T(8,128)(2,1)S(1)} %slice_bitcast_fusion), channel_id=1, source_target_pairs={{0,112},{8,120},{16,0},{24,8},{32,16},{40,24},{48,32},{56,40},{64,... | collective-permute-start | bytes 393224 | tf_op jit(solution)/shard_map/ppermute | solution.py:153
  33.7 0.0 collective-permute-done.6
  33.8 0.1 collective-permute-start.7
  33.9 2.0 %collective-permute-done.8 = bf16[8,16,512]{2,1,0:T(8,128)(2,1)S(1)} collective-permute-done((bf16[8,16,512]{2,1,0:T(8,128)(2,1)S(1)}, bf16[8,16,512]{2,1,0:T(8,128)(2,1)S(1)}, u32[]{:S(2)}, u32[]{:S(2)}) %collective-permute-start.8) | collective-permute-done | bytes 131104 | tf_op jit(solution)/shard_map/ppermute | solution.py:153
  35.9 3.5 %collective-permute-done.7 = bf16[8,16,512]{2,1,0:T(8,128)(2,1)S(1)} collective-permute-done((bf16[8,16,512]{2,1,0:T(8,128)(2,1)S(1)}, bf16[8,16,512]{2,1,0:T(8,128)(2,1)S(1)}, u32[]{:S(2)}, u32[]{:S(2)}) %collective-permute-start.7) | collective-permute-done | bytes 131104 | tf_op jit(solution)/shard_map/ppermute | solution.py:153
  39.5 6.2 %collective-permute-start.9 = (bf16[16,8,16,512]{3,2,1,0:T(8,128)(2,1)S(1)}, bf16[16,8,16,512]{3,2,1,0:T(8,128)(2,1)}, u32[]{:S(2)}, u32[]{:S(2)}) collective-permute-start(bf16[16,8,16,512]{3,2,1,0:T(8,128)(2,1)S(1)} %bitcast.46), channel_id=1, source_target_pairs={{0,8},{8,0},{16,24},{24,16},{32,40},{40,32},{48,56},{56,48},{64,72... | collective-permute-start | bytes 6291464 | tf_op jit(solution)/shard_map/ppermute | solution.py:157
  45.7 4.4 %reshape.26.resp_ref = bf16[4,512,512]{2,1,0:T(8,128)(2,1)} reshape(bf16[4,512,2,256]{3,2,1,0:T(2,128)(2,1)} %param.6) | data formatting | bytes 4194304 | tf_op jit(solution)/shard_map/reshape | solution.py:176
  50.2 16.8 %shard_map.55 = bf16[8,4,256,128]{3,2,1,0:T(8,128)(2,1)S(1)} custom-call(s32[4]{0:T(128)S(1)} %copy-done, s32[16]{0:T(128)S(1)} %fusion.4.table_ref, s32[1]{0:T(128)} %bitcast.swap_ref, bf16[16,8,16,512]{3,2,1,0:T(8,128)(2,1)S(1)} %bitcast.47, bf16[16,8,16,512]{3,2,1,0:T(8,128)(2,1)} %collective-permute-done.9.theirs_ref, ...), custom_call_target="tpu_custom_call" | custom-call | flops 8589934592 | bytes 8912896 | tf_op jit(solution)/shard_map/pallas_call | solution.py:99
  67.0 34.6 %all_to_all.4 = bf16[4,8,256,128]{3,2,0,1:T(8,128)(2,1)S(1)} all-to-all(bf16[4,8,256,128]{3,2,0,1:T(8,128)(2,1)S(1)} %bitcast.45), channel_id=1, replica_groups=mesh['dm'=32,'beam'=8] {'beam'}, dimensions={1} | all-to-all | bytes 4194304 | tf_op jit(solution)/shard_map/all_to_all | solution.py:178
  101.6 0.1 copy.8
  101.8 2.1 %reshape.27 = bf16[4,1,262144]{2,0,1:T(4,128)(2,1)} reshape(bf16[4,8,256,128]{3,2,1,0:T(8,128)(2,1)S(1)} %copy.8) | data formatting | bytes 4194304 | tf_op jit(solution)/shard_map/reshape | solution.py:179
  (20 shorter events, 0.3 us)
Async XLA Ops:
  2.3 4.5 %collective-permute-start = (bf16[8,16,512]{2,1,0:T(8,128)(2,1)S(1)}, bf16[8,16,512]{2,1,0:T(8,128)(2,1)S(1)}, u32[]{:S(2)}, u32[]{:S(2)}) collective-permute-start(bf16[8,16,512]{2,1,0:T(8,128)(2,1)S(1)} %bitcast.48), channel_id=1, source_target_pairs={{0,128},{8,136},{16,144},{24,152},{32,160},{40,168},{48,176},{56,1... | collective-permute-start | bytes 393224 | tf_op jit(solution)/shard_map/ppermute | solution.py:146
  6.8 10.6 %collective-permute-start.1 = (bf16[2,8,16,512]{3,2,1,0:T(8,128)(2,1)S(1)}, bf16[2,8,16,512]{3,2,1,0:T(8,128)(2,1)S(1)}, u32[]{:S(2)}, u32[]{:S(2)}) collective-permute-start(bf16[2,8,16,512]{3,2,1,0:T(8,128)(2,1)S(1)} %pad_maximum_fusion), channel_id=1, source_target_pairs={{0,112},{8,120},{16,0},{24,8},{32,16},{40,24},{48,32},{56,40},{64,... | collective-permute-start | bytes 786440 | tf_op jit(solution)/shard_map/ppermute | solution.py:151
  13.2 7.5 %collective-permute-start.4 = (bf16[2,8,16,512]{3,2,1,0:T(8,128)(2,1)S(1)}, bf16[2,8,16,512]{3,2,1,0:T(8,128)(2,1)S(1)}, u32[]{:S(2)}, u32[]{:S(2)}) collective-permute-start(bf16[2,8,16,512]{3,2,1,0:T(8,128)(2,1)S(1)} %pad_maximum_fusion), channel_id=1, source_target_pairs={{0,16},{8,24},{16,32},{24,40},{32,48},{40,56},{48,64},{56,72},{64,... | collective-permute-start | bytes 786440 | tf_op jit(solution)/shard_map/ppermute | solution.py:150
  17.4 6.7 %collective-permute-start.2 = (bf16[2,8,16,512]{3,2,1,0:T(8,128)(2,1)S(1)}, bf16[2,8,16,512]{3,2,1,0:T(8,128)(2,1)S(1)}, u32[]{:S(2)}, u32[]{:S(2)}) collective-permute-start(bf16[2,8,16,512]{3,2,1,0:T(8,128)(2,1)S(1)} %collective-permute-done.1), channel_id=1, source_target_pairs={{0,112},{8,120},{16,0},{24,8},{32,16},{40,24},{48,32},{56,40},{64,... | collective-permute-start | bytes 786440 | tf_op jit(solution)/shard_map/ppermute | solution.py:151
  20.8 6.5 %collective-permute-start.5 = (bf16[2,8,16,512]{3,2,1,0:T(8,128)(2,1)S(1)}, bf16[2,8,16,512]{3,2,1,0:T(8,128)(2,1)S(1)}, u32[]{:S(2)}, u32[]{:S(2)}) collective-permute-start(bf16[2,8,16,512]{3,2,1,0:T(8,128)(2,1)S(1)} %collective-permute-done.4), channel_id=1, source_target_pairs={{0,16},{8,24},{16,32},{24,40},{32,48},{40,56},{48,64},{56,72},{64,... | collective-permute-start | bytes 786440 | tf_op jit(solution)/shard_map/ppermute | solution.py:150
  24.1 6.4 %collective-permute-start.3 = (bf16[2,8,16,512]{3,2,1,0:T(8,128)(2,1)S(1)}, bf16[2,8,16,512]{3,2,1,0:T(8,128)(2,1)S(1)}, u32[]{:S(2)}, u32[]{:S(2)}) collective-permute-start(bf16[2,8,16,512]{3,2,1,0:T(8,128)(2,1)S(1)} %collective-permute-done.2), channel_id=1, source_target_pairs={{0,112},{8,120},{16,0},{24,8},{32,16},{40,24},{48,32},{56,40},{64,... | collective-permute-start | bytes 786440 | tf_op jit(solution)/shard_map/ppermute | solution.py:151
  27.2 6.5 %collective-permute-start.6 = (bf16[2,8,16,512]{3,2,1,0:T(8,128)(2,1)S(1)}, bf16[2,8,16,512]{3,2,1,0:T(8,128)(2,1)S(1)}, u32[]{:S(2)}, u32[]{:S(2)}) collective-permute-start(bf16[2,8,16,512]{3,2,1,0:T(8,128)(2,1)S(1)} %collective-permute-done.5), channel_id=1, source_target_pairs={{0,16},{8,24},{16,32},{24,40},{32,48},{40,56},{48,64},{56,72},{64,... | collective-permute-start | bytes 786440 | tf_op jit(solution)/shard_map/ppermute | solution.py:150
  30.5 5.4 %collective-permute-start.8 = (bf16[8,16,512]{2,1,0:T(8,128)(2,1)S(1)}, bf16[8,16,512]{2,1,0:T(8,128)(2,1)S(1)}, u32[]{:S(2)}, u32[]{:S(2)}) collective-permute-start(bf16[8,16,512]{2,1,0:T(8,128)(2,1)S(1)} %slice_bitcast_fusion), channel_id=1, source_target_pairs={{0,112},{8,120},{16,0},{24,8},{32,16},{40,24},{48,32},{56,40},{64,... | collective-permute-start | bytes 393224 | tf_op jit(solution)/shard_map/ppermute | solution.py:153
  33.8 5.7 %collective-permute-start.7 = (bf16[8,16,512]{2,1,0:T(8,128)(2,1)S(1)}, bf16[8,16,512]{2,1,0:T(8,128)(2,1)S(1)}, u32[]{:S(2)}, u32[]{:S(2)}) collective-permute-start(bf16[8,16,512]{2,1,0:T(8,128)(2,1)S(1)} %slice_bitcast_fusion.1), channel_id=1, source_target_pairs={{0,16},{8,24},{16,32},{24,40},{32,48},{40,56},{48,64},{56,72},{64,... | collective-permute-start | bytes 393224 | tf_op jit(solution)/shard_map/ppermute | solution.py:153
  39.5 10.7 %collective-permute-start.9 = (bf16[16,8,16,512]{3,2,1,0:T(8,128)(2,1)S(1)}, bf16[16,8,16,512]{3,2,1,0:T(8,128)(2,1)}, u32[]{:S(2)}, u32[]{:S(2)}) collective-permute-start(bf16[16,8,16,512]{3,2,1,0:T(8,128)(2,1)S(1)} %bitcast.46), channel_id=1, source_target_pairs={{0,8},{8,0},{16,24},{24,16},{32,40},{40,32},{48,56},{56,48},{64,72... | collective-permute-start | bytes 6291464 | tf_op jit(solution)/shard_map/ppermute | solution.py:157
  45.7 4.5 %copy-start = (s32[4]{0:T(128)S(1)}, s32[4]{0:T(128)}, u32[]{:S(2)}) copy-start(s32[4]{0:T(128)} %chirp_ref.1) | copy-start | bytes 52
  45.7 4.5 %copy-start.1 = (bf16[512,512]{1,0:T(8,128)(2,1)S(1)}, bf16[512,512]{1,0:T(8,128)(2,1)}, u32[]{:S(2)}) copy-start(bf16[512,512]{1,0:T(8,128)(2,1)} %constant.84.clone.back_ref) | copy-start | bytes 1572868

commit v9 on v8

--- a/solution.py
+++ b/solution.py
@@ -53,16 +53,22 @@
     return rate * (pos % bins) + pos // bins
 
 
-def detect_kernel(chirp_ref, table_ref, swap_ref, mine_ref, theirs_ref, resp_ref, back_ref, out_ref, pair_ref):
-    _, beams, chans_local, width = mine_ref.shape
+def detect_kernel(
+    chirp_ref, table_ref, swap_ref, mine0_ref, theirs0_ref, mine1_ref, theirs1_ref, resp_ref, back_ref, out_ref,
+    pair_ref,
+):
+    _, beams, chans_local, width = mine0_ref.shape
     trials = resp_ref.shape[0]
     length = width // 2
     bins = length // RATE
-    chans = 2 * chans_local
+    chans = 4 * chans_local
     keep = swap_ref[0] == 0
-    mine = mine_ref[0]
-    theirs = theirs_ref[0]
-    x = jnp.concatenate([jnp.where(keep, mine, theirs), jnp.where(keep, theirs, mine)], axis=1)
+    pieces = []
+    for mine_ref, theirs_ref in ((mine0_ref, theirs0_ref), (mine1_ref, theirs1_ref)):
+        mine = mine_ref[0]
+        theirs = theirs_ref[0]
+        pieces += [jnp.where(keep, mine, theirs), jnp.where(keep, theirs, mine)]
+    x = jnp.concatenate(pieces, axis=1)
     xr = x[:, :, :length].astype(jnp.float32)
     xi = x[:, :, length:].astype(jnp.float32)
     back = back_ref[...]
@@ -93,7 +99,7 @@
     trials, chans = responses.shape[0], responses.shape[1]
     length = width // 2
     bins = length // RATE
-    step = 2 * chans_local
+    step = 4 * chans_local
     flops = 2 * trials * beams * chans * width * width
     bytes_accessed = 2 * (2 * mine.size + responses.size + backward.size + trials * beams * chans * bins)
     return pl.pallas_call(
@@ -103,8 +109,10 @@
             num_scalar_prefetch=3,
             grid=(chans // step,),
             in_specs=[
-                pl.BlockSpec((1, beams, chans_local, width), lambda n, cl, tb, sw: (tb[n], 0, 0, 0)),
-                pl.BlockSpec((1, beams, chans_local, width), lambda n, cl, tb, sw: (tb[n], 0, 0, 0)),
+                pl.BlockSpec((1, beams, chans_local, width), lambda n, cl, tb, sw: (tb[2 * n], 0, 0, 0)),
+                pl.BlockSpec((1, beams, chans_local, width), lambda n, cl, tb, sw: (tb[2 * n], 0, 0, 0)),
+                pl.BlockSpec((1, beams, chans_local, width), lambda n, cl, tb, sw: (tb[2 * n + 1], 0, 0, 0)),
+                pl.BlockSpec((1, beams, chans_local, width), lambda n, cl, tb, sw: (tb[2 * n + 1], 0, 0, 0)),
                 pl.BlockSpec((trials, step, width), lambda n, cl, tb, sw: (0, n, 0)),
                 pl.BlockSpec((width, width), lambda n, cl, tb, sw: (0, 0)),
             ],
@@ -117,7 +125,7 @@
             dimension_semantics=("arbitrary",), vmem_limit_bytes=48 * 1024 * 1024
         ),
         cost_estimate=pl.CostEstimate(flops=flops, transcendentals=0, bytes_accessed=bytes_accessed),
-    )(chirp_len, table, swap, mine, theirs, responses, backward)
+    )(chirp_len, table, swap, mine, theirs, mine, theirs, responses, backward)
 
 
 def coords(index, z_count):

time: 104 us -> 102 us (0.981)
  Pallas kernels: 16.8 us -> 14.2 us
    pallas_call x1, Pallas kernels: 16.8 us -> 14.2 us  [detect(): pl.pallas_call(detect_kernel, out_shape=jax.ShapeDtypeStruct((beams, tria...]
where the time goes in v9:
time: 102 us; the launch traced here: 101 us
  blocking collectives  34.6 us (34%)
  starting transfers between devices  24.7 us (24%)
  waiting for transfers between devices  18.5 us (18%)
  Pallas kernels  14.2 us (14%)
  local copies, waits for them, and re-layouts  7.77 us (8%)
  matrix products  1.27 us (1%)
    all_to_all x1, blocking collectives, shards(): lax.all_to_all(detected.transpose(1, 0, 2, 3), 'beam', split_axis=1, conc...  34.6 us
    pallas_call x1, Pallas kernels, detect(): pl.pallas_call(detect_kernel, out_shape=jax.ShapeDtypeStruct((beams, tria...  14.2 us
    ppermute x3, starting transfers between devices, gather_spectra(): from_above.append(lax.ppermute(from_above[-1], 'dm', down))  13 us
    ppermute x3, waiting for transfers between devices, gather_spectra(): from_above.append(lax.ppermute(from_above[-1], 'dm', down))  10.6 us
    ppermute x1, starting transfers between devices, gather_spectra(): return (column, lax.ppermute(column, 'dm', partner))  6.2 us
    reshape x1, local copies, waits for them, and re-layouts, shards(): responses.reshape(trials, chans, 2 * length)  4.43 us
    ppermute x1, waiting for transfers between devices, gather_spectra(): lax.ppermute(from_below[-1][0], 'dm', up)  3.51 us
    ppermute x1, starting transfers between devices, gather_spectra(): lax.ppermute(from_above[-1][1], 'dm', down)  3.19 us
  transfers between devices with their start and end apart: 10, of which 6 were waited for; matrix products, arithmetic and copies ran while one was open for 4% of the time, Pallas kernels for 0%

profile of v9, /device:TPU:1, one launch (start us, length us, event | category | flops | bytes accessed | tf_op | source)
XLA Modules:
  0.0 101.3 jit_solution(18382505480706288103)
XLA Ops:
  0.0 0.9 copy.9
  0.9 1.3 %fusion = bf16[16,8,512]{2,1,0:T(8,128)(2,1)S(1)} fusion(bf16[128,512]{1,0:T(8,128)(2,1)S(1)} %bitcast.52, bf16[512,512]{1,0:T(8,128)(2,1)} %constant.83.clone), kind=kOutput, calls=%fused_computation.1 | convolution fusion | flops 67174400 | bytes 786432 | tf_op jit(solution)/shard_map/dot_general | solution.py:174
  2.3 2.1 %collective-permute-start = (bf16[8,16,512]{2,1,0:T(8,128)(2,1)S(1)}, bf16[8,16,512]{2,1,0:T(8,128)(2,1)S(1)}, u32[]{:S(2)}, u32[]{:S(2)}) collective-permute-start(bf16[8,16,512]{2,1,0:T(8,128)(2,1)S(1)} %bitcast.49), channel_id=1, source_target_pairs={{0,128},{8,136},{16,144},{24,152},{32,160},{40,168},{48,176},{56,1... | collective-permute-start | bytes 393224 | tf_op jit(solution)/shard_map/ppermute | solution.py:154
  4.4 2.4 %collective-permute-done = bf16[8,16,512]{2,1,0:T(8,128)(2,1)S(1)} collective-permute-done((bf16[8,16,512]{2,1,0:T(8,128)(2,1)S(1)}, bf16[8,16,512]{2,1,0:T(8,128)(2,1)S(1)}, u32[]{:S(2)}, u32[]{:S(2)}) %collective-permute-start) | collective-permute-done | bytes 131104 | tf_op jit(solution)/shard_map/ppermute | solution.py:154
  6.8 6.5 %collective-permute-start.1 = (bf16[2,8,16,512]{3,2,1,0:T(8,128)(2,1)S(1)}, bf16[2,8,16,512]{3,2,1,0:T(8,128)(2,1)S(1)}, u32[]{:S(2)}, u32[]{:S(2)}) collective-permute-start(bf16[2,8,16,512]{3,2,1,0:T(8,128)(2,1)S(1)} %pad_maximum_fusion), channel_id=1, source_target_pairs={{0,112},{8,120},{16,0},{24,8},{32,16},{40,24},{48,32},{56,40},{64,... | collective-permute-start | bytes 786440 | tf_op jit(solution)/shard_map/ppermute | solution.py:159
  13.2 0.0 collective-permute-start.4
  13.2 4.1 %collective-permute-done.1 = bf16[2,8,16,512]{3,2,1,0:T(8,128)(2,1)S(1)} collective-permute-done((bf16[2,8,16,512]{3,2,1,0:T(8,128)(2,1)S(1)}, bf16[2,8,16,512]{3,2,1,0:T(8,128)(2,1)S(1)}, u32[]{:S(2)}, u32[]{:S(2)}) %collective-permute-start.1) | collective-permute-done | bytes 262176 | tf_op jit(solution)/shard_map/ppermute | solution.py:159
  17.4 3.4 %collective-permute-start.2 = (bf16[2,8,16,512]{3,2,1,0:T(8,128)(2,1)S(1)}, bf16[2,8,16,512]{3,2,1,0:T(8,128)(2,1)S(1)}, u32[]{:S(2)}, u32[]{:S(2)}) collective-permute-start(bf16[2,8,16,512]{3,2,1,0:T(8,128)(2,1)S(1)} %collective-permute-done.1), channel_id=1, source_target_pairs={{0,112},{8,120},{16,0},{24,8},{32,16},{40,24},{48,32},{56,40},{64,... | collective-permute-start | bytes 786440 | tf_op jit(solution)/shard_map/ppermute | solution.py:159
  20.8 3.3 %collective-permute-done.2 = bf16[2,8,16,512]{3,2,1,0:T(8,128)(2,1)S(1)} collective-permute-done((bf16[2,8,16,512]{3,2,1,0:T(8,128)(2,1)S(1)}, bf16[2,8,16,512]{3,2,1,0:T(8,128)(2,1)S(1)}, u32[]{:S(2)}, u32[]{:S(2)}) %collective-permute-start.2) | collective-permute-done | bytes 262176 | tf_op jit(solution)/shard_map/ppermute | solution.py:159
  24.1 3.1 %collective-permute-start.3 = (bf16[2,8,16,512]{3,2,1,0:T(8,128)(2,1)S(1)}, bf16[2,8,16,512]{3,2,1,0:T(8,128)(2,1)S(1)}, u32[]{:S(2)}, u32[]{:S(2)}) collective-permute-start(bf16[2,8,16,512]{3,2,1,0:T(8,128)(2,1)S(1)} %collective-permute-done.2), channel_id=1, source_target_pairs={{0,112},{8,120},{16,0},{24,8},{32,16},{40,24},{48,32},{56,40},{64,... | collective-permute-start | bytes 786440 | tf_op jit(solution)/shard_map/ppermute | solution.py:159
  27.2 0.1 collective-permute-start.6
  27.4 3.2 %collective-permute-done.3 = bf16[2,8,16,512]{3,2,1,0:T(8,128)(2,1)S(1)} collective-permute-done((bf16[2,8,16,512]{3,2,1,0:T(8,128)(2,1)S(1)}, bf16[2,8,16,512]{3,2,1,0:T(8,128)(2,1)S(1)}, u32[]{:S(2)}, u32[]{:S(2)}) %collective-permute-start.3) | collective-permute-done | bytes 262176 | tf_op jit(solution)/shard_map/ppermute | solution.py:159
  30.5 3.2 %collective-permute-start.8 = (bf16[8,16,512]{2,1,0:T(8,128)(2,1)S(1)}, bf16[8,16,512]{2,1,0:T(8,128)(2,1)S(1)}, u32[]{:S(2)}, u32[]{:S(2)}) collective-permute-start(bf16[8,16,512]{2,1,0:T(8,128)(2,1)S(1)} %slice_bitcast_fusion), channel_id=1, source_target_pairs={{0,112},{8,120},{16,0},{24,8},{32,16},{40,24},{48,32},{56,40},{64,... | collective-permute-start | bytes 393224 | tf_op jit(solution)/shard_map/ppermute | solution.py:161
  33.7 0.0 collective-permute-done.6
  33.8 0.1 collective-permute-start.7
  33.9 2.0 %collective-permute-done.8 = bf16[8,16,512]{2,1,0:T(8,128)(2,1)S(1)} collective-permute-done((bf16[8,16,512]{2,1,0:T(8,128)(2,1)S(1)}, bf16[8,16,512]{2,1,0:T(8,128)(2,1)S(1)}, u32[]{:S(2)}, u32[]{:S(2)}) %collective-permute-start.8) | collective-permute-done | bytes 131104 | tf_op jit(solution)/shard_map/ppermute | solution.py:161
  35.9 3.5 %collective-permute-done.7 = bf16[8,16,512]{2,1,0:T(8,128)(2,1)S(1)} collective-permute-done((bf16[8,16,512]{2,1,0:T(8,128)(2,1)S(1)}, bf16[8,16,512]{2,1,0:T(8,128)(2,1)S(1)}, u32[]{:S(2)}, u32[]{:S(2)}) %collective-permute-start.7) | collective-permute-done | bytes 131104 | tf_op jit(solution)/shard_map/ppermute | solution.py:161
  39.5 6.2 %collective-permute-start.9 = (bf16[16,8,16,512]{3,2,1,0:T(8,128)(2,1)S(1)}, bf16[16,8,16,512]{3,2,1,0:T(8,128)(2,1)}, u32[]{:S(2)}, u32[]{:S(2)}) collective-permute-start(bf16[16,8,16,512]{3,2,1,0:T(8,128)(2,1)S(1)} %bitcast.46), channel_id=1, source_target_pairs={{0,8},{8,0},{16,24},{24,16},{32,40},{40,32},{48,56},{56,48},{64,72... | collective-permute-start | bytes 6291464 | tf_op jit(solution)/shard_map/ppermute | solution.py:165
  45.7 4.4 %reshape.26.resp_ref = bf16[4,512,512]{2,1,0:T(8,128)(2,1)} reshape(bf16[4,512,2,256]{3,2,1,0:T(2,128)(2,1)} %param.6) | data formatting | bytes 4194304 | tf_op jit(solution)/shard_map/reshape | solution.py:184
  50.2 0.0 collective-permute-done.9.theirs0_ref.theirs1_ref
  50.2 14.2 %shard_map.55 = bf16[8,4,256,128]{3,2,1,0:T(8,128)(2,1)S(1)} custom-call(s32[4]{0:T(128)S(1)} %copy-done, s32[16]{0:T(128)S(1)} %fusion.4.table_ref, s32[1]{0:T(128)} %bitcast.swap_ref, bf16[16,8,16,512]{3,2,1,0:T(8,128)(2,1)S(1)} %bitcast.47, bf16[16,8,16,512]{3,2,1,0:T(8,128)(2,1)} %collective-permute-done.9.theirs0_ref.theirs1_ref, ...), custom_call_target="tpu_custom_call" | custom-call | flops 8589934592 | bytes 8912896 | tf_op jit(solution)/shard_map/pallas_call | solution.py:105
  64.4 34.6 %all_to_all.4 = bf16[4,8,256,128]{3,2,0,1:T(8,128)(2,1)S(1)} all-to-all(bf16[4,8,256,128]{3,2,0,1:T(8,128)(2,1)S(1)} %bitcast.45), channel_id=1, replica_groups=mesh['dm'=32,'beam'=8] {'beam'}, dimensions={1} | all-to-all | bytes 4194304 | tf_op jit(solution)/shard_map/all_to_all | solution.py:186
  99.1 0.1 copy.8
  99.2 2.1 %reshape.27 = bf16[4,1,262144]{2,0,1:T(4,128)(2,1)} reshape(bf16[4,8,256,128]{3,2,1,0:T(8,128)(2,1)S(1)} %copy.8) | data formatting | bytes 4194304 | tf_op jit(solution)/shard_map/reshape | solution.py:187
  (20 shorter events, 0.3 us)
Async XLA Ops:
  2.3 4.5 %collective-permute-start = (bf16[8,16,512]{2,1,0:T(8,128)(2,1)S(1)}, bf16[8,16,512]{2,1,0:T(8,128)(2,1)S(1)}, u32[]{:S(2)}, u32[]{:S(2)}) collective-permute-start(bf16[8,16,512]{2,1,0:T(8,128)(2,1)S(1)} %bitcast.49), channel_id=1, source_target_pairs={{0,128},{8,136},{16,144},{24,152},{32,160},{40,168},{48,176},{56,1... | collective-permute-start | bytes 393224 | tf_op jit(solution)/shard_map/ppermute | solution.py:154
  6.8 10.6 %collective-permute-start.1 = (bf16[2,8,16,512]{3,2,1,0:T(8,128)(2,1)S(1)}, bf16[2,8,16,512]{3,2,1,0:T(8,128)(2,1)S(1)}, u32[]{:S(2)}, u32[]{:S(2)}) collective-permute-start(bf16[2,8,16,512]{3,2,1,0:T(8,128)(2,1)S(1)} %pad_maximum_fusion), channel_id=1, source_target_pairs={{0,112},{8,120},{16,0},{24,8},{32,16},{40,24},{48,32},{56,40},{64,... | collective-permute-start | bytes 786440 | tf_op jit(solution)/shard_map/ppermute | solution.py:159
  13.2 7.5 %collective-permute-start.4 = (bf16[2,8,16,512]{3,2,1,0:T(8,128)(2,1)S(1)}, bf16[2,8,16,512]{3,2,1,0:T(8,128)(2,1)S(1)}, u32[]{:S(2)}, u32[]{:S(2)}) collective-permute-start(bf16[2,8,16,512]{3,2,1,0:T(8,128)(2,1)S(1)} %pad_maximum_fusion), channel_id=1, source_target_pairs={{0,16},{8,24},{16,32},{24,40},{32,48},{40,56},{48,64},{56,72},{64,... | collective-permute-start | bytes 786440 | tf_op jit(solution)/shard_map/ppermute | solution.py:158
  17.4 6.7 %collective-permute-start.2 = (bf16[2,8,16,512]{3,2,1,0:T(8,128)(2,1)S(1)}, bf16[2,8,16,512]{3,2,1,0:T(8,128)(2,1)S(1)}, u32[]{:S(2)}, u32[]{:S(2)}) collective-permute-start(bf16[2,8,16,512]{3,2,1,0:T(8,128)(2,1)S(1)} %collective-permute-done.1), channel_id=1, source_target_pairs={{0,112},{8,120},{16,0},{24,8},{32,16},{40,24},{48,32},{56,40},{64,... | collective-permute-start | bytes 786440 | tf_op jit(solution)/shard_map/ppermute | solution.py:159
  20.8 6.5 %collective-permute-start.5 = (bf16[2,8,16,512]{3,2,1,0:T(8,128)(2,1)S(1)}, bf16[2,8,16,512]{3,2,1,0:T(8,128)(2,1)S(1)}, u32[]{:S(2)}, u32[]{:S(2)}) collective-permute-start(bf16[2,8,16,512]{3,2,1,0:T(8,128)(2,1)S(1)} %collective-permute-done.4), channel_id=1, source_target_pairs={{0,16},{8,24},{16,32},{24,40},{32,48},{40,56},{48,64},{56,72},{64,... | collective-permute-start | bytes 786440 | tf_op jit(solution)/shard_map/ppermute | solution.py:158
  24.1 6.4 %collective-permute-start.3 = (bf16[2,8,16,512]{3,2,1,0:T(8,128)(2,1)S(1)}, bf16[2,8,16,512]{3,2,1,0:T(8,128)(2,1)S(1)}, u32[]{:S(2)}, u32[]{:S(2)}) collective-permute-start(bf16[2,8,16,512]{3,2,1,0:T(8,128)(2,1)S(1)} %collective-permute-done.2), channel_id=1, source_target_pairs={{0,112},{8,120},{16,0},{24,8},{32,16},{40,24},{48,32},{56,40},{64,... | collective-permute-start | bytes 786440 | tf_op jit(solution)/shard_map/ppermute | solution.py:159
  27.2 6.5 %collective-permute-start.6 = (bf16[2,8,16,512]{3,2,1,0:T(8,128)(2,1)S(1)}, bf16[2,8,16,512]{3,2,1,0:T(8,128)(2,1)S(1)}, u32[]{:S(2)}, u32[]{:S(2)}) collective-permute-start(bf16[2,8,16,512]{3,2,1,0:T(8,128)(2,1)S(1)} %collective-permute-done.5), channel_id=1, source_target_pairs={{0,16},{8,24},{16,32},{24,40},{32,48},{40,56},{48,64},{56,72},{64,... | collective-permute-start | bytes 786440 | tf_op jit(solution)/shard_map/ppermute | solution.py:158
  30.5 5.4 %collective-permute-start.8 = (bf16[8,16,512]{2,1,0:T(8,128)(2,1)S(1)}, bf16[8,16,512]{2,1,0:T(8,128)(2,1)S(1)}, u32[]{:S(2)}, u32[]{:S(2)}) collective-permute-start(bf16[8,16,512]{2,1,0:T(8,128)(2,1)S(1)} %slice_bitcast_fusion), channel_id=1, source_target_pairs={{0,112},{8,120},{16,0},{24,8},{32,16},{40,24},{48,32},{56,40},{64,... | collective-permute-start | bytes 393224 | tf_op jit(solution)/shard_map/ppermute | solution.py:161
  33.8 5.7 %collective-permute-start.7 = (bf16[8,16,512]{2,1,0:T(8,128)(2,1)S(1)}, bf16[8,16,512]{2,1,0:T(8,128)(2,1)S(1)}, u32[]{:S(2)}, u32[]{:S(2)}) collective-permute-start(bf16[8,16,512]{2,1,0:T(8,128)(2,1)S(1)} %slice_bitcast_fusion.1), channel_id=1, source_target_pairs={{0,16},{8,24},{16,32},{24,40},{32,48},{40,56},{48,64},{56,72},{64,... | collective-permute-start | bytes 393224 | tf_op jit(solution)/shard_map/ppermute | solution.py:161
  39.5 10.7 %collective-permute-start.9 = (bf16[16,8,16,512]{3,2,1,0:T(8,128)(2,1)S(1)}, bf16[16,8,16,512]{3,2,1,0:T(8,128)(2,1)}, u32[]{:S(2)}, u32[]{:S(2)}) collective-permute-start(bf16[16,8,16,512]{3,2,1,0:T(8,128)(2,1)S(1)} %bitcast.46), channel_id=1, source_target_pairs={{0,8},{8,0},{16,24},{24,16},{32,40},{40,32},{48,56},{56,48},{64,72... | collective-permute-start | bytes 6291464 | tf_op jit(solution)/shard_map/ppermute | solution.py:165
  45.7 4.5 %copy-start = (s32[4]{0:T(128)S(1)}, s32[4]{0:T(128)}, u32[]{:S(2)}) copy-start(s32[4]{0:T(128)} %chirp_ref.1) | copy-start | bytes 52
  45.7 4.5 %copy-start.1 = (bf16[512,512]{1,0:T(8,128)(2,1)S(1)}, bf16[512,512]{1,0:T(8,128)(2,1)}, u32[]{:S(2)}) copy-start(bf16[512,512]{1,0:T(8,128)(2,1)} %constant.84.clone.back_ref) | copy-start | bytes 1572868

commit v10 on v8

--- a/solution.py
+++ b/solution.py
@@ -12,6 +12,7 @@
 
 RATE = 4
 CHAN_BLOCK = 256
+GROUP = 4
 
 
 def dft_tables(length):
@@ -53,16 +54,21 @@
     return rate * (pos % bins) + pos // bins
 
 
-def detect_kernel(chirp_ref, table_ref, swap_ref, mine_ref, theirs_ref, resp_ref, back_ref, out_ref, pair_ref):
-    _, beams, chans_local, width = mine_ref.shape
+def detect_kernel(chirp_ref, table_ref, swap_ref, *refs):
+    spec_refs = refs[: 2 * GROUP]
+    resp_ref, back_ref, out_ref, pair_ref = refs[2 * GROUP :]
+    _, beams, chans_local, width = spec_refs[0].shape
     trials = resp_ref.shape[0]
     length = width // 2
     bins = length // RATE
-    chans = 2 * chans_local
+    chans = 2 * GROUP * chans_local
     keep = swap_ref[0] == 0
-    mine = mine_ref[0]
-    theirs = theirs_ref[0]
-    x = jnp.concatenate([jnp.where(keep, mine, theirs), jnp.where(keep, theirs, mine)], axis=1)
+    pieces = []
+    for g in range(GROUP):
+        mine = spec_refs[2 * g][0]
+        theirs = spec_refs[2 * g + 1][0]
+        pieces += [jnp.where(keep, mine, theirs), jnp.where(keep, theirs, mine)]
+    x = jnp.concatenate(pieces, axis=1)
     xr = x[:, :, :length].astype(jnp.float32)
     xi = x[:, :, length:].astype(jnp.float32)
     back = back_ref[...]
@@ -93,18 +99,22 @@
     trials, chans = responses.shape[0], responses.shape[1]
     length = width // 2
     bins = length // RATE
-    step = 2 * chans_local
+    step = 2 * GROUP * chans_local
     flops = 2 * trials * beams * chans * width * width
     bytes_accessed = 2 * (2 * mine.size + responses.size + backward.size + trials * beams * chans * bins)
+    spec_specs = []
+    for g in range(GROUP):
+        spec = pl.BlockSpec(
+            (1, beams, chans_local, width), lambda n, cl, tb, sw, g=g: (tb[GROUP * n + g], 0, 0, 0)
+        )
+        spec_specs += [spec, spec]
     return pl.pallas_call(
         detect_kernel,
         out_shape=jax.ShapeDtypeStruct((beams, trials, chans // 2, 2 * bins), jnp.bfloat16),
         grid_spec=pltpu.PrefetchScalarGridSpec(
             num_scalar_prefetch=3,
             grid=(chans // step,),
-            in_specs=[
-                pl.BlockSpec((1, beams, chans_local, width), lambda n, cl, tb, sw: (tb[n], 0, 0, 0)),
-                pl.BlockSpec((1, beams, chans_local, width), lambda n, cl, tb, sw: (tb[n], 0, 0, 0)),
+            in_specs=spec_specs + [
                 pl.BlockSpec((trials, step, width), lambda n, cl, tb, sw: (0, n, 0)),
                 pl.BlockSpec((width, width), lambda n, cl, tb, sw: (0, 0)),
             ],
@@ -117,7 +127,7 @@
             dimension_semantics=("arbitrary",), vmem_limit_bytes=48 * 1024 * 1024
         ),
         cost_estimate=pl.CostEstimate(flops=flops, transcendentals=0, bytes_accessed=bytes_accessed),
-    )(chirp_len, table, swap, mine, theirs, responses, backward)
+    )(chirp_len, table, swap, *([mine, theirs] * GROUP), responses, backward)
 
 
 def coords(index, z_count):

time: 104 us -> 101 us (0.971)
  Pallas kernels: 16.8 us -> 13.5 us
    pallas_call x1, Pallas kernels: 16.8 us -> 13.5 us  [detect(): pl.pallas_call(detect_kernel, out_shape=jax.ShapeDtypeStruct((beams, tria...]
  transfers between devices with their start and end apart: 10 -> 10, of which waited for: 6 -> 6; matrix products, arithmetic and copies ran while one was open for 4% -> 5% of each run, Pallas kernels for 0% -> 0%
where the time goes in v10:
time: 101 us
  blocking collectives  34.6 us (34%)
  starting transfers between devices  24.7 us (24%)
  waiting for transfers between devices  18.5 us (18%)
  Pallas kernels  13.5 us (13%)
  local copies, waits for them, and re-layouts  7.77 us (8%)
  matrix products  1.27 us (1%)
    all_to_all x1, blocking collectives, shards(): lax.all_to_all(detected.transpose(1, 0, 2, 3), 'beam', split_axis=1, conc...  34.6 us
    pallas_call x1, Pallas kernels, detect(): pl.pallas_call(detect_kernel, out_shape=jax.ShapeDtypeStruct((beams, tria...  13.5 us
    ppermute x3, starting transfers between devices, gather_spectra(): from_above.append(lax.ppermute(from_above[-1], 'dm', down))  13 us
    ppermute x3, waiting for transfers between devices, gather_spectra(): from_above.append(lax.ppermute(from_above[-1], 'dm', down))  10.6 us
    ppermute x1, starting transfers between devices, gather_spectra(): return (column, lax.ppermute(column, 'dm', partner))  6.2 us
    reshape x1, local copies, waits for them, and re-layouts, shards(): responses.reshape(trials, chans, 2 * length)  4.43 us
    ppermute x1, waiting for transfers between devices, gather_spectra(): lax.ppermute(from_below[-1][0], 'dm', up)  3.51 us
    ppermute x1, starting transfers between devices, gather_spectra(): lax.ppermute(from_above[-1][1], 'dm', down)  3.19 us
  transfers between devices with their start and end apart: 10, of which 6 were waited for; matrix products, arithmetic and copies ran while one was open for 5% of the time, Pallas kernels for 0%

profile of v10, /device:TPU:1, one launch (start us, length us, event | category | flops | bytes accessed | tf_op | source)
XLA Modules:
  0.0 100.6 jit_solution(3714709437058962109)
XLA Ops:
  0.0 0.9 copy.9
  0.9 1.3 %fusion = bf16[16,8,512]{2,1,0:T(8,128)(2,1)S(1)} fusion(bf16[128,512]{1,0:T(8,128)(2,1)S(1)} %bitcast.54, bf16[512,512]{1,0:T(8,128)(2,1)} %constant.83.clone), kind=kOutput, calls=%fused_computation.1 | convolution fusion | flops 67174400 | bytes 786432 | tf_op jit(solution)/shard_map/dot_general | solution.py:176
  2.3 2.1 %collective-permute-start = (bf16[8,16,512]{2,1,0:T(8,128)(2,1)S(1)}, bf16[8,16,512]{2,1,0:T(8,128)(2,1)S(1)}, u32[]{:S(2)}, u32[]{:S(2)}) collective-permute-start(bf16[8,16,512]{2,1,0:T(8,128)(2,1)S(1)} %bitcast.51), channel_id=1, source_target_pairs={{0,128},{8,136},{16,144},{24,152},{32,160},{40,168},{48,176},{56,1... | collective-permute-start | bytes 393224 | tf_op jit(solution)/shard_map/ppermute | solution.py:156
  4.4 2.4 %collective-permute-done = bf16[8,16,512]{2,1,0:T(8,128)(2,1)S(1)} collective-permute-done((bf16[8,16,512]{2,1,0:T(8,128)(2,1)S(1)}, bf16[8,16,512]{2,1,0:T(8,128)(2,1)S(1)}, u32[]{:S(2)}, u32[]{:S(2)}) %collective-permute-start) | collective-permute-done | bytes 131104 | tf_op jit(solution)/shard_map/ppermute | solution.py:156
  6.8 6.5 %collective-permute-start.1 = (bf16[2,8,16,512]{3,2,1,0:T(8,128)(2,1)S(1)}, bf16[2,8,16,512]{3,2,1,0:T(8,128)(2,1)S(1)}, u32[]{:S(2)}, u32[]{:S(2)}) collective-permute-start(bf16[2,8,16,512]{3,2,1,0:T(8,128)(2,1)S(1)} %pad_maximum_fusion), channel_id=1, source_target_pairs={{0,112},{8,120},{16,0},{24,8},{32,16},{40,24},{48,32},{56,40},{64,... | collective-permute-start | bytes 786440 | tf_op jit(solution)/shard_map/ppermute | solution.py:161
  13.2 0.0 collective-permute-start.4
  13.2 4.1 %collective-permute-done.1 = bf16[2,8,16,512]{3,2,1,0:T(8,128)(2,1)S(1)} collective-permute-done((bf16[2,8,16,512]{3,2,1,0:T(8,128)(2,1)S(1)}, bf16[2,8,16,512]{3,2,1,0:T(8,128)(2,1)S(1)}, u32[]{:S(2)}, u32[]{:S(2)}) %collective-permute-start.1) | collective-permute-done | bytes 262176 | tf_op jit(solution)/shard_map/ppermute | solution.py:161
  17.4 3.4 %collective-permute-start.2 = (bf16[2,8,16,512]{3,2,1,0:T(8,128)(2,1)S(1)}, bf16[2,8,16,512]{3,2,1,0:T(8,128)(2,1)S(1)}, u32[]{:S(2)}, u32[]{:S(2)}) collective-permute-start(bf16[2,8,16,512]{3,2,1,0:T(8,128)(2,1)S(1)} %collective-permute-done.1), channel_id=1, source_target_pairs={{0,112},{8,120},{16,0},{24,8},{32,16},{40,24},{48,32},{56,40},{64,... | collective-permute-start | bytes 786440 | tf_op jit(solution)/shard_map/ppermute | solution.py:161
  20.8 3.3 %collective-permute-done.2 = bf16[2,8,16,512]{3,2,1,0:T(8,128)(2,1)S(1)} collective-permute-done((bf16[2,8,16,512]{3,2,1,0:T(8,128)(2,1)S(1)}, bf16[2,8,16,512]{3,2,1,0:T(8,128)(2,1)S(1)}, u32[]{:S(2)}, u32[]{:S(2)}) %collective-permute-start.2) | collective-permute-done | bytes 262176 | tf_op jit(solution)/shard_map/ppermute | solution.py:161
  24.1 3.1 %collective-permute-start.3 = (bf16[2,8,16,512]{3,2,1,0:T(8,128)(2,1)S(1)}, bf16[2,8,16,512]{3,2,1,0:T(8,128)(2,1)S(1)}, u32[]{:S(2)}, u32[]{:S(2)}) collective-permute-start(bf16[2,8,16,512]{3,2,1,0:T(8,128)(2,1)S(1)} %collective-permute-done.2), channel_id=1, source_target_pairs={{0,112},{8,120},{16,0},{24,8},{32,16},{40,24},{48,32},{56,40},{64,... | collective-permute-start | bytes 786440 | tf_op jit(solution)/shard_map/ppermute | solution.py:161
  27.2 0.1 collective-permute-start.6
  27.4 3.2 %collective-permute-done.3 = bf16[2,8,16,512]{3,2,1,0:T(8,128)(2,1)S(1)} collective-permute-done((bf16[2,8,16,512]{3,2,1,0:T(8,128)(2,1)S(1)}, bf16[2,8,16,512]{3,2,1,0:T(8,128)(2,1)S(1)}, u32[]{:S(2)}, u32[]{:S(2)}) %collective-permute-start.3) | collective-permute-done | bytes 262176 | tf_op jit(solution)/shard_map/ppermute | solution.py:161
  30.5 3.2 %collective-permute-start.8 = (bf16[8,16,512]{2,1,0:T(8,128)(2,1)S(1)}, bf16[8,16,512]{2,1,0:T(8,128)(2,1)S(1)}, u32[]{:S(2)}, u32[]{:S(2)}) collective-permute-start(bf16[8,16,512]{2,1,0:T(8,128)(2,1)S(1)} %slice_bitcast_fusion), channel_id=1, source_target_pairs={{0,112},{8,120},{16,0},{24,8},{32,16},{40,24},{48,32},{56,40},{64,... | collective-permute-start | bytes 393224 | tf_op jit(solution)/shard_map/ppermute | solution.py:163
  33.7 0.0 collective-permute-done.6
  33.8 0.1 collective-permute-start.7
  33.9 2.0 %collective-permute-done.8 = bf16[8,16,512]{2,1,0:T(8,128)(2,1)S(1)} collective-permute-done((bf16[8,16,512]{2,1,0:T(8,128)(2,1)S(1)}, bf16[8,16,512]{2,1,0:T(8,128)(2,1)S(1)}, u32[]{:S(2)}, u32[]{:S(2)}) %collective-permute-start.8) | collective-permute-done | bytes 131104 | tf_op jit(solution)/shard_map/ppermute | solution.py:163
  35.9 3.5 %collective-permute-done.7 = bf16[8,16,512]{2,1,0:T(8,128)(2,1)S(1)} collective-permute-done((bf16[8,16,512]{2,1,0:T(8,128)(2,1)S(1)}, bf16[8,16,512]{2,1,0:T(8,128)(2,1)S(1)}, u32[]{:S(2)}, u32[]{:S(2)}) %collective-permute-start.7) | collective-permute-done | bytes 131104 | tf_op jit(solution)/shard_map/ppermute | solution.py:163
  39.5 6.2 %collective-permute-start.9 = (bf16[16,8,16,512]{3,2,1,0:T(8,128)(2,1)S(1)}, bf16[16,8,16,512]{3,2,1,0:T(8,128)(2,1)}, u32[]{:S(2)}, u32[]{:S(2)}) collective-permute-start(bf16[16,8,16,512]{3,2,1,0:T(8,128)(2,1)S(1)} %bitcast.46), channel_id=1, source_target_pairs={{0,8},{8,0},{16,24},{24,16},{32,40},{40,32},{48,56},{56,48},{64,72... | collective-permute-start | bytes 6291464 | tf_op jit(solution)/shard_map/ppermute | solution.py:167
  45.7 4.4 %reshape.26.refs_8_ = bf16[4,512,512]{2,1,0:T(8,128)(2,1)} reshape(bf16[4,512,2,256]{3,2,1,0:T(2,128)(2,1)} %param.6) | data formatting | bytes 4194304 | tf_op jit(solution)/shard_map/reshape | solution.py:186
  50.2 0.0 collective-permute-done.9.refs_1_.refs_3_.refs_5_.refs_7_
  50.2 13.5 %shard_map.55 = bf16[8,4,256,128]{3,2,1,0:T(8,128)(2,1)S(1)} custom-call(s32[4]{0:T(128)S(1)} %copy-done, s32[16]{0:T(128)S(1)} %fusion.4.table_ref, s32[1]{0:T(128)} %bitcast.swap_ref, bf16[16,8,16,512]{3,2,1,0:T(8,128)(2,1)S(1)} %bitcast.47, bf16[16,8,16,512]{3,2,1,0:T(8,128)(2,1)} %collective-permute-done.9.refs_1_.refs_3_.refs_5_.refs_7_, ...), custom_call_target="tpu_custom_call" | custom-call | flops 8589934592 | bytes 8912896 | tf_op jit(solution)/shard_map/pallas_call | solution.py:111
  63.7 34.6 %all_to_all.4 = bf16[4,8,256,128]{3,2,0,1:T(8,128)(2,1)S(1)} all-to-all(bf16[4,8,256,128]{3,2,0,1:T(8,128)(2,1)S(1)} %bitcast.45), channel_id=1, replica_groups=mesh['dm'=32,'beam'=8] {'beam'}, dimensions={1} | all-to-all | bytes 4194304 | tf_op jit(solution)/shard_map/all_to_all | solution.py:188
  98.3 0.1 copy.8
  98.5 2.1 %reshape.27 = bf16[4,1,262144]{2,0,1:T(4,128)(2,1)} reshape(bf16[4,8,256,128]{3,2,1,0:T(8,128)(2,1)S(1)} %copy.8) | data formatting | bytes 4194304 | tf_op jit(solution)/shard_map/reshape | solution.py:189
  (20 shorter events, 0.3 us)
Async XLA Ops:
  2.3 4.5 %collective-permute-start = (bf16[8,16,512]{2,1,0:T(8,128)(2,1)S(1)}, bf16[8,16,512]{2,1,0:T(8,128)(2,1)S(1)}, u32[]{:S(2)}, u32[]{:S(2)}) collective-permute-start(bf16[8,16,512]{2,1,0:T(8,128)(2,1)S(1)} %bitcast.51), channel_id=1, source_target_pairs={{0,128},{8,136},{16,144},{24,152},{32,160},{40,168},{48,176},{56,1... | collective-permute-start | bytes 393224 | tf_op jit(solution)/shard_map/ppermute | solution.py:156
  6.8 10.6 %collective-permute-start.1 = (bf16[2,8,16,512]{3,2,1,0:T(8,128)(2,1)S(1)}, bf16[2,8,16,512]{3,2,1,0:T(8,128)(2,1)S(1)}, u32[]{:S(2)}, u32[]{:S(2)}) collective-permute-start(bf16[2,8,16,512]{3,2,1,0:T(8,128)(2,1)S(1)} %pad_maximum_fusion), channel_id=1, source_target_pairs={{0,112},{8,120},{16,0},{24,8},{32,16},{40,24},{48,32},{56,40},{64,... | collective-permute-start | bytes 786440 | tf_op jit(solution)/shard_map/ppermute | solution.py:161
  13.2 7.5 %collective-permute-start.4 = (bf16[2,8,16,512]{3,2,1,0:T(8,128)(2,1)S(1)}, bf16[2,8,16,512]{3,2,1,0:T(8,128)(2,1)S(1)}, u32[]{:S(2)}, u32[]{:S(2)}) collective-permute-start(bf16[2,8,16,512]{3,2,1,0:T(8,128)(2,1)S(1)} %pad_maximum_fusion), channel_id=1, source_target_pairs={{0,16},{8,24},{16,32},{24,40},{32,48},{40,56},{48,64},{56,72},{64,... | collective-permute-start | bytes 786440 | tf_op jit(solution)/shard_map/ppermute | solution.py:160
  17.4 6.7 %collective-permute-start.2 = (bf16[2,8,16,512]{3,2,1,0:T(8,128)(2,1)S(1)}, bf16[2,8,16,512]{3,2,1,0:T(8,128)(2,1)S(1)}, u32[]{:S(2)}, u32[]{:S(2)}) collective-permute-start(bf16[2,8,16,512]{3,2,1,0:T(8,128)(2,1)S(1)} %collective-permute-done.1), channel_id=1, source_target_pairs={{0,112},{8,120},{16,0},{24,8},{32,16},{40,24},{48,32},{56,40},{64,... | collective-permute-start | bytes 786440 | tf_op jit(solution)/shard_map/ppermute | solution.py:161
  20.8 6.5 %collective-permute-start.5 = (bf16[2,8,16,512]{3,2,1,0:T(8,128)(2,1)S(1)}, bf16[2,8,16,512]{3,2,1,0:T(8,128)(2,1)S(1)}, u32[]{:S(2)}, u32[]{:S(2)}) collective-permute-start(bf16[2,8,16,512]{3,2,1,0:T(8,128)(2,1)S(1)} %collective-permute-done.4), channel_id=1, source_target_pairs={{0,16},{8,24},{16,32},{24,40},{32,48},{40,56},{48,64},{56,72},{64,... | collective-permute-start | bytes 786440 | tf_op jit(solution)/shard_map/ppermute | solution.py:160
  24.1 6.4 %collective-permute-start.3 = (bf16[2,8,16,512]{3,2,1,0:T(8,128)(2,1)S(1)}, bf16[2,8,16,512]{3,2,1,0:T(8,128)(2,1)S(1)}, u32[]{:S(2)}, u32[]{:S(2)}) collective-permute-start(bf16[2,8,16,512]{3,2,1,0:T(8,128)(2,1)S(1)} %collective-permute-done.2), channel_id=1, source_target_pairs={{0,112},{8,120},{16,0},{24,8},{32,16},{40,24},{48,32},{56,40},{64,... | collective-permute-start | bytes 786440 | tf_op jit(solution)/shard_map/ppermute | solution.py:161
  27.2 6.5 %collective-permute-start.6 = (bf16[2,8,16,512]{3,2,1,0:T(8,128)(2,1)S(1)}, bf16[2,8,16,512]{3,2,1,0:T(8,128)(2,1)S(1)}, u32[]{:S(2)}, u32[]{:S(2)}) collective-permute-start(bf16[2,8,16,512]{3,2,1,0:T(8,128)(2,1)S(1)} %collective-permute-done.5), channel_id=1, source_target_pairs={{0,16},{8,24},{16,32},{24,40},{32,48},{40,56},{48,64},{56,72},{64,... | collective-permute-start | bytes 786440 | tf_op jit(solution)/shard_map/ppermute | solution.py:160
  30.5 5.4 %collective-permute-start.8 = (bf16[8,16,512]{2,1,0:T(8,128)(2,1)S(1)}, bf16[8,16,512]{2,1,0:T(8,128)(2,1)S(1)}, u32[]{:S(2)}, u32[]{:S(2)}) collective-permute-start(bf16[8,16,512]{2,1,0:T(8,128)(2,1)S(1)} %slice_bitcast_fusion), channel_id=1, source_target_pairs={{0,112},{8,120},{16,0},{24,8},{32,16},{40,24},{48,32},{56,40},{64,... | collective-permute-start | bytes 393224 | tf_op jit(solution)/shard_map/ppermute | solution.py:163
  33.8 5.7 %collective-permute-start.7 = (bf16[8,16,512]{2,1,0:T(8,128)(2,1)S(1)}, bf16[8,16,512]{2,1,0:T(8,128)(2,1)S(1)}, u32[]{:S(2)}, u32[]{:S(2)}) collective-permute-start(bf16[8,16,512]{2,1,0:T(8,128)(2,1)S(1)} %slice_bitcast_fusion.1), channel_id=1, source_target_pairs={{0,16},{8,24},{16,32},{24,40},{32,48},{40,56},{48,64},{56,72},{64,... | collective-permute-start | bytes 393224 | tf_op jit(solution)/shard_map/ppermute | solution.py:163
  39.5 10.7 %collective-permute-start.9 = (bf16[16,8,16,512]{3,2,1,0:T(8,128)(2,1)S(1)}, bf16[16,8,16,512]{3,2,1,0:T(8,128)(2,1)}, u32[]{:S(2)}, u32[]{:S(2)}) collective-permute-start(bf16[16,8,16,512]{3,2,1,0:T(8,128)(2,1)S(1)} %bitcast.46), channel_id=1, source_target_pairs={{0,8},{8,0},{16,24},{24,16},{32,40},{40,32},{48,56},{56,48},{64,72... | collective-permute-start | bytes 6291464 | tf_op jit(solution)/shard_map/ppermute | solution.py:167
  45.7 4.5 %copy-start = (s32[4]{0:T(128)S(1)}, s32[4]{0:T(128)}, u32[]{:S(2)}) copy-start(s32[4]{0:T(128)} %chirp_ref.1) | copy-start | bytes 52
  45.7 4.5 %copy-start.1 = (bf16[512,512]{1,0:T(8,128)(2,1)S(1)}, bf16[512,512]{1,0:T(8,128)(2,1)}, u32[]{:S(2)}) copy-start(bf16[512,512]{1,0:T(8,128)(2,1)} %constant.84.clone.refs_9_) | copy-start | bytes 1572868

commit v11 on v10

--- a/solution.py
+++ b/solution.py
@@ -147,7 +147,7 @@
     return pairs
 
 
-def gather_spectra(own, count):
+def gather_spectra(own, count, carried):
     z_count = count // 4
     across = moves(count, lambda x, z, c, n: flat(1 - x, z, c, n))
     up = moves(count, lambda x, z, c, n: flat(x, z + 1, c, n))
@@ -156,15 +156,19 @@
     pair = jnp.stack([own, lax.ppermute(own, "dm", across)])
     from_below = [pair]
     from_above = [pair]
-    for _ in range(z_count // 2 - 1):
+    for k in range(z_count // 2 - 1):
         from_below.append(lax.ppermute(from_below[-1], "dm", up))
         from_above.append(lax.ppermute(from_above[-1], "dm", down))
+        if k == 0:
+            from_below[-1], from_above[-1], carried = lax.optimization_barrier(
+                (from_below[-1], from_above[-1], carried)
+            )
     far = jnp.stack(
         [lax.ppermute(from_below[-1][0], "dm", up), lax.ppermute(from_above[-1][1], "dm", down)]
     )
     column = jnp.stack(from_above + [far] + from_below[:0:-1])
     column = column.reshape((2 * z_count,) + own.shape)
-    return column, lax.ppermute(column, "dm", partner)
+    return column, lax.ppermute(column, "dm", partner), carried
 
 
 def shards(voltages, responses, chirp_len):
@@ -177,13 +181,14 @@
         voltages.reshape(-1, 2 * length), forward, preferred_element_type=jnp.float32
     ).astype(jnp.bfloat16)
     local = local.reshape(chans_local, beams, 2 * length).transpose(1, 0, 2)
-    mine, theirs = gather_spectra(local, count)
+    resp = responses.reshape(trials, chans, 2 * length)
+    mine, theirs, resp = gather_spectra(local, count, resp)
     x_me, z_me, c_me = coords(lax.axis_index("dm"), z_count)
     block = jnp.arange(count // 2, dtype=jnp.int32)
     table = ((block % z_count - z_me) % z_count) * 2 + ((block // z_count) ^ x_me)
     swap = jnp.reshape(c_me, (1,)).astype(jnp.int32)
     detected = detect(
-        table, swap, mine, theirs, responses.reshape(trials, chans, 2 * length), chirp_len, backward
+        table, swap, mine, theirs, resp, chirp_len, backward
     )
     moved = lax.all_to_all(detected.transpose(1, 0, 2, 3), "beam", split_axis=1, concat_axis=2, tiled=True)
     return moved.reshape(trials, 1, -1)

time: 101 us -> 99.8 us (0.988)
    ppermute x3, waiting for transfers between devices: 10.6 us -> 6.44 us  [gather_spectra(): from_above.append(lax.ppermute(from_above[-1], 'dm', down))]
    ppermute x1, waiting for transfers between devices: 0.01 us -> 3.9 us  [gather_spectra(): return (column, lax.ppermute(column, 'dm', partner), carried)]
    ppermute x3, starting transfers between devices: 13 us -> 9.63 us  [gather_spectra(): from_above.append(lax.ppermute(from_above[-1], 'dm', down))]
    ppermute x3, starting transfers between devices: 0.09 us -> 2.61 us  [gather_spectra(): from_below.append(lax.ppermute(from_below[-1], 'dm', up))]
  transfers between devices with their start and end apart: 10 -> 10, of which waited for: 6 -> 7; matrix products, arithmetic and copies ran while one was open for 5% -> 4% of each run, Pallas kernels for 0% -> 0%
where the time goes in v11:
time: 99.8 us; the launch traced here: 99.5 us
  blocking collectives  34 us (34%)
  starting transfers between devices  23.8 us (24%)
  waiting for transfers between devices  19 us (19%)
  Pallas kernels  13.5 us (14%)
  local copies, waits for them, and re-layouts  7.71 us (8%)
  matrix products  1.27 us (1%)
    all_to_all x1, blocking collectives, shards(): lax.all_to_all(detected.transpose(1, 0, 2, 3), 'beam', split_axis=1, conc...  34 us
    pallas_call x1, Pallas kernels, detect(): pl.pallas_call(detect_kernel, out_shape=jax.ShapeDtypeStruct((beams, tria...  13.5 us
    ppermute x3, starting transfers between devices, gather_spectra(): from_above.append(lax.ppermute(from_above[-1], 'dm', down))  9.63 us
    ppermute x3, waiting for transfers between devices, gather_spectra(): from_above.append(lax.ppermute(from_above[-1], 'dm', down))  6.44 us
    ppermute x1, starting transfers between devices, gather_spectra(): return (column, lax.ppermute(column, 'dm', partner), carried)  6.2 us
    reshape x1, local copies, waits for them, and re-layouts, shards(): resp = responses.reshape(trials, chans, 2 * length)  4.37 us
    ppermute x1, waiting for transfers between devices, gather_spectra(): return (column, lax.ppermute(column, 'dm', partner), carried)  3.9 us
    ppermute x1, waiting for transfers between devices, gather_spectra(): lax.ppermute(from_below[-1][0], 'dm', up)  3.51 us
  transfers between devices with their start and end apart: 10, of which 7 were waited for; matrix products, arithmetic and copies ran while one was open for 4% of the time, Pallas kernels for 0%

profile of v11, /device:TPU:1, one launch (start us, length us, event | category | flops | bytes accessed | tf_op | source)
XLA Modules:
  0.0 99.5 jit_solution(6451059756355868175)
XLA Ops:
  0.0 0.9 copy.9
  0.9 1.3 %fusion = bf16[16,8,512]{2,1,0:T(8,128)(2,1)S(1)} fusion(bf16[128,512]{1,0:T(8,128)(2,1)S(1)} %bitcast.54, bf16[512,512]{1,0:T(8,128)(2,1)} %constant.83.clone), kind=kOutput, calls=%fused_computation.1 | convolution fusion | flops 67174400 | bytes 786432 | tf_op jit(solution)/shard_map/dot_general | solution.py:180
  2.3 2.1 %collective-permute-start = (bf16[8,16,512]{2,1,0:T(8,128)(2,1)S(1)}, bf16[8,16,512]{2,1,0:T(8,128)(2,1)S(1)}, u32[]{:S(2)}, u32[]{:S(2)}) collective-permute-start(bf16[8,16,512]{2,1,0:T(8,128)(2,1)S(1)} %bitcast.51), channel_id=1, source_target_pairs={{0,128},{8,136},{16,144},{24,152},{32,160},{40,168},{48,176},{56,1... | collective-permute-start | bytes 393224 | tf_op jit(solution)/shard_map/ppermute | solution.py:156
  4.4 2.4 %collective-permute-done = bf16[8,16,512]{2,1,0:T(8,128)(2,1)S(1)} collective-permute-done((bf16[8,16,512]{2,1,0:T(8,128)(2,1)S(1)}, bf16[8,16,512]{2,1,0:T(8,128)(2,1)S(1)}, u32[]{:S(2)}, u32[]{:S(2)}) %collective-permute-start) | collective-permute-done | bytes 131104 | tf_op jit(solution)/shard_map/ppermute | solution.py:156
  6.8 2.5 %collective-permute-start.1 = (bf16[2,8,16,512]{3,2,1,0:T(8,128)(2,1)S(1)}, bf16[2,8,16,512]{3,2,1,0:T(8,128)(2,1)S(1)}, u32[]{:S(2)}, u32[]{:S(2)}) collective-permute-start(bf16[2,8,16,512]{3,2,1,0:T(8,128)(2,1)S(1)} %pad_maximum_fusion), channel_id=1, source_target_pairs={{0,16},{8,24},{16,32},{24,40},{32,48},{40,56},{48,64},{56,72},{64,... | collective-permute-start | bytes 786440 | tf_op jit(solution)/shard_map/ppermute | solution.py:160
  9.3 4.0 %collective-permute-start.2 = (bf16[2,8,16,512]{3,2,1,0:T(8,128)(2,1)S(1)}, bf16[2,8,16,512]{3,2,1,0:T(8,128)(2,1)S(1)}, u32[]{:S(2)}, u32[]{:S(2)}) collective-permute-start(bf16[2,8,16,512]{3,2,1,0:T(8,128)(2,1)S(1)} %pad_maximum_fusion), channel_id=1, source_target_pairs={{0,112},{8,120},{16,0},{24,8},{32,16},{40,24},{48,32},{56,40},{64,... | collective-permute-start | bytes 786440 | tf_op jit(solution)/shard_map/ppermute | solution.py:161
  13.3 4.4 %reshape.25.refs_8_ = bf16[4,512,512]{2,1,0:T(8,128)(2,1)} reshape(bf16[4,512,2,256]{3,2,1,0:T(2,128)(2,1)} %param.6) | data formatting | bytes 4194304 | tf_op jit(solution)/shard_map/reshape | solution.py:184
  17.7 0.7 collective-permute-done.1
  18.4 2.5 %collective-permute-start.3 = (bf16[2,8,16,512]{3,2,1,0:T(8,128)(2,1)S(1)}, bf16[2,8,16,512]{3,2,1,0:T(8,128)(2,1)S(1)}, u32[]{:S(2)}, u32[]{:S(2)}) collective-permute-start(bf16[2,8,16,512]{3,2,1,0:T(8,128)(2,1)S(1)} %collective-permute-done.2), channel_id=1, source_target_pairs={{0,112},{8,120},{16,0},{24,8},{32,16},{40,24},{48,32},{56,40},{64,... | collective-permute-start | bytes 786440 | tf_op jit(solution)/shard_map/ppermute | solution.py:161
  20.9 3.3 %collective-permute-done.3 = bf16[2,8,16,512]{3,2,1,0:T(8,128)(2,1)S(1)} collective-permute-done((bf16[2,8,16,512]{3,2,1,0:T(8,128)(2,1)S(1)}, bf16[2,8,16,512]{3,2,1,0:T(8,128)(2,1)S(1)}, u32[]{:S(2)}, u32[]{:S(2)}) %collective-permute-start.3) | collective-permute-done | bytes 262176 | tf_op jit(solution)/shard_map/ppermute | solution.py:161
  24.2 3.1 %collective-permute-start.4 = (bf16[2,8,16,512]{3,2,1,0:T(8,128)(2,1)S(1)}, bf16[2,8,16,512]{3,2,1,0:T(8,128)(2,1)S(1)}, u32[]{:S(2)}, u32[]{:S(2)}) collective-permute-start(bf16[2,8,16,512]{3,2,1,0:T(8,128)(2,1)S(1)} %collective-permute-done.3), channel_id=1, source_target_pairs={{0,112},{8,120},{16,0},{24,8},{32,16},{40,24},{48,32},{56,40},{64,... | collective-permute-start | bytes 786440 | tf_op jit(solution)/shard_map/ppermute | solution.py:161
  27.3 0.1 collective-permute-start.6
  27.4 3.2 %collective-permute-done.4 = bf16[2,8,16,512]{3,2,1,0:T(8,128)(2,1)S(1)} collective-permute-done((bf16[2,8,16,512]{3,2,1,0:T(8,128)(2,1)S(1)}, bf16[2,8,16,512]{3,2,1,0:T(8,128)(2,1)S(1)}, u32[]{:S(2)}, u32[]{:S(2)}) %collective-permute-start.4) | collective-permute-done | bytes 262176 | tf_op jit(solution)/shard_map/ppermute | solution.py:161
  30.6 3.2 %collective-permute-start.8 = (bf16[8,16,512]{2,1,0:T(8,128)(2,1)S(1)}, bf16[8,16,512]{2,1,0:T(8,128)(2,1)S(1)}, u32[]{:S(2)}, u32[]{:S(2)}) collective-permute-start(bf16[8,16,512]{2,1,0:T(8,128)(2,1)S(1)} %slice_bitcast_fusion), channel_id=1, source_target_pairs={{0,112},{8,120},{16,0},{24,8},{32,16},{40,24},{48,32},{56,40},{64,... | collective-permute-start | bytes 393224 | tf_op jit(solution)/shard_map/ppermute | solution.py:167
  33.8 0.0 collective-permute-done.6
  33.8 0.1 collective-permute-start.7
  34.0 2.0 %collective-permute-done.8 = bf16[8,16,512]{2,1,0:T(8,128)(2,1)S(1)} collective-permute-done((bf16[8,16,512]{2,1,0:T(8,128)(2,1)S(1)}, bf16[8,16,512]{2,1,0:T(8,128)(2,1)S(1)}, u32[]{:S(2)}, u32[]{:S(2)}) %collective-permute-start.8) | collective-permute-done | bytes 131104 | tf_op jit(solution)/shard_map/ppermute | solution.py:167
  36.0 3.5 %collective-permute-done.7 = bf16[8,16,512]{2,1,0:T(8,128)(2,1)S(1)} collective-permute-done((bf16[8,16,512]{2,1,0:T(8,128)(2,1)S(1)}, bf16[8,16,512]{2,1,0:T(8,128)(2,1)S(1)}, u32[]{:S(2)}, u32[]{:S(2)}) %collective-permute-start.7) | collective-permute-done | bytes 131104 | tf_op jit(solution)/shard_map/ppermute | solution.py:167
  39.6 6.2 %collective-permute-start.9 = (bf16[16,8,16,512]{3,2,1,0:T(8,128)(2,1)S(1)}, bf16[16,8,16,512]{3,2,1,0:T(8,128)(2,1)}, u32[]{:S(2)}, u32[]{:S(2)}) collective-permute-start(bf16[16,8,16,512]{3,2,1,0:T(8,128)(2,1)S(1)} %bitcast.46), channel_id=1, source_target_pairs={{0,8},{8,0},{16,24},{24,16},{32,40},{40,32},{48,56},{56,48},{64,72... | collective-permute-start | bytes 6291464 | tf_op jit(solution)/shard_map/ppermute | solution.py:171
  45.8 3.9 %collective-permute-done.9.refs_1_.refs_3_.refs_5_.refs_7_ = bf16[16,8,16,512]{3,2,1,0:T(8,128)(2,1)} collective-permute-done((bf16[16,8,16,512]{3,2,1,0:T(8,128)(2,1)S(1)}, bf16[16,8,16,512]{3,2,1,0:T(8,128)(2,1)}, u32[]{:S(2)}, u32[]{:S(2)}) %collective-permute-start.9) | collective-permute-done | bytes 2097184 | tf_op jit(solution)/shard_map/ppermute | solution.py:171
  49.7 13.5 %shard_map.55 = bf16[8,4,256,128]{3,2,1,0:T(8,128)(2,1)S(1)} custom-call(s32[4]{0:T(128)S(1)} %copy-done, s32[16]{0:T(128)S(1)} %fusion.4.table_ref, s32[1]{0:T(128)} %bitcast.swap_ref, bf16[16,8,16,512]{3,2,1,0:T(8,128)(2,1)S(1)} %bitcast.47, bf16[16,8,16,512]{3,2,1,0:T(8,128)(2,1)} %collective-permute-done.9.refs_1_.refs_3_.refs_5_.refs_7_, ...), custom_call_target="tpu_custom_call" | custom-call | flops 8589934592 | bytes 8912896 | tf_op jit(solution)/shard_map/pallas_call | solution.py:111
  63.2 34.0 %all_to_all.4 = bf16[4,8,256,128]{3,2,0,1:T(8,128)(2,1)S(1)} all-to-all(bf16[4,8,256,128]{3,2,0,1:T(8,128)(2,1)S(1)} %bitcast.45), channel_id=1, replica_groups=mesh['dm'=32,'beam'=8] {'beam'}, dimensions={1} | all-to-all | bytes 4194304 | tf_op jit(solution)/shard_map/all_to_all | solution.py:193
  97.2 0.1 copy.8
  97.4 2.1 %reshape.27 = bf16[4,1,262144]{2,0,1:T(4,128)(2,1)} reshape(bf16[4,8,256,128]{3,2,1,0:T(8,128)(2,1)S(1)} %copy.8) | data formatting | bytes 4194304 | tf_op jit(solution)/shard_map/reshape | solution.py:194
  (20 shorter events, 0.3 us)
Async XLA Ops:
  2.3 4.5 %collective-permute-start = (bf16[8,16,512]{2,1,0:T(8,128)(2,1)S(1)}, bf16[8,16,512]{2,1,0:T(8,128)(2,1)S(1)}, u32[]{:S(2)}, u32[]{:S(2)}) collective-permute-start(bf16[8,16,512]{2,1,0:T(8,128)(2,1)S(1)} %bitcast.51), channel_id=1, source_target_pairs={{0,128},{8,136},{16,144},{24,152},{32,160},{40,168},{48,176},{56,1... | collective-permute-start | bytes 393224 | tf_op jit(solution)/shard_map/ppermute | solution.py:156
  6.8 11.6 %collective-permute-start.1 = (bf16[2,8,16,512]{3,2,1,0:T(8,128)(2,1)S(1)}, bf16[2,8,16,512]{3,2,1,0:T(8,128)(2,1)S(1)}, u32[]{:S(2)}, u32[]{:S(2)}) collective-permute-start(bf16[2,8,16,512]{3,2,1,0:T(8,128)(2,1)S(1)} %pad_maximum_fusion), channel_id=1, source_target_pairs={{0,16},{8,24},{16,32},{24,40},{32,48},{40,56},{48,64},{56,72},{64,... | collective-permute-start | bytes 786440 | tf_op jit(solution)/shard_map/ppermute | solution.py:160
  9.3 9.1 %collective-permute-start.2 = (bf16[2,8,16,512]{3,2,1,0:T(8,128)(2,1)S(1)}, bf16[2,8,16,512]{3,2,1,0:T(8,128)(2,1)S(1)}, u32[]{:S(2)}, u32[]{:S(2)}) collective-permute-start(bf16[2,8,16,512]{3,2,1,0:T(8,128)(2,1)S(1)} %pad_maximum_fusion), channel_id=1, source_target_pairs={{0,112},{8,120},{16,0},{24,8},{32,16},{40,24},{48,32},{56,40},{64,... | collective-permute-start | bytes 786440 | tf_op jit(solution)/shard_map/ppermute | solution.py:161
  18.4 5.8 %collective-permute-start.3 = (bf16[2,8,16,512]{3,2,1,0:T(8,128)(2,1)S(1)}, bf16[2,8,16,512]{3,2,1,0:T(8,128)(2,1)S(1)}, u32[]{:S(2)}, u32[]{:S(2)}) collective-permute-start(bf16[2,8,16,512]{3,2,1,0:T(8,128)(2,1)S(1)} %collective-permute-done.2), channel_id=1, source_target_pairs={{0,112},{8,120},{16,0},{24,8},{32,16},{40,24},{48,32},{56,40},{64,... | collective-permute-start | bytes 786440 | tf_op jit(solution)/shard_map/ppermute | solution.py:161
  20.9 6.5 %collective-permute-start.5 = (bf16[2,8,16,512]{3,2,1,0:T(8,128)(2,1)S(1)}, bf16[2,8,16,512]{3,2,1,0:T(8,128)(2,1)S(1)}, u32[]{:S(2)}, u32[]{:S(2)}) collective-permute-start(bf16[2,8,16,512]{3,2,1,0:T(8,128)(2,1)S(1)} %collective-permute-done.1), channel_id=1, source_target_pairs={{0,16},{8,24},{16,32},{24,40},{32,48},{40,56},{48,64},{56,72},{64,... | collective-permute-start | bytes 786440 | tf_op jit(solution)/shard_map/ppermute | solution.py:160
  20.9 28.9 %copy-start = (s32[4]{0:T(128)S(1)}, s32[4]{0:T(128)}, u32[]{:S(2)}) copy-start(s32[4]{0:T(128)} %chirp_ref.1) | copy-start | bytes 52
  20.9 28.8 %copy-start.1 = (bf16[512,512]{1,0:T(8,128)(2,1)S(1)}, bf16[512,512]{1,0:T(8,128)(2,1)}, u32[]{:S(2)}) copy-start(bf16[512,512]{1,0:T(8,128)(2,1)} %constant.84.clone.refs_9_) | copy-start | bytes 1572868
  24.2 6.4 %collective-permute-start.4 = (bf16[2,8,16,512]{3,2,1,0:T(8,128)(2,1)S(1)}, bf16[2,8,16,512]{3,2,1,0:T(8,128)(2,1)S(1)}, u32[]{:S(2)}, u32[]{:S(2)}) collective-permute-start(bf16[2,8,16,512]{3,2,1,0:T(8,128)(2,1)S(1)} %collective-permute-done.3), channel_id=1, source_target_pairs={{0,112},{8,120},{16,0},{24,8},{32,16},{40,24},{48,32},{56,40},{64,... | collective-permute-start | bytes 786440 | tf_op jit(solution)/shard_map/ppermute | solution.py:161
  27.3 6.5 %collective-permute-start.6 = (bf16[2,8,16,512]{3,2,1,0:T(8,128)(2,1)S(1)}, bf16[2,8,16,512]{3,2,1,0:T(8,128)(2,1)S(1)}, u32[]{:S(2)}, u32[]{:S(2)}) collective-permute-start(bf16[2,8,16,512]{3,2,1,0:T(8,128)(2,1)S(1)} %collective-permute-done.5), channel_id=1, source_target_pairs={{0,16},{8,24},{16,32},{24,40},{32,48},{40,56},{48,64},{56,72},{64,... | collective-permute-start | bytes 786440 | tf_op jit(solution)/shard_map/ppermute | solution.py:160
  30.6 5.4 %collective-permute-start.8 = (bf16[8,16,512]{2,1,0:T(8,128)(2,1)S(1)}, bf16[8,16,512]{2,1,0:T(8,128)(2,1)S(1)}, u32[]{:S(2)}, u32[]{:S(2)}) collective-permute-start(bf16[8,16,512]{2,1,0:T(8,128)(2,1)S(1)} %slice_bitcast_fusion), channel_id=1, source_target_pairs={{0,112},{8,120},{16,0},{24,8},{32,16},{40,24},{48,32},{56,40},{64,... | collective-permute-start | bytes 393224 | tf_op jit(solution)/shard_map/ppermute | solution.py:167
  33.8 5.7 %collective-permute-start.7 = (bf16[8,16,512]{2,1,0:T(8,128)(2,1)S(1)}, bf16[8,16,512]{2,1,0:T(8,128)(2,1)S(1)}, u32[]{:S(2)}, u32[]{:S(2)}) collective-permute-start(bf16[8,16,512]{2,1,0:T(8,128)(2,1)S(1)} %slice_bitcast_fusion.1), channel_id=1, source_target_pairs={{0,16},{8,24},{16,32},{24,40},{32,48},{40,56},{48,64},{56,72},{64,... | collective-permute-start | bytes 393224 | tf_op jit(solution)/shard_map/ppermute | solution.py:167
  39.6 10.1 %collective-permute-start.9 = (bf16[16,8,16,512]{3,2,1,0:T(8,128)(2,1)S(1)}, bf16[16,8,16,512]{3,2,1,0:T(8,128)(2,1)}, u32[]{:S(2)}, u32[]{:S(2)}) collective-permute-start(bf16[16,8,16,512]{3,2,1,0:T(8,128)(2,1)S(1)} %bitcast.46), channel_id=1, source_target_pairs={{0,8},{8,0},{16,24},{24,16},{32,40},{40,32},{48,56},{56,48},{64,72... | collective-permute-start | bytes 6291464 | tf_op jit(solution)/shard_map/ppermute | solution.py:171

commit v12 on v11

--- a/solution.py
+++ b/solution.py
@@ -54,9 +54,9 @@
     return rate * (pos % bins) + pos // bins
 
 
-def detect_kernel(chirp_ref, table_ref, swap_ref, *refs):
-    spec_refs = refs[: 2 * GROUP]
-    resp_ref, back_ref, out_ref, pair_ref = refs[2 * GROUP :]
+def detect_kernel(chirp_ref, table_ref, early_ref, late_ref, flag_ref, swap_ref, *refs):
+    spec_refs = refs[: 3 * GROUP]
+    resp_ref, back_ref, out_ref, pair_ref = refs[3 * GROUP :]
     _, beams, chans_local, width = spec_refs[0].shape
     trials = resp_ref.shape[0]
     length = width // 2
@@ -65,8 +65,9 @@
     keep = swap_ref[0] == 0
     pieces = []
     for g in range(GROUP):
-        mine = spec_refs[2 * g][0]
-        theirs = spec_refs[2 * g + 1][0]
+        mine = spec_refs[3 * g][0]
+        late = flag_ref[GROUP * pl.program_id(0) + g] != 0
+        theirs = jnp.where(late, spec_refs[3 * g + 2][0], spec_refs[3 * g + 1][0])
         pieces += [jnp.where(keep, mine, theirs), jnp.where(keep, theirs, mine)]
     x = jnp.concatenate(pieces, axis=1)
     xr = x[:, :, :length].astype(jnp.float32)
@@ -94,7 +95,7 @@
         out_ref[:, d] = both.reshape(beams, chans // 2, 2 * bins).astype(out_ref.dtype)
 
 
-def detect(table, swap, mine, theirs, responses, chirp_len, backward):
+def detect(tables, swap, mine, theirs_early, theirs_late, responses, chirp_len, backward):
     blocks, beams, chans_local, width = mine.shape
     trials, chans = responses.shape[0], responses.shape[1]
     length = width // 2
@@ -104,22 +105,27 @@
     bytes_accessed = 2 * (2 * mine.size + responses.size + backward.size + trials * beams * chans * bins)
     spec_specs = []
     for g in range(GROUP):
-        spec = pl.BlockSpec(
-            (1, beams, chans_local, width), lambda n, cl, tb, sw, g=g: (tb[GROUP * n + g], 0, 0, 0)
-        )
-        spec_specs += [spec, spec]
+        for which in range(3):
+            spec_specs.append(
+                pl.BlockSpec(
+                    (1, beams, chans_local, width),
+                    lambda n, cl, tb, te, tl, fl, sw, g=g, which=which: (
+                        (tb, te, tl)[which][GROUP * n + g], 0, 0, 0
+                    ),
+                )
+            )
     return pl.pallas_call(
         detect_kernel,
         out_shape=jax.ShapeDtypeStruct((beams, trials, chans // 2, 2 * bins), jnp.bfloat16),
         grid_spec=pltpu.PrefetchScalarGridSpec(
-            num_scalar_prefetch=3,
+            num_scalar_prefetch=6,
             grid=(chans // step,),
             in_specs=spec_specs + [
-                pl.BlockSpec((trials, step, width), lambda n, cl, tb, sw: (0, n, 0)),
-                pl.BlockSpec((width, width), lambda n, cl, tb, sw: (0, 0)),
+                pl.BlockSpec((trials, step, width), lambda n, cl, tb, te, tl, fl, sw: (0, n, 0)),
+                pl.BlockSpec((width, width), lambda n, cl, tb, te, tl, fl, sw: (0, 0)),
             ],
             out_specs=pl.BlockSpec(
-                (beams, trials, step // 2, 2 * bins), lambda n, cl, tb, sw: (0, 0, n, 0)
+                (beams, trials, step // 2, 2 * bins), lambda n, cl, tb, te, tl, fl, sw: (0, 0, n, 0)
             ),
             scratch_shapes=[pltpu.VMEM((beams * step, 2 * bins), jnp.float32)],
         ),
@@ -127,7 +133,7 @@
             dimension_semantics=("arbitrary",), vmem_limit_bytes=48 * 1024 * 1024
         ),
         cost_estimate=pl.CostEstimate(flops=flops, transcendentals=0, bytes_accessed=bytes_accessed),
-    )(chirp_len, table, swap, *([mine, theirs] * GROUP), responses, backward)
+    )(chirp_len, *tables, swap, *([mine, theirs_early, theirs_late] * GROUP), responses, backward)
 
 
 def coords(index, z_count):
@@ -166,9 +172,14 @@
     far = jnp.stack(
         [lax.ppermute(from_below[-1][0], "dm", up), lax.ppermute(from_above[-1][1], "dm", down)]
     )
+    near = z_count // 4 + 1
+    early = jnp.stack(from_above[:near] + from_below[near - 1 : 0 : -1])
+    early = early.reshape((-1,) + own.shape)
+    theirs_early = lax.ppermute(early, "dm", partner)
     column = jnp.stack(from_above + [far] + from_below[:0:-1])
     column = column.reshape((2 * z_count,) + own.shape)
-    return column, lax.ppermute(column, "dm", partner), carried
+    late = column[2 * near : 2 * (z_count - near + 1)]
+    return column, theirs_early, lax.ppermute(late, "dm", partner), carried
 
 
 def shards(voltages, responses, chirp_len):
@@ -182,14 +193,22 @@
     ).astype(jnp.bfloat16)
     local = local.reshape(chans_local, beams, 2 * length).transpose(1, 0, 2)
     resp = responses.reshape(trials, chans, 2 * length)
-    mine, theirs, resp = gather_spectra(local, count, resp)
+    mine, theirs_early, theirs_late, resp = gather_spectra(local, count, resp)
     x_me, z_me, c_me = coords(lax.axis_index("dm"), z_count)
     block = jnp.arange(count // 2, dtype=jnp.int32)
     table = ((block % z_count - z_me) % z_count) * 2 + ((block // z_count) ^ x_me)
     swap = jnp.reshape(c_me, (1,)).astype(jnp.int32)
-    detected = detect(
-        table, swap, mine, theirs, resp, chirp_len, backward
-    )
+    near = z_count // 4 + 1
+    z_rel, x_rel = table // 2, table % 2
+    is_late = (z_rel >= near) & (z_rel <= z_count - near)
+    early_index = jnp.where(z_rel < near, z_rel, z_rel - (z_count - 2 * near + 1))
+    tables = (
+        table,
+        jnp.where(is_late, 0, early_index * 2 + x_rel),
+        jnp.where(is_late, (z_rel - near) * 2 + x_rel, 0),
+        is_late.astype(jnp.int32),
+    )
+    detected = detect(tables, swap, mine, theirs_early, theirs_late, resp, chirp_len, backward)
     moved = lax.all_to_all(detected.transpose(1, 0, 2, 3), "beam", split_axis=1, concat_axis=2, tiled=True)
     return moved.reshape(trials, 1, -1)
 

time: 99.8 us -> 99.5 us (level)
  waiting for transfers between devices: 19 us -> 13.4 us
  local copies, waits for them, and re-layouts: 7.71 us -> 10.6 us
    ppermute x3, waiting for transfers between devices: 6.44 us -> 0.2 us  [gather_spectra(): from_above.append(lax.ppermute(from_above[-1], 'dm', down))]
    ppermute x3, waiting for transfers between devices: 0.72 us -> 6.49 us  [gather_spectra(): from_below.append(lax.ppermute(from_below[-1], 'dm', up))]
    unnamed x10 -> x12, local copies, waits for them, and re-layouts: 1.03 us -> 3.21 us
    ppermute x1, waiting for transfers between devices: 3.51 us -> 1.59 us  [gather_spectra(): lax.ppermute(from_below[-1][0], 'dm', up)]
    ppermute x1, waiting for transfers between devices: 2.04 us -> 0.33 us  [gather_spectra(): lax.ppermute(from_above[-1][1], 'dm', down)]
    ppermute x1 -> x2, waiting for transfers between devices: 3.9 us -> 2.47 us  [the longest x1 2.47 us: gather_spectra(): return (column, theirs_early, lax.ppermute(late, 'dm', partner), carried)]
    ppermute x1 -> x2, starting transfers between devices: 6.2 us -> 6.91 us  [the longest x1 5.55 us: gather_spectra(): theirs_early = lax.ppermute(early, 'dm', partner)]
  transfers between devices with their start and end apart: 10 -> 11, of which waited for: 7 -> 8; matrix products, arithmetic and copies ran while one was open for 4% -> 7% of each run, Pallas kernels for 0% -> 0%
where the time goes in v12:
time: 99.5 us; the launch traced here: 98.3 us
  blocking collectives  34 us (34%)
  starting transfers between devices  24.2 us (24%)
  Pallas kernels  13.6 us (14%)
  waiting for transfers between devices  13.4 us (13%)
  local copies, waits for them, and re-layouts  10.6 us (11%)
  matrix products  1.27 us (1%)
    all_to_all x1, blocking collectives, shards(): lax.all_to_all(detected.transpose(1, 0, 2, 3), 'beam', split_axis=1, conc...  34 us
    pallas_call x1, Pallas kernels, detect(): pl.pallas_call(detect_kernel, out_shape=jax.ShapeDtypeStruct((beams, tria...  13.6 us
    ppermute x3, starting transfers between devices, gather_spectra(): from_above.append(lax.ppermute(from_above[-1], 'dm', down))  9.38 us
    ppermute x3, waiting for transfers between devices, gather_spectra(): from_below.append(lax.ppermute(from_below[-1], 'dm', up))  6.49 us
    ppermute x1, starting transfers between devices, gather_spectra(): theirs_early = lax.ppermute(early, 'dm', partner)  5.55 us
    reshape x1, local copies, waits for them, and re-layouts, shards(): resp = responses.reshape(trials, chans, 2 * length)  4.4 us
    unnamed x12, local copies, waits for them, and re-layouts  3.21 us
    ppermute x1, starting transfers between devices, gather_spectra(): lax.ppermute(from_above[-1][1], 'dm', down)  3.19 us
  transfers between devices with their start and end apart: 11, of which 8 were waited for; matrix products, arithmetic and copies ran while one was open for 7% of the time, Pallas kernels for 0%

profile of v12, /device:TPU:1, one launch (start us, length us, event | category | flops | bytes accessed | tf_op | source)
XLA Modules:
  0.0 98.3 jit_solution(16883020130953883571)
XLA Ops:
  0.0 0.9 copy.9
  0.9 1.3 %fusion = bf16[16,8,512]{2,1,0:T(8,128)(2,1)S(1)} fusion(bf16[128,512]{1,0:T(8,128)(2,1)S(1)} %bitcast.59, bf16[512,512]{1,0:T(8,128)(2,1)} %constant.101.clone), kind=kOutput, calls=%fused_computation.1 | convolution fusion | flops 67174400 | bytes 786432 | tf_op jit(solution)/shard_map/dot_general | solution.py:191
  2.3 2.1 %collective-permute-start = (bf16[8,16,512]{2,1,0:T(8,128)(2,1)S(1)}, bf16[8,16,512]{2,1,0:T(8,128)(2,1)S(1)}, u32[]{:S(2)}, u32[]{:S(2)}) collective-permute-start(bf16[8,16,512]{2,1,0:T(8,128)(2,1)S(1)} %bitcast.55), channel_id=1, source_target_pairs={{0,128},{8,136},{16,144},{24,152},{32,160},{40,168},{48,176},{56,1... | collective-permute-start | bytes 393224 | tf_op jit(solution)/shard_map/ppermute | solution.py:162
  4.4 2.4 %collective-permute-done = bf16[8,16,512]{2,1,0:T(8,128)(2,1)S(1)} collective-permute-done((bf16[8,16,512]{2,1,0:T(8,128)(2,1)S(1)}, bf16[8,16,512]{2,1,0:T(8,128)(2,1)S(1)}, u32[]{:S(2)}, u32[]{:S(2)}) %collective-permute-start) | collective-permute-done | bytes 131104 | tf_op jit(solution)/shard_map/ppermute | solution.py:162
  6.8 2.5 %collective-permute-start.1 = (bf16[2,8,16,512]{3,2,1,0:T(8,128)(2,1)S(1)}, bf16[2,8,16,512]{3,2,1,0:T(8,128)(2,1)S(1)}, u32[]{:S(2)}, u32[]{:S(2)}) collective-permute-start(bf16[2,8,16,512]{3,2,1,0:T(8,128)(2,1)S(1)} %pad_maximum_fusion.1), channel_id=1, source_target_pairs={{0,16},{8,24},{16,32},{24,40},{32,48},{40,56},{48,64},{56,72},{64,... | collective-permute-start | bytes 786440 | tf_op jit(solution)/shard_map/ppermute | solution.py:166
  9.3 4.0 %collective-permute-start.2 = (bf16[2,8,16,512]{3,2,1,0:T(8,128)(2,1)S(1)}, bf16[2,8,16,512]{3,2,1,0:T(8,128)(2,1)S(1)}, u32[]{:S(2)}, u32[]{:S(2)}) collective-permute-start(bf16[2,8,16,512]{3,2,1,0:T(8,128)(2,1)S(1)} %pad_maximum_fusion.1), channel_id=1, source_target_pairs={{0,112},{8,120},{16,0},{24,8},{32,16},{40,24},{48,32},{56,40},{64,... | collective-permute-start | bytes 786440 | tf_op jit(solution)/shard_map/ppermute | solution.py:167
  13.3 4.4 %reshape.29.refs_12_ = bf16[4,512,512]{2,1,0:T(8,128)(2,1)} reshape(bf16[4,512,2,256]{3,2,1,0:T(2,128)(2,1)} %param.6) | data formatting | bytes 4194304 | tf_op jit(solution)/shard_map/reshape | solution.py:195
  18.4 2.7 %collective-permute-start.3 = (bf16[2,8,16,512]{3,2,1,0:T(8,128)(2,1)S(1)}, bf16[2,8,16,512]{3,2,1,0:T(8,128)(2,1)S(1)}, u32[]{:S(2)}, u32[]{:S(2)}) collective-permute-start(bf16[2,8,16,512]{3,2,1,0:T(8,128)(2,1)S(1)} %collective-permute-done.2), channel_id=1, source_target_pairs={{0,112},{8,120},{16,0},{24,8},{32,16},{40,24},{48,32},{56,40},{64,... | collective-permute-start | bytes 786440 | tf_op jit(solution)/shard_map/ppermute | solution.py:167
  21.1 0.7 bitcast_dynamic-update-slice_fusion.8
  21.8 3.6 %collective-permute-done.5 = bf16[2,8,16,512]{3,2,1,0:T(8,128)(2,1)S(1)} collective-permute-done((bf16[2,8,16,512]{3,2,1,0:T(8,128)(2,1)S(1)}, bf16[2,8,16,512]{3,2,1,0:T(8,128)(2,1)S(1)}, u32[]{:S(2)}, u32[]{:S(2)}) %collective-permute-start.5) | collective-permute-done | bytes 262176 | tf_op jit(solution)/shard_map/ppermute | solution.py:166
  25.4 0.7 bitcast_dynamic-update-slice_fusion.6
  26.1 2.7 %collective-permute-start.4 = (bf16[2,8,16,512]{3,2,1,0:T(8,128)(2,1)S(1)}, bf16[2,8,16,512]{3,2,1,0:T(8,128)(2,1)S(1)}, u32[]{:S(2)}, u32[]{:S(2)}) collective-permute-start(bf16[2,8,16,512]{3,2,1,0:T(8,128)(2,1)S(1)} %collective-permute-done.3), channel_id=1, source_target_pairs={{0,112},{8,120},{16,0},{24,8},{32,16},{40,24},{48,32},{56,40},{64,... | collective-permute-start | bytes 786440 | tf_op jit(solution)/shard_map/ppermute | solution.py:167
  28.8 0.8 bitcast_dynamic-update-slice_fusion.4
  29.5 2.3 %collective-permute-done.6 = bf16[2,8,16,512]{3,2,1,0:T(8,128)(2,1)S(1)} collective-permute-done((bf16[2,8,16,512]{3,2,1,0:T(8,128)(2,1)S(1)}, bf16[2,8,16,512]{3,2,1,0:T(8,128)(2,1)S(1)}, u32[]{:S(2)}, u32[]{:S(2)}) %collective-permute-start.6) | collective-permute-done | bytes 262176 | tf_op jit(solution)/shard_map/ppermute | solution.py:166
  32.1 3.2 %collective-permute-start.8 = (bf16[8,16,512]{2,1,0:T(8,128)(2,1)S(1)}, bf16[8,16,512]{2,1,0:T(8,128)(2,1)S(1)}, u32[]{:S(2)}, u32[]{:S(2)}) collective-permute-start(bf16[8,16,512]{2,1,0:T(8,128)(2,1)S(1)} %slice_bitcast_fusion), channel_id=1, source_target_pairs={{0,112},{8,120},{16,0},{24,8},{32,16},{40,24},{48,32},{56,40},{64,... | collective-permute-start | bytes 393224 | tf_op jit(solution)/shard_map/ppermute | solution.py:173
  35.3 1.6 %collective-permute-done.7 = bf16[8,16,512]{2,1,0:T(8,128)(2,1)S(1)} collective-permute-done((bf16[8,16,512]{2,1,0:T(8,128)(2,1)S(1)}, bf16[8,16,512]{2,1,0:T(8,128)(2,1)S(1)}, u32[]{:S(2)}, u32[]{:S(2)}) %collective-permute-start.7) | collective-permute-done | bytes 131104 | tf_op jit(solution)/shard_map/ppermute | solution.py:173
  37.3 0.7 bitcast_dynamic-update-slice_fusion.2
  38.1 0.7 bitcast_dynamic-update-slice_fusion
  38.8 5.6 %collective-permute-start.9 = (bf16[10,8,16,512]{3,2,1,0:T(8,128)(2,1)}, bf16[10,8,16,512]{3,2,1,0:T(8,128)(2,1)S(1)}, u32[]{:S(2)}, u32[]{:S(2)}) collective-permute-start(bf16[10,8,16,512]{3,2,1,0:T(8,128)(2,1)} %bitcast.19), channel_id=1, source_target_pairs={{0,8},{8,0},{16,24},{24,16},{32,40},{40,32},{48,56},{56,48},{64,72... | collective-permute-start | bytes 3932168 | tf_op jit(solution)/shard_map/ppermute | solution.py:178
  44.5 1.4 %collective-permute-start.10 = (bf16[6,8,16,512]{3,2,1,0:T(8,128)(2,1)S(1)}, bf16[6,8,16,512]{3,2,1,0:T(8,128)(2,1)S(1)}, u32[]{:S(2)}, u32[]{:S(2)}) collective-permute-start(bf16[6,8,16,512]{3,2,1,0:T(8,128)(2,1)S(1)} %bitcast.58), channel_id=1, source_target_pairs={{0,8},{8,0},{16,24},{24,16},{32,40},{40,32},{48,56},{56,48},{64,72... | collective-permute-start | bytes 2359304 | tf_op jit(solution)/shard_map/ppermute | solution.py:182
  45.9 2.5 %collective-permute-done.10.refs_2_.refs_5_.refs_8_.refs_11_ = bf16[6,8,16,512]{3,2,1,0:T(8,128)(2,1)S(1)} collective-permute-done((bf16[6,8,16,512]{3,2,1,0:T(8,128)(2,1)S(1)}, bf16[6,8,16,512]{3,2,1,0:T(8,128)(2,1)S(1)}, u32[]{:S(2)}, u32[]{:S(2)}) %collective-permute-start.10) | collective-permute-done | bytes 786464 | tf_op jit(solution)/shard_map/ppermute | solution.py:182
  48.4 13.6 %shard_map.55 = bf16[8,4,256,128]{3,2,1,0:T(8,128)(2,1)S(1)} custom-call(s32[4]{0:T(128)S(1)} %copy-done, s32[16]{0:T(128)S(1)} %get-tuple-element.14.table_ref, s32[16]{0:T(128)S(1)} %get-tuple-element.28.early_ref, s32[16]{0:T(128)S(1)} %get-tuple-element.27.late_ref, s32[16]{0:T(128)S(1)} %get-tuple-element.11.flag_ref, s32[1]{0:T(128)} %bitcast.swap_ref, ...), custom_call_target="tpu_custom_call" | custom-call | flops 8589934592 | bytes 8912896 | tf_op jit(solution)/shard_map/pallas_call | solution.py:117
  62.0 34.0 %all_to_all.4 = bf16[4,8,256,128]{3,2,0,1:T(8,128)(2,1)S(1)} all-to-all(bf16[4,8,256,128]{3,2,0,1:T(8,128)(2,1)S(1)} %bitcast.52), channel_id=1, replica_groups=mesh['dm'=32,'beam'=8] {'beam'}, dimensions={1} | all-to-all | bytes 4194304 | tf_op jit(solution)/shard_map/all_to_all | solution.py:212
  96.2 2.1 %reshape.32 = bf16[4,1,262144]{2,0,1:T(4,128)(2,1)} reshape(bf16[4,8,256,128]{3,2,1,0:T(8,128)(2,1)S(1)} %copy.8) | data formatting | bytes 4194304 | tf_op jit(solution)/shard_map/reshape | solution.py:213
  (27 shorter events, 1.7 us)
Async XLA Ops:
  2.3 4.5 %collective-permute-start = (bf16[8,16,512]{2,1,0:T(8,128)(2,1)S(1)}, bf16[8,16,512]{2,1,0:T(8,128)(2,1)S(1)}, u32[]{:S(2)}, u32[]{:S(2)}) collective-permute-start(bf16[8,16,512]{2,1,0:T(8,128)(2,1)S(1)} %bitcast.55), channel_id=1, source_target_pairs={{0,128},{8,136},{16,144},{24,152},{32,160},{40,168},{48,176},{56,1... | collective-permute-start | bytes 393224 | tf_op jit(solution)/shard_map/ppermute | solution.py:162
  6.8 11.6 %collective-permute-start.1 = (bf16[2,8,16,512]{3,2,1,0:T(8,128)(2,1)S(1)}, bf16[2,8,16,512]{3,2,1,0:T(8,128)(2,1)S(1)}, u32[]{:S(2)}, u32[]{:S(2)}) collective-permute-start(bf16[2,8,16,512]{3,2,1,0:T(8,128)(2,1)S(1)} %pad_maximum_fusion.1), channel_id=1, source_target_pairs={{0,16},{8,24},{16,32},{24,40},{32,48},{40,56},{48,64},{56,72},{64,... | collective-permute-start | bytes 786440 | tf_op jit(solution)/shard_map/ppermute | solution.py:166
  9.3 9.1 %collective-permute-start.2 = (bf16[2,8,16,512]{3,2,1,0:T(8,128)(2,1)S(1)}, bf16[2,8,16,512]{3,2,1,0:T(8,128)(2,1)S(1)}, u32[]{:S(2)}, u32[]{:S(2)}) collective-permute-start(bf16[2,8,16,512]{3,2,1,0:T(8,128)(2,1)S(1)} %pad_maximum_fusion.1), channel_id=1, source_target_pairs={{0,112},{8,120},{16,0},{24,8},{32,16},{40,24},{48,32},{56,40},{64,... | collective-permute-start | bytes 786440 | tf_op jit(solution)/shard_map/ppermute | solution.py:167
  18.4 7.0 %collective-permute-start.5 = (bf16[2,8,16,512]{3,2,1,0:T(8,128)(2,1)S(1)}, bf16[2,8,16,512]{3,2,1,0:T(8,128)(2,1)S(1)}, u32[]{:S(2)}, u32[]{:S(2)}) collective-permute-start(bf16[2,8,16,512]{3,2,1,0:T(8,128)(2,1)S(1)} %collective-permute-done.1), channel_id=1, source_target_pairs={{0,16},{8,24},{16,32},{24,40},{32,48},{40,56},{48,64},{56,72},{64,... | collective-permute-start | bytes 786440 | tf_op jit(solution)/shard_map/ppermute | solution.py:166
  18.4 7.7 %collective-permute-start.3 = (bf16[2,8,16,512]{3,2,1,0:T(8,128)(2,1)S(1)}, bf16[2,8,16,512]{3,2,1,0:T(8,128)(2,1)S(1)}, u32[]{:S(2)}, u32[]{:S(2)}) collective-permute-start(bf16[2,8,16,512]{3,2,1,0:T(8,128)(2,1)S(1)} %collective-permute-done.2), channel_id=1, source_target_pairs={{0,112},{8,120},{16,0},{24,8},{32,16},{40,24},{48,32},{56,40},{64,... | collective-permute-start | bytes 786440 | tf_op jit(solution)/shard_map/ppermute | solution.py:167
  25.4 6.4 %collective-permute-start.6 = (bf16[2,8,16,512]{3,2,1,0:T(8,128)(2,1)S(1)}, bf16[2,8,16,512]{3,2,1,0:T(8,128)(2,1)S(1)}, u32[]{:S(2)}, u32[]{:S(2)}) collective-permute-start(bf16[2,8,16,512]{3,2,1,0:T(8,128)(2,1)S(1)} %collective-permute-done.5), channel_id=1, source_target_pairs={{0,16},{8,24},{16,32},{24,40},{32,48},{40,56},{48,64},{56,72},{64,... | collective-permute-start | bytes 786440 | tf_op jit(solution)/shard_map/ppermute | solution.py:166
  26.1 6.0 %collective-permute-start.4 = (bf16[2,8,16,512]{3,2,1,0:T(8,128)(2,1)S(1)}, bf16[2,8,16,512]{3,2,1,0:T(8,128)(2,1)S(1)}, u32[]{:S(2)}, u32[]{:S(2)}) collective-permute-start(bf16[2,8,16,512]{3,2,1,0:T(8,128)(2,1)S(1)} %collective-permute-done.3), channel_id=1, source_target_pairs={{0,112},{8,120},{16,0},{24,8},{32,16},{40,24},{48,32},{56,40},{64,... | collective-permute-start | bytes 786440 | tf_op jit(solution)/shard_map/ppermute | solution.py:167
  31.8 5.1 %collective-permute-start.7 = (bf16[8,16,512]{2,1,0:T(8,128)(2,1)S(1)}, bf16[8,16,512]{2,1,0:T(8,128)(2,1)S(1)}, u32[]{:S(2)}, u32[]{:S(2)}) collective-permute-start(bf16[8,16,512]{2,1,0:T(8,128)(2,1)S(1)} %slice_bitcast_fusion.1), channel_id=1, source_target_pairs={{0,16},{8,24},{16,32},{24,40},{32,48},{40,56},{48,64},{56,72},{64,... | collective-permute-start | bytes 393224 | tf_op jit(solution)/shard_map/ppermute | solution.py:173
  32.1 5.1 %collective-permute-start.8 = (bf16[8,16,512]{2,1,0:T(8,128)(2,1)S(1)}, bf16[8,16,512]{2,1,0:T(8,128)(2,1)S(1)}, u32[]{:S(2)}, u32[]{:S(2)}) collective-permute-start(bf16[8,16,512]{2,1,0:T(8,128)(2,1)S(1)} %slice_bitcast_fusion), channel_id=1, source_target_pairs={{0,112},{8,120},{16,0},{24,8},{32,16},{40,24},{48,32},{56,40},{64,... | collective-permute-start | bytes 393224 | tf_op jit(solution)/shard_map/ppermute | solution.py:173
  37.3 11.1 %copy-start = (s32[4]{0:T(128)S(1)}, s32[4]{0:T(128)}, u32[]{:S(2)}) copy-start(s32[4]{0:T(128)} %chirp_ref.1) | copy-start | bytes 52
  37.3 11.1 %copy-start.1 = (bf16[512,512]{1,0:T(8,128)(2,1)S(1)}, bf16[512,512]{1,0:T(8,128)(2,1)}, u32[]{:S(2)}) copy-start(bf16[512,512]{1,0:T(8,128)(2,1)} %constant.102.clone.refs_13_) | copy-start | bytes 1572868
  38.8 5.6 %copy-start.2 = (bf16[8,2,8,16,512]{4,3,2,1,0:T(8,128)(2,1)}, bf16[8,2,8,16,512]{4,3,2,1,0:T(8,128)(2,1)S(1)}, u32[]{:S(2)}) copy-start(bf16[8,2,8,16,512]{4,3,2,1,0:T(8,128)(2,1)S(1)} %get-tuple-element.16) | copy-start | bytes 6291460
  38.8 9.6 %collective-permute-start.9 = (bf16[10,8,16,512]{3,2,1,0:T(8,128)(2,1)}, bf16[10,8,16,512]{3,2,1,0:T(8,128)(2,1)S(1)}, u32[]{:S(2)}, u32[]{:S(2)}) collective-permute-start(bf16[10,8,16,512]{3,2,1,0:T(8,128)(2,1)} %bitcast.19), channel_id=1, source_target_pairs={{0,8},{8,0},{16,24},{24,16},{32,40},{40,32},{48,56},{56,48},{64,72... | collective-permute-start | bytes 3932168 | tf_op jit(solution)/shard_map/ppermute | solution.py:178
  44.5 3.9 %collective-permute-start.10 = (bf16[6,8,16,512]{3,2,1,0:T(8,128)(2,1)S(1)}, bf16[6,8,16,512]{3,2,1,0:T(8,128)(2,1)S(1)}, u32[]{:S(2)}, u32[]{:S(2)}) collective-permute-start(bf16[6,8,16,512]{3,2,1,0:T(8,128)(2,1)S(1)} %bitcast.58), channel_id=1, source_target_pairs={{0,8},{8,0},{16,24},{24,16},{32,40},{40,32},{48,56},{56,48},{64,72... | collective-permute-start | bytes 2359304 | tf_op jit(solution)/shard_map/ppermute | solution.py:182

commit v13 on v12

--- a/solution.py
+++ b/solution.py
@@ -169,13 +169,16 @@
             from_below[-1], from_above[-1], carried = lax.optimization_barrier(
                 (from_below[-1], from_above[-1], carried)
             )
-    far = jnp.stack(
-        [lax.ppermute(from_below[-1][0], "dm", up), lax.ppermute(from_above[-1][1], "dm", down)]
-    )
     near = z_count // 4 + 1
     early = jnp.stack(from_above[:near] + from_below[near - 1 : 0 : -1])
     early = early.reshape((-1,) + own.shape)
     theirs_early = lax.ppermute(early, "dm", partner)
+    from_below[-1], from_above[-1], theirs_early = lax.optimization_barrier(
+        (from_below[-1], from_above[-1], theirs_early)
+    )
+    far = jnp.stack(
+        [lax.ppermute(from_below[-1][0], "dm", up), lax.ppermute(from_above[-1][1], "dm", down)]
+    )
     column = jnp.stack(from_above + [far] + from_below[:0:-1])
     column = column.reshape((2 * z_count,) + own.shape)
     late = column[2 * near : 2 * (z_count - near + 1)]

time: 99.5 us -> 106 us (1.065); the launches traced: 98.3 us -> 106 us
  waiting for transfers between devices: 13.4 us -> 18.4 us
  local copies, waits for them, and re-layouts: 10.6 us -> 13.6 us
  starting transfers between devices: 24.2 us -> 22.9 us
    ppermute x3, waiting for transfers between devices: 6.49 us -> 10.1 us  [gather_spectra(): from_below.append(lax.ppermute(from_below[-1], 'dm', up))]
    ppermute x1, waiting for transfers between devices: 2.47 us -> 0.01 us  [gather_spectra(): return (column, theirs_early, lax.ppermute(late, 'dm', partner), carried)]
    unnamed x12 -> x11, local copies, waits for them, and re-layouts: 3.21 us -> 5.51 us
    ppermute x1, starting transfers between devices: 5.55 us -> 3.82 us  [gather_spectra(): theirs_early = lax.ppermute(early, 'dm', partner)]
    ppermute x1, waiting for transfers between devices: 1.59 us -> 3.17 us  [gather_spectra(): lax.ppermute(from_below[-1][0], 'dm', up)]
    ppermute x3, waiting for transfers between devices: 0.2 us -> 1.61 us  [gather_spectra(): from_above.append(lax.ppermute(from_above[-1], 'dm', down))]
    ppermute x1, starting transfers between devices: 1.36 us -> 2.66 us  [gather_spectra(): return (column, theirs_early, lax.ppermute(late, 'dm', partner), carried)]
  transfers between devices with their start and end apart: 11 -> 11, of which waited for: 8 -> 7; matrix products, arithmetic and copies ran while one was open for 7% -> 10% of each run, Pallas kernels for 0% -> 0%
where the time goes in v13:
time: 106 us
  blocking collectives  34.7 us (33%)
  starting transfers between devices  22.9 us (22%)
  waiting for transfers between devices  18.4 us (17%)
  local copies, waits for them, and re-layouts  13.6 us (13%)
  Pallas kernels  13.3 us (13%)
  other arithmetic  1.74 us (2%)
  matrix products  1.27 us (1%)
    all_to_all x1, blocking collectives, shards(): lax.all_to_all(detected.transpose(1, 0, 2, 3), 'beam', split_axis=1, conc...  34.7 us
    pallas_call x1, Pallas kernels, detect(): pl.pallas_call(detect_kernel, out_shape=jax.ShapeDtypeStruct((beams, tria...  13.3 us
    ppermute x3, waiting for transfers between devices, gather_spectra(): from_below.append(lax.ppermute(from_below[-1], 'dm', up))  10.1 us
    ppermute x3, starting transfers between devices, gather_spectra(): from_above.append(lax.ppermute(from_above[-1], 'dm', down))  9.18 us
    unnamed x11, local copies, waits for them, and re-layouts  5.51 us
    reshape x1, local copies, waits for them, and re-layouts, shards(): resp = responses.reshape(trials, chans, 2 * length)  4.39 us
    ppermute x1, starting transfers between devices, gather_spectra(): theirs_early = lax.ppermute(early, 'dm', partner)  3.82 us
    ppermute x1, waiting for transfers between devices, gather_spectra(): lax.ppermute(from_below[-1][0], 'dm', up)  3.17 us
  transfers between devices with their start and end apart: 11, of which 7 were waited for; matrix products, arithmetic and copies ran while one was open for 10% of the time, Pallas kernels for 0%

profile of v13, /device:TPU:1, one launch (start us, length us, event | category | flops | bytes accessed | tf_op | source)
XLA Modules:
  0.0 106.0 jit_solution(8226913358852922296)
XLA Ops:
  0.0 0.9 copy.9
  0.9 1.3 %fusion = bf16[16,8,512]{2,1,0:T(8,128)(2,1)S(1)} fusion(bf16[128,512]{1,0:T(8,128)(2,1)S(1)} %bitcast.59, bf16[512,512]{1,0:T(8,128)(2,1)} %constant.101.clone), kind=kOutput, calls=%fused_computation.1 | convolution fusion | flops 67174400 | bytes 786432 | tf_op jit(solution)/shard_map/dot_general | solution.py:194
  2.3 2.1 %collective-permute-start = (bf16[8,16,512]{2,1,0:T(8,128)(2,1)S(1)}, bf16[8,16,512]{2,1,0:T(8,128)(2,1)S(1)}, u32[]{:S(2)}, u32[]{:S(2)}) collective-permute-start(bf16[8,16,512]{2,1,0:T(8,128)(2,1)S(1)} %bitcast.55), channel_id=1, source_target_pairs={{0,128},{8,136},{16,144},{24,152},{32,160},{40,168},{48,176},{56,1... | collective-permute-start | bytes 393224 | tf_op jit(solution)/shard_map/ppermute | solution.py:162
  4.4 2.4 %collective-permute-done = bf16[8,16,512]{2,1,0:T(8,128)(2,1)S(1)} collective-permute-done((bf16[8,16,512]{2,1,0:T(8,128)(2,1)S(1)}, bf16[8,16,512]{2,1,0:T(8,128)(2,1)S(1)}, u32[]{:S(2)}, u32[]{:S(2)}) %collective-permute-start) | collective-permute-done | bytes 131104 | tf_op jit(solution)/shard_map/ppermute | solution.py:162
  6.8 2.5 %collective-permute-start.1 = (bf16[2,8,16,512]{3,2,1,0:T(8,128)(2,1)S(1)}, bf16[2,8,16,512]{3,2,1,0:T(8,128)(2,1)S(1)}, u32[]{:S(2)}, u32[]{:S(2)}) collective-permute-start(bf16[2,8,16,512]{3,2,1,0:T(8,128)(2,1)S(1)} %pad_maximum_fusion.1), channel_id=1, source_target_pairs={{0,16},{8,24},{16,32},{24,40},{32,48},{40,56},{48,64},{56,72},{64,... | collective-permute-start | bytes 786440 | tf_op jit(solution)/shard_map/ppermute | solution.py:166
  9.3 4.0 %collective-permute-start.2 = (bf16[2,8,16,512]{3,2,1,0:T(8,128)(2,1)S(1)}, bf16[2,8,16,512]{3,2,1,0:T(8,128)(2,1)S(1)}, u32[]{:S(2)}, u32[]{:S(2)}) collective-permute-start(bf16[2,8,16,512]{3,2,1,0:T(8,128)(2,1)S(1)} %pad_maximum_fusion.1), channel_id=1, source_target_pairs={{0,112},{8,120},{16,0},{24,8},{32,16},{40,24},{48,32},{56,40},{64,... | collective-permute-start | bytes 786440 | tf_op jit(solution)/shard_map/ppermute | solution.py:167
  13.3 4.4 %reshape.29.refs_12_ = bf16[4,512,512]{2,1,0:T(8,128)(2,1)} reshape(bf16[4,512,2,256]{3,2,1,0:T(2,128)(2,1)} %param.6) | data formatting | bytes 4194304 | tf_op jit(solution)/shard_map/reshape | solution.py:198
  18.4 2.5 %collective-permute-start.3 = (bf16[2,8,16,512]{3,2,1,0:T(8,128)(2,1)S(1)}, bf16[2,8,16,512]{3,2,1,0:T(8,128)(2,1)S(1)}, u32[]{:S(2)}, u32[]{:S(2)}) collective-permute-start(bf16[2,8,16,512]{3,2,1,0:T(8,128)(2,1)S(1)} %collective-permute-done.2), channel_id=1, source_target_pairs={{0,112},{8,120},{16,0},{24,8},{32,16},{40,24},{48,32},{56,40},{64,... | collective-permute-start | bytes 786440 | tf_op jit(solution)/shard_map/ppermute | solution.py:167
  20.9 0.9 bitcast_dynamic-update-slice_fusion.9
  21.7 0.9 bitcast_dynamic-update-slice_fusion.7
  22.6 1.6 %collective-permute-done.3 = bf16[2,8,16,512]{3,2,1,0:T(8,128)(2,1)S(1)} collective-permute-done((bf16[2,8,16,512]{3,2,1,0:T(8,128)(2,1)S(1)}, bf16[2,8,16,512]{3,2,1,0:T(8,128)(2,1)S(1)}, u32[]{:S(2)}, u32[]{:S(2)}) %collective-permute-start.3) | collective-permute-done | bytes 262176 | tf_op jit(solution)/shard_map/ppermute | solution.py:167
  24.2 0.8 bitcast_dynamic-update-slice_fusion.5
  25.0 3.1 %collective-permute-done.4 = bf16[2,8,16,512]{3,2,1,0:T(8,128)(2,1)S(1)} collective-permute-done((bf16[2,8,16,512]{3,2,1,0:T(8,128)(2,1)S(1)}, bf16[2,8,16,512]{3,2,1,0:T(8,128)(2,1)S(1)}, u32[]{:S(2)}, u32[]{:S(2)}) %collective-permute-start.4) | collective-permute-done | bytes 262176 | tf_op jit(solution)/shard_map/ppermute | solution.py:166
  29.6 3.8 %collective-permute-start.7 = (bf16[10,8,16,512]{3,2,1,0:T(8,128)(2,1)}, bf16[10,8,16,512]{3,2,1,0:T(8,128)(2,1)S(1)}, u32[]{:S(2)}, u32[]{:S(2)}) collective-permute-start(bf16[10,8,16,512]{3,2,1,0:T(8,128)(2,1)} %bitcast.11), channel_id=1, source_target_pairs={{0,8},{8,0},{16,24},{24,16},{32,40},{40,32},{48,56},{56,48},{64,72... | collective-permute-start | bytes 3932168 | tf_op jit(solution)/shard_map/ppermute | solution.py:175
  33.4 2.7 %collective-permute-start.6 = (bf16[2,8,16,512]{3,2,1,0:T(8,128)(2,1)S(1)}, bf16[2,8,16,512]{3,2,1,0:T(8,128)(2,1)S(1)}, u32[]{:S(2)}, u32[]{:S(2)}) collective-permute-start(bf16[2,8,16,512]{3,2,1,0:T(8,128)(2,1)S(1)} %collective-permute-done.3), channel_id=1, source_target_pairs={{0,112},{8,120},{16,0},{24,8},{32,16},{40,24},{48,32},{56,40},{64,... | collective-permute-start | bytes 786440 | tf_op jit(solution)/shard_map/ppermute | solution.py:167
  36.1 6.3 %collective-permute-done.5 = bf16[2,8,16,512]{3,2,1,0:T(8,128)(2,1)S(1)} collective-permute-done((bf16[2,8,16,512]{3,2,1,0:T(8,128)(2,1)S(1)}, bf16[2,8,16,512]{3,2,1,0:T(8,128)(2,1)S(1)}, u32[]{:S(2)}, u32[]{:S(2)}) %collective-permute-start.5) | collective-permute-done | bytes 262176 | tf_op jit(solution)/shard_map/ppermute | solution.py:166
  42.5 2.5 %collective-permute-start.9 = (bf16[8,16,512]{2,1,0:T(8,128)(2,1)S(1)}, bf16[8,16,512]{2,1,0:T(8,128)(2,1)S(1)}, u32[]{:S(2)}, u32[]{:S(2)}) collective-permute-start(bf16[8,16,512]{2,1,0:T(8,128)(2,1)S(1)} %slice_bitcast_fusion), channel_id=1, source_target_pairs={{0,112},{8,120},{16,0},{24,8},{32,16},{40,24},{48,32},{56,40},{64,... | collective-permute-start | bytes 393224 | tf_op jit(solution)/shard_map/ppermute | solution.py:180
  45.1 0.7 constant_dynamic-update-slice_fusion.2
  45.8 1.1 %collective-permute-done.9 = bf16[8,16,512]{2,1,0:T(8,128)(2,1)S(1)} collective-permute-done((bf16[8,16,512]{2,1,0:T(8,128)(2,1)S(1)}, bf16[8,16,512]{2,1,0:T(8,128)(2,1)S(1)}, u32[]{:S(2)}, u32[]{:S(2)}) %collective-permute-start.9) | collective-permute-done | bytes 131104 | tf_op jit(solution)/shard_map/ppermute | solution.py:180
  46.9 3.2 %collective-permute-done.8 = bf16[8,16,512]{2,1,0:T(8,128)(2,1)S(1)} collective-permute-done((bf16[8,16,512]{2,1,0:T(8,128)(2,1)S(1)}, bf16[8,16,512]{2,1,0:T(8,128)(2,1)S(1)}, u32[]{:S(2)}, u32[]{:S(2)}) %collective-permute-start.8) | collective-permute-done | bytes 131104 | tf_op jit(solution)/shard_map/ppermute | solution.py:180
  50.2 2.7 %collective-permute-start.10 = (bf16[6,8,16,512]{3,2,1,0:T(8,128)(2,1)S(1)}, bf16[6,8,16,512]{3,2,1,0:T(8,128)(2,1)S(1)}, u32[]{:S(2)}, u32[]{:S(2)}) collective-permute-start(bf16[6,8,16,512]{3,2,1,0:T(8,128)(2,1)S(1)} %bitcast.58), channel_id=1, source_target_pairs={{0,8},{8,0},{16,24},{24,16},{32,40},{40,32},{48,56},{56,48},{64,72... | collective-permute-start | bytes 2359304 | tf_op jit(solution)/shard_map/ppermute | solution.py:185
  55.8 13.3 %shard_map.55 = bf16[8,4,256,128]{3,2,1,0:T(8,128)(2,1)S(1)} custom-call(s32[4]{0:T(128)S(1)} %copy-done, s32[16]{0:T(128)S(1)} %get-tuple-element.20.table_ref, s32[16]{0:T(128)S(1)} %get-tuple-element.30.early_ref, s32[16]{0:T(128)S(1)} %get-tuple-element.29.late_ref, s32[16]{0:T(128)S(1)} %get-tuple-element.17.flag_ref, s32[1]{0:T(128)} %bitcast.swap_ref, ...), custom_call_target="tpu_custom_call" | custom-call | flops 8589934592 | bytes 8912896 | tf_op jit(solution)/shard_map/pallas_call | solution.py:117
  69.1 34.7 %all_to_all.4 = bf16[4,8,256,128]{3,2,0,1:T(8,128)(2,1)S(1)} all-to-all(bf16[4,8,256,128]{3,2,0,1:T(8,128)(2,1)S(1)} %bitcast.52), channel_id=1, replica_groups=mesh['dm'=32,'beam'=8] {'beam'}, dimensions={1} | all-to-all | bytes 4194304 | tf_op jit(solution)/shard_map/all_to_all | solution.py:215
  103.9 2.1 %reshape.32 = bf16[4,1,262144]{2,0,1:T(4,128)(2,1)} reshape(bf16[4,8,256,128]{3,2,1,0:T(8,128)(2,1)S(1)} %copy.8) | data formatting | bytes 4194304 | tf_op jit(solution)/shard_map/reshape | solution.py:216
  (27 shorter events, 5.5 us)
Async XLA Ops:
  2.3 4.5 %collective-permute-start = (bf16[8,16,512]{2,1,0:T(8,128)(2,1)S(1)}, bf16[8,16,512]{2,1,0:T(8,128)(2,1)S(1)}, u32[]{:S(2)}, u32[]{:S(2)}) collective-permute-start(bf16[8,16,512]{2,1,0:T(8,128)(2,1)S(1)} %bitcast.55), channel_id=1, source_target_pairs={{0,128},{8,136},{16,144},{24,152},{32,160},{40,168},{48,176},{56,1... | collective-permute-start | bytes 393224 | tf_op jit(solution)/shard_map/ppermute | solution.py:162
  6.8 11.6 %collective-permute-start.1 = (bf16[2,8,16,512]{3,2,1,0:T(8,128)(2,1)S(1)}, bf16[2,8,16,512]{3,2,1,0:T(8,128)(2,1)S(1)}, u32[]{:S(2)}, u32[]{:S(2)}) collective-permute-start(bf16[2,8,16,512]{3,2,1,0:T(8,128)(2,1)S(1)} %pad_maximum_fusion.1), channel_id=1, source_target_pairs={{0,16},{8,24},{16,32},{24,40},{32,48},{40,56},{48,64},{56,72},{64,... | collective-permute-start | bytes 786440 | tf_op jit(solution)/shard_map/ppermute | solution.py:166
  9.3 9.1 %collective-permute-start.2 = (bf16[2,8,16,512]{3,2,1,0:T(8,128)(2,1)S(1)}, bf16[2,8,16,512]{3,2,1,0:T(8,128)(2,1)S(1)}, u32[]{:S(2)}, u32[]{:S(2)}) collective-permute-start(bf16[2,8,16,512]{3,2,1,0:T(8,128)(2,1)S(1)} %pad_maximum_fusion.1), channel_id=1, source_target_pairs={{0,112},{8,120},{16,0},{24,8},{32,16},{40,24},{48,32},{56,40},{64,... | collective-permute-start | bytes 786440 | tf_op jit(solution)/shard_map/ppermute | solution.py:167
  18.4 5.8 %collective-permute-start.3 = (bf16[2,8,16,512]{3,2,1,0:T(8,128)(2,1)S(1)}, bf16[2,8,16,512]{3,2,1,0:T(8,128)(2,1)S(1)}, u32[]{:S(2)}, u32[]{:S(2)}) collective-permute-start(bf16[2,8,16,512]{3,2,1,0:T(8,128)(2,1)S(1)} %collective-permute-done.2), channel_id=1, source_target_pairs={{0,112},{8,120},{16,0},{24,8},{32,16},{40,24},{48,32},{56,40},{64,... | collective-permute-start | bytes 786440 | tf_op jit(solution)/shard_map/ppermute | solution.py:167
  21.7 6.4 %collective-permute-start.4 = (bf16[2,8,16,512]{3,2,1,0:T(8,128)(2,1)S(1)}, bf16[2,8,16,512]{3,2,1,0:T(8,128)(2,1)S(1)}, u32[]{:S(2)}, u32[]{:S(2)}) collective-permute-start(bf16[2,8,16,512]{3,2,1,0:T(8,128)(2,1)S(1)} %collective-permute-done.1), channel_id=1, source_target_pairs={{0,16},{8,24},{16,32},{24,40},{32,48},{40,56},{48,64},{56,72},{64,... | collective-permute-start | bytes 786440 | tf_op jit(solution)/shard_map/ppermute | solution.py:166
  29.6 12.9 %collective-permute-start.7 = (bf16[10,8,16,512]{3,2,1,0:T(8,128)(2,1)}, bf16[10,8,16,512]{3,2,1,0:T(8,128)(2,1)S(1)}, u32[]{:S(2)}, u32[]{:S(2)}) collective-permute-start(bf16[10,8,16,512]{3,2,1,0:T(8,128)(2,1)} %bitcast.11), channel_id=1, source_target_pairs={{0,8},{8,0},{16,24},{24,16},{32,40},{40,32},{48,56},{56,48},{64,72... | collective-permute-start | bytes 3932168 | tf_op jit(solution)/shard_map/ppermute | solution.py:175
  33.4 9.1 %collective-permute-start.5 = (bf16[2,8,16,512]{3,2,1,0:T(8,128)(2,1)S(1)}, bf16[2,8,16,512]{3,2,1,0:T(8,128)(2,1)S(1)}, u32[]{:S(2)}, u32[]{:S(2)}) collective-permute-start(bf16[2,8,16,512]{3,2,1,0:T(8,128)(2,1)S(1)} %collective-permute-done.4), channel_id=1, source_target_pairs={{0,16},{8,24},{16,32},{24,40},{32,48},{40,56},{48,64},{56,72},{64,... | collective-permute-start | bytes 786440 | tf_op jit(solution)/shard_map/ppermute | solution.py:166
  33.4 9.1 %collective-permute-start.6 = (bf16[2,8,16,512]{3,2,1,0:T(8,128)(2,1)S(1)}, bf16[2,8,16,512]{3,2,1,0:T(8,128)(2,1)S(1)}, u32[]{:S(2)}, u32[]{:S(2)}) collective-permute-start(bf16[2,8,16,512]{3,2,1,0:T(8,128)(2,1)S(1)} %collective-permute-done.3), channel_id=1, source_target_pairs={{0,112},{8,120},{16,0},{24,8},{32,16},{40,24},{48,32},{56,40},{64,... | collective-permute-start | bytes 786440 | tf_op jit(solution)/shard_map/ppermute | solution.py:167
  42.5 4.4 %collective-permute-start.9 = (bf16[8,16,512]{2,1,0:T(8,128)(2,1)S(1)}, bf16[8,16,512]{2,1,0:T(8,128)(2,1)S(1)}, u32[]{:S(2)}, u32[]{:S(2)}) collective-permute-start(bf16[8,16,512]{2,1,0:T(8,128)(2,1)S(1)} %slice_bitcast_fusion), channel_id=1, source_target_pairs={{0,112},{8,120},{16,0},{24,8},{32,16},{40,24},{48,32},{56,40},{64,... | collective-permute-start | bytes 393224 | tf_op jit(solution)/shard_map/ppermute | solution.py:180
  45.0 5.1 %collective-permute-start.8 = (bf16[8,16,512]{2,1,0:T(8,128)(2,1)S(1)}, bf16[8,16,512]{2,1,0:T(8,128)(2,1)S(1)}, u32[]{:S(2)}, u32[]{:S(2)}) collective-permute-start(bf16[8,16,512]{2,1,0:T(8,128)(2,1)S(1)} %slice_bitcast_fusion.1), channel_id=1, source_target_pairs={{0,16},{8,24},{16,32},{24,40},{32,48},{40,56},{48,64},{56,72},{64,... | collective-permute-start | bytes 393224 | tf_op jit(solution)/shard_map/ppermute | solution.py:180
  50.1 5.7 %copy-start = (s32[4]{0:T(128)S(1)}, s32[4]{0:T(128)}, u32[]{:S(2)}) copy-start(s32[4]{0:T(128)} %chirp_ref.1) | copy-start | bytes 52
  50.1 5.7 %copy-start.1 = (bf16[512,512]{1,0:T(8,128)(2,1)S(1)}, bf16[512,512]{1,0:T(8,128)(2,1)}, u32[]{:S(2)}) copy-start(bf16[512,512]{1,0:T(8,128)(2,1)} %constant.102.clone.refs_13_) | copy-start | bytes 1572868
  50.2 5.5 %collective-permute-start.10 = (bf16[6,8,16,512]{3,2,1,0:T(8,128)(2,1)S(1)}, bf16[6,8,16,512]{3,2,1,0:T(8,128)(2,1)S(1)}, u32[]{:S(2)}, u32[]{:S(2)}) collective-permute-start(bf16[6,8,16,512]{3,2,1,0:T(8,128)(2,1)S(1)} %bitcast.58), channel_id=1, source_target_pairs={{0,8},{8,0},{16,24},{24,16},{32,40},{40,32},{48,56},{56,48},{64,72... | collective-permute-start | bytes 2359304 | tf_op jit(solution)/shard_map/ppermute | solution.py:185

commit v14 on v12

--- a/solution.py
+++ b/solution.py
@@ -12,7 +12,7 @@
 
 RATE = 4
 CHAN_BLOCK = 256
-GROUP = 4
+GROUP = 8
 
 
 def dft_tables(length):

time: 99.5 us -> 102 us (1.025)
  local copies, waits for them, and re-layouts: 10.6 us -> 12 us
  waiting for transfers between devices: 13.4 us -> 14.5 us
  starting transfers between devices: 24.2 us -> 23.1 us
    unnamed x12, local copies, waits for them, and re-layouts: 3.21 us -> 4.53 us
    ppermute x1, starting transfers between devices: 1.36 us -> 0.27 us  [gather_spectra(): return (column, theirs_early, lax.ppermute(late, 'dm', partner), carried)]
    ppermute x1, waiting for transfers between devices: 2.47 us -> 3.51 us  [gather_spectra(): return (column, theirs_early, lax.ppermute(late, 'dm', partner), carried)]
where the time goes in v14:
time: 102 us; the launch traced here: 100 us
  blocking collectives  34 us (33%)
  starting transfers between devices  23.1 us (23%)
  waiting for transfers between devices  14.5 us (14%)
  Pallas kernels  14.4 us (14%)
  local copies, waits for them, and re-layouts  12 us (12%)
  matrix products  1.27 us (1%)
    all_to_all x1, blocking collectives, shards(): lax.all_to_all(detected.transpose(1, 0, 2, 3), 'beam', split_axis=1, conc...  34 us
    pallas_call x1, Pallas kernels, detect(): pl.pallas_call(detect_kernel, out_shape=jax.ShapeDtypeStruct((beams, tria...  14.4 us
    ppermute x3, starting transfers between devices, gather_spectra(): from_above.append(lax.ppermute(from_above[-1], 'dm', down))  9.37 us
    ppermute x3, waiting for transfers between devices, gather_spectra(): from_below.append(lax.ppermute(from_below[-1], 'dm', up))  6.48 us
    ppermute x1, starting transfers between devices, gather_spectra(): theirs_early = lax.ppermute(early, 'dm', partner)  5.57 us
    unnamed x12, local copies, waits for them, and re-layouts  4.53 us
    reshape x1, local copies, waits for them, and re-layouts, shards(): resp = responses.reshape(trials, chans, 2 * length)  4.4 us
    ppermute x1, waiting for transfers between devices, gather_spectra(): return (column, theirs_early, lax.ppermute(late, 'dm', partner), carried)  3.51 us
  transfers between devices with their start and end apart: 11, of which 8 were waited for; matrix products, arithmetic and copies ran while one was open for 7% of the time, Pallas kernels for 0%

profile of v14, /device:TPU:1, one launch (start us, length us, event | category | flops | bytes accessed | tf_op | source)
XLA Modules:
  0.0 100.4 jit_solution(12706081045284161758)
XLA Ops:
  0.0 0.9 copy.9
  0.9 1.3 %fusion = bf16[16,8,512]{2,1,0:T(8,128)(2,1)S(1)} fusion(bf16[128,512]{1,0:T(8,128)(2,1)S(1)} %bitcast.67, bf16[512,512]{1,0:T(8,128)(2,1)} %constant.101.clone), kind=kOutput, calls=%fused_computation.1 | convolution fusion | flops 67174400 | bytes 786432 | tf_op jit(solution)/shard_map/dot_general | solution.py:191
  2.3 2.1 %collective-permute-start = (bf16[8,16,512]{2,1,0:T(8,128)(2,1)S(1)}, bf16[8,16,512]{2,1,0:T(8,128)(2,1)S(1)}, u32[]{:S(2)}, u32[]{:S(2)}) collective-permute-start(bf16[8,16,512]{2,1,0:T(8,128)(2,1)S(1)} %bitcast.63), channel_id=1, source_target_pairs={{0,128},{8,136},{16,144},{24,152},{32,160},{40,168},{48,176},{56,1... | collective-permute-start | bytes 393224 | tf_op jit(solution)/shard_map/ppermute | solution.py:162
  4.4 2.4 %collective-permute-done = bf16[8,16,512]{2,1,0:T(8,128)(2,1)S(1)} collective-permute-done((bf16[8,16,512]{2,1,0:T(8,128)(2,1)S(1)}, bf16[8,16,512]{2,1,0:T(8,128)(2,1)S(1)}, u32[]{:S(2)}, u32[]{:S(2)}) %collective-permute-start) | collective-permute-done | bytes 131104 | tf_op jit(solution)/shard_map/ppermute | solution.py:162
  6.8 2.5 %collective-permute-start.1 = (bf16[2,8,16,512]{3,2,1,0:T(8,128)(2,1)S(1)}, bf16[2,8,16,512]{3,2,1,0:T(8,128)(2,1)S(1)}, u32[]{:S(2)}, u32[]{:S(2)}) collective-permute-start(bf16[2,8,16,512]{3,2,1,0:T(8,128)(2,1)S(1)} %pad_maximum_fusion.1), channel_id=1, source_target_pairs={{0,16},{8,24},{16,32},{24,40},{32,48},{40,56},{48,64},{56,72},{64,... | collective-permute-start | bytes 786440 | tf_op jit(solution)/shard_map/ppermute | solution.py:166
  9.3 4.0 %collective-permute-start.2 = (bf16[2,8,16,512]{3,2,1,0:T(8,128)(2,1)S(1)}, bf16[2,8,16,512]{3,2,1,0:T(8,128)(2,1)S(1)}, u32[]{:S(2)}, u32[]{:S(2)}) collective-permute-start(bf16[2,8,16,512]{3,2,1,0:T(8,128)(2,1)S(1)} %pad_maximum_fusion.1), channel_id=1, source_target_pairs={{0,112},{8,120},{16,0},{24,8},{32,16},{40,24},{48,32},{56,40},{64,... | collective-permute-start | bytes 786440 | tf_op jit(solution)/shard_map/ppermute | solution.py:167
  13.3 4.4 %reshape.29.refs_24_ = bf16[4,512,512]{2,1,0:T(8,128)(2,1)} reshape(bf16[4,512,2,256]{3,2,1,0:T(2,128)(2,1)} %param.6) | data formatting | bytes 4194304 | tf_op jit(solution)/shard_map/reshape | solution.py:195
  18.4 2.7 %collective-permute-start.3 = (bf16[2,8,16,512]{3,2,1,0:T(8,128)(2,1)S(1)}, bf16[2,8,16,512]{3,2,1,0:T(8,128)(2,1)S(1)}, u32[]{:S(2)}, u32[]{:S(2)}) collective-permute-start(bf16[2,8,16,512]{3,2,1,0:T(8,128)(2,1)S(1)} %collective-permute-done.2), channel_id=1, source_target_pairs={{0,112},{8,120},{16,0},{24,8},{32,16},{40,24},{48,32},{56,40},{64,... | collective-permute-start | bytes 786440 | tf_op jit(solution)/shard_map/ppermute | solution.py:167
  21.0 0.7 bitcast_dynamic-update-slice_fusion.8
  21.8 3.6 %collective-permute-done.5 = bf16[2,8,16,512]{3,2,1,0:T(8,128)(2,1)S(1)} collective-permute-done((bf16[2,8,16,512]{3,2,1,0:T(8,128)(2,1)S(1)}, bf16[2,8,16,512]{3,2,1,0:T(8,128)(2,1)S(1)}, u32[]{:S(2)}, u32[]{:S(2)}) %collective-permute-start.5) | collective-permute-done | bytes 262176 | tf_op jit(solution)/shard_map/ppermute | solution.py:166
  25.3 0.7 bitcast_dynamic-update-slice_fusion.6
  26.1 2.7 %collective-permute-start.4 = (bf16[2,8,16,512]{3,2,1,0:T(8,128)(2,1)S(1)}, bf16[2,8,16,512]{3,2,1,0:T(8,128)(2,1)S(1)}, u32[]{:S(2)}, u32[]{:S(2)}) collective-permute-start(bf16[2,8,16,512]{3,2,1,0:T(8,128)(2,1)S(1)} %collective-permute-done.3), channel_id=1, source_target_pairs={{0,112},{8,120},{16,0},{24,8},{32,16},{40,24},{48,32},{56,40},{64,... | collective-permute-start | bytes 786440 | tf_op jit(solution)/shard_map/ppermute | solution.py:167
  28.8 0.8 bitcast_dynamic-update-slice_fusion.4
  29.5 2.3 %collective-permute-done.6 = bf16[2,8,16,512]{3,2,1,0:T(8,128)(2,1)S(1)} collective-permute-done((bf16[2,8,16,512]{3,2,1,0:T(8,128)(2,1)S(1)}, bf16[2,8,16,512]{3,2,1,0:T(8,128)(2,1)S(1)}, u32[]{:S(2)}, u32[]{:S(2)}) %collective-permute-start.6) | collective-permute-done | bytes 262176 | tf_op jit(solution)/shard_map/ppermute | solution.py:166
  32.1 3.2 %collective-permute-start.8 = (bf16[8,16,512]{2,1,0:T(8,128)(2,1)S(1)}, bf16[8,16,512]{2,1,0:T(8,128)(2,1)S(1)}, u32[]{:S(2)}, u32[]{:S(2)}) collective-permute-start(bf16[8,16,512]{2,1,0:T(8,128)(2,1)S(1)} %slice_bitcast_fusion), channel_id=1, source_target_pairs={{0,112},{8,120},{16,0},{24,8},{32,16},{40,24},{48,32},{56,40},{64,... | collective-permute-start | bytes 393224 | tf_op jit(solution)/shard_map/ppermute | solution.py:173
  35.3 1.6 %collective-permute-done.7 = bf16[8,16,512]{2,1,0:T(8,128)(2,1)S(1)} collective-permute-done((bf16[8,16,512]{2,1,0:T(8,128)(2,1)S(1)}, bf16[8,16,512]{2,1,0:T(8,128)(2,1)S(1)}, u32[]{:S(2)}, u32[]{:S(2)}) %collective-permute-start.7) | collective-permute-done | bytes 131104 | tf_op jit(solution)/shard_map/ppermute | solution.py:173
  37.3 0.7 bitcast_dynamic-update-slice_fusion.2
  38.0 0.7 bitcast_dynamic-update-slice_fusion
  38.8 1.3 %copy-done.2 = bf16[8,2,8,16,512]{4,3,2,1,0:T(8,128)(2,1)} copy-done((bf16[8,2,8,16,512]{4,3,2,1,0:T(8,128)(2,1)}, bf16[8,2,8,16,512]{4,3,2,1,0:T(8,128)(2,1)S(1)}, u32[]{:S(2)}) %copy-start.2) | copy-done | bytes 2097176
  40.1 5.6 %collective-permute-start.9 = (bf16[10,8,16,512]{3,2,1,0:T(8,128)(2,1)}, bf16[10,8,16,512]{3,2,1,0:T(8,128)(2,1)S(1)}, u32[]{:S(2)}, u32[]{:S(2)}) collective-permute-start(bf16[10,8,16,512]{3,2,1,0:T(8,128)(2,1)} %bitcast.19), channel_id=1, source_target_pairs={{0,8},{8,0},{16,24},{24,16},{32,40},{40,32},{48,56},{56,48},{64,72... | collective-permute-start | bytes 3932168 | tf_op jit(solution)/shard_map/ppermute | solution.py:178
  46.2 3.5 %collective-permute-done.10.refs_2_.refs_5_.refs_8_.refs_11_.refs_14_.refs_17_.refs_20_.refs_23_ = bf16[6,8,16,512]{3,2,1,0:T(8,128)(2,1)S(1)} collective-permute-done((bf16[6,8,16,512]{3,2,1,0:T(8,128)(2,1)S(1)}, bf16[6,8,16,512]{3,2,1,0:T(8,128)(2,1)S(1)}, u32[]{:S(2)}, u32[]{:S(2)}) %collective-permute-start.10) | collective-permute-done | bytes 786464 | tf_op jit(solution)/shard_map/ppermute | solution.py:182
  49.7 14.4 %shard_map.55 = bf16[8,4,256,128]{3,2,1,0:T(8,128)(2,1)S(1)} custom-call(s32[4]{0:T(128)S(1)} %copy-done.1, s32[16]{0:T(128)S(1)} %get-tuple-element.14.table_ref, s32[16]{0:T(128)S(1)} %get-tuple-element.28.early_ref, s32[16]{0:T(128)S(1)} %get-tuple-element.27.late_ref, s32[16]{0:T(128)S(1)} %get-tuple-element.11.flag_ref, s32[1]{0:T(128)} %bitcast.swap_ref, ...), custom_call_target="tpu_custom_call" | custom-call | flops 8589934592 | bytes 8912896 | tf_op jit(solution)/shard_map/pallas_call | solution.py:117
  64.1 34.0 %all_to_all.4 = bf16[4,8,256,128]{3,2,0,1:T(8,128)(2,1)S(1)} all-to-all(bf16[4,8,256,128]{3,2,0,1:T(8,128)(2,1)S(1)} %bitcast.52), channel_id=1, replica_groups=mesh['dm'=32,'beam'=8] {'beam'}, dimensions={1} | all-to-all | bytes 4194304 | tf_op jit(solution)/shard_map/all_to_all | solution.py:212
  98.3 2.1 %reshape.32 = bf16[4,1,262144]{2,0,1:T(4,128)(2,1)} reshape(bf16[4,8,256,128]{3,2,1,0:T(8,128)(2,1)S(1)} %copy.8) | data formatting | bytes 4194304 | tf_op jit(solution)/shard_map/reshape | solution.py:213
  (27 shorter events, 2.0 us)
Async XLA Ops:
  2.3 4.5 %collective-permute-start = (bf16[8,16,512]{2,1,0:T(8,128)(2,1)S(1)}, bf16[8,16,512]{2,1,0:T(8,128)(2,1)S(1)}, u32[]{:S(2)}, u32[]{:S(2)}) collective-permute-start(bf16[8,16,512]{2,1,0:T(8,128)(2,1)S(1)} %bitcast.63), channel_id=1, source_target_pairs={{0,128},{8,136},{16,144},{24,152},{32,160},{40,168},{48,176},{56,1... | collective-permute-start | bytes 393224 | tf_op jit(solution)/shard_map/ppermute | solution.py:162
  6.8 11.6 %collective-permute-start.1 = (bf16[2,8,16,512]{3,2,1,0:T(8,128)(2,1)S(1)}, bf16[2,8,16,512]{3,2,1,0:T(8,128)(2,1)S(1)}, u32[]{:S(2)}, u32[]{:S(2)}) collective-permute-start(bf16[2,8,16,512]{3,2,1,0:T(8,128)(2,1)S(1)} %pad_maximum_fusion.1), channel_id=1, source_target_pairs={{0,16},{8,24},{16,32},{24,40},{32,48},{40,56},{48,64},{56,72},{64,... | collective-permute-start | bytes 786440 | tf_op jit(solution)/shard_map/ppermute | solution.py:166
  9.3 9.1 %collective-permute-start.2 = (bf16[2,8,16,512]{3,2,1,0:T(8,128)(2,1)S(1)}, bf16[2,8,16,512]{3,2,1,0:T(8,128)(2,1)S(1)}, u32[]{:S(2)}, u32[]{:S(2)}) collective-permute-start(bf16[2,8,16,512]{3,2,1,0:T(8,128)(2,1)S(1)} %pad_maximum_fusion.1), channel_id=1, source_target_pairs={{0,112},{8,120},{16,0},{24,8},{32,16},{40,24},{48,32},{56,40},{64,... | collective-permute-start | bytes 786440 | tf_op jit(solution)/shard_map/ppermute | solution.py:167
  18.4 7.0 %collective-permute-start.5 = (bf16[2,8,16,512]{3,2,1,0:T(8,128)(2,1)S(1)}, bf16[2,8,16,512]{3,2,1,0:T(8,128)(2,1)S(1)}, u32[]{:S(2)}, u32[]{:S(2)}) collective-permute-start(bf16[2,8,16,512]{3,2,1,0:T(8,128)(2,1)S(1)} %collective-permute-done.1), channel_id=1, source_target_pairs={{0,16},{8,24},{16,32},{24,40},{32,48},{40,56},{48,64},{56,72},{64,... | collective-permute-start | bytes 786440 | tf_op jit(solution)/shard_map/ppermute | solution.py:166
  18.4 7.7 %collective-permute-start.3 = (bf16[2,8,16,512]{3,2,1,0:T(8,128)(2,1)S(1)}, bf16[2,8,16,512]{3,2,1,0:T(8,128)(2,1)S(1)}, u32[]{:S(2)}, u32[]{:S(2)}) collective-permute-start(bf16[2,8,16,512]{3,2,1,0:T(8,128)(2,1)S(1)} %collective-permute-done.2), channel_id=1, source_target_pairs={{0,112},{8,120},{16,0},{24,8},{32,16},{40,24},{48,32},{56,40},{64,... | collective-permute-start | bytes 786440 | tf_op jit(solution)/shard_map/ppermute | solution.py:167
  25.3 6.4 %collective-permute-start.6 = (bf16[2,8,16,512]{3,2,1,0:T(8,128)(2,1)S(1)}, bf16[2,8,16,512]{3,2,1,0:T(8,128)(2,1)S(1)}, u32[]{:S(2)}, u32[]{:S(2)}) collective-permute-start(bf16[2,8,16,512]{3,2,1,0:T(8,128)(2,1)S(1)} %collective-permute-done.5), channel_id=1, source_target_pairs={{0,16},{8,24},{16,32},{24,40},{32,48},{40,56},{48,64},{56,72},{64,... | collective-permute-start | bytes 786440 | tf_op jit(solution)/shard_map/ppermute | solution.py:166
  26.1 6.0 %collective-permute-start.4 = (bf16[2,8,16,512]{3,2,1,0:T(8,128)(2,1)S(1)}, bf16[2,8,16,512]{3,2,1,0:T(8,128)(2,1)S(1)}, u32[]{:S(2)}, u32[]{:S(2)}) collective-permute-start(bf16[2,8,16,512]{3,2,1,0:T(8,128)(2,1)S(1)} %collective-permute-done.3), channel_id=1, source_target_pairs={{0,112},{8,120},{16,0},{24,8},{32,16},{40,24},{48,32},{56,40},{64,... | collective-permute-start | bytes 786440 | tf_op jit(solution)/shard_map/ppermute | solution.py:167
  31.8 5.1 %collective-permute-start.7 = (bf16[8,16,512]{2,1,0:T(8,128)(2,1)S(1)}, bf16[8,16,512]{2,1,0:T(8,128)(2,1)S(1)}, u32[]{:S(2)}, u32[]{:S(2)}) collective-permute-start(bf16[8,16,512]{2,1,0:T(8,128)(2,1)S(1)} %slice_bitcast_fusion.1), channel_id=1, source_target_pairs={{0,16},{8,24},{16,32},{24,40},{32,48},{40,56},{48,64},{56,72},{64,... | collective-permute-start | bytes 393224 | tf_op jit(solution)/shard_map/ppermute | solution.py:173
  32.1 5.1 %collective-permute-start.8 = (bf16[8,16,512]{2,1,0:T(8,128)(2,1)S(1)}, bf16[8,16,512]{2,1,0:T(8,128)(2,1)S(1)}, u32[]{:S(2)}, u32[]{:S(2)}) collective-permute-start(bf16[8,16,512]{2,1,0:T(8,128)(2,1)S(1)} %slice_bitcast_fusion), channel_id=1, source_target_pairs={{0,112},{8,120},{16,0},{24,8},{32,16},{40,24},{48,32},{56,40},{64,... | collective-permute-start | bytes 393224 | tf_op jit(solution)/shard_map/ppermute | solution.py:173
  37.2 12.4 %copy-start = (bf16[512,512]{1,0:T(8,128)(2,1)S(1)}, bf16[512,512]{1,0:T(8,128)(2,1)}, u32[]{:S(2)}) copy-start(bf16[512,512]{1,0:T(8,128)(2,1)} %constant.102.clone.refs_25_) | copy-start | bytes 1572868
  37.3 12.4 %copy-start.1 = (s32[4]{0:T(128)S(1)}, s32[4]{0:T(128)}, u32[]{:S(2)}) copy-start(s32[4]{0:T(128)} %chirp_ref.1) | copy-start | bytes 52
  38.8 1.3 %copy-start.2 = (bf16[8,2,8,16,512]{4,3,2,1,0:T(8,128)(2,1)}, bf16[8,2,8,16,512]{4,3,2,1,0:T(8,128)(2,1)S(1)}, u32[]{:S(2)}) copy-start(bf16[8,2,8,16,512]{4,3,2,1,0:T(8,128)(2,1)S(1)} %get-tuple-element.16) | copy-start | bytes 6291460
  40.1 9.6 %collective-permute-start.9 = (bf16[10,8,16,512]{3,2,1,0:T(8,128)(2,1)}, bf16[10,8,16,512]{3,2,1,0:T(8,128)(2,1)S(1)}, u32[]{:S(2)}, u32[]{:S(2)}) collective-permute-start(bf16[10,8,16,512]{3,2,1,0:T(8,128)(2,1)} %bitcast.19), channel_id=1, source_target_pairs={{0,8},{8,0},{16,24},{24,16},{32,40},{40,32},{48,56},{56,48},{64,72... | collective-permute-start | bytes 3932168 | tf_op jit(solution)/shard_map/ppermute | solution.py:178
  45.8 3.9 %collective-permute-start.10 = (bf16[6,8,16,512]{3,2,1,0:T(8,128)(2,1)S(1)}, bf16[6,8,16,512]{3,2,1,0:T(8,128)(2,1)S(1)}, u32[]{:S(2)}, u32[]{:S(2)}) collective-permute-start(bf16[6,8,16,512]{3,2,1,0:T(8,128)(2,1)S(1)} %bitcast.66), channel_id=1, source_target_pairs={{0,8},{8,0},{16,24},{24,16},{32,40},{40,32},{48,56},{56,48},{64,72... | collective-permute-start | bytes 2359304 | tf_op jit(solution)/shard_map/ppermute | solution.py:182

commit v15 on v12

--- a/solution.py
+++ b/solution.py
@@ -92,7 +92,7 @@
         even = pair_ref[pl.ds(0, rows, stride=2), :]
         odd = pair_ref[pl.ds(1, rows, stride=2), :]
         both = jnp.where(lane < bins, even, odd) / RATE
-        out_ref[:, d] = both.reshape(beams, chans // 2, 2 * bins).astype(out_ref.dtype)
+        out_ref[:, :, d] = both.reshape(beams, chans // 2, 2 * bins).astype(out_ref.dtype)
 
 
 def detect(tables, swap, mine, theirs_early, theirs_late, responses, chirp_len, backward):
@@ -116,7 +116,7 @@
             )
     return pl.pallas_call(
         detect_kernel,
-        out_shape=jax.ShapeDtypeStruct((beams, trials, chans // 2, 2 * bins), jnp.bfloat16),
+        out_shape=jax.ShapeDtypeStruct((beams, chans // 2, trials, 2 * bins), jnp.bfloat16),
         grid_spec=pltpu.PrefetchScalarGridSpec(
             num_scalar_prefetch=6,
             grid=(chans // step,),
@@ -125,7 +125,7 @@
                 pl.BlockSpec((width, width), lambda n, cl, tb, te, tl, fl, sw: (0, 0)),
             ],
             out_specs=pl.BlockSpec(
-                (beams, trials, step // 2, 2 * bins), lambda n, cl, tb, te, tl, fl, sw: (0, 0, n, 0)
+                (beams, step // 2, trials, 2 * bins), lambda n, cl, tb, te, tl, fl, sw: (0, n, 0, 0)
             ),
             scratch_shapes=[pltpu.VMEM((beams * step, 2 * bins), jnp.float32)],
         ),
@@ -209,8 +209,8 @@
         is_late.astype(jnp.int32),
     )
     detected = detect(tables, swap, mine, theirs_early, theirs_late, resp, chirp_len, backward)
-    moved = lax.all_to_all(detected.transpose(1, 0, 2, 3), "beam", split_axis=1, concat_axis=2, tiled=True)
-    return moved.reshape(trials, 1, -1)
+    moved = lax.all_to_all(detected, "beam", split_axis=0, concat_axis=1, tiled=True)
+    return moved[0].transpose(1, 0, 2).reshape(trials, 1, -1)
 
 
 def solution(mesh):

time: 99.5 us -> 103 us (1.035)
  Pallas kernels: 13.6 us -> 18.4 us
    pallas_call x1, Pallas kernels: 13.6 us -> 18.4 us  [detect(): pl.pallas_call(detect_kernel, out_shape=jax.ShapeDtypeStruct((beams, chan...]
    reshape x1 -> x0, local copies, waits for them, and re-layouts: 2.09 us -> none  [shards(): return moved.reshape(trials, 1, -1)]
    unnamed x12 -> x13, local copies, waits for them, and re-layouts: 3.21 us -> 4.53 us
where the time goes in v15:
time: 103 us; the launch traced here: 102 us
  blocking collectives  34 us (33%)
  starting transfers between devices  24.4 us (24%)
  Pallas kernels  18.4 us (18%)
  waiting for transfers between devices  13.2 us (13%)
  local copies, waits for them, and re-layouts  9.73 us (9%)
  matrix products  1.27 us (1%)
    all_to_all x1, blocking collectives, shards(): lax.all_to_all(detected, 'beam', split_axis=0, concat_axis=1, tiled=True)  34 us
    pallas_call x1, Pallas kernels, detect(): pl.pallas_call(detect_kernel, out_shape=jax.ShapeDtypeStruct((beams, chan...  18.4 us
    ppermute x3, starting transfers between devices, gather_spectra(): from_above.append(lax.ppermute(from_above[-1], 'dm', down))  9.37 us
    ppermute x3, waiting for transfers between devices, gather_spectra(): from_below.append(lax.ppermute(from_below[-1], 'dm', up))  6.48 us
    ppermute x1, starting transfers between devices, gather_spectra(): theirs_early = lax.ppermute(early, 'dm', partner)  5.57 us
    unnamed x13, local copies, waits for them, and re-layouts  4.53 us
    reshape x1, local copies, waits for them, and re-layouts, shards(): resp = responses.reshape(trials, chans, 2 * length)  4.4 us
    ppermute x1, starting transfers between devices, gather_spectra(): lax.ppermute(from_above[-1][1], 'dm', down)  3.19 us
  transfers between devices with their start and end apart: 11, of which 8 were waited for; matrix products, arithmetic and copies ran while one was open for 7% of the time, Pallas kernels for 0%

profile of v15, /device:TPU:1, one launch (start us, length us, event | category | flops | bytes accessed | tf_op | source)
XLA Modules:
  0.0 102.1 jit_solution(11147069512398763520)
XLA Ops:
  0.0 0.9 copy.8
  0.9 1.3 %fusion = bf16[16,8,512]{2,1,0:T(8,128)(2,1)S(1)} fusion(bf16[128,512]{1,0:T(8,128)(2,1)S(1)} %bitcast.61, bf16[512,512]{1,0:T(8,128)(2,1)} %constant.101.clone), kind=kOutput, calls=%fused_computation.1 | convolution fusion | flops 67174400 | bytes 786432 | tf_op jit(solution)/shard_map/dot_general | solution.py:191
  2.3 2.1 %collective-permute-start = (bf16[8,16,512]{2,1,0:T(8,128)(2,1)S(1)}, bf16[8,16,512]{2,1,0:T(8,128)(2,1)S(1)}, u32[]{:S(2)}, u32[]{:S(2)}) collective-permute-start(bf16[8,16,512]{2,1,0:T(8,128)(2,1)S(1)} %bitcast.57), channel_id=1, source_target_pairs={{0,128},{8,136},{16,144},{24,152},{32,160},{40,168},{48,176},{56,1... | collective-permute-start | bytes 393224 | tf_op jit(solution)/shard_map/ppermute | solution.py:162
  4.4 2.4 %collective-permute-done = bf16[8,16,512]{2,1,0:T(8,128)(2,1)S(1)} collective-permute-done((bf16[8,16,512]{2,1,0:T(8,128)(2,1)S(1)}, bf16[8,16,512]{2,1,0:T(8,128)(2,1)S(1)}, u32[]{:S(2)}, u32[]{:S(2)}) %collective-permute-start) | collective-permute-done | bytes 131104 | tf_op jit(solution)/shard_map/ppermute | solution.py:162
  6.8 2.5 %collective-permute-start.1 = (bf16[2,8,16,512]{3,2,1,0:T(8,128)(2,1)S(1)}, bf16[2,8,16,512]{3,2,1,0:T(8,128)(2,1)S(1)}, u32[]{:S(2)}, u32[]{:S(2)}) collective-permute-start(bf16[2,8,16,512]{3,2,1,0:T(8,128)(2,1)S(1)} %pad_maximum_fusion.1), channel_id=1, source_target_pairs={{0,16},{8,24},{16,32},{24,40},{32,48},{40,56},{48,64},{56,72},{64,... | collective-permute-start | bytes 786440 | tf_op jit(solution)/shard_map/ppermute | solution.py:166
  9.3 4.0 %collective-permute-start.2 = (bf16[2,8,16,512]{3,2,1,0:T(8,128)(2,1)S(1)}, bf16[2,8,16,512]{3,2,1,0:T(8,128)(2,1)S(1)}, u32[]{:S(2)}, u32[]{:S(2)}) collective-permute-start(bf16[2,8,16,512]{3,2,1,0:T(8,128)(2,1)S(1)} %pad_maximum_fusion.1), channel_id=1, source_target_pairs={{0,112},{8,120},{16,0},{24,8},{32,16},{40,24},{48,32},{56,40},{64,... | collective-permute-start | bytes 786440 | tf_op jit(solution)/shard_map/ppermute | solution.py:167
  13.3 4.4 %reshape.29.refs_12_ = bf16[4,512,512]{2,1,0:T(8,128)(2,1)} reshape(bf16[4,512,2,256]{3,2,1,0:T(2,128)(2,1)} %param.6) | data formatting | bytes 4194304 | tf_op jit(solution)/shard_map/reshape | solution.py:195
  18.4 2.7 %collective-permute-start.3 = (bf16[2,8,16,512]{3,2,1,0:T(8,128)(2,1)S(1)}, bf16[2,8,16,512]{3,2,1,0:T(8,128)(2,1)S(1)}, u32[]{:S(2)}, u32[]{:S(2)}) collective-permute-start(bf16[2,8,16,512]{3,2,1,0:T(8,128)(2,1)S(1)} %collective-permute-done.2), channel_id=1, source_target_pairs={{0,112},{8,120},{16,0},{24,8},{32,16},{40,24},{48,32},{56,40},{64,... | collective-permute-start | bytes 786440 | tf_op jit(solution)/shard_map/ppermute | solution.py:167
  21.0 0.7 bitcast_dynamic-update-slice_fusion.8
  21.8 3.6 %collective-permute-done.5 = bf16[2,8,16,512]{3,2,1,0:T(8,128)(2,1)S(1)} collective-permute-done((bf16[2,8,16,512]{3,2,1,0:T(8,128)(2,1)S(1)}, bf16[2,8,16,512]{3,2,1,0:T(8,128)(2,1)S(1)}, u32[]{:S(2)}, u32[]{:S(2)}) %collective-permute-start.5) | collective-permute-done | bytes 262176 | tf_op jit(solution)/shard_map/ppermute | solution.py:166
  25.3 0.7 bitcast_dynamic-update-slice_fusion.6
  26.1 2.7 %collective-permute-start.4 = (bf16[2,8,16,512]{3,2,1,0:T(8,128)(2,1)S(1)}, bf16[2,8,16,512]{3,2,1,0:T(8,128)(2,1)S(1)}, u32[]{:S(2)}, u32[]{:S(2)}) collective-permute-start(bf16[2,8,16,512]{3,2,1,0:T(8,128)(2,1)S(1)} %collective-permute-done.3), channel_id=1, source_target_pairs={{0,112},{8,120},{16,0},{24,8},{32,16},{40,24},{48,32},{56,40},{64,... | collective-permute-start | bytes 786440 | tf_op jit(solution)/shard_map/ppermute | solution.py:167
  28.8 0.8 bitcast_dynamic-update-slice_fusion.4
  29.5 2.3 %collective-permute-done.6 = bf16[2,8,16,512]{3,2,1,0:T(8,128)(2,1)S(1)} collective-permute-done((bf16[2,8,16,512]{3,2,1,0:T(8,128)(2,1)S(1)}, bf16[2,8,16,512]{3,2,1,0:T(8,128)(2,1)S(1)}, u32[]{:S(2)}, u32[]{:S(2)}) %collective-permute-start.6) | collective-permute-done | bytes 262176 | tf_op jit(solution)/shard_map/ppermute | solution.py:166
  32.1 3.2 %collective-permute-start.8 = (bf16[8,16,512]{2,1,0:T(8,128)(2,1)S(1)}, bf16[8,16,512]{2,1,0:T(8,128)(2,1)S(1)}, u32[]{:S(2)}, u32[]{:S(2)}) collective-permute-start(bf16[8,16,512]{2,1,0:T(8,128)(2,1)S(1)} %slice_bitcast_fusion), channel_id=1, source_target_pairs={{0,112},{8,120},{16,0},{24,8},{32,16},{40,24},{48,32},{56,40},{64,... | collective-permute-start | bytes 393224 | tf_op jit(solution)/shard_map/ppermute | solution.py:173
  35.3 1.6 %collective-permute-done.7 = bf16[8,16,512]{2,1,0:T(8,128)(2,1)S(1)} collective-permute-done((bf16[8,16,512]{2,1,0:T(8,128)(2,1)S(1)}, bf16[8,16,512]{2,1,0:T(8,128)(2,1)S(1)}, u32[]{:S(2)}, u32[]{:S(2)}) %collective-permute-start.7) | collective-permute-done | bytes 131104 | tf_op jit(solution)/shard_map/ppermute | solution.py:173
  37.3 0.7 bitcast_dynamic-update-slice_fusion.2
  38.0 0.7 bitcast_dynamic-update-slice_fusion
  38.8 5.6 %collective-permute-start.9 = (bf16[10,8,16,512]{3,2,1,0:T(8,128)(2,1)}, bf16[10,8,16,512]{3,2,1,0:T(8,128)(2,1)S(1)}, u32[]{:S(2)}, u32[]{:S(2)}) collective-permute-start(bf16[10,8,16,512]{3,2,1,0:T(8,128)(2,1)} %bitcast.19), channel_id=1, source_target_pairs={{0,8},{8,0},{16,24},{24,16},{32,40},{40,32},{48,56},{56,48},{64,72... | collective-permute-start | bytes 3932168 | tf_op jit(solution)/shard_map/ppermute | solution.py:178
  44.5 1.5 %collective-permute-start.10 = (bf16[6,8,16,512]{3,2,1,0:T(8,128)(2,1)S(1)}, bf16[6,8,16,512]{3,2,1,0:T(8,128)(2,1)S(1)}, u32[]{:S(2)}, u32[]{:S(2)}) collective-permute-start(bf16[6,8,16,512]{3,2,1,0:T(8,128)(2,1)S(1)} %bitcast.60), channel_id=1, source_target_pairs={{0,8},{8,0},{16,24},{24,16},{32,40},{40,32},{48,56},{56,48},{64,72... | collective-permute-start | bytes 2359304 | tf_op jit(solution)/shard_map/ppermute | solution.py:182
  46.1 2.3 %collective-permute-done.10.refs_2_.refs_5_.refs_8_.refs_11_ = bf16[6,8,16,512]{3,2,1,0:T(8,128)(2,1)S(1)} collective-permute-done((bf16[6,8,16,512]{3,2,1,0:T(8,128)(2,1)S(1)}, bf16[6,8,16,512]{3,2,1,0:T(8,128)(2,1)S(1)}, u32[]{:S(2)}, u32[]{:S(2)}) %collective-permute-start.10) | collective-permute-done | bytes 786464 | tf_op jit(solution)/shard_map/ppermute | solution.py:182
  48.4 18.4 %shard_map.55 = bf16[8,256,4,128]{3,2,1,0:T(4,128)(2,1)S(1)} custom-call(s32[4]{0:T(128)S(1)} %copy-done, s32[16]{0:T(128)S(1)} %get-tuple-element.14.table_ref, s32[16]{0:T(128)S(1)} %get-tuple-element.28.early_ref, s32[16]{0:T(128)S(1)} %get-tuple-element.27.late_ref, s32[16]{0:T(128)S(1)} %get-tuple-element.11.flag_ref, s32[1]{0:T(128)} %bitcast.swap_ref, ...), custom_call_target="tpu_custom_call" | custom-call | flops 8589934592 | bytes 8912896 | tf_op jit(solution)/shard_map/pallas_call | solution.py:117
  66.8 34.0 %all_to_all.4 = bf16[8,256,4,128]{3,2,1,0:T(4,128)(2,1)S(1)} all-to-all(bf16[8,256,4,128]{3,2,1,0:T(4,128)(2,1)S(1)} %shard_map.55), channel_id=1, replica_groups=mesh['dm'=32,'beam'=8] {'beam'}, dimensions={0} | all-to-all | bytes 4194304 | tf_op jit(solution)/shard_map/all_to_all | solution.py:212
  100.8 1.3 %copy.24 = bf16[4,1,262144]{2,0,1:T(4,128)(2,1)} copy(bf16[4,1,262144]{2,0,1:T(4,128)(2,1)S(1)} %bitcast.54) | data formatting | bytes 4194304
  (26 shorter events, 1.6 us)
Async XLA Ops:
  2.3 4.5 %collective-permute-start = (bf16[8,16,512]{2,1,0:T(8,128)(2,1)S(1)}, bf16[8,16,512]{2,1,0:T(8,128)(2,1)S(1)}, u32[]{:S(2)}, u32[]{:S(2)}) collective-permute-start(bf16[8,16,512]{2,1,0:T(8,128)(2,1)S(1)} %bitcast.57), channel_id=1, source_target_pairs={{0,128},{8,136},{16,144},{24,152},{32,160},{40,168},{48,176},{56,1... | collective-permute-start | bytes 393224 | tf_op jit(solution)/shard_map/ppermute | solution.py:162
  6.8 11.6 %collective-permute-start.1 = (bf16[2,8,16,512]{3,2,1,0:T(8,128)(2,1)S(1)}, bf16[2,8,16,512]{3,2,1,0:T(8,128)(2,1)S(1)}, u32[]{:S(2)}, u32[]{:S(2)}) collective-permute-start(bf16[2,8,16,512]{3,2,1,0:T(8,128)(2,1)S(1)} %pad_maximum_fusion.1), channel_id=1, source_target_pairs={{0,16},{8,24},{16,32},{24,40},{32,48},{40,56},{48,64},{56,72},{64,... | collective-permute-start | bytes 786440 | tf_op jit(solution)/shard_map/ppermute | solution.py:166
  9.3 9.1 %collective-permute-start.2 = (bf16[2,8,16,512]{3,2,1,0:T(8,128)(2,1)S(1)}, bf16[2,8,16,512]{3,2,1,0:T(8,128)(2,1)S(1)}, u32[]{:S(2)}, u32[]{:S(2)}) collective-permute-start(bf16[2,8,16,512]{3,2,1,0:T(8,128)(2,1)S(1)} %pad_maximum_fusion.1), channel_id=1, source_target_pairs={{0,112},{8,120},{16,0},{24,8},{32,16},{40,24},{48,32},{56,40},{64,... | collective-permute-start | bytes 786440 | tf_op jit(solution)/shard_map/ppermute | solution.py:167
  18.4 7.0 %collective-permute-start.5 = (bf16[2,8,16,512]{3,2,1,0:T(8,128)(2,1)S(1)}, bf16[2,8,16,512]{3,2,1,0:T(8,128)(2,1)S(1)}, u32[]{:S(2)}, u32[]{:S(2)}) collective-permute-start(bf16[2,8,16,512]{3,2,1,0:T(8,128)(2,1)S(1)} %collective-permute-done.1), channel_id=1, source_target_pairs={{0,16},{8,24},{16,32},{24,40},{32,48},{40,56},{48,64},{56,72},{64,... | collective-permute-start | bytes 786440 | tf_op jit(solution)/shard_map/ppermute | solution.py:166
  18.4 7.7 %collective-permute-start.3 = (bf16[2,8,16,512]{3,2,1,0:T(8,128)(2,1)S(1)}, bf16[2,8,16,512]{3,2,1,0:T(8,128)(2,1)S(1)}, u32[]{:S(2)}, u32[]{:S(2)}) collective-permute-start(bf16[2,8,16,512]{3,2,1,0:T(8,128)(2,1)S(1)} %collective-permute-done.2), channel_id=1, source_target_pairs={{0,112},{8,120},{16,0},{24,8},{32,16},{40,24},{48,32},{56,40},{64,... | collective-permute-start | bytes 786440 | tf_op jit(solution)/shard_map/ppermute | solution.py:167
  25.3 6.4 %collective-permute-start.6 = (bf16[2,8,16,512]{3,2,1,0:T(8,128)(2,1)S(1)}, bf16[2,8,16,512]{3,2,1,0:T(8,128)(2,1)S(1)}, u32[]{:S(2)}, u32[]{:S(2)}) collective-permute-start(bf16[2,8,16,512]{3,2,1,0:T(8,128)(2,1)S(1)} %collective-permute-done.5), channel_id=1, source_target_pairs={{0,16},{8,24},{16,32},{24,40},{32,48},{40,56},{48,64},{56,72},{64,... | collective-permute-start | bytes 786440 | tf_op jit(solution)/shard_map/ppermute | solution.py:166
  26.1 6.0 %collective-permute-start.4 = (bf16[2,8,16,512]{3,2,1,0:T(8,128)(2,1)S(1)}, bf16[2,8,16,512]{3,2,1,0:T(8,128)(2,1)S(1)}, u32[]{:S(2)}, u32[]{:S(2)}) collective-permute-start(bf16[2,8,16,512]{3,2,1,0:T(8,128)(2,1)S(1)} %collective-permute-done.3), channel_id=1, source_target_pairs={{0,112},{8,120},{16,0},{24,8},{32,16},{40,24},{48,32},{56,40},{64,... | collective-permute-start | bytes 786440 | tf_op jit(solution)/shard_map/ppermute | solution.py:167
  31.8 5.1 %collective-permute-start.7 = (bf16[8,16,512]{2,1,0:T(8,128)(2,1)S(1)}, bf16[8,16,512]{2,1,0:T(8,128)(2,1)S(1)}, u32[]{:S(2)}, u32[]{:S(2)}) collective-permute-start(bf16[8,16,512]{2,1,0:T(8,128)(2,1)S(1)} %slice_bitcast_fusion.1), channel_id=1, source_target_pairs={{0,16},{8,24},{16,32},{24,40},{32,48},{40,56},{48,64},{56,72},{64,... | collective-permute-start | bytes 393224 | tf_op jit(solution)/shard_map/ppermute | solution.py:173
  32.1 5.1 %collective-permute-start.8 = (bf16[8,16,512]{2,1,0:T(8,128)(2,1)S(1)}, bf16[8,16,512]{2,1,0:T(8,128)(2,1)S(1)}, u32[]{:S(2)}, u32[]{:S(2)}) collective-permute-start(bf16[8,16,512]{2,1,0:T(8,128)(2,1)S(1)} %slice_bitcast_fusion), channel_id=1, source_target_pairs={{0,112},{8,120},{16,0},{24,8},{32,16},{40,24},{48,32},{56,40},{64,... | collective-permute-start | bytes 393224 | tf_op jit(solution)/shard_map/ppermute | solution.py:173
  37.2 11.1 %copy-start = (s32[4]{0:T(128)S(1)}, s32[4]{0:T(128)}, u32[]{:S(2)}) copy-start(s32[4]{0:T(128)} %chirp_ref.1) | copy-start | bytes 52
  37.3 11.1 %copy-start.1 = (bf16[512,512]{1,0:T(8,128)(2,1)S(1)}, bf16[512,512]{1,0:T(8,128)(2,1)}, u32[]{:S(2)}) copy-start(bf16[512,512]{1,0:T(8,128)(2,1)} %constant.102.clone.refs_13_) | copy-start | bytes 1572868
  38.8 5.6 %copy-start.2 = (bf16[8,2,8,16,512]{4,3,2,1,0:T(8,128)(2,1)}, bf16[8,2,8,16,512]{4,3,2,1,0:T(8,128)(2,1)S(1)}, u32[]{:S(2)}) copy-start(bf16[8,2,8,16,512]{4,3,2,1,0:T(8,128)(2,1)S(1)} %get-tuple-element.16) | copy-start | bytes 6291460
  38.8 9.6 %collective-permute-start.9 = (bf16[10,8,16,512]{3,2,1,0:T(8,128)(2,1)}, bf16[10,8,16,512]{3,2,1,0:T(8,128)(2,1)S(1)}, u32[]{:S(2)}, u32[]{:S(2)}) collective-permute-start(bf16[10,8,16,512]{3,2,1,0:T(8,128)(2,1)} %bitcast.19), channel_id=1, source_target_pairs={{0,8},{8,0},{16,24},{24,16},{32,40},{40,32},{48,56},{56,48},{64,72... | collective-permute-start | bytes 3932168 | tf_op jit(solution)/shard_map/ppermute | solution.py:178
  44.5 3.9 %collective-permute-start.10 = (bf16[6,8,16,512]{3,2,1,0:T(8,128)(2,1)S(1)}, bf16[6,8,16,512]{3,2,1,0:T(8,128)(2,1)S(1)}, u32[]{:S(2)}, u32[]{:S(2)}) collective-permute-start(bf16[6,8,16,512]{3,2,1,0:T(8,128)(2,1)S(1)} %bitcast.60), channel_id=1, source_target_pairs={{0,8},{8,0},{16,24},{24,16},{32,40},{40,32},{48,56},{56,48},{64,72... | collective-permute-start | bytes 2359304 | tf_op jit(solution)/shard_map/ppermute | solution.py:182

commit v16 on v12

--- a/solution.py
+++ b/solution.py
@@ -136,6 +136,83 @@
     )(chirp_len, *tables, swap, *([mine, theirs_early, theirs_late] * GROUP), responses, backward)
 
 
+def split_kernel(chirp_ref, index_ref, block_ref, swap_ref, mine_ref, theirs_ref, resp_ref, back_ref, *rest):
+    out_ref, pair_ref = rest[-2], rest[-1]
+    _, beams, chans_local, width = mine_ref.shape
+    trials = resp_ref.shape[0]
+    length = width // 2
+    bins = length // RATE
+    chans = 2 * chans_local
+    keep = swap_ref[0] == 0
+    mine = mine_ref[0]
+    theirs = theirs_ref[0]
+    x = jnp.concatenate([jnp.where(keep, mine, theirs), jnp.where(keep, theirs, mine)], axis=1)
+    xr = x[:, :, :length].astype(jnp.float32)
+    xi = x[:, :, length:].astype(jnp.float32)
+    back = back_ref[...]
+    pos = lax.broadcasted_iota(jnp.int32, (1, length), 1)
+    t = RATE * (pos % bins) + pos // bins
+    lane = lax.broadcasted_iota(jnp.int32, (1, 2 * bins), 1)
+    rows = beams * chans // 2
+    for d in range(trials):
+        h = resp_ref[d]
+        hr = h[:, :length].astype(jnp.float32)[None]
+        hi = h[:, length:].astype(jnp.float32)[None]
+        fr = hr * xr - hi * xi
+        fi = hr * xi + hi * xr
+        joined = jnp.concatenate([fr, fi], -1).reshape(beams * chans, width).astype(jnp.bfloat16)
+        series = jnp.dot(joined, back, preferred_element_type=jnp.float32)
+        powers = series[:, :length] ** 2 + series[:, length:] ** 2
+        powers = jnp.where(t >= chirp_ref[d], powers, jnp.float32(0.0))
+        half = powers[:, : length // 2] + powers[:, length // 2 :]
+        pair_ref[...] = half + pltpu.roll(half, bins, 1)
+        even = pair_ref[pl.ds(0, rows, stride=2), :]
+        odd = pair_ref[pl.ds(1, rows, stride=2), :]
+        both = jnp.where(lane < bins, even, odd) / RATE
+        out_ref[:, d] = both.reshape(beams, chans // 2, 2 * bins).astype(out_ref.dtype)
+
+
+def detect_part(index, block, swap, mine, theirs, responses, chirp_len, backward, previous):
+    _, beams, chans_local, width = mine.shape
+    trials, chans = responses.shape[0], responses.shape[1]
+    bins = width // 2 // RATE
+    step = 2 * chans_local
+    count = index.shape[0]
+    flops = 2 * trials * beams * count * step * width * width
+    bytes_accessed = 2 * count * (2 * beams * chans_local * width + trials * step * width + trials * beams * step * bins)
+    spec = pl.BlockSpec((1, beams, chans_local, width), lambda n, cl, ix, bk, sw: (ix[n], 0, 0, 0))
+    in_specs = [
+        spec,
+        spec,
+        pl.BlockSpec((trials, step, width), lambda n, cl, ix, bk, sw: (0, bk[n], 0)),
+        pl.BlockSpec((width, width), lambda n, cl, ix, bk, sw: (0, 0)),
+    ]
+    args = [chirp_len, index, block, swap, mine, theirs, responses, backward]
+    aliases = {}
+    if previous is not None:
+        in_specs.append(pl.BlockSpec(memory_space=pl.ANY))
+        args.append(previous)
+        aliases = {len(args) - 1: 0}
+    return pl.pallas_call(
+        split_kernel,
+        out_shape=jax.ShapeDtypeStruct((beams, trials, chans // 2, 2 * bins), jnp.bfloat16),
+        grid_spec=pltpu.PrefetchScalarGridSpec(
+            num_scalar_prefetch=4,
+            grid=(count,),
+            in_specs=in_specs,
+            out_specs=pl.BlockSpec(
+                (beams, trials, step // 2, 2 * bins), lambda n, cl, ix, bk, sw: (0, 0, bk[n], 0)
+            ),
+            scratch_shapes=[pltpu.VMEM((beams * step, 2 * bins), jnp.float32)],
+        ),
+        input_output_aliases=aliases,
+        compiler_params=pltpu.CompilerParams(
+            dimension_semantics=("arbitrary",), vmem_limit_bytes=48 * 1024 * 1024
+        ),
+        cost_estimate=pl.CostEstimate(flops=flops, transcendentals=0, bytes_accessed=bytes_accessed),
+    )(*args)
+
+
 def coords(index, z_count):
     return index // (2 * z_count), (index // 2) % z_count, index % 2
 
@@ -179,7 +256,7 @@
     column = jnp.stack(from_above + [far] + from_below[:0:-1])
     column = column.reshape((2 * z_count,) + own.shape)
     late = column[2 * near : 2 * (z_count - near + 1)]
-    return column, theirs_early, lax.ppermute(late, "dm", partner), carried
+    return early, late, theirs_early, lax.ppermute(late, "dm", partner), carried
 
 
 def shards(voltages, responses, chirp_len):
@@ -193,22 +270,23 @@
     ).astype(jnp.bfloat16)
     local = local.reshape(chans_local, beams, 2 * length).transpose(1, 0, 2)
     resp = responses.reshape(trials, chans, 2 * length)
-    mine, theirs_early, theirs_late, resp = gather_spectra(local, count, resp)
+    mine_early, mine_late, theirs_early, theirs_late, resp = gather_spectra(local, count, resp)
     x_me, z_me, c_me = coords(lax.axis_index("dm"), z_count)
-    block = jnp.arange(count // 2, dtype=jnp.int32)
-    table = ((block % z_count - z_me) % z_count) * 2 + ((block // z_count) ^ x_me)
     swap = jnp.reshape(c_me, (1,)).astype(jnp.int32)
     near = z_count // 4 + 1
-    z_rel, x_rel = table // 2, table % 2
-    is_late = (z_rel >= near) & (z_rel <= z_count - near)
-    early_index = jnp.where(z_rel < near, z_rel, z_rel - (z_count - 2 * near + 1))
-    tables = (
-        table,
-        jnp.where(is_late, 0, early_index * 2 + x_rel),
-        jnp.where(is_late, (z_rel - near) * 2 + x_rel, 0),
-        is_late.astype(jnp.int32),
-    )
-    detected = detect(tables, swap, mine, theirs_early, theirs_late, resp, chirp_len, backward)
+    x_rel = jnp.arange(2, dtype=jnp.int32)[None, :]
+    early_z = jnp.array(list(range(near)) + [z_count - k for k in range(near - 1, 0, -1)], jnp.int32)
+    late_z = jnp.arange(near, z_count - near + 1, dtype=jnp.int32)
+    early_block = (((x_rel ^ x_me) * z_count) + (z_me + early_z[:, None]) % z_count).reshape(-1)
+    late_block = (((x_rel ^ x_me) * z_count) + (z_me + late_z[:, None]) % z_count).reshape(-1)
+    first = detect_part(
+        jnp.arange(early_block.shape[0], dtype=jnp.int32), early_block, swap,
+        mine_early, theirs_early, resp, chirp_len, backward, None,
+    )
+    detected = detect_part(
+        jnp.arange(late_block.shape[0], dtype=jnp.int32), late_block, swap,
+        mine_late, theirs_late, resp, chirp_len, backward, first,
+    )
     moved = lax.all_to_all(detected.transpose(1, 0, 2, 3), "beam", split_axis=1, concat_axis=2, tiled=True)
     return moved.reshape(trials, 1, -1)
 

time: 99.5 us -> 107 us (1.075)
  Pallas kernels: 13.6 us -> 17.6 us
  waiting for transfers between devices: 13.4 us -> 16.8 us
  other arithmetic: 0.92 us -> 2.26 us
    pallas_call x1 -> x2, Pallas kernels: 13.6 us -> 17.6 us  [detect_part(): pl.pallas_call(split_kernel, out_shape=jax.ShapeDtypeStruct((beams, trial...]
    ppermute x1, waiting for transfers between devices: 1.59 us -> 4.86 us  [gather_spectra(): lax.ppermute(from_below[-1][0], 'dm', up)]
    ppermute x3, waiting for transfers between devices: 0.2 us -> 3.25 us  [gather_spectra(): from_above.append(lax.ppermute(from_above[-1], 'dm', down))]
    ppermute x1, waiting for transfers between devices: 2.47 us -> 0.01 us  [gather_spectra(): lax.ppermute(late, 'dm', partner)]
    another operation x2, other arithmetic: 0.11 us -> 2.05 us  [gather_spectra(): column = jnp.stack(from_above + [far] + from_below[:0:-1])]
    ppermute x1, starting transfers between devices: 5.55 us -> 3.9 us  [gather_spectra(): theirs_early = lax.ppermute(early, 'dm', partner)]
    unnamed x12 -> x14, local copies, waits for them, and re-layouts: 3.21 us -> 3.01 us
  transfers between devices with their start and end apart: 11 -> 11, of which waited for: 8 -> 5; matrix products, arithmetic and copies ran while one was open for 7% -> 8% of each run, Pallas kernels for 0% -> 10%
where the time goes in v16:
time: 107 us
  blocking collectives  34.7 us (32%)
  starting transfers between devices  23.2 us (22%)
  Pallas kernels  17.6 us (16%)
  waiting for transfers between devices  16.8 us (16%)
  local copies, waits for them, and re-layouts  10.5 us (10%)
  other arithmetic  2.26 us (2%)
  matrix products  1.27 us (1%)
    all_to_all x1, blocking collectives, shards(): lax.all_to_all(detected.transpose(1, 0, 2, 3), 'beam', split_axis=1, conc...  34.7 us
    pallas_call x2, Pallas kernels, detect_part(): pl.pallas_call(split_kernel, out_shape=jax.ShapeDtypeStruct((beams, trial...  17.6 us
    ppermute x3, starting transfers between devices, gather_spectra(): from_above.append(lax.ppermute(from_above[-1], 'dm', down))  9.66 us
    ppermute x3, waiting for transfers between devices, gather_spectra(): from_below.append(lax.ppermute(from_below[-1], 'dm', up))  6.29 us
    ppermute x1, waiting for transfers between devices, gather_spectra(): lax.ppermute(from_below[-1][0], 'dm', up)  4.86 us
    reshape x1, local copies, waits for them, and re-layouts, shards(): resp = responses.reshape(trials, chans, 2 * length)  4.38 us
    ppermute x1, starting transfers between devices, gather_spectra(): theirs_early = lax.ppermute(early, 'dm', partner)  3.9 us
    ppermute x3, waiting for transfers between devices, gather_spectra(): from_above.append(lax.ppermute(from_above[-1], 'dm', down))  3.25 us
  transfers between devices with their start and end apart: 11, of which 5 were waited for; matrix products, arithmetic and copies ran while one was open for 8% of the time, Pallas kernels for 10%

profile of v16, /device:TPU:1, one launch (start us, length us, event | category | flops | bytes accessed | tf_op | source)
XLA Modules:
  0.0 106.6 jit_solution(7283590225757834727)
XLA Ops:
  0.0 0.9 copy.11
  0.9 1.3 %fusion = bf16[16,8,512]{2,1,0:T(8,128)(2,1)S(1)} fusion(bf16[128,512]{1,0:T(8,128)(2,1)S(1)} %bitcast.52, bf16[512,512]{1,0:T(8,128)(2,1)} %constant.76.clone), kind=kOutput, calls=%fused_computation.1 | convolution fusion | flops 67174400 | bytes 786432 | tf_op jit(solution)/shard_map/dot_general | solution.py:268
  2.3 2.1 %collective-permute-start = (bf16[8,16,512]{2,1,0:T(8,128)(2,1)S(1)}, bf16[8,16,512]{2,1,0:T(8,128)(2,1)S(1)}, u32[]{:S(2)}, u32[]{:S(2)}) collective-permute-start(bf16[8,16,512]{2,1,0:T(8,128)(2,1)S(1)} %bitcast.47), channel_id=1, source_target_pairs={{0,128},{8,136},{16,144},{24,152},{32,160},{40,168},{48,176},{56,1... | collective-permute-start | bytes 393224 | tf_op jit(solution)/shard_map/ppermute | solution.py:239
  4.4 2.4 %collective-permute-done = bf16[8,16,512]{2,1,0:T(8,128)(2,1)S(1)} collective-permute-done((bf16[8,16,512]{2,1,0:T(8,128)(2,1)S(1)}, bf16[8,16,512]{2,1,0:T(8,128)(2,1)S(1)}, u32[]{:S(2)}, u32[]{:S(2)}) %collective-permute-start) | collective-permute-done | bytes 131104 | tf_op jit(solution)/shard_map/ppermute | solution.py:239
  6.8 2.5 %collective-permute-start.1 = (bf16[2,8,16,512]{3,2,1,0:T(8,128)(2,1)S(1)}, bf16[2,8,16,512]{3,2,1,0:T(8,128)(2,1)S(1)}, u32[]{:S(2)}, u32[]{:S(2)}) collective-permute-start(bf16[2,8,16,512]{3,2,1,0:T(8,128)(2,1)S(1)} %pad_maximum_fusion.1), channel_id=1, source_target_pairs={{0,16},{8,24},{16,32},{24,40},{32,48},{40,56},{48,64},{56,72},{64,... | collective-permute-start | bytes 786440 | tf_op jit(solution)/shard_map/ppermute | solution.py:243
  9.3 4.0 %collective-permute-start.2 = (bf16[2,8,16,512]{3,2,1,0:T(8,128)(2,1)S(1)}, bf16[2,8,16,512]{3,2,1,0:T(8,128)(2,1)S(1)}, u32[]{:S(2)}, u32[]{:S(2)}) collective-permute-start(bf16[2,8,16,512]{3,2,1,0:T(8,128)(2,1)S(1)} %pad_maximum_fusion.1), channel_id=1, source_target_pairs={{0,112},{8,120},{16,0},{24,8},{32,16},{40,24},{48,32},{56,40},{64,... | collective-permute-start | bytes 786440 | tf_op jit(solution)/shard_map/ppermute | solution.py:244
  13.3 4.4 %reshape.73.resp_ref = bf16[4,512,512]{2,1,0:T(8,128)(2,1)} reshape(bf16[4,512,2,256]{3,2,1,0:T(2,128)(2,1)} %param.7) | data formatting | bytes 4194304 | tf_op jit(solution)/shard_map/reshape | solution.py:272
  17.7 0.7 collective-permute-done.1
  18.4 2.5 %collective-permute-start.3 = (bf16[2,8,16,512]{3,2,1,0:T(8,128)(2,1)S(1)}, bf16[2,8,16,512]{3,2,1,0:T(8,128)(2,1)}, u32[]{:S(2)}, u32[]{:S(2)}) collective-permute-start(bf16[2,8,16,512]{3,2,1,0:T(8,128)(2,1)S(1)} %collective-permute-done.2), channel_id=1, source_target_pairs={{0,112},{8,120},{16,0},{24,8},{32,16},{40,24},{48,32},{56,40},{64,... | collective-permute-start | bytes 786440 | tf_op jit(solution)/shard_map/ppermute | solution.py:244
  21.0 3.2 %collective-permute-done.3 = bf16[2,8,16,512]{3,2,1,0:T(8,128)(2,1)} collective-permute-done((bf16[2,8,16,512]{3,2,1,0:T(8,128)(2,1)S(1)}, bf16[2,8,16,512]{3,2,1,0:T(8,128)(2,1)}, u32[]{:S(2)}, u32[]{:S(2)}) %collective-permute-start.3) | collective-permute-done | bytes 262176 | tf_op jit(solution)/shard_map/ppermute | solution.py:244
  24.2 3.2 %collective-permute-start.4 = (bf16[2,8,16,512]{3,2,1,0:T(8,128)(2,1)}, bf16[2,8,16,512]{3,2,1,0:T(8,128)(2,1)S(1)}, u32[]{:S(2)}, u32[]{:S(2)}) collective-permute-start(bf16[2,8,16,512]{3,2,1,0:T(8,128)(2,1)} %collective-permute-done.3), channel_id=1, source_target_pairs={{0,112},{8,120},{16,0},{24,8},{32,16},{40,24},{48,32},{56,40},{64,... | collective-permute-start | bytes 786440 | tf_op jit(solution)/shard_map/ppermute | solution.py:244
  27.4 1.0 bitcast_dynamic-update-slice_fusion.2
  28.5 3.9 %collective-permute-start.10 = (bf16[10,8,16,512]{3,2,1,0:T(8,128)(2,1)S(1)}, bf16[10,8,16,512]{3,2,1,0:T(8,128)(2,1)S(1)}, u32[]{:S(2)}, u32[]{:S(2)}) collective-permute-start(bf16[10,8,16,512]{3,2,1,0:T(8,128)(2,1)S(1)} %bitcast.45), channel_id=1, source_target_pairs={{0,8},{8,0},{16,24},{24,16},{32,40},{40,32},{48,56},{56,48},{64,72... | collective-permute-start | bytes 3932168 | tf_op jit(solution)/shard_map/ppermute | solution.py:255
  33.1 2.7 %collective-permute-start.8 = (bf16[8,16,512]{2,1,0:T(8,128)(2,1)}, bf16[8,16,512]{2,1,0:T(8,128)(2,1)}, u32[]{:S(2)}, u32[]{:S(2)}) collective-permute-start(bf16[8,16,512]{2,1,0:T(8,128)(2,1)} %slice_bitcast_fusion), channel_id=1, source_target_pairs={{0,112},{8,120},{16,0},{24,8},{32,16},{40,24},{48,32},{56,40},{64,... | collective-permute-start | bytes 393224 | tf_op jit(solution)/shard_map/ppermute | solution.py:250
  35.7 5.6 %collective-permute-done.6 = bf16[2,8,16,512]{3,2,1,0:T(8,128)(2,1)S(1)} collective-permute-done((bf16[2,8,16,512]{3,2,1,0:T(8,128)(2,1)S(1)}, bf16[2,8,16,512]{3,2,1,0:T(8,128)(2,1)S(1)}, u32[]{:S(2)}, u32[]{:S(2)}) %collective-permute-start.6) | collective-permute-done | bytes 262176 | tf_op jit(solution)/shard_map/ppermute | solution.py:243
  41.6 4.9 %collective-permute-done.7 = bf16[8,16,512]{2,1,0:T(8,128)(2,1)S(1)} collective-permute-done((bf16[8,16,512]{2,1,0:T(8,128)(2,1)S(1)}, bf16[8,16,512]{2,1,0:T(8,128)(2,1)S(1)}, u32[]{:S(2)}, u32[]{:S(2)}) %collective-permute-start.7) | collective-permute-done | bytes 131104 | tf_op jit(solution)/shard_map/ppermute | solution.py:250
  46.5 0.9 maximum_bitcast_fusion
  47.4 1.1 %pad_maximum_fusion = bf16[3,2,8,16,512]{4,3,2,1,0:T(8,128)(2,1)S(1)} fusion(bf16[1,2,8,16,512]{4,3,2,1,0:T(8,128)(2,1)} %bitcast.51, bf16[1,2,8,16,512]{4,3,2,1,0:T(8,128)(2,1)S(1)} %maximum_bitcast_fusion, bf16[1,2,8,16,512]{4,3,2,1,0:T(8,128)(2,1)} %bitcast.50), kind=kLoop, calls=%fused_computation.2 | loop fusion | flops 786432 | bytes 1572864 | tf_op jit(solution)/shard_map/stack | solution.py:256
  48.5 2.2 %collective-permute-start.9 = (bf16[6,8,16,512]{3,2,1,0:T(8,128)(2,1)S(1)}, bf16[6,8,16,512]{3,2,1,0:T(8,128)(2,1)}, u32[]{:S(2)}, u32[]{:S(2)}) collective-permute-start(bf16[6,8,16,512]{3,2,1,0:T(8,128)(2,1)S(1)} %bitcast.43), channel_id=1, source_target_pairs={{0,8},{8,0},{16,24},{24,16},{32,40},{40,32},{48,56},{56,48},{64,72... | collective-permute-start | bytes 2359304 | tf_op jit(solution)/shard_map/ppermute | solution.py:259
  50.9 1.0 copy-done.1
  52.0 10.5 %shard_map.64.rest_0_ = bf16[8,4,256,128]{3,2,1,0:T(8,128)(2,1)S(1)} custom-call(s32[4]{0:T(128)S(1)} %copy-done, s32[10]{0:T(128)S(1)} %iota.19.index_ref, s32[10]{0:T(128)S(1)} %add.102.block_ref, s32[1]{0:T(128)} %bitcast.swap_ref, bf16[10,8,16,512]{3,2,1,0:T(8,128)(2,1)S(1)} %bitcast.46, bf16[10,8,16,512]{3,2,1,0:T(8,128)(2,1)S(1)} %collective-permute-done.10.theirs_ref, ...), custom_call_target="tpu_custom_call" | custom-call | flops 5368709120 | bytes 5242880 | tf_op jit(solution)/shard_map/pallas_call | solution.py:196
  62.5 7.1 %shard_map.65 = bf16[8,4,256,128]{3,2,1,0:T(8,128)(2,1)S(1)} custom-call(s32[4]{0:T(128)S(1)} %copy-done, s32[6]{0:T(128)S(1)} %iota.16.index_ref, s32[6]{0:T(128)S(1)} %add.94.block_ref, s32[1]{0:T(128)} %bitcast.swap_ref, bf16[6,8,16,512]{3,2,1,0:T(8,128)(2,1)S(1)} %bitcast.44, ...), custom_call_target="tpu_custom_call", output_to_operand_aliasing={{}: (8, {})} | custom-call | flops 3221225472 | bytes 3145728 | tf_op jit(solution)/shard_map/pallas_call | solution.py:196
  69.6 34.7 %all_to_all.4 = bf16[4,8,256,128]{3,2,0,1:T(8,128)(2,1)S(1)} all-to-all(bf16[4,8,256,128]{3,2,0,1:T(8,128)(2,1)S(1)} %bitcast.42), channel_id=1, replica_groups=mesh['dm'=32,'beam'=8] {'beam'}, dimensions={1} | all-to-all | bytes 4194304 | tf_op jit(solution)/shard_map/all_to_all | solution.py:290
  104.5 2.1 %reshape.75 = bf16[4,1,262144]{2,0,1:T(4,128)(2,1)} reshape(bf16[4,8,256,128]{3,2,1,0:T(8,128)(2,1)S(1)} %copy.10) | data formatting | bytes 4194304 | tf_op jit(solution)/shard_map/reshape | solution.py:291
  (36 shorter events, 1.5 us)
Async XLA Ops:
  2.3 4.5 %collective-permute-start = (bf16[8,16,512]{2,1,0:T(8,128)(2,1)S(1)}, bf16[8,16,512]{2,1,0:T(8,128)(2,1)S(1)}, u32[]{:S(2)}, u32[]{:S(2)}) collective-permute-start(bf16[8,16,512]{2,1,0:T(8,128)(2,1)S(1)} %bitcast.47), channel_id=1, source_target_pairs={{0,128},{8,136},{16,144},{24,152},{32,160},{40,168},{48,176},{56,1... | collective-permute-start | bytes 393224 | tf_op jit(solution)/shard_map/ppermute | solution.py:239
  6.8 11.6 %collective-permute-start.1 = (bf16[2,8,16,512]{3,2,1,0:T(8,128)(2,1)S(1)}, bf16[2,8,16,512]{3,2,1,0:T(8,128)(2,1)S(1)}, u32[]{:S(2)}, u32[]{:S(2)}) collective-permute-start(bf16[2,8,16,512]{3,2,1,0:T(8,128)(2,1)S(1)} %pad_maximum_fusion.1), channel_id=1, source_target_pairs={{0,16},{8,24},{16,32},{24,40},{32,48},{40,56},{48,64},{56,72},{64,... | collective-permute-start | bytes 786440 | tf_op jit(solution)/shard_map/ppermute | solution.py:243
  9.3 9.1 %collective-permute-start.2 = (bf16[2,8,16,512]{3,2,1,0:T(8,128)(2,1)S(1)}, bf16[2,8,16,512]{3,2,1,0:T(8,128)(2,1)S(1)}, u32[]{:S(2)}, u32[]{:S(2)}) collective-permute-start(bf16[2,8,16,512]{3,2,1,0:T(8,128)(2,1)S(1)} %pad_maximum_fusion.1), channel_id=1, source_target_pairs={{0,112},{8,120},{16,0},{24,8},{32,16},{40,24},{48,32},{56,40},{64,... | collective-permute-start | bytes 786440 | tf_op jit(solution)/shard_map/ppermute | solution.py:244
  13.3 4.4 %copy-start.4 = (s32[5]{0:T(128)S(1)}, s32[5]{0:T(128)}, u32[]{:S(2)}) copy-start(s32[5]{0:T(128)} %constant.78.clone) | copy-start | bytes 64
  18.4 5.9 %collective-permute-start.3 = (bf16[2,8,16,512]{3,2,1,0:T(8,128)(2,1)S(1)}, bf16[2,8,16,512]{3,2,1,0:T(8,128)(2,1)}, u32[]{:S(2)}, u32[]{:S(2)}) collective-permute-start(bf16[2,8,16,512]{3,2,1,0:T(8,128)(2,1)S(1)} %collective-permute-done.2), channel_id=1, source_target_pairs={{0,112},{8,120},{16,0},{24,8},{32,16},{40,24},{48,32},{56,40},{64,... | collective-permute-start | bytes 786440 | tf_op jit(solution)/shard_map/ppermute | solution.py:244
  20.9 7.5 %collective-permute-start.5 = (bf16[2,8,16,512]{3,2,1,0:T(8,128)(2,1)S(1)}, bf16[2,8,16,512]{3,2,1,0:T(8,128)(2,1)S(1)}, u32[]{:S(2)}, u32[]{:S(2)}) collective-permute-start(bf16[2,8,16,512]{3,2,1,0:T(8,128)(2,1)S(1)} %collective-permute-done.1), channel_id=1, source_target_pairs={{0,16},{8,24},{16,32},{24,40},{32,48},{40,56},{48,64},{56,72},{64,... | collective-permute-start | bytes 786440 | tf_op jit(solution)/shard_map/ppermute | solution.py:243
  24.2 8.1 %collective-permute-start.4 = (bf16[2,8,16,512]{3,2,1,0:T(8,128)(2,1)}, bf16[2,8,16,512]{3,2,1,0:T(8,128)(2,1)S(1)}, u32[]{:S(2)}, u32[]{:S(2)}) collective-permute-start(bf16[2,8,16,512]{3,2,1,0:T(8,128)(2,1)} %collective-permute-done.3), channel_id=1, source_target_pairs={{0,112},{8,120},{16,0},{24,8},{32,16},{40,24},{48,32},{56,40},{64,... | collective-permute-start | bytes 786440 | tf_op jit(solution)/shard_map/ppermute | solution.py:244
  28.5 22.4 %collective-permute-start.10 = (bf16[10,8,16,512]{3,2,1,0:T(8,128)(2,1)S(1)}, bf16[10,8,16,512]{3,2,1,0:T(8,128)(2,1)S(1)}, u32[]{:S(2)}, u32[]{:S(2)}) collective-permute-start(bf16[10,8,16,512]{3,2,1,0:T(8,128)(2,1)S(1)} %bitcast.45), channel_id=1, source_target_pairs={{0,8},{8,0},{16,24},{24,16},{32,40},{40,32},{48,56},{56,48},{64,72... | collective-permute-start | bytes 3932168 | tf_op jit(solution)/shard_map/ppermute | solution.py:255
  32.4 9.0 %collective-permute-start.6 = (bf16[2,8,16,512]{3,2,1,0:T(8,128)(2,1)S(1)}, bf16[2,8,16,512]{3,2,1,0:T(8,128)(2,1)S(1)}, u32[]{:S(2)}, u32[]{:S(2)}) collective-permute-start(bf16[2,8,16,512]{3,2,1,0:T(8,128)(2,1)S(1)} %collective-permute-done.5), channel_id=1, source_target_pairs={{0,16},{8,24},{16,32},{24,40},{32,48},{40,56},{48,64},{56,72},{64,... | collective-permute-start | bytes 786440 | tf_op jit(solution)/shard_map/ppermute | solution.py:243
  32.4 18.5 %copy-start = (s32[4]{0:T(128)S(1)}, s32[4]{0:T(128)}, u32[]{:S(2)}) copy-start(s32[4]{0:T(128)} %chirp_ref.3) | copy-start | bytes 52
  32.4 15.0 %copy-start.2 = (bf16[2,8,16,512]{3,2,1,0:T(8,128)(2,1)}, bf16[2,8,16,512]{3,2,1,0:T(8,128)(2,1)S(1)}, u32[]{:S(2)}) copy-start(bf16[2,8,16,512]{3,2,1,0:T(8,128)(2,1)S(1)} %collective-permute-done.4) | copy-start | bytes 786436
  33.1 8.6 %collective-permute-start.8 = (bf16[8,16,512]{2,1,0:T(8,128)(2,1)}, bf16[8,16,512]{2,1,0:T(8,128)(2,1)}, u32[]{:S(2)}, u32[]{:S(2)}) collective-permute-start(bf16[8,16,512]{2,1,0:T(8,128)(2,1)} %slice_bitcast_fusion), channel_id=1, source_target_pairs={{0,112},{8,120},{16,0},{24,8},{32,16},{40,24},{48,32},{56,40},{64,... | collective-permute-start | bytes 393224 | tf_op jit(solution)/shard_map/ppermute | solution.py:250
  41.4 6.1 %copy-start.3 = (bf16[2,8,16,512]{3,2,1,0:T(8,128)(2,1)}, bf16[2,8,16,512]{3,2,1,0:T(8,128)(2,1)S(1)}, u32[]{:S(2)}) copy-start(bf16[2,8,16,512]{3,2,1,0:T(8,128)(2,1)S(1)} %collective-permute-done.6) | copy-start | bytes 786436
  41.4 5.1 %collective-permute-start.7 = (bf16[8,16,512]{2,1,0:T(8,128)(2,1)S(1)}, bf16[8,16,512]{2,1,0:T(8,128)(2,1)S(1)}, u32[]{:S(2)}, u32[]{:S(2)}) collective-permute-start(bf16[8,16,512]{2,1,0:T(8,128)(2,1)S(1)} %slice_bitcast_fusion.1), channel_id=1, source_target_pairs={{0,16},{8,24},{16,32},{24,40},{32,48},{40,56},{48,64},{56,72},{64,... | collective-permute-start | bytes 393224 | tf_op jit(solution)/shard_map/ppermute | solution.py:250
  48.5 13.9 %collective-permute-start.9 = (bf16[6,8,16,512]{3,2,1,0:T(8,128)(2,1)S(1)}, bf16[6,8,16,512]{3,2,1,0:T(8,128)(2,1)}, u32[]{:S(2)}, u32[]{:S(2)}) collective-permute-start(bf16[6,8,16,512]{3,2,1,0:T(8,128)(2,1)S(1)} %bitcast.43), channel_id=1, source_target_pairs={{0,8},{8,0},{16,24},{24,16},{32,40},{40,32},{48,56},{56,48},{64,72... | collective-permute-start | bytes 2359304 | tf_op jit(solution)/shard_map/ppermute | solution.py:259
  50.9 1.0 copy-start.1
